TPU v7x, 32 devices: a whole 2x2x4 slice. The times are simulated.
32 devices in a mesh: layer: 8 (over z, x), feat: 4 (over y, core).
Axes of the slice: x: 2, y: 2, z: 4, core: 2. Of those that a mesh axis runs over, the one named last changes fastest.
Arguments:
- resid: bfloat16 [8, 128, 2304], P('layer', None, 'feat'), may hold values from -6 to 6
- encoder: bfloat16 [8, 2304, 4096], P('layer', None, 'feat'), may hold values from -0.125 to 0.125
- encoder_bias: float32 [8, 4096], P('layer', 'feat'), may hold values from -3 to 3
- decoder: bfloat16 [8, 4, 4096, 2304], P('layer', None, 'feat'), may hold values from -0.5 to 0.5
- decoder_bias: float32 [4, 2304], P(None, 'feat'), may hold values from -3 to 3
- topk_index: int32 [4, 256, 64], replicated, may hold values from 0 to 8191, all different within a row
- target: bfloat16 [4, 256, 2304], P(None, 'layer', 'feat'), may hold values from -6 to 6
Outputs:
- recon_error: bfloat16 [4, 256, 2304], P(None, 'layer', 'feat')
- grad_resid: bfloat16 [8, 128, 2304], P('layer', None, 'feat')
Inputs may be any that keep to these rules, and one draw needn't show every extreme that they name: `topk_index`: each row names 64 distinct features of its layer, and every feature is named by some row of some layer.
All inputs are finite; a program needn't handle non-finite values.
Results may differ from a plain program's by a relative error of at most 0.0058.
Values may be sent and summed in bfloat16 or wider, within the bound.
No kernel may reach another device: no remote copies, remote signals or barrier semaphores. Data moves between devices by JAX's collectives and lax.ppermute only.
A program may use at most 128 MiB of HBM per device.

v0:
```python
import jax
import jax.numpy as jnp
from jax import lax
from jax.sharding import PartitionSpec as P

FEAT = 8192


def swapped(value, axis, stride):
    mask = 2**stride
    pairs = [(source, source ^ mask) for source in range(lax.axis_size(axis))]
    return lax.ppermute(value, axis, pairs)


def local(resid, encoder, encoder_bias, decoder, decoder_bias, topk_index, target):
    slot_index = lax.axis_index("layer")
    layer_id = slot_index // 2
    half_bit = slot_index % 2
    feat_pos = lax.axis_index("feat")
    layer_count = decoder.shape[1]
    feat_dev = encoder.shape[2]
    half_rows = resid.shape[1]
    columns = lax.all_gather(resid[0], "feat", axis=1, tiled=True)
    partner = swapped(columns, "layer", 0)
    first_half = jnp.where(half_bit == 0, columns, partner)
    second_half = jnp.where(half_bit == 0, partner, columns)
    tokens_all = jnp.concatenate([first_half, second_half], axis=0)
    pre = jnp.dot(tokens_all, encoder[0], preferred_element_type=jnp.float32) + encoder_bias[0]
    first_feat = half_bit * (FEAT // 2) + feat_pos * feat_dev
    feat_ids = first_feat + lax.iota(jnp.int32, feat_dev)
    layer_index = lax.dynamic_index_in_dim(topk_index, layer_id, 0, keepdims=False)
    selected = jnp.any(layer_index[:, :, None] == feat_ids[None, None, :], axis=1).astype(
        jnp.float32
    )
    acts = (selected * pre).astype(jnp.bfloat16)
    live_layers = lax.iota(jnp.int32, layer_count) >= layer_id
    partial_value = jnp.einsum("tf,lfd->ltd", acts, decoder[0], preferred_element_type=jnp.float32)
    partial_value = jnp.where(live_layers[:, None, None], partial_value, 0.0)
    summed_cols = lax.psum_scatter(partial_value, "feat", scatter_dimension=2, tiled=True)
    recon = lax.psum_scatter(summed_cols, "layer", scatter_dimension=1, tiled=True)
    recon = recon + decoder_bias[:, None, :]
    error = (recon - target.astype(jnp.float32)).astype(jnp.bfloat16)
    error_cols = lax.all_gather(error, "feat", axis=2, tiled=True)
    piece = lax.all_gather(error_cols, "layer", axis=1, tiled=True)
    kept = jnp.where(live_layers[:, None, None], piece, jnp.zeros_like(piece))
    grad_act = jnp.einsum("ltd,lfd->tf", kept, decoder[0], preferred_element_type=jnp.float32)
    grad_pre = (selected * grad_act).astype(jnp.bfloat16)
    grad_part = lax.dot_general(
        grad_pre, encoder[0], (((1,), (1,)), ((), ())), preferred_element_type=jnp.float32
    )
    own_start = half_bit * half_rows
    other_start = (1 - half_bit) * half_rows
    own_rows = lax.dynamic_slice_in_dim(grad_part, own_start, half_rows, 0)
    other_rows = lax.dynamic_slice_in_dim(grad_part, other_start, half_rows, 0)
    received = swapped(other_rows, "layer", 0)
    grad_sum = lax.psum_scatter(own_rows + received, "feat", scatter_dimension=1, tiled=True)
    return (error, grad_sum.astype(jnp.bfloat16)[None])


def solution(mesh):
    in_specs = (
        P("layer", None, "feat"),
        P("layer", None, "feat"),
        P("layer", "feat"),
        P("layer", None, "feat", None),
        P(None, "feat"),
        P(),
        P(None, "layer", "feat"),
    )
    out_specs = (P(None, "layer", "feat"), P("layer", None, "feat"))
    return jax.shard_map(local, mesh=mesh, in_specs=in_specs, out_specs=out_specs, check_vma=False)
```

profile of v0, /device:TPU:0, one launch (start us, length us, event | category | flops | bytes accessed | tf_op | source)
XLA Modules:
  0.0 538.2 jit_solution(14545535078416521851)
XLA Ops:
  7.2 0.0 copy-start
  7.2 0.0 all-reduce.5.cloned.1.call-start
  7.2 9.4 %all-gather = bf16[1,128,2304]{1,2,0:T(8,128)(2,1)S(1)} all-gather(bf16[1,128,576]{1,2,0:T(8,128)(2,1)} %param.7), channel_id=2, replica_groups=mesh['layer'=8,'feat'=4] {'feat'}, dimensions={2}, use_global_device_ids=true | all-gather | bytes 737280 | tf_op jit(solution)/shard_map/all_gather | solution.py:23
  16.6 1.5 collective-permute-start
  18.1 0.0 copy-done
  18.1 0.1 copy.28
  18.2 9.4 %compare_reduce_fusion = pred[256,1024]{1,0:T(8,128)(4,1)S(1)} fusion(s32[1024]{0:T(1024)S(1)} %iota_add_fusion, s32[256,64]{1,0:T(8,128)S(1)} %copy.28), kind=kLoop, calls=%fused_computation | loop fusion | flops 33292288 | bytes 331776 | tf_op jit(solution)/shard_map/reduce_or | solution.py:32
  27.7 0.0 copy-start.3
  27.7 4.5 collective-permute-done
  32.2 0.1 broadcast_select_fusion.2
  32.3 0.0 copy-done.3
  32.3 3.8 fusion.35
  36.1 13.9 %select_bitcast_fusion = f32[4,256,2304]{2,1,0:T(8,128)} fusion(bf16[256,1024,1]{1,0,2:T(8,128)(2,1)S(1)} %fusion.35, bf16[1,4,1024,2304]{3,2,1,0:T(8,128)(2,1)} %param.10, pred[4]{0:T(512)(128)(4,1)S(1)} %iota_compare_fusion), kind=kOutput, calls=%fused_computation.5 | convolution fusion | flops 4834197504 | bytes 28835844 | tf_op jit(solution)/shard_map/tf,lfd->ltd/dot_general | solution.py:37
  50.0 11.9 %copy.29 = f32[4,256,2304]{1,0,2:T(4,128)} copy(f32[4,256,2304]{2,1,0:T(8,128)} %select_bitcast_fusion) | data formatting | bytes 18874368 | tf_op jit(solution)/shard_map/jit(_where)/select_n | solution.py:38
  61.9 0.0 copy-start.8
  61.9 0.0 all-reduce.5.cloned.1.call-update
  61.9 0.0 all-reduce.7.cloned.1.call-start
  62.0 0.6 copy-done.8
  62.5 0.6 dynamic-slice
  63.8 168.9 %all-reduce.5.cloned.1.call-done = f32[4,256,2304]{1,0,2:T(4,128)} async-done(((f32[4,256,2304]{1,0,2:T(4,128)}), f32[4,256,2304]{1,0,2:T(4,128)}) %all-reduce.5.cloned.1.call-update) | async-done | bytes 9437200
  232.7 2.1 constant_dynamic-slice_fusion
  234.7 0.0 copy-start.7
  234.8 0.0 copy-start.5
  234.8 0.0 copy-start.6
  234.8 3.0 copy.30
  237.8 0.0 all-reduce.7.cloned.1.call-update
  237.8 0.0 all-gather.3.cloned.1.call-start
  237.8 0.0 copy-done.7
  237.8 0.6 dynamic-slice.2
  239.1 115.0 %all-reduce.7.cloned.1.call-done = f32[4,256,576]{2,0,1:T(4,128)} async-done(((f32[4,256,576]{2,0,1:T(4,128)}), f32[4,256,576]{2,0,1:T(4,128)}) %all-reduce.7.cloned.1.call-update) | async-done | bytes 2359312
  354.1 0.0 copy-done.5
  354.1 0.0 copy-done.6
  354.1 1.1 fusion.47
  355.2 0.4 copy.32
  355.5 17.1 %all_gather.10 = bf16[4,32,2304]{1,0,2:T(4,128)(2,1)S(1)} all-gather(bf16[4,32,576]{1,0,2:T(4,128)(2,1)S(1)} %copy.32), channel_id=1, replica_groups=mesh['layer'=8,'feat'=4] {'feat'}, dimensions={2}, use_global_device_ids=true | all-gather | bytes 737280 | tf_op jit(solution)/shard_map/all_gather | solution.py:43
  372.7 3.5 copy.33
  376.2 0.0 all-gather.3.cloned.1.call-update
  376.2 0.2 reduce-scatter.4.cloned.1.call-start
  376.5 0.0 copy-start.4
  376.5 77.7 %all-gather.3.cloned.1.call-done = bf16[4,256,2304]{2,0,1:T(4,128)(2,1)} async-done(((bf16[4,32,2304]{2,0,1:T(4,128)(2,1)}), bf16[4,256,2304]{2,0,1:T(4,128)(2,1)}) %all-gather.3.cloned.1.call-update) | async-done | bytes 4718608 | tf_op jit(solution)/shard_map/all_gather | solution.py:44
  454.2 6.5 %broadcast_select_fusion = bf16[4,256,2304]{2,0,1:T(4,128)(2,1)} fusion(bf16[4,256,2304]{2,0,1:T(4,128)(2,1)} %all-gather.3.cloned.1.call-done, pred[4]{0:T(512)(128)(4,1)S(1)} %iota_compare_fusion), kind=kLoop, calls=%fused_computation.11 | loop fusion | flops 2359296 | bytes 9437188 | tf_op jit(solution)/shard_map/jit(_where)/select_n | solution.py:45
  460.7 0.0 copy-done.4
  460.7 0.0 copy-start.1
  460.7 12.5 %fusion.6 = f32[256,2304]{1,0:T(8,128)S(1)} fusion(bf16[1,2304,1024]{2,1,0:T(8,128)(2,1)} %param.8, pred[256,1024]{1,0:T(8,128)(4,1)S(1)} %copy-done.4, bf16[1,4,1024,2304]{3,2,1,0:T(8,128)(2,1)} %param.10, bf16[4,256,2304]{2,0,1:T(4,128)(2,1)} %broadcast_select_fusion), kind=kOutput, calls=%fused_computation.6 | convolution fusion | flops 6040322048 | bytes 30932992 | tf_op jit(solution)/shard_map/dot_general | solution.py:48
  473.2 0.0 copy-start.2
  473.2 1.2 constant_dynamic-slice_fusion.1
  474.4 0.6 collective-permute-start.1
  475.0 0.1 copy-done.2
  475.1 26.0 %collective-permute-done.1 = f32[128,2304]{1,0:T(8,128)} collective-permute-done((f32[128,2304]{1,0:T(8,128)}, f32[128,2304]{1,0:T(8,128)}, u32[]{:S(2)}, u32[]{:S(2)}) %collective-permute-start.1) | collective-permute-done | bytes 1179680 | tf_op jit(solution)/shard_map/ppermute | solution.py:12
  501.1 1.7 dynamic-slice_add_fusion
  502.8 1.4 copy.37
  504.2 0.0 reduce-scatter.4.cloned.1.call-update
  504.2 0.7 copy.35
  504.9 24.8 %reduce-scatter.4.cloned.1.call-done = f32[576,128]{1,0:T(8,128)} async-done(((f32[2304,128]{1,0:T(8,128)}), f32[576,128]{1,0:T(8,128)}) %reduce-scatter.4.cloned.1.call-update) | async-done | bytes 294928
  529.7 1.1 copy.38
  530.8 0.8 copy.36
  531.6 0.0 copy-done.1
  (3 shorter events, 0.0 us)
Async XLA Ops:
  7.2 10.9 %copy-start = (s32[4,256,64]{1,2,0:T(8,128)S(1)}, s32[4,256,64]{1,2,0:T(8,128)}, u32[]{:S(2)}) copy-start(s32[4,256,64]{1,2,0:T(8,128)} %param.12) | copy-start | bytes 786436
  7.2 225.5 %all-reduce.5.cloned.1.call-start = ((), (), s32[]{:S(2)}) async-start(), calls=%async_computation.3 | async-start | bytes 18874368
  16.6 15.6 %collective-permute-start = (bf16[128,2304]{0,1:T(8,128)(2,1)S(1)}, bf16[128,2304]{0,1:T(8,128)(2,1)S(1)}, u32[]{:S(2)}, u32[]{:S(2)}) collective-permute-start(bf16[128,2304]{0,1:T(8,128)(2,1)S(1)} %bitcast.55), channel_id=1, source_target_pairs={{0,4},{4,0},{8,12},{12,8},{16,20},{20,16},{24,28},{28,24},{1,5},{5... | collective-permute-start | bytes 1769480 | tf_op jit(solution)/shard_map/ppermute | solution.py:12
  27.7 4.6 copy-start.3
  61.9 0.7 copy-start.8
  61.9 292.2 %all-reduce.7.cloned.1.call-start = ((), (), s32[]{:S(2)}) async-start(), calls=%async_computation.4 | async-start | bytes 5242880
  234.7 3.1 copy-start.7
  234.8 119.3 %copy-start.5 = (bf16[4,32,576]{2,1,0:T(8,128)(2,1)S(1)}, bf16[4,32,576]{2,1,0:T(8,128)(2,1)}, u32[]{:S(2)}) copy-start(bf16[4,32,576]{2,1,0:T(8,128)(2,1)} %param.13) | copy-start | bytes 442372
  234.8 119.3 %copy-start.6 = (f32[4,576]{1,0:T(4,128)S(1)}, f32[4,576]{1,0:T(4,128)}, u32[]{:S(2)}) copy-start(f32[4,576]{1,0:T(4,128)} %param.11) | copy-start | bytes 27652
  237.8 216.4 %all-gather.3.cloned.1.call-start = ((), (), s32[]{:S(2)}) async-start(), calls=%async_computation.1 | async-start | bytes 5308416 | tf_op jit(solution)/shard_map/all_gather | solution.py:44
  376.2 153.5 %reduce-scatter.4.cloned.1.call-start = ((), (), s32[]{:S(2)}) async-start(), calls=%async_computation.2 | async-start | bytes 1474560
  376.5 84.2 %copy-start.4 = (pred[256,1024]{1,0:T(8,128)(4,1)S(1)}, pred[256,1024]{1,0:T(8,128)(4,1)}, u32[]{:S(2)}) copy-start(pred[256,1024]{1,0:T(8,128)(4,1)} %copy-done.3) | copy-start | bytes 786436
  460.7 71.0 %copy-start.1 = (s32[4,256,64]{1,2,0:T(8,128)S(1)}, s32[4,256,64]{1,2,0:T(8,128)}, u32[]{:S(2)}) copy-start(s32[4,256,64]{1,2,0:T(8,128)} %param.12) | copy-start | bytes 786436
  473.2 1.8 copy-start.2
  474.4 26.6 %collective-permute-start.1 = (f32[128,2304]{1,0:T(8,128)}, f32[128,2304]{1,0:T(8,128)}, u32[]{:S(2)}, u32[]{:S(2)}) collective-permute-start(f32[128,2304]{1,0:T(8,128)} %constant_dynamic-slice_fusion.1), channel_id=1, source_target_pairs={{0,4},{4,0},{8,12},{12,8},{16,20},{20,16},{24,28},{28,24},{1,5},{5... | collective-permute-start | bytes 3538952 | tf_op jit(solution)/shard_map/ppermute | solution.py:12
Sparse Core Ops, SparseCore 0:
  62.0 170.6 all-reduce.4
  237.9 116.1 all-reduce.6
  376.3 77.8 all-gather.2
  504.4 25.3 reduce-scatter.3
where the time goes:
time: 539 us; the launch traced here: 538 us
  waiting for transfers between devices  417 us (77%)
  matrix products  30.2 us (6%)
  local copies, waits for them, and re-layouts  28 us (5%)
  blocking collectives  26.5 us (5%)
  other arithmetic  18.8 us (3%)
  between operations  15.2 us (3%)
    unnamed x7, waiting for transfers between devices  309 us
    all_gather x1, waiting for transfers between devices, local(): piece = lax.all_gather(error_cols, 'layer', axis=1, tiled=True)  77.7 us
    ppermute x2, waiting for transfers between devices, swapped(): return lax.ppermute(value, axis, pairs)  30.5 us
    all_gather x1, blocking collectives, local(): error_cols = lax.all_gather(error, 'feat', axis=2, tiled=True)  17.1 us
    dot_general x1, matrix products, local(): jnp.einsum('tf,lfd->ltd', acts, decoder[0], preferred_element_type=jnp.fl...  13.9 us
    dot_general x1, matrix products, local(): lax.dot_general(grad_pre, encoder[0], (((1,), (1,)), ((), ())), preferred...  12.5 us
    select_n x1, local copies, waits for them, and re-layouts, local(): partial_value = jnp.where(live_layers[:, None, None], partial_value, 0.0)  11.9 us
  transfers between devices with their start and end apart: 6, of which 6 were waited for; matrix products, arithmetic and copies ran while one was open for 2% of the time, Pallas kernels for 0%

commit v1 on v0

v1 whole, which is shorter than its diff:
```python
import jax
import jax.numpy as jnp
from jax import lax
from jax.sharding import Mesh
from jax.sharding import PartitionSpec as P

PLANE = ("lx", "feat")
EVERY = ("lz", "lx", "feat")


def local(resid, encoder, encoder_bias, decoder, decoder_bias, topk_index, target):
    planes = lax.axis_size("lz")
    feat_parts = lax.axis_size("feat")
    layer_id = lax.axis_index("lz")
    half_bit = lax.axis_index("lx")
    feat_pos = lax.axis_index("feat")
    layer_count = decoder.shape[1]
    feat_dev = encoder.shape[2]
    half_rows = resid.shape[1]
    cols = resid.shape[2]
    tokens = 2 * half_rows
    width = cols * feat_parts
    slots = 2 * planes
    slot_rows = tokens // slots
    feat_total = 2 * feat_parts * feat_dev

    gathered = lax.all_gather(resid[0], PLANE, axis=0, tiled=False)
    tokens_all = (
        gathered.reshape(2, feat_parts, half_rows, cols).transpose(0, 2, 1, 3).reshape(tokens, width)
    )
    pre = jnp.dot(tokens_all, encoder[0], preferred_element_type=jnp.float32) + encoder_bias[0]
    first_feat = half_bit * (feat_total // 2) + feat_pos * feat_dev
    feat_ids = first_feat + lax.iota(jnp.int32, feat_dev)
    layer_index = lax.dynamic_index_in_dim(topk_index, layer_id, 0, keepdims=False)
    selected = jnp.any(layer_index[:, :, None] == feat_ids[None, None, :], axis=1).astype(
        jnp.float32
    )
    acts = (selected * pre).astype(jnp.bfloat16)
    live_layers = lax.iota(jnp.int32, layer_count) >= layer_id
    partial_value = jnp.einsum("tf,lfd->ltd", acts, decoder[0], preferred_element_type=jnp.float32)
    partial_value = jnp.where(live_layers[:, None, None], partial_value, 0.0)
    blocks = (
        partial_value.reshape(layer_count, slots, slot_rows, feat_parts, cols)
        .transpose(1, 3, 0, 2, 4)
        .reshape(slots * feat_parts, layer_count, slot_rows, cols)
    )
    recon = lax.psum_scatter(blocks, EVERY, scatter_dimension=0, tiled=True)[0]
    recon = recon + decoder_bias[:, None, :]
    error = (recon - target.astype(jnp.float32)).astype(jnp.bfloat16)
    pieces = lax.all_gather(error, EVERY, axis=0, tiled=False)
    piece = (
        pieces.reshape(slots, feat_parts, layer_count, slot_rows, cols)
        .transpose(2, 0, 3, 1, 4)
        .reshape(layer_count, tokens, width)
    )
    kept = jnp.where(live_layers[:, None, None], piece, jnp.zeros_like(piece))
    grad_act = jnp.einsum("ltd,lfd->tf", kept, decoder[0], preferred_element_type=jnp.float32)
    grad_pre = (selected * grad_act).astype(jnp.bfloat16)
    grad_part = lax.dot_general(
        grad_pre, encoder[0], (((1,), (1,)), ((), ())), preferred_element_type=jnp.float32
    )
    grad_blocks = (
        grad_part.reshape(2, half_rows, feat_parts, cols)
        .transpose(0, 2, 1, 3)
        .reshape(2 * feat_parts, half_rows, cols)
    )
    grad_sum = lax.psum_scatter(grad_blocks, PLANE, scatter_dimension=0, tiled=True)
    return (error, grad_sum.astype(jnp.bfloat16))


def solution(mesh):
    layer_n = mesh.shape["layer"]
    feat_n = mesh.shape["feat"]
    split = Mesh(mesh.devices.reshape(layer_n // 2, 2, feat_n), ("lz", "lx", "feat"))
    slot = ("lz", "lx")
    in_specs = (
        P(slot, None, "feat"),
        P(slot, None, "feat"),
        P(slot, "feat"),
        P(slot, None, "feat", None),
        P(None, "feat"),
        P(),
        P(None, slot, "feat"),
    )
    out_specs = (P(None, slot, "feat"), P(slot, None, "feat"))
    return jax.shard_map(local, mesh=split, in_specs=in_specs, out_specs=out_specs, check_vma=False)
```

time: 539 us -> 383 us (0.71)
  waiting for transfers between devices: 417 us -> 278 us
  blocking collectives: 26.5 us -> 0 us
  local copies, waits for them, and re-layouts: 28 us -> 43.9 us
  other arithmetic: 18.8 us -> 12.8 us
    unnamed x7 -> x4, waiting for transfers between devices: 309 us -> 0.73 us
    reduce_scatter x0 -> x2, waiting for transfers between devices: none -> 195 us  [the longest x1 154 us: local(): recon = lax.psum_scatter(blocks, EVERY, scatter_dimension=0, tiled=True)[0]]
    ppermute x2 -> x0, waiting for transfers between devices: 30.5 us -> none  [swapped(): return lax.ppermute(value, axis, pairs)]
    all_gather x2 -> x0, blocking collectives: 26.5 us -> none  [the longest x1 17.1 us: local(): error_cols = lax.all_gather(error, 'feat', axis=2, tiled=True)]
    reshape x0 -> x3, local copies, waits for them, and re-layouts: none -> 25.4 us  [the longest x1 13.2 us: local(): partial_value.reshape(layer_count, slots, slot_rows, feat_parts, cols)]
    transpose x0 -> x2, local copies, waits for them, and re-layouts: none -> 18.2 us  [the longest x1 9.33 us: local(): blocks = partial_value.reshape(layer_count, slots, slot_rows, feat_parts,...]
    select_n x1 -> x0, local copies, waits for them, and re-layouts: 11.9 us -> none  [local(): partial_value = jnp.where(live_layers[:, None, None], partial_value, 0.0)]
    dot_general x0 -> x1, matrix products: none -> 10.4 us  [local(): jnp.einsum('ltd,lfd->tf', kept, decoder[0], preferred_element_type=jnp.fl...]
  transfers between devices with their start and end apart: 6 -> 4, of which waited for: 6 -> 4; matrix products, arithmetic and copies ran while one was open for 2% -> 2% of each run, Pallas kernels for 0% -> 0%
where the time goes in v1:
time: 383 us; the launch traced here: 382 us
  waiting for transfers between devices  278 us (73%)
  local copies, waits for them, and re-layouts  43.9 us (11%)
  matrix products  33.2 us (9%)
  between operations  13.8 us (4%)
  other arithmetic  12.8 us (3%)
    reduce_scatter x1, waiting for transfers between devices, local(): recon = lax.psum_scatter(blocks, EVERY, scatter_dimension=0, tiled=True)[0]  154 us
    all_gather x1, waiting for transfers between devices, local(): pieces = lax.all_gather(error, EVERY, axis=0, tiled=False)  63.3 us
    reduce_scatter x1, waiting for transfers between devices, local(): lax.psum_scatter(grad_blocks, PLANE, scatter_dimension=0, tiled=True)  41 us
    all_gather x1, waiting for transfers between devices, local(): gathered = lax.all_gather(resid[0], PLANE, axis=0, tiled=False)  18.9 us
    dot_general x1, matrix products, local(): jnp.einsum('tf,lfd->ltd', acts, decoder[0], preferred_element_type=jnp.fl...  13.9 us
    reshape x1, local copies, waits for them, and re-layouts, local(): partial_value.reshape(layer_count, slots, slot_rows, feat_parts, cols)  13.2 us
    dot_general x1, matrix products, local(): jnp.einsum('ltd,lfd->tf', kept, decoder[0], preferred_element_type=jnp.fl...  10.4 us
    reshape x1, local copies, waits for them, and re-layouts, local(): piece = pieces.reshape(slots, feat_parts, layer_count, slot_rows, cols).t...  9.81 us
  transfers between devices with their start and end apart: 4, of which 4 were waited for; matrix products, arithmetic and copies ran while one was open for 2% of the time, Pallas kernels for 0%

profile of v1, /device:TPU:0, one launch (start us, length us, event | category | flops | bytes accessed | tf_op | source)
XLA Modules:
  0.0 382.1 jit_solution(18166649742462273024)
XLA Ops:
  7.2 0.0 copy-start
  7.2 0.0 all-gather.4.cloned.1.call-start
  7.2 0.7 all-gather.4.cloned.1.call-update
  7.9 0.0 reduce-scatter.3.cloned.1.call-start
  8.0 0.2 copy-done
  8.1 0.1 copy.19
  8.3 9.4 %compare_reduce_fusion = pred[256,1024]{1,0:T(8,128)(4,1)S(1)} fusion(s32[1024]{0:T(1024)S(1)} %iota_add_fusion, s32[256,64]{1,0:T(8,128)S(1)} %copy.19), kind=kLoop, calls=%fused_computation | loop fusion | flops 33292288 | bytes 331776 | tf_op jit(solution)/shard_map/reduce_or | solution.py:35
  17.7 18.9 %all-gather.4.cloned.1.call-done = bf16[8,128,576]{1,2,0:T(8,128)(2,1)} async-done(((bf16[1,128,576]{1,2,0:T(8,128)(2,1)}), bf16[8,128,576]{1,2,0:T(8,128)(2,1)}) %all-gather.4.cloned.1.call-update) | async-done | bytes 1179664 | tf_op jit(solution)/shard_map/all_gather | solution.py:27
  36.5 2.5 copy.20
  39.0 3.8 fusion.35
  42.8 13.9 %select_bitcast_fusion = f32[4,256,2304]{2,1,0:T(8,128)} fusion(bf16[256,1024,1]{1,0,2:T(8,128)(2,1)S(1)} %fusion.35, bf16[1,4,1024,2304]{3,2,1,0:T(8,128)(2,1)} %param.10, pred[4]{0:T(512)(128)(4,1)S(1)} %iota_compare_fusion), kind=kOutput, calls=%fused_computation.5 | convolution fusion | flops 4834197504 | bytes 28835844 | tf_op jit(solution)/shard_map/tf,lfd->ltd/dot_general | solution.py:40
  56.7 13.2 %reshape.42 = f32[4,8,32,4,576]{4,3,2,1,0:T(4,128)} reshape(f32[4,256,2304]{2,1,0:T(8,128)} %select_bitcast_fusion) | data formatting | bytes 18874368 | tf_op jit(solution)/shard_map/reshape | solution.py:43
  69.9 9.3 %copy.21 = f32[8,4,4,32,576]{4,3,2,1,0:T(8,128)} copy(f32[8,4,4,32,576]{4,1,3,0,2:T(4,128)} %bitcast.72) | data formatting | bytes 18874368 | tf_op jit(solution)/shard_map/transpose | solution.py:44
  79.2 0.0 copy-start.2
  79.2 0.0 copy-start.3
  79.2 0.0 reduce-scatter.3.cloned.1.call-update
  79.2 0.0 all-gather.6.cloned.1.call-start
  79.3 154.1 %reduce-scatter.3.cloned.1.call-done = f32[1,4,32,576]{3,2,1,0:T(8,128)} async-done(((f32[32,4,32,576]{3,2,1,0:T(8,128)}), f32[1,4,32,576]{3,2,1,0:T(8,128)}) %reduce-scatter.3.cloned.1.call-update) | async-done | bytes 294928 | tf_op jit(solution)/shard_map/reduce_scatter | solution.py:47
  233.4 0.0 copy-done.2
  233.4 0.0 copy-done.3
  233.4 1.7 fusion.41
  235.1 0.0 all-gather.6.cloned.1.call-update
  235.1 0.2 reduce-scatter.5.cloned.1.call-start
  235.3 63.3 %all-gather.6.cloned.1.call-done = bf16[128,32,576]{2,1,0:T(8,128)(2,1)} async-done(((bf16[4,32,576]{2,1,0:T(8,128)(2,1)}), bf16[128,32,576]{2,1,0:T(8,128)(2,1)}) %all-gather.6.cloned.1.call-update) | async-done | bytes 4718608 | tf_op jit(solution)/shard_map/all_gather | solution.py:50
  298.6 8.8 %copy.22 = bf16[4,8,32,4,576]{4,3,2,1,0:T(4,128)(2,1)} copy(bf16[4,8,32,4,576]{4,2,0,3,1:T(8,128)(2,1)} %bitcast.73) | data formatting | bytes 9437184 | tf_op jit(solution)/shard_map/transpose | solution.py:53
  307.5 9.8 %reshape.45 = bf16[4,256,2304]{2,1,0:T(8,128)(2,1)} reshape(bf16[4,8,32,4,576]{4,3,2,1,0:T(4,128)(2,1)} %copy.22) | data formatting | bytes 9437184 | tf_op jit(solution)/shard_map/reshape | solution.py:54
  317.3 10.4 %fusion.30 = bf16[256,1024]{1,0:T(8,128)(2,1)S(1)} fusion(pred[256,1024]{1,0:T(8,128)(4,1)S(1)} %compare_reduce_fusion, bf16[1,4,1024,2304]{3,2,1,0:T(8,128)(2,1)} %param.10, bf16[4,256,2304]{2,1,0:T(8,128)(2,1)} %reshape.45, pred[4]{0:T(512)(128)(4,1)S(1)} %iota_compare_fusion), kind=kOutput, calls=%fused_computation.16 | convolution fusion | flops 4834721792 | bytes 24379396 | tf_op jit(solution)/shard_map/ltd,lfd->tf/dot_general | solution.py:57
  327.6 0.0 copy-start.1
  327.6 5.2 %fusion.43 = f32[2,128,4,576]{1,3,2,0:T(8,128)} fusion(bf16[2,128,1024,1]{2,1,3,0:T(8,128)(2,1)S(1)} %bitcast.79, bf16[4,576,1024,1]{2,1,0,3:T(8,128)(2,1)} %bitcast.77), kind=kOutput, calls=%fused_computation.27 | convolution fusion | flops 1207959552 | bytes 7602176 | tf_op jit(solution)/shard_map/dot_general | solution.py:59
  332.9 0.0 reduce-scatter.5.cloned.1.call-update
  332.9 41.0 %reduce-scatter.5.cloned.1.call-done = f32[1,128,576]{1,2,0:T(8,128)} async-done(((f32[8,128,576]{1,2,0:T(8,128)}), f32[1,128,576]{1,2,0:T(8,128)}) %reduce-scatter.5.cloned.1.call-update) | async-done | bytes 294928 | tf_op jit(solution)/shard_map/reduce_scatter | solution.py:67
  373.9 1.6 convert_element_type.20
  375.5 0.0 copy-done.1
  (3 shorter events, 0.0 us)
Async XLA Ops:
  7.2 1.0 copy-start
  7.2 29.4 %all-gather.4.cloned.1.call-start = ((), (), s32[]{:S(2)}) async-start(), calls=%async_computation.2 | async-start | bytes 1327104 | tf_op jit(solution)/shard_map/all_gather | solution.py:27
  7.9 225.5 %reduce-scatter.3.cloned.1.call-start = ((), (), s32[]{:S(2)}) async-start(), calls=%async_computation.3 | async-start | bytes 10813440 | tf_op jit(solution)/shard_map/reduce_scatter | solution.py:47
  79.2 154.2 %copy-start.2 = (bf16[4,32,576]{2,1,0:T(8,128)(2,1)S(1)}, bf16[4,32,576]{2,1,0:T(8,128)(2,1)}, u32[]{:S(2)}) copy-start(bf16[4,32,576]{2,1,0:T(8,128)(2,1)} %param.13) | copy-start | bytes 442372
  79.2 154.2 %copy-start.3 = (f32[4,576]{1,0:T(4,128)S(1)}, f32[4,576]{1,0:T(4,128)}, u32[]{:S(2)}) copy-start(f32[4,576]{1,0:T(4,128)} %param.11) | copy-start | bytes 27652
  79.2 219.4 %all-gather.6.cloned.1.call-start = ((), (), s32[]{:S(2)}) async-start(), calls=%async_computation.5 | async-start | bytes 5406720 | tf_op jit(solution)/shard_map/all_gather | solution.py:50
  235.1 138.8 %reduce-scatter.5.cloned.1.call-start = ((), (), s32[]{:S(2)}) async-start(), calls=%async_computation.4 | async-start | bytes 2654208 | tf_op jit(solution)/shard_map/reduce_scatter | solution.py:67
  327.6 47.9 %copy-start.1 = (s32[4,256,64]{1,2,0:T(8,128)S(1)}, s32[4,256,64]{1,2,0:T(8,128)}, u32[]{:S(2)}) copy-start(s32[4,256,64]{1,2,0:T(8,128)} %param.12) | copy-start | bytes 786436
Sparse Core Ops, SparseCore 0:
  9.9 26.6 all-gather.3
  79.3 153.9 reduce-scatter.2
  236.8 61.7 all-gather.5
  333.0 40.8 reduce-scatter.4

commit v2 on v1

--- a/solution.py
+++ b/solution.py
@@ -44,8 +44,8 @@
         .transpose(1, 3, 0, 2, 4)
         .reshape(slots * feat_parts, layer_count, slot_rows, cols)
     )
-    recon = lax.psum_scatter(blocks, EVERY, scatter_dimension=0, tiled=True)[0]
-    recon = recon + decoder_bias[:, None, :]
+    recon = lax.psum_scatter(blocks.astype(jnp.bfloat16), EVERY, scatter_dimension=0, tiled=True)[0]
+    recon = recon.astype(jnp.float32) + decoder_bias[:, None, :]
     error = (recon - target.astype(jnp.float32)).astype(jnp.bfloat16)
     pieces = lax.all_gather(error, EVERY, axis=0, tiled=False)
     piece = (
@@ -64,7 +64,7 @@
         .transpose(0, 2, 1, 3)
         .reshape(2 * feat_parts, half_rows, cols)
     )
-    grad_sum = lax.psum_scatter(grad_blocks, PLANE, scatter_dimension=0, tiled=True)
+    grad_sum = lax.psum_scatter(grad_blocks.astype(jnp.bfloat16), PLANE, scatter_dimension=0, tiled=True)
     return (error, grad_sum.astype(jnp.bfloat16))
 
 

time: 383 us -> 359 us (0.937)
  waiting for transfers between devices: 278 us -> 262 us
  local copies, waits for them, and re-layouts: 43.9 us -> 38.8 us
    convert_element_type x0 -> x2, local copies, waits for them, and re-layouts: none -> 17.4 us  [local(): blocks.astype(jnp.bfloat16)]
    reduce_scatter x2, waiting for transfers between devices: 195 us -> 180 us  [the longest x1 145 us: local(): lax.psum_scatter(blocks.astype(jnp.bfloat16), EVERY, scatter_dimension=0,...]
    reshape x1 -> x0, local copies, waits for them, and re-layouts: 13.2 us -> none  [local(): partial_value.reshape(layer_count, slots, slot_rows, feat_parts, cols)]
    transpose x1 -> x0, local copies, waits for them, and re-layouts: 9.33 us -> none  [local(): blocks = partial_value.reshape(layer_count, slots, slot_rows, feat_parts,...]
  transfers between devices with their start and end apart: 4 -> 4, of which waited for: 4 -> 4; matrix products, arithmetic and copies ran while one was open for 2% -> 3% of each run, Pallas kernels for 0% -> 0%
where the time goes in v2:
time: 359 us; the launch traced here: 358 us
  waiting for transfers between devices  262 us (73%)
  local copies, waits for them, and re-layouts  38.8 us (11%)
  matrix products  32.1 us (9%)
  between operations  13.8 us (4%)
  other arithmetic  11.1 us (3%)
    reduce_scatter x1, waiting for transfers between devices, local(): lax.psum_scatter(blocks.astype(jnp.bfloat16), EVERY, scatter_dimension=0,...  145 us
    all_gather x1, waiting for transfers between devices, local(): pieces = lax.all_gather(error, EVERY, axis=0, tiled=False)  62.7 us
    reduce_scatter x1, waiting for transfers between devices, local(): lax.psum_scatter(grad_blocks.astype(jnp.bfloat16), PLANE, scatter_dimensi...  35.3 us
    all_gather x1, waiting for transfers between devices, local(): gathered = lax.all_gather(resid[0], PLANE, axis=0, tiled=False)  18.9 us
    convert_element_type x2, local copies, waits for them, and re-layouts, local(): blocks.astype(jnp.bfloat16)  17.4 us
    dot_general x1, matrix products, local(): jnp.einsum('tf,lfd->ltd', acts, decoder[0], preferred_element_type=jnp.fl...  13.1 us
    dot_general x1, matrix products, local(): jnp.einsum('ltd,lfd->tf', kept, decoder[0], preferred_element_type=jnp.fl...  10.4 us
    reshape x1, local copies, waits for them, and re-layouts, local(): piece = pieces.reshape(slots, feat_parts, layer_count, slot_rows, cols).t...  9.81 us
  transfers between devices with their start and end apart: 4, of which 4 were waited for; matrix products, arithmetic and copies ran while one was open for 3% of the time, Pallas kernels for 0%

profile of v2, /device:TPU:0, one launch (start us, length us, event | category | flops | bytes accessed | tf_op | source)
XLA Modules:
  0.0 358.4 jit_solution(6869624745375756821)
XLA Ops:
  7.2 0.0 copy-start
  7.2 0.0 all-gather.4.cloned.1.call-start
  7.2 0.7 all-gather.4.cloned.1.call-update
  7.9 0.0 reduce-scatter.3.cloned.1.call-start
  8.0 0.2 copy-done
  8.1 0.1 copy.19
  8.3 9.4 %compare_reduce_fusion = pred[256,1024]{1,0:T(8,128)(4,1)S(1)} fusion(s32[1024]{0:T(1024)S(1)} %iota_add_fusion, s32[256,64]{1,0:T(8,128)S(1)} %copy.19), kind=kLoop, calls=%fused_computation | loop fusion | flops 33292288 | bytes 331776 | tf_op jit(solution)/shard_map/reduce_or | solution.py:35
  17.7 18.9 %all-gather.4.cloned.1.call-done = bf16[8,128,576]{1,2,0:T(8,128)(2,1)} async-done(((bf16[1,128,576]{1,2,0:T(8,128)(2,1)}), bf16[8,128,576]{1,2,0:T(8,128)(2,1)}) %all-gather.4.cloned.1.call-update) | async-done | bytes 1179664 | tf_op jit(solution)/shard_map/all_gather | solution.py:27
  36.5 2.5 copy.20
  39.0 3.8 %fusion.38 = bf16[256,1024,1]{1,0,2:T(8,128)(2,1)S(1)} fusion(pred[256,1024]{1,0:T(8,128)(4,1)S(1)} %compare_reduce_fusion, bf16[1,2304,1024]{2,1,0:T(8,128)(2,1)} %param.8, bf16[288,8,2,128]{3,2,1,0:T(2,128)(2,1)S(1)} %bitcast.75, f32[1024]{0:T(1024)} %bitcast.77), kind=kOutput, calls=%fused_computation.19 | convolution fusion | flops 1208745984 | bytes 6688768 | tf_op jit(solution)/shard_map/dot_general | solution.py:31
  42.8 13.1 %fusion.6 = bf16[4,256,2304]{2,1,0:T(8,128)(2,1)} fusion(bf16[256,1024,1]{1,0,2:T(8,128)(2,1)S(1)} %fusion.38, bf16[1,4,1024,2304]{3,2,1,0:T(8,128)(2,1)} %param.10, pred[4]{0:T(512)(128)(4,1)S(1)} %iota_compare_fusion), kind=kOutput, calls=%fused_computation.6 | convolution fusion | flops 4836556800 | bytes 24117252 | tf_op jit(solution)/shard_map/tf,lfd->ltd/dot_general | solution.py:40
  55.9 11.5 %convert_element_type.46 = bf16[4,8,32,4,576]{4,3,2,1,0:T(4,128)(2,1)} reshape(bf16[4,256,2304]{2,1,0:T(8,128)(2,1)} %fusion.6) | data formatting | bytes 9437184 | tf_op jit(solution)/shard_map/convert_element_type | solution.py:47
  67.4 5.9 %copy.21 = bf16[8,4,4,32,576]{4,3,2,1,0:T(8,128)(2,1)} copy(bf16[8,4,4,32,576]{4,1,3,0,2:T(4,128)(2,1)} %bitcast.71) | data formatting | bytes 9437184 | tf_op jit(solution)/shard_map/convert_element_type | solution.py:47
  73.4 0.0 copy-start.1
  73.4 0.0 copy-start.2
  73.4 0.0 reduce-scatter.3.cloned.1.call-update
  73.4 0.0 all-gather.6.cloned.1.call-start
  73.4 144.7 %reduce-scatter.3.cloned.1.call-done = bf16[1,4,32,576]{3,2,1,0:T(8,128)(2,1)} async-done(((bf16[32,4,32,576]{3,2,1,0:T(8,128)(2,1)}), bf16[1,4,32,576]{3,2,1,0:T(8,128)(2,1)}) %reduce-scatter.3.cloned.1.call-update) | async-done | bytes 147472 | tf_op jit(solution)/shard_map/reduce_scatter | solution.py:47
  218.1 0.0 copy-done.1
  218.1 0.0 copy-done.2
  218.1 1.6 fusion.44
  219.7 0.0 all-gather.6.cloned.1.call-update
  219.8 0.2 reduce-scatter.5.cloned.1.call-start
  220.0 62.7 %all-gather.6.cloned.1.call-done = bf16[128,32,576]{2,1,0:T(8,128)(2,1)} async-done(((bf16[4,32,576]{2,1,0:T(8,128)(2,1)}), bf16[128,32,576]{2,1,0:T(8,128)(2,1)}) %all-gather.6.cloned.1.call-update) | async-done | bytes 4718608 | tf_op jit(solution)/shard_map/all_gather | solution.py:50
  282.7 8.8 %copy.22 = bf16[4,8,32,4,576]{4,3,2,1,0:T(4,128)(2,1)} copy(bf16[4,8,32,4,576]{4,2,0,3,1:T(8,128)(2,1)} %bitcast.72) | data formatting | bytes 9437184 | tf_op jit(solution)/shard_map/transpose | solution.py:53
  291.5 9.8 %reshape.42 = bf16[4,256,2304]{2,1,0:T(8,128)(2,1)} reshape(bf16[4,8,32,4,576]{4,3,2,1,0:T(4,128)(2,1)} %copy.22) | data formatting | bytes 9437184 | tf_op jit(solution)/shard_map/reshape | solution.py:54
  301.4 10.4 %fusion.33 = bf16[256,1024]{1,0:T(8,128)(2,1)S(1)} fusion(pred[256,1024]{1,0:T(8,128)(4,1)S(1)} %compare_reduce_fusion, bf16[1,4,1024,2304]{3,2,1,0:T(8,128)(2,1)} %param.10, bf16[4,256,2304]{2,1,0:T(8,128)(2,1)} %reshape.42, pred[4]{0:T(512)(128)(4,1)S(1)} %iota_compare_fusion), kind=kOutput, calls=%fused_computation.18 | convolution fusion | flops 4834721792 | bytes 24379396 | tf_op jit(solution)/shard_map/ltd,lfd->tf/dot_general | solution.py:57
  311.7 4.8 %convolution_convert_fusion = bf16[2,128,4,576]{1,3,2,0:T(8,128)(2,1)} fusion(bf16[2,128,1024,1]{2,1,3,0:T(8,128)(2,1)S(1)} %bitcast.78, bf16[4,576,1024,1]{2,1,0,3:T(8,128)(2,1)} %bitcast.76), kind=kOutput, calls=%fused_computation.12 | convolution fusion | flops 1208549376 | bytes 6422528 | tf_op jit(solution)/shard_map/dot_general | solution.py:59
  316.5 0.0 reduce-scatter.5.cloned.1.call-update
  316.5 35.3 %reduce-scatter.5.cloned.1.call-done = bf16[1,128,576]{1,2,0:T(8,128)(2,1)} async-done(((bf16[8,128,576]{1,2,0:T(8,128)(2,1)}), bf16[1,128,576]{1,2,0:T(8,128)(2,1)}) %reduce-scatter.5.cloned.1.call-update) | async-done | bytes 147472 | tf_op jit(solution)/shard_map/reduce_scatter | solution.py:67
  (3 shorter events, 0.0 us)
Async XLA Ops:
  7.2 1.0 copy-start
  7.2 29.4 %all-gather.4.cloned.1.call-start = ((), (), s32[]{:S(2)}) async-start(), calls=%async_computation.2 | async-start | bytes 1327104 | tf_op jit(solution)/shard_map/all_gather | solution.py:27
  7.9 210.2 %reduce-scatter.3.cloned.1.call-start = ((), (), s32[]{:S(2)}) async-start(), calls=%async_computation.3 | async-start | bytes 5406720 | tf_op jit(solution)/shard_map/reduce_scatter | solution.py:47
  73.4 144.7 %copy-start.1 = (bf16[4,32,576]{2,1,0:T(8,128)(2,1)S(1)}, bf16[4,32,576]{2,1,0:T(8,128)(2,1)}, u32[]{:S(2)}) copy-start(bf16[4,32,576]{2,1,0:T(8,128)(2,1)} %param.13) | copy-start | bytes 442372
  73.4 144.7 %copy-start.2 = (f32[4,576]{1,0:T(4,128)S(1)}, f32[4,576]{1,0:T(4,128)}, u32[]{:S(2)}) copy-start(f32[4,576]{1,0:T(4,128)} %param.11) | copy-start | bytes 27652
  73.4 209.3 %all-gather.6.cloned.1.call-start = ((), (), s32[]{:S(2)}) async-start(), calls=%async_computation.5 | async-start | bytes 5406720 | tf_op jit(solution)/shard_map/all_gather | solution.py:50
  219.8 132.1 %reduce-scatter.5.cloned.1.call-start = ((), (), s32[]{:S(2)}) async-start(), calls=%async_computation.4 | async-start | bytes 1327104 | tf_op jit(solution)/shard_map/reduce_scatter | solution.py:67
Sparse Core Ops, SparseCore 0:
  9.9 26.6 all-gather.3
  73.5 144.5 reduce-scatter.2
  221.5 61.1 all-gather.5
  316.7 35.1 reduce-scatter.4

commit v3 on v1

--- a/solution.py
+++ b/solution.py
@@ -6,6 +6,99 @@
 
 PLANE = ("lx", "feat")
 EVERY = ("lz", "lx", "feat")
+
+
+def bit_labels(axes):
+    labels = []
+    for axis in axes:
+        size = lax.axis_size(axis)
+        bits = size.bit_length() - 1
+        assert 1 << bits == size
+        labels += [(axis, b) for b in reversed(range(bits))]
+    return labels
+
+
+def plan(axes):
+    labels = bit_labels(axes)
+    prefix = [("feat", 0)]
+    suffix = [("lz", lax.axis_size("lz").bit_length() - 2)] if "lz" in axes else []
+    rotation = [label for label in labels if label not in prefix + suffix]
+    orders = [rotation[p:] + rotation[:p] for p in range(len(rotation))]
+    return labels, prefix, orders, suffix
+
+
+def row_split(rows, parts):
+    base = (rows // (8 * parts)) * 8
+    sizes = [base] * parts
+    extra = rows - base * parts
+    i = 0
+    while extra >= 8:
+        sizes[i % parts] += 8
+        extra -= 8
+        i += 1
+    sizes[0] += extra
+    return sizes
+
+
+def partner(axis, bit):
+    return [(i, i ^ (1 << bit)) for i in range(lax.axis_size(axis))]
+
+
+def halve(x, labels, label):
+    axis, bit = label
+    dim = labels.index(label)
+    own = (lax.axis_index(axis) >> bit) & 1
+    keep = lax.dynamic_index_in_dim(x, own, dim, keepdims=False)
+    send = lax.dynamic_index_in_dim(x, 1 - own, dim, keepdims=False)
+    recv = lax.ppermute(send, axis, partner(axis, bit))
+    return keep + recv, [l for l in labels if l != label]
+
+
+def double(x, labels, label):
+    axis, bit = label
+    own = (lax.axis_index(axis) >> bit) & 1
+    recv = lax.ppermute(x, axis, partner(axis, bit))
+    low = jnp.where(own == 0, x, recv)
+    high = jnp.where(own == 0, recv, x)
+    return jnp.stack([low, high]), [label] + labels
+
+
+def reduce_scatter(blocks, axes):
+    labels, prefix, orders, suffix = plan(axes)
+    n, rows, cols = blocks.shape
+    x = blocks.reshape([2] * len(labels) + [rows, cols])
+    cur = list(labels)
+    for label in prefix:
+        x, cur = halve(x, cur, label)
+    sizes = row_split(rows, len(orders))
+    starts = [sum(sizes[:i]) for i in range(len(sizes))]
+    parts = [lax.slice_in_dim(x, s, s + z, axis=x.ndim - 2) for s, z in zip(starts, sizes)]
+    curs = [list(cur) for _ in parts]
+    for step in range(len(orders[0]) + len(suffix)):
+        for p in range(len(parts)):
+            label = (orders[p] + suffix)[step]
+            parts[p], curs[p] = halve(parts[p], curs[p], label)
+    return jnp.concatenate(parts, axis=0)
+
+
+def all_gather(block, axes):
+    labels, prefix, orders, suffix = plan(axes)
+    rows, cols = block.shape
+    sizes = row_split(rows, len(orders))
+    starts = [sum(sizes[:i]) for i in range(len(sizes))]
+    parts = [lax.slice_in_dim(block, s, s + z, axis=0) for s, z in zip(starts, sizes)]
+    curs = [[] for _ in parts]
+    for step in range(len(orders[0]) + len(suffix)):
+        for p in range(len(parts)):
+            label = list(reversed(orders[p] + suffix))[step]
+            parts[p], curs[p] = double(parts[p], curs[p], label)
+    cur = curs[0]
+    parts = [jnp.transpose(x, [c.index(l) for l in cur] + [x.ndim - 2, x.ndim - 1]) for x, c in zip(parts, curs)]
+    x = jnp.concatenate(parts, axis=-2)
+    for label in reversed(prefix):
+        x, cur = double(x, cur, label)
+    x = jnp.transpose(x, [cur.index(l) for l in labels] + [x.ndim - 2, x.ndim - 1])
+    return x.reshape(-1, rows, cols)
 
 
 def local(resid, encoder, encoder_bias, decoder, decoder_bias, topk_index, target):
@@ -24,7 +117,7 @@
     slot_rows = tokens // slots
     feat_total = 2 * feat_parts * feat_dev
 
-    gathered = lax.all_gather(resid[0], PLANE, axis=0, tiled=False)
+    gathered = all_gather(resid[0], PLANE)
     tokens_all = (
         gathered.reshape(2, feat_parts, half_rows, cols).transpose(0, 2, 1, 3).reshape(tokens, width)
     )
@@ -42,12 +135,12 @@
     blocks = (
         partial_value.reshape(layer_count, slots, slot_rows, feat_parts, cols)
         .transpose(1, 3, 0, 2, 4)
-        .reshape(slots * feat_parts, layer_count, slot_rows, cols)
+        .reshape(slots * feat_parts, layer_count * slot_rows, cols)
     )
-    recon = lax.psum_scatter(blocks, EVERY, scatter_dimension=0, tiled=True)[0]
+    recon = reduce_scatter(blocks, EVERY).reshape(layer_count, slot_rows, cols)
     recon = recon + decoder_bias[:, None, :]
     error = (recon - target.astype(jnp.float32)).astype(jnp.bfloat16)
-    pieces = lax.all_gather(error, EVERY, axis=0, tiled=False)
+    pieces = all_gather(error.reshape(layer_count * slot_rows, cols), EVERY)
     piece = (
         pieces.reshape(slots, feat_parts, layer_count, slot_rows, cols)
         .transpose(2, 0, 3, 1, 4)
@@ -64,8 +157,8 @@
         .transpose(0, 2, 1, 3)
         .reshape(2 * feat_parts, half_rows, cols)
     )
-    grad_sum = lax.psum_scatter(grad_blocks, PLANE, scatter_dimension=0, tiled=True)
-    return (error, grad_sum.astype(jnp.bfloat16))
+    grad_sum = reduce_scatter(grad_blocks, PLANE)
+    return (error, grad_sum.astype(jnp.bfloat16)[None])
 
 
 def solution(mesh):

time: 383 us -> 274 us (0.72)
  waiting for transfers between devices: 278 us -> 87.5 us
  local copies, waits for them, and re-layouts: 43.9 us -> 93.4 us
  starting transfers between devices: 0.34 us -> 40.7 us
  other arithmetic: 12.8 us -> 26.6 us
  between operations: 13.8 us -> 1.43 us
  matrix products: 33.2 us -> 23.2 us
    reduce_scatter x2 -> x0, waiting for transfers between devices: 195 us -> none  [the longest x1 154 us: local(): recon = lax.psum_scatter(blocks, EVERY, scatter_dimension=0, tiled=True)[0]]
    ppermute x0 -> x36, waiting for transfers between devices: none -> 87.5 us  [the longest x18 53.1 us: halve(): recv = lax.ppermute(send, axis, partner(axis, bit))]
    all_gather x2 -> x0, waiting for transfers between devices: 82.2 us -> none  [the longest x1 63.3 us: local(): pieces = lax.all_gather(error, EVERY, axis=0, tiled=False)]
    dynamic_slice x0 -> x18, local copies, waits for them, and re-layouts: none -> 43.3 us  [the longest x12 28.7 us: halve(): keep = lax.dynamic_index_in_dim(x, own, dim, keepdims=False)]
    ppermute x0 -> x36, starting transfers between devices: none -> 40.7 us  [the longest x18 20.7 us: double(): recv = lax.ppermute(x, axis, partner(axis, bit))]
    add x0 -> x16, other arithmetic: none -> 9.56 us  [halve(): return (keep + recv, [l for l in labels if l != label])]
    transpose x1, local copies, waits for them, and re-layouts: 9.33 us -> 1.22 us  [local(): gathered.reshape(2, feat_parts, half_rows, cols).transpose(0, 2, 1, 3)]
    another operation x0 -> x30, other arithmetic: none -> 6.51 us  [double(): return (jnp.stack([low, high]), [label] + labels)]
  transfers between devices with their start and end apart: 4 -> 36, of which waited for: 4 -> 26; matrix products, arithmetic and copies ran while one was open for 2% -> 16% of each run, Pallas kernels for 0% -> 0%
where the time goes in v3:
time: 274 us; the launch traced here: 273 us
  local copies, waits for them, and re-layouts  93.4 us (34%)
  waiting for transfers between devices  87.5 us (32%)
  starting transfers between devices  40.7 us (15%)
  other arithmetic  26.6 us (10%)
  matrix products  23.2 us (8%)
    ppermute x18, waiting for transfers between devices, halve(): recv = lax.ppermute(send, axis, partner(axis, bit))  53.1 us
    ppermute x18, waiting for transfers between devices, double(): recv = lax.ppermute(x, axis, partner(axis, bit))  34.4 us
    dynamic_slice x12, local copies, waits for them, and re-layouts, halve(): keep = lax.dynamic_index_in_dim(x, own, dim, keepdims=False)  28.7 us
    ppermute x18, starting transfers between devices, double(): recv = lax.ppermute(x, axis, partner(axis, bit))  20.7 us
    ppermute x18, starting transfers between devices, halve(): recv = lax.ppermute(send, axis, partner(axis, bit))  20 us
    reshape x2, local copies, waits for them, and re-layouts, local(): partial_value.reshape(layer_count, slots, slot_rows, feat_parts, cols)  18.7 us
    dynamic_slice x6, local copies, waits for them, and re-layouts, halve(): send = lax.dynamic_index_in_dim(x, 1 - own, dim, keepdims=False)  14.6 us
    dot_general x1, matrix products, local(): jnp.einsum('ltd,lfd->tf', kept, decoder[0], preferred_element_type=jnp.fl...  10.5 us
  transfers between devices with their start and end apart: 36, of which 26 were waited for; matrix products, arithmetic and copies ran while one was open for 16% of the time, Pallas kernels for 0%

profile of v3, /device:TPU:0, one launch (start us, length us, event | category | flops | bytes accessed | tf_op | source)
XLA Modules:
  0.0 272.8 jit_solution(962101543520388745)
XLA Ops:
  1.8 3.1 %collective-permute-start = (bf16[64,576]{0,1:T(8,128)(2,1)S(1)}, bf16[64,576]{0,1:T(8,128)(2,1)S(1)}, u32[]{:S(2)}, u32[]{:S(2)}) collective-permute-start(bf16[64,576]{0,1:T(8,128)(2,1)S(1)} %get-tuple-element.63), channel_id=1, source_target_pairs={{0,2},{1,3},{2,0},{3,1},{4,6},{5,7},{6,4},{7,5},{8,10},{9,11},{10,... | collective-permute-start | bytes 221192 | tf_op jit(solution)/shard_map/ppermute | solution.py:60
  4.8 1.5 collective-permute-start.2
  6.4 2.3 collective-permute-done
  8.7 1.5 collective-permute-done.2
  11.9 1.7 collective-permute-start.1
  13.6 5.4 %collective-permute-done.3 = bf16[2,64,576]{1,2,0:T(8,128)(2,1)S(1)} collective-permute-done((bf16[2,64,576]{1,2,0:T(8,128)(2,1)S(1)}, bf16[2,64,576]{1,2,0:T(8,128)(2,1)S(1)}, u32[]{:S(2)}, u32[]{:S(2)}) %collective-permute-start.3) | collective-permute-done | bytes 147488 | tf_op jit(solution)/shard_map/ppermute | solution.py:60
  20.1 9.4 %compare_reduce_fusion = pred[256,1024]{1,0:T(8,128)(4,1)S(1)} fusion(s32[1024]{0:T(1024)S(1)} %iota_add_fusion, s32[256,64]{1,0:T(8,128)S(1)} %copy.110), kind=kLoop, calls=%fused_computation | loop fusion | flops 33292288 | bytes 331776 | tf_op jit(solution)/shard_map/reduce_or | solution.py:128
  31.4 3.8 %fusion.35 = bf16[256,1024,1]{1,0,2:T(8,128)(2,1)S(1)} fusion(pred[256,1024]{1,0:T(8,128)(4,1)S(1)} %compare_reduce_fusion, bf16[1,2304,1024]{2,1,0:T(8,128)(2,1)} %param.8, bf16[288,8,2,128]{3,2,1,0:T(2,128)(2,1)S(1)} %bitcast.267, f32[1024]{0:T(1024)S(1)} %bitcast.274), kind=kOutput, calls=%fused_computation.22 | convolution fusion | flops 1208745984 | bytes 6688768 | tf_op jit(solution)/shard_map/dot_general | solution.py:124
  35.2 7.4 %select_bitcast_fusion = f32[4,256,2304]{2,1,0:T(8,128)} fusion(bf16[256,1024,1]{1,0,2:T(8,128)(2,1)S(1)} %fusion.35, bf16[1,4,1024,2304]{3,2,1,0:T(8,128)(2,1)S(1)} %copy-done.12, pred[4]{0:T(512)(128)(4,1)S(1)} %iota_compare_fusion), kind=kOutput, calls=%fused_computation.5 | convolution fusion | flops 4834197504 | bytes 28835844 | tf_op jit(solution)/shard_map/tf,lfd->ltd/dot_general | solution.py:133
  42.6 13.2 %reshape.68 = f32[4,8,32,4,576]{4,3,2,1,0:T(4,128)} reshape(f32[4,256,2304]{2,1,0:T(8,128)} %select_bitcast_fusion) | data formatting | bytes 18874368 | tf_op jit(solution)/shard_map/reshape | solution.py:136
  55.8 5.5 %copy.114 = f32[4,8,32,4,576]{4,2,0,3,1:T(8,128)S(1)} copy(f32[4,8,32,4,576]{4,3,2,1,0:T(4,128)} %reshape.68) | data formatting | bytes 18874368 | tf_op jit(solution)/shard_map/reshape | solution.py:136
  61.3 4.7 %constant_dynamic-slice_fusion.11 = (f32[2,2,2,2,1,128,576]{6,5,4,3,2,1,0:T(8,128)}, f32[2,2,2,2,1,128,576]{6,5,4,3,2,1,0:T(8,128)}) fusion(f32[2,2,2,2,2,128,576]{6,5,4,3,2,1,0:T(8,128)S(1)} %bitcast.255, s32[]{:T(128)S(6)} %select_n.306, s32[]{:T(128)S(6)} %select_n.307), kind=kLoop, calls=%fused_computation.126 | loop fusion | bytes 18874376 | tf_op jit(solution)/shard_map/jit(dynamic_index_in_dim)/dynamic_slice | solution.py:51
  66.0 5.8 %copy.116 = f32[2,2,2,2,1,128,576]{5,6,4,3,2,1,0:T(8,128)} copy(f32[2,2,2,2,1,128,576]{6,5,4,3,2,1,0:T(8,128)} %get-tuple-element.9) | data formatting | bytes 9437184 | tf_op jit(solution)/shard_map/jit(dynamic_index_in_dim)/dynamic_slice | solution.py:52
  72.3 5.8 %copy.115 = f32[2,2,2,2,1,128,576]{5,6,4,3,2,1,0:T(8,128)} copy(f32[2,2,2,2,1,128,576]{6,5,4,3,2,1,0:T(8,128)} %get-tuple-element.8) | data formatting | bytes 9437184 | tf_op jit(solution)/shard_map/jit(dynamic_index_in_dim)/dynamic_slice | solution.py:51
  78.1 2.1 collective-permute-done.5
  80.2 4.3 %bitcast_add_fusion = f32[2,2,2,2,128,576]{4,5,3,2,1,0:T(8,128)S(1)} fusion(f32[2,2,2,2,128,576]{4,5,3,2,1,0:T(8,128)} %collective-permute-done.5, f32[2,2,2,2,1,128,576]{5,6,4,3,2,1,0:T(8,128)} %copy.115), kind=kLoop, calls=%fused_computation.7 | loop fusion | flops 1179648 | bytes 14155776 | tf_op jit(solution)/shard_map/add | solution.py:54
  84.5 4.7 %fusion.45 = (f32[2,2,2,2,40,576]{4,5,3,2,1,0:T(8,128)S(1)}, f32[2,2,2,2,40,576]{4,5,3,2,1,0:T(8,128)}) fusion(f32[2,2,2,2,128,576]{4,5,3,2,1,0:T(8,128)S(1)} %bitcast_add_fusion), kind=kLoop, calls=%fused_computation.130 | loop fusion | bytes 5898240 | tf_op jit(solution)/shard_map/slice | solution.py:75
  89.2 1.8 constant_dynamic-slice_fusion.7
  90.9 2.8 %copy.120 = f32[2,2,1,2,40,576]{5,4,3,1,0,2:T(8,128)} copy(f32[2,2,1,2,40,576]{4,5,3,2,1,0:T(8,128)} %get-tuple-element.15) | data formatting | bytes 1474560 | tf_op jit(solution)/shard_map/jit(dynamic_index_in_dim)/dynamic_slice | solution.py:52
  93.7 1.4 collective-permute-start.10
  95.1 5.0 %constant_dynamic-slice_fusion.5 = (f32[2,2,2,1,40,576]{4,5,3,2,1,0:T(8,128)}, f32[2,2,2,1,40,576]{4,5,3,2,1,0:T(8,128)}) fusion(f32[2,2,2,2,40,576]{4,5,3,2,1,0:T(8,128)} %get-tuple-element.17, s32[]{:T(128)S(6)} %select_n.312, s32[]{:T(128)S(6)} %select_n.313), kind=kLoop, calls=%fused_computation.120 | loop fusion | bytes 2949128 | tf_op jit(solution)/shard_map/jit(dynamic_index_in_dim)/dynamic_slice | solution.py:51
  100.2 2.8 %copy.122 = f32[2,2,2,1,40,576]{5,4,2,1,0,3:T(8,128)} copy(f32[2,2,2,1,40,576]{4,5,3,2,1,0:T(8,128)} %get-tuple-element.19) | data formatting | bytes 1474560 | tf_op jit(solution)/shard_map/jit(dynamic_index_in_dim)/dynamic_slice | solution.py:52
  103.0 1.5 collective-permute-start.14
  104.4 5.0 %constant_dynamic-slice_fusion.9 = (f32[2,1,2,2,48,576]{4,5,3,2,1,0:T(8,128)}, f32[2,1,2,2,48,576]{4,5,3,2,1,0:T(8,128)}) fusion(f32[2,2,2,2,48,576]{4,5,3,2,1,0:T(8,128)} %bitcast.254, s32[]{:T(128)S(6)} %select_n.308, s32[]{:T(128)S(6)} %select_n.309), kind=kLoop, calls=%fused_computation.124 | loop fusion | bytes 3538952 | tf_op jit(solution)/shard_map/jit(dynamic_index_in_dim)/dynamic_slice | solution.py:51
  109.4 2.8 %copy.118 = f32[2,1,2,2,48,576]{5,4,3,2,0,1:T(8,128)} copy(f32[2,1,2,2,48,576]{4,5,3,2,1,0:T(8,128)} %get-tuple-element.13) | data formatting | bytes 1769472 | tf_op jit(solution)/shard_map/jit(dynamic_index_in_dim)/dynamic_slice | solution.py:52
  112.3 1.6 collective-permute-start.6
  113.8 2.8 %copy.117 = f32[2,1,2,2,48,576]{5,4,3,2,0,1:T(8,128)} copy(f32[2,1,2,2,48,576]{4,5,3,2,1,0:T(8,128)} %get-tuple-element.12) | data formatting | bytes 1769472 | tf_op jit(solution)/shard_map/jit(dynamic_index_in_dim)/dynamic_slice | solution.py:51
  117.6 2.0 copy.121
  119.6 1.2 bitcast_add_fusion.4
  121.6 2.3 collective-permute-done.14
  123.8 1.2 bitcast_add_fusion.3
  125.1 2.2 collective-permute-start.15
  127.3 9.9 %collective-permute-done.6 = f32[2,2,2,48,576]{4,3,2,1,0:T(8,128)} collective-permute-done((f32[2,2,2,48,576]{4,3,2,1,0:T(8,128)}, f32[2,2,2,48,576]{4,3,2,1,0:T(8,128)}, u32[]{:S(2)}, u32[]{:S(2)}) %collective-permute-start.6) | collective-permute-done | bytes 884768 | tf_op jit(solution)/shard_map/ppermute | solution.py:53
  137.2 1.3 bitcast_add_fusion.2
  139.2 1.6 collective-permute-start.12
  140.9 5.0 %collective-permute-done.15 = f32[2,2,40,576]{3,2,1,0:T(8,128)S(1)} collective-permute-done((f32[2,2,40,576]{3,2,1,0:T(8,128)S(1)}, f32[2,2,40,576]{3,2,1,0:T(8,128)S(1)}, u32[]{:S(2)}, u32[]{:S(2)}) %collective-permute-start.15) | collective-permute-done | bytes 368672 | tf_op jit(solution)/shard_map/ppermute | solution.py:53
  146.5 2.6 collective-permute-done.12
  149.2 2.7 collective-permute-start.13
  151.8 2.1 collective-permute-done.16
  154.0 2.7 collective-permute-start.17
  157.7 5.4 %collective-permute-done.8 = f32[2,48,576]{2,1,0:T(8,128)S(1)} collective-permute-done((f32[2,48,576]{2,1,0:T(8,128)S(1)}, f32[2,48,576]{2,1,0:T(8,128)S(1)}, u32[]{:S(2)}, u32[]{:S(2)}) %collective-permute-start.8) | collective-permute-done | bytes 221216 | tf_op jit(solution)/shard_map/ppermute | solution.py:53
  163.5 8.3 %collective-permute-done.9 = f32[48,576]{1,0:T(8,128)S(1)} collective-permute-done((f32[48,576]{1,0:T(8,128)S(1)}, f32[48,576]{1,0:T(8,128)S(1)}, u32[]{:S(2)}, u32[]{:S(2)}) %collective-permute-start.9) | collective-permute-done | bytes 110624 | tf_op jit(solution)/shard_map/ppermute | solution.py:53
  172.1 2.9 %collective-permute-start.18 = (bf16[48,576]{1,0:T(8,128)(2,1)S(1)}, bf16[48,576]{1,0:T(8,128)(2,1)S(1)}, u32[]{:S(2)}, u32[]{:S(2)}) collective-permute-start(bf16[48,576]{1,0:T(8,128)(2,1)S(1)} %slice.51), channel_id=1, source_target_pairs={{0,16},{8,24},{16,0},{24,8},{1,17},{9,25},{17,1},{25,9},{2,18},{10... | collective-permute-start | bytes 165896 | tf_op jit(solution)/shard_map/ppermute | solution.py:60
  175.0 2.8 %collective-permute-done.22 = bf16[40,576]{1,0:T(8,128)(2,1)S(1)} collective-permute-done((bf16[40,576]{1,0:T(8,128)(2,1)S(1)}, bf16[40,576]{1,0:T(8,128)(2,1)S(1)}, u32[]{:S(2)}, u32[]{:S(2)}) %collective-permute-start.22) | collective-permute-done | bytes 46112 | tf_op jit(solution)/shard_map/ppermute | solution.py:60
  177.9 2.2 collective-permute-start.26
  180.8 2.3 collective-permute-done.26
  186.1 2.9 %collective-permute-done.27 = bf16[2,40,576]{2,1,0:T(8,128)(2,1)S(1)} collective-permute-done((bf16[2,40,576]{2,1,0:T(8,128)(2,1)S(1)}, bf16[2,40,576]{2,1,0:T(8,128)(2,1)S(1)}, u32[]{:S(2)}, u32[]{:S(2)}) %collective-permute-start.27) | collective-permute-done | bytes 92192 | tf_op jit(solution)/shard_map/ppermute | solution.py:60
  189.1 2.5 collective-permute-start.28
  191.7 1.6 collective-permute-start.25
  193.2 3.5 %collective-permute-done.28 = bf16[2,2,40,576]{3,2,0,1:T(8,128)(2,1)S(1)} collective-permute-done((bf16[2,2,40,576]{3,2,0,1:T(8,128)(2,1)S(1)}, bf16[2,2,40,576]{3,2,0,1:T(8,128)(2,1)S(1)}, u32[]{:S(2)}, u32[]{:S(2)}) %collective-permute-start.28) | collective-permute-done | bytes 184352 | tf_op jit(solution)/shard_map/ppermute | solution.py:60
  196.9 1.4 collective-permute-start.29
  199.9 4.9 %collective-permute-done.29 = bf16[2,2,2,40,576]{4,3,1,0,2:T(8,128)(2,1)S(1)} collective-permute-done((bf16[2,2,2,40,576]{4,3,1,0,2:T(8,128)(2,1)S(1)}, bf16[2,2,2,40,576]{4,3,1,0,2:T(8,128)(2,1)S(1)}, u32[]{:S(2)}, u32[]{:S(2)}) %collective-permute-start.29) | collective-permute-done | bytes 368672 | tf_op jit(solution)/shard_map/ppermute | solution.py:60
  205.1 2.1 collective-permute-done.21
  208.5 2.6 copy.128
  211.1 4.9 %collective-permute-done.30 = bf16[2,2,2,2,128,576]{4,5,3,2,1,0:T(8,128)(2,1)} collective-permute-done((bf16[2,2,2,2,128,576]{4,5,3,2,1,0:T(8,128)(2,1)}, bf16[2,2,2,2,128,576]{4,5,3,2,1,0:T(8,128)(2,1)}, u32[]{:S(2)}, u32[]{:S(2)}) %collective-permute-start.30) | collective-permute-done | bytes 2359328 | tf_op jit(solution)/shard_map/ppermute | solution.py:60
  216.0 3.1 %copy.129 = bf16[2,2,2,2,128,576]{5,4,2,1,0,3:T(8,128)(2,1)S(1)} copy(bf16[2,2,2,2,128,576]{4,5,3,2,1,0:T(8,128)(2,1)} %collective-permute-done.30) | data formatting | bytes 4718592 | tf_op jit(solution)/shard_map/ppermute | solution.py:60
  219.1 2.7 select_bitcast_fusion.2
  222.5 6.4 %copy.132 = bf16[4,8,32,4,576]{4,3,2,1,0:T(4,128)(2,1)} copy(bf16[4,8,32,4,576]{4,2,0,3,1:T(8,128)(2,1)S(1)} %bitcast.256) | data formatting | bytes 9437184 | tf_op jit(solution)/shard_map/transpose | solution.py:146
  228.9 9.9 %reshape.71 = bf16[4,256,2304]{2,1,0:T(8,128)(2,1)} reshape(bf16[4,8,32,4,576]{4,3,2,1,0:T(4,128)(2,1)} %copy.132) | data formatting | bytes 9437184 | tf_op jit(solution)/shard_map/reshape | solution.py:147
  238.8 10.5 %fusion.30 = bf16[256,1024]{1,0:T(8,128)(2,1)S(1)} fusion(pred[256,1024]{1,0:T(8,128)(4,1)S(1)} %copy-done.9, bf16[1,4,1024,2304]{3,2,1,0:T(8,128)(2,1)} %param.10, bf16[4,256,2304]{2,1,0:T(8,128)(2,1)} %reshape.71, pred[4]{0:T(512)(128)(4,1)S(1)} %iota_compare_fusion), kind=kOutput, calls=%fused_computation.21 | convolution fusion | flops 4834721792 | bytes 24379396 | tf_op jit(solution)/shard_map/ltd,lfd->tf/dot_general | solution.py:150
  249.4 1.5 fusion.47
  251.2 2.7 collective-permute-done.31
  256.9 7.8 %collective-permute-done.32 = f32[2,64,576]{2,1,0:T(8,128)} collective-permute-done((f32[2,64,576]{2,1,0:T(8,128)S(1)}, f32[2,64,576]{2,1,0:T(8,128)}, u32[]{:S(2)}, u32[]{:S(2)}) %collective-permute-start.32) | collective-permute-done | bytes 294944 | tf_op jit(solution)/shard_map/ppermute | solution.py:53
  267.2 4.0 %collective-permute-done.33 = f32[64,576]{1,0:T(8,128)S(1)} collective-permute-done((f32[64,576]{1,0:T(8,128)S(1)}, f32[64,576]{1,0:T(8,128)S(1)}, u32[]{:S(2)}, u32[]{:S(2)}) %collective-permute-start.33) | collective-permute-done | bytes 147488 | tf_op jit(solution)/shard_map/ppermute | solution.py:53
  (149 shorter events, 26.4 us)
Async XLA Ops:
  0.6 5.7 %copy-start = (s32[4,256,64]{1,2,0:T(8,128)S(1)}, s32[4,256,64]{1,2,0:T(8,128)}, u32[]{:S(2)}) copy-start(s32[4,256,64]{1,2,0:T(8,128)} %param.12) | copy-start | bytes 786436
  1.8 6.9 %collective-permute-start = (bf16[64,576]{0,1:T(8,128)(2,1)S(1)}, bf16[64,576]{0,1:T(8,128)(2,1)S(1)}, u32[]{:S(2)}, u32[]{:S(2)}) collective-permute-start(bf16[64,576]{0,1:T(8,128)(2,1)S(1)} %get-tuple-element.63), channel_id=1, source_target_pairs={{0,2},{1,3},{2,0},{3,1},{4,6},{5,7},{6,4},{7,5},{8,10},{9,11},{10,... | collective-permute-start | bytes 221192 | tf_op jit(solution)/shard_map/ppermute | solution.py:60
  4.8 5.3 %collective-permute-start.2 = (bf16[64,576]{0,1:T(8,128)(2,1)S(1)}, bf16[64,576]{0,1:T(8,128)(2,1)S(1)}, u32[]{:S(2)}, u32[]{:S(2)}) collective-permute-start(bf16[64,576]{0,1:T(8,128)(2,1)S(1)} %get-tuple-element.64), channel_id=1, source_target_pairs={{0,4},{4,0},{1,5},{5,1},{2,6},{6,2},{3,7},{7,3},{8,12},{12,8},{9,1... | collective-permute-start | bytes 221192 | tf_op jit(solution)/shard_map/ppermute | solution.py:60
  11.3 7.7 %collective-permute-start.3 = (bf16[2,64,576]{1,2,0:T(8,128)(2,1)S(1)}, bf16[2,64,576]{1,2,0:T(8,128)(2,1)S(1)}, u32[]{:S(2)}, u32[]{:S(2)}) collective-permute-start(bf16[2,64,576]{1,2,0:T(8,128)(2,1)S(1)} %pad_maximum_fusion.10), channel_id=1, source_target_pairs={{0,2},{1,3},{2,0},{3,1},{4,6},{5,7},{6,4},{7,5},{8,10},{9,11},{10,... | collective-permute-start | bytes 442376 | tf_op jit(solution)/shard_map/ppermute | solution.py:60
  11.9 7.7 %collective-permute-start.1 = (bf16[2,64,576]{1,2,0:T(8,128)(2,1)S(1)}, bf16[2,64,576]{1,2,0:T(8,128)(2,1)S(1)}, u32[]{:S(2)}, u32[]{:S(2)}) collective-permute-start(bf16[2,64,576]{1,2,0:T(8,128)(2,1)S(1)} %pad_maximum_fusion.9), channel_id=1, source_target_pairs={{0,4},{4,0},{1,5},{5,1},{2,6},{6,2},{3,7},{7,3},{8,12},{12,8},{9,1... | collective-permute-start | bytes 442376 | tf_op jit(solution)/shard_map/ppermute | solution.py:60
  19.6 11.8 %copy-start.13 = (f32[1,1024]{1,0:T(1,128)S(1)}, f32[1,1024]{1,0:T(1,128)}, u32[]{:S(2)}) copy-start(f32[1,1024]{1,0:T(1,128)} %param.9) | copy-start | bytes 12292
  19.7 15.5 %copy-start.12 = (bf16[1,4,1024,2304]{3,2,1,0:T(8,128)(2,1)S(1)}, bf16[1,4,1024,2304]{3,2,1,0:T(8,128)(2,1)}, u32[]{:S(2)}) copy-start(bf16[1,4,1024,2304]{3,2,1,0:T(8,128)(2,1)} %param.10) | copy-start | bytes 56623108
  20.0 9.5 %collective-permute-start.4 = (bf16[2,2,128,576]{2,3,1,0:T(8,128)(2,1)S(1)}, bf16[2,2,128,576]{2,3,1,0:T(8,128)(2,1)S(1)}, u32[]{:S(2)}, u32[]{:S(2)}) collective-permute-start(bf16[2,2,128,576]{2,3,1,0:T(8,128)(2,1)S(1)} %pad_maximum_fusion.4), channel_id=1, source_target_pairs={{0,1},{1,0},{2,3},{3,2},{4,5},{5,4},{6,7},{7,6},{8,9},{9,8},{10,11... | collective-permute-start | bytes 1769480 | tf_op jit(solution)/shard_map/ppermute | solution.py:60
  29.6 1.9 copy-start.8
  71.8 8.4 %collective-permute-start.5 = (f32[2,2,2,2,128,576]{4,5,3,2,1,0:T(8,128)}, f32[2,2,2,2,128,576]{4,5,3,2,1,0:T(8,128)}, u32[]{:S(2)}, u32[]{:S(2)}) collective-permute-start(f32[2,2,2,2,128,576]{4,5,3,2,1,0:T(8,128)} %bitcast.257), channel_id=1, source_target_pairs={{0,1},{1,0},{2,3},{3,2},{4,5},{5,4},{6,7},{7,6},{8,9},{9,8},{10,11... | collective-permute-start | bytes 14155784 | tf_op jit(solution)/shard_map/ppermute | solution.py:53
  84.5 4.7 %copy-start.2 = (f32[2,2,2,2,128,576]{4,5,3,2,1,0:T(8,128)}, f32[2,2,2,2,128,576]{4,5,3,2,1,0:T(8,128)S(1)}, u32[]{:S(2)}) copy-start(f32[2,2,2,2,128,576]{4,5,3,2,1,0:T(8,128)S(1)} %bitcast_add_fusion) | copy-start | bytes 14155780
  93.7 25.9 %collective-permute-start.10 = (f32[2,2,2,40,576]{4,3,2,1,0:T(8,128)}, f32[2,2,2,40,576]{4,3,2,1,0:T(8,128)}, u32[]{:S(2)}, u32[]{:S(2)}) collective-permute-start(f32[2,2,2,40,576]{4,3,2,1,0:T(8,128)} %bitcast.38), channel_id=1, source_target_pairs={{0,4},{4,0},{1,5},{5,1},{2,6},{6,2},{3,7},{7,3},{8,12},{12,8},{9,1... | collective-permute-start | bytes 2211848 | tf_op jit(solution)/shard_map/ppermute | solution.py:53
  103.0 20.9 %collective-permute-start.14 = (f32[2,2,2,40,576]{4,3,2,1,0:T(8,128)}, f32[2,2,2,40,576]{4,3,2,1,0:T(8,128)}, u32[]{:S(2)}, u32[]{:S(2)}) collective-permute-start(f32[2,2,2,40,576]{4,3,2,1,0:T(8,128)} %bitcast.46), channel_id=1, source_target_pairs={{0,2},{1,3},{2,0},{3,1},{4,6},{5,7},{6,4},{7,5},{8,10},{9,11},{10,... | collective-permute-start | bytes 2211848 | tf_op jit(solution)/shard_map/ppermute | solution.py:53
  112.3 24.9 %collective-permute-start.6 = (f32[2,2,2,48,576]{4,3,2,1,0:T(8,128)}, f32[2,2,2,48,576]{4,3,2,1,0:T(8,128)}, u32[]{:S(2)}, u32[]{:S(2)}) collective-permute-start(f32[2,2,2,48,576]{4,3,2,1,0:T(8,128)} %bitcast.268), channel_id=1, source_target_pairs={{0,8},{8,0},{16,24},{24,16},{1,9},{9,1},{17,25},{25,17},{2,10},{10... | collective-permute-start | bytes 2654216 | tf_op jit(solution)/shard_map/ppermute | solution.py:53
  120.9 16.3 %copy-start.6 = (f32[2,1,2,2,48,576]{5,4,3,2,0,1:T(8,128)S(1)}, f32[2,1,2,2,48,576]{5,4,3,2,0,1:T(8,128)}, u32[]{:S(2)}) copy-start(f32[2,1,2,2,48,576]{5,4,3,2,0,1:T(8,128)} %copy.117) | copy-start | bytes 2654212
  120.9 18.2 %collective-permute-start.11 = (f32[2,2,40,576]{3,2,1,0:T(8,128)S(1)}, f32[2,2,40,576]{3,2,1,0:T(8,128)S(1)}, u32[]{:S(2)}, u32[]{:S(2)}) collective-permute-start(f32[2,2,40,576]{3,2,1,0:T(8,128)S(1)} %dynamic-slice_bitcast_fusion.3), channel_id=1, source_target_pairs={{0,2},{1,3},{2,0},{3,1},{4,6},{5,7},{6,4},{7,5},{8,10},{9,11},{10,... | collective-permute-start | bytes 1105928 | tf_op jit(solution)/shard_map/ppermute | solution.py:53
  125.1 20.8 %collective-permute-start.15 = (f32[2,2,40,576]{3,2,1,0:T(8,128)S(1)}, f32[2,2,40,576]{3,2,1,0:T(8,128)S(1)}, u32[]{:S(2)}, u32[]{:S(2)}) collective-permute-start(f32[2,2,40,576]{3,2,1,0:T(8,128)S(1)} %dynamic-slice_bitcast_fusion.2), channel_id=1, source_target_pairs={{0,8},{8,0},{16,24},{24,16},{1,9},{9,1},{17,25},{25,17},{2,10},{10... | collective-permute-start | bytes 1105928 | tf_op jit(solution)/shard_map/ppermute | solution.py:53
  138.6 18.1 %collective-permute-start.7 = (f32[2,2,48,576]{3,2,1,0:T(8,128)S(1)}, f32[2,2,48,576]{3,2,1,0:T(8,128)S(1)}, u32[]{:S(2)}, u32[]{:S(2)}) collective-permute-start(f32[2,2,48,576]{3,2,1,0:T(8,128)S(1)} %dynamic-slice_bitcast_fusion.1), channel_id=1, source_target_pairs={{0,4},{4,0},{1,5},{5,1},{2,6},{6,2},{3,7},{7,3},{8,12},{12,8},{9,1... | collective-permute-start | bytes 1327112 | tf_op jit(solution)/shard_map/ppermute | solution.py:53
  139.2 9.9 %collective-permute-start.12 = (f32[2,40,576]{2,1,0:T(8,128)S(1)}, f32[2,40,576]{2,1,0:T(8,128)S(1)}, u32[]{:S(2)}, u32[]{:S(2)}) collective-permute-start(f32[2,40,576]{2,1,0:T(8,128)S(1)} %dynamic-slice_bitcast_fusion.6), channel_id=1, source_target_pairs={{0,8},{8,0},{16,24},{24,16},{1,9},{9,1},{17,25},{25,17},{2,10},{10... | collective-permute-start | bytes 552968 | tf_op jit(solution)/shard_map/ppermute | solution.py:53
  145.9 8.0 %collective-permute-start.16 = (f32[2,40,576]{2,1,0:T(8,128)S(1)}, f32[2,40,576]{2,1,0:T(8,128)S(1)}, u32[]{:S(2)}, u32[]{:S(2)}) collective-permute-start(f32[2,40,576]{2,1,0:T(8,128)S(1)} %dynamic-slice_bitcast_fusion.5), channel_id=1, source_target_pairs={{0,4},{4,0},{1,5},{5,1},{2,6},{6,2},{3,7},{7,3},{8,12},{12,8},{9,1... | collective-permute-start | bytes 552968 | tf_op jit(solution)/shard_map/ppermute | solution.py:53
  149.2 22.7 %copy-start.10 = (bf16[4,32,576]{2,1,0:T(8,128)(2,1)S(1)}, bf16[4,32,576]{2,1,0:T(8,128)(2,1)}, u32[]{:S(2)}) copy-start(bf16[4,32,576]{2,1,0:T(8,128)(2,1)} %param.13) | copy-start | bytes 442372
  149.2 22.7 %copy-start.11 = (f32[4,576]{1,0:T(4,128)S(1)}, f32[4,576]{1,0:T(4,128)}, u32[]{:S(2)}) copy-start(f32[4,576]{1,0:T(4,128)} %param.11) | copy-start | bytes 27652
  149.2 8.5 %collective-permute-start.13 = (f32[40,576]{1,0:T(8,128)S(1)}, f32[40,576]{1,0:T(8,128)S(1)}, u32[]{:S(2)}, u32[]{:S(2)}) collective-permute-start(f32[40,576]{1,0:T(8,128)S(1)} %dynamic-slice_bitcast_fusion.11), channel_id=1, source_target_pairs={{0,16},{8,24},{16,0},{24,8},{1,17},{9,25},{17,1},{25,9},{2,18},{10... | collective-permute-start | bytes 276488 | tf_op jit(solution)/shard_map/ppermute | solution.py:53
  154.0 9.5 %collective-permute-start.17 = (f32[40,576]{1,0:T(8,128)S(1)}, f32[40,576]{1,0:T(8,128)S(1)}, u32[]{:S(2)}, u32[]{:S(2)}) collective-permute-start(f32[40,576]{1,0:T(8,128)S(1)} %dynamic-slice_bitcast_fusion.10), channel_id=1, source_target_pairs={{0,16},{8,24},{16,0},{24,8},{1,17},{9,25},{17,1},{25,9},{2,18},{10... | collective-permute-start | bytes 276488 | tf_op jit(solution)/shard_map/ppermute | solution.py:53
  156.8 6.3 %collective-permute-start.8 = (f32[2,48,576]{2,1,0:T(8,128)S(1)}, f32[2,48,576]{2,1,0:T(8,128)S(1)}, u32[]{:S(2)}, u32[]{:S(2)}) collective-permute-start(f32[2,48,576]{2,1,0:T(8,128)S(1)} %dynamic-slice_bitcast_fusion.4), channel_id=1, source_target_pairs={{0,2},{1,3},{2,0},{3,1},{4,6},{5,7},{6,4},{7,5},{8,10},{9,11},{10,... | collective-permute-start | bytes 663560 | tf_op jit(solution)/shard_map/ppermute | solution.py:53
  163.1 8.7 %collective-permute-start.9 = (f32[48,576]{1,0:T(8,128)S(1)}, f32[48,576]{1,0:T(8,128)S(1)}, u32[]{:S(2)}, u32[]{:S(2)}) collective-permute-start(f32[48,576]{1,0:T(8,128)S(1)} %dynamic-slice_bitcast_fusion.9), channel_id=1, source_target_pairs={{0,16},{8,24},{16,0},{24,8},{1,17},{9,25},{17,1},{25,9},{2,18},{10... | collective-permute-start | bytes 331784 | tf_op jit(solution)/shard_map/ppermute | solution.py:53
  171.9 19.7 %copy-start.7 = (bf16[4,32,576]{2,1,0:T(8,128)(2,1)}, bf16[4,32,576]{2,1,0:T(8,128)(2,1)S(1)}, u32[]{:S(2)}) copy-start(bf16[4,32,576]{2,1,0:T(8,128)(2,1)S(1)} %subtract_convert_fusion) | copy-start | bytes 442372
  172.0 5.8 %collective-permute-start.22 = (bf16[40,576]{1,0:T(8,128)(2,1)S(1)}, bf16[40,576]{1,0:T(8,128)(2,1)S(1)}, u32[]{:S(2)}, u32[]{:S(2)}) collective-permute-start(bf16[40,576]{1,0:T(8,128)(2,1)S(1)} %slice.52), channel_id=1, source_target_pairs={{0,16},{8,24},{16,0},{24,8},{1,17},{9,25},{17,1},{25,9},{2,18},{10... | collective-permute-start | bytes 138248 | tf_op jit(solution)/shard_map/ppermute | solution.py:60
  172.1 8.1 %collective-permute-start.18 = (bf16[48,576]{1,0:T(8,128)(2,1)S(1)}, bf16[48,576]{1,0:T(8,128)(2,1)S(1)}, u32[]{:S(2)}, u32[]{:S(2)}) collective-permute-start(bf16[48,576]{1,0:T(8,128)(2,1)S(1)} %slice.51), channel_id=1, source_target_pairs={{0,16},{8,24},{16,0},{24,8},{1,17},{9,25},{17,1},{25,9},{2,18},{10... | collective-permute-start | bytes 165896 | tf_op jit(solution)/shard_map/ppermute | solution.py:60
  177.9 5.9 %collective-permute-start.23 = (bf16[2,40,576]{2,1,0:T(8,128)(2,1)S(1)}, bf16[2,40,576]{2,1,0:T(8,128)(2,1)S(1)}, u32[]{:S(2)}, u32[]{:S(2)}) collective-permute-start(bf16[2,40,576]{2,1,0:T(8,128)(2,1)S(1)} %pad_maximum_fusion.16), channel_id=1, source_target_pairs={{0,8},{8,0},{16,24},{24,16},{1,9},{9,1},{17,25},{25,17},{2,10},{10... | collective-permute-start | bytes 276488 | tf_op jit(solution)/shard_map/ppermute | solution.py:60
  177.9 5.2 %collective-permute-start.26 = (bf16[40,576]{1,0:T(8,128)(2,1)S(1)}, bf16[40,576]{1,0:T(8,128)(2,1)S(1)}, u32[]{:S(2)}, u32[]{:S(2)}) collective-permute-start(bf16[40,576]{1,0:T(8,128)(2,1)S(1)} %get-tuple-element.60), channel_id=1, source_target_pairs={{0,16},{8,24},{16,0},{24,8},{1,17},{9,25},{17,1},{25,9},{2,18},{10... | collective-permute-start | bytes 138248 | tf_op jit(solution)/shard_map/ppermute | solution.py:60
  180.2 4.9 %collective-permute-start.19 = (bf16[2,48,576]{2,1,0:T(8,128)(2,1)S(1)}, bf16[2,48,576]{2,1,0:T(8,128)(2,1)S(1)}, u32[]{:S(2)}, u32[]{:S(2)}) collective-permute-start(bf16[2,48,576]{2,1,0:T(8,128)(2,1)S(1)} %pad_maximum_fusion.15), channel_id=1, source_target_pairs={{0,2},{1,3},{2,0},{3,1},{4,6},{5,7},{6,4},{7,5},{8,10},{9,11},{10,... | collective-permute-start | bytes 331784 | tf_op jit(solution)/shard_map/ppermute | solution.py:60
  183.2 5.8 %collective-permute-start.27 = (bf16[2,40,576]{2,1,0:T(8,128)(2,1)S(1)}, bf16[2,40,576]{2,1,0:T(8,128)(2,1)S(1)}, u32[]{:S(2)}, u32[]{:S(2)}) collective-permute-start(bf16[2,40,576]{2,1,0:T(8,128)(2,1)S(1)} %pad_maximum_fusion.17), channel_id=1, source_target_pairs={{0,4},{4,0},{1,5},{5,1},{2,6},{6,2},{3,7},{7,3},{8,12},{12,8},{9,1... | collective-permute-start | bytes 276488 | tf_op jit(solution)/shard_map/ppermute | solution.py:60
  183.8 7.7 %collective-permute-start.24 = (bf16[2,2,40,576]{3,2,1,0:T(8,128)(2,1)S(1)}, bf16[2,2,40,576]{3,2,1,0:T(8,128)(2,1)S(1)}, u32[]{:S(2)}, u32[]{:S(2)}) collective-permute-start(bf16[2,2,40,576]{3,2,1,0:T(8,128)(2,1)S(1)} %pad_maximum_fusion.12), channel_id=1, source_target_pairs={{0,2},{1,3},{2,0},{3,1},{4,6},{5,7},{6,4},{7,5},{8,10},{9,11},{10,... | collective-permute-start | bytes 552968 | tf_op jit(solution)/shard_map/ppermute | solution.py:60
  185.2 13.0 %collective-permute-start.20 = (bf16[2,2,48,576]{3,2,1,0:T(8,128)(2,1)S(1)}, bf16[2,2,48,576]{3,2,1,0:T(8,128)(2,1)S(1)}, u32[]{:S(2)}, u32[]{:S(2)}) collective-permute-start(bf16[2,2,48,576]{3,2,1,0:T(8,128)(2,1)S(1)} %pad_maximum_fusion.11), channel_id=1, source_target_pairs={{0,4},{4,0},{1,5},{5,1},{2,6},{6,2},{3,7},{7,3},{8,12},{12,8},{9,1... | collective-permute-start | bytes 663560 | tf_op jit(solution)/shard_map/ppermute | solution.py:60
  189.1 7.7 %collective-permute-start.28 = (bf16[2,2,40,576]{3,2,0,1:T(8,128)(2,1)S(1)}, bf16[2,2,40,576]{3,2,0,1:T(8,128)(2,1)S(1)}, u32[]{:S(2)}, u32[]{:S(2)}) collective-permute-start(bf16[2,2,40,576]{3,2,0,1:T(8,128)(2,1)S(1)} %pad_maximum_fusion.13), channel_id=1, source_target_pairs={{0,8},{8,0},{16,24},{24,16},{1,9},{9,1},{17,25},{25,17},{2,10},{10... | collective-permute-start | bytes 552968 | tf_op jit(solution)/shard_map/ppermute | solution.py:60
  191.7 8.0 %collective-permute-start.25 = (bf16[2,2,2,40,576]{4,3,2,1,0:T(8,128)(2,1)S(1)}, bf16[2,2,2,40,576]{4,3,2,1,0:T(8,128)(2,1)S(1)}, u32[]{:S(2)}, u32[]{:S(2)}) collective-permute-start(bf16[2,2,2,40,576]{4,3,2,1,0:T(8,128)(2,1)S(1)} %pad_maximum_fusion.6), channel_id=1, source_target_pairs={{0,4},{4,0},{1,5},{5,1},{2,6},{6,2},{3,7},{7,3},{8,12},{12,8},{9,1... | collective-permute-start | bytes 1105928 | tf_op jit(solution)/shard_map/ppermute | solution.py:60
  196.9 8.0 %collective-permute-start.29 = (bf16[2,2,2,40,576]{4,3,1,0,2:T(8,128)(2,1)S(1)}, bf16[2,2,2,40,576]{4,3,1,0,2:T(8,128)(2,1)S(1)}, u32[]{:S(2)}, u32[]{:S(2)}) collective-permute-start(bf16[2,2,2,40,576]{4,3,1,0,2:T(8,128)(2,1)S(1)} %pad_maximum_fusion.7), channel_id=1, source_target_pairs={{0,2},{1,3},{2,0},{3,1},{4,6},{5,7},{6,4},{7,5},{8,10},{9,11},{10,... | collective-permute-start | bytes 1105928 | tf_op jit(solution)/shard_map/ppermute | solution.py:60
  198.4 8.9 %collective-permute-start.21 = (bf16[2,2,2,48,576]{4,3,2,1,0:T(8,128)(2,1)S(1)}, bf16[2,2,2,48,576]{4,3,2,1,0:T(8,128)(2,1)S(1)}, u32[]{:S(2)}, u32[]{:S(2)}) collective-permute-start(bf16[2,2,2,48,576]{4,3,2,1,0:T(8,128)(2,1)S(1)} %pad_maximum_fusion.5), channel_id=1, source_target_pairs={{0,8},{8,0},{16,24},{24,16},{1,9},{9,1},{17,25},{25,17},{2,10},{10... | collective-permute-start | bytes 1327112 | tf_op jit(solution)/shard_map/ppermute | solution.py:60
  199.9 7.5 %copy-start.3 = (bf16[2,2,2,2,40,576]{5,4,3,0,2,1:T(8,128)(2,1)}, bf16[2,2,2,2,40,576]{5,4,3,0,2,1:T(8,128)(2,1)S(1)}, u32[]{:S(2)}) copy-start(bf16[2,2,2,2,40,576]{5,4,3,0,2,1:T(8,128)(2,1)S(1)} %maximum_bitcast_fusion) | copy-start | bytes 2211844
  205.1 2.3 copy-start.4
  207.4 0.8 copy-start.5
  211.1 4.9 %collective-permute-start.30 = (bf16[2,2,2,2,128,576]{4,5,3,2,1,0:T(8,128)(2,1)}, bf16[2,2,2,2,128,576]{4,5,3,2,1,0:T(8,128)(2,1)}, u32[]{:S(2)}, u32[]{:S(2)}) collective-permute-start(bf16[2,2,2,2,128,576]{4,5,3,2,1,0:T(8,128)(2,1)} %copy.128), channel_id=1, source_target_pairs={{0,1},{1,0},{2,3},{3,2},{4,5},{5,4},{6,7},{7,6},{8,9},{9,8},{10,11... | collective-permute-start | bytes 7077896 | tf_op jit(solution)/shard_map/ppermute | solution.py:60
  228.9 9.9 %copy-start.9 = (pred[256,1024]{1,0:T(8,128)(4,1)S(1)}, pred[256,1024]{1,0:T(8,128)(4,1)}, u32[]{:S(2)}) copy-start(pred[256,1024]{1,0:T(8,128)(4,1)} %copy-done.8) | copy-start | bytes 786436
  228.9 20.5 %slice-start = ((s8[4718592]{0:T(1024)(128)(4,1)}), s8[524288]{0:T(1024)(128)(4,1)S(1)}, s32[]{:S(2)}) async-start(s8[4718592]{0:T(1024)(128)(4,1)} %bitcast.271), calls=%async_computation | async-start | bytes 1048576
  238.8 10.6 %slice-start.1 = ((s8[4718592]{0:T(1024)(128)(4,1)}), s8[4194304]{0:T(1024)(128)(4,1)S(1)}, s32[]{:S(2)}) async-start(s8[4718592]{0:T(1024)(128)(4,1)} %bitcast.271), calls=%async_computation.1 | async-start | bytes 8388608
  251.0 2.9 %collective-permute-start.31 = (f32[2,2,128,576]{2,3,1,0:T(8,128)S(1)}, f32[2,2,128,576]{2,3,1,0:T(8,128)S(1)}, u32[]{:S(2)}, u32[]{:S(2)}) collective-permute-start(f32[2,2,128,576]{2,3,1,0:T(8,128)S(1)} %dynamic-slice_bitcast_fusion), channel_id=1, source_target_pairs={{0,1},{1,0},{2,3},{3,2},{4,5},{5,4},{6,7},{7,6},{8,9},{9,8},{10,11... | collective-permute-start | bytes 3538952 | tf_op jit(solution)/shard_map/ppermute | solution.py:53
  254.8 9.9 %collective-permute-start.32 = (f32[2,64,576]{2,1,0:T(8,128)S(1)}, f32[2,64,576]{2,1,0:T(8,128)}, u32[]{:S(2)}, u32[]{:S(2)}) collective-permute-start(f32[2,64,576]{2,1,0:T(8,128)S(1)} %bitcast.269), channel_id=1, source_target_pairs={{0,4},{4,0},{1,5},{5,1},{2,6},{6,2},{3,7},{7,3},{8,12},{12,8},{9,1... | collective-permute-start | bytes 884744 | tf_op jit(solution)/shard_map/ppermute | solution.py:53
  255.7 17.1 %copy-start.1 = (s32[4,256,64]{1,2,0:T(8,128)S(1)}, s32[4,256,64]{1,2,0:T(8,128)}, u32[]{:S(2)}) copy-start(s32[4,256,64]{1,2,0:T(8,128)} %param.12) | copy-start | bytes 786436
  255.9 10.6 %collective-permute-start.34 = (f32[2,64,576]{2,1,0:T(8,128)S(1)}, f32[2,64,576]{2,1,0:T(8,128)S(1)}, u32[]{:S(2)}, u32[]{:S(2)}) collective-permute-start(f32[2,64,576]{2,1,0:T(8,128)S(1)} %bitcast.270), channel_id=1, source_target_pairs={{0,2},{1,3},{2,0},{3,1},{4,6},{5,7},{6,4},{7,5},{8,10},{9,11},{10,... | collective-permute-start | bytes 884744 | tf_op jit(solution)/shard_map/ppermute | solution.py:53
  265.7 5.5 %collective-permute-start.33 = (f32[64,576]{1,0:T(8,128)S(1)}, f32[64,576]{1,0:T(8,128)S(1)}, u32[]{:S(2)}, u32[]{:S(2)}) collective-permute-start(f32[64,576]{1,0:T(8,128)S(1)} %dynamic-slice_bitcast_fusion.8), channel_id=1, source_target_pairs={{0,2},{1,3},{2,0},{3,1},{4,6},{5,7},{6,4},{7,5},{8,10},{9,11},{10,... | collective-permute-start | bytes 442376 | tf_op jit(solution)/shard_map/ppermute | solution.py:53
  266.6 5.4 %collective-permute-start.35 = (f32[64,576]{1,0:T(8,128)S(1)}, f32[64,576]{1,0:T(8,128)S(1)}, u32[]{:S(2)}, u32[]{:S(2)}) collective-permute-start(f32[64,576]{1,0:T(8,128)S(1)} %dynamic-slice_bitcast_fusion.7), channel_id=1, source_target_pairs={{0,4},{4,0},{1,5},{5,1},{2,6},{6,2},{3,7},{7,3},{8,12},{12,8},{9,1... | collective-permute-start | bytes 442376 | tf_op jit(solution)/shard_map/ppermute | solution.py:53

commit v4 on v3

--- a/solution.py
+++ b/solution.py
@@ -44,61 +44,54 @@
     return [(i, i ^ (1 << bit)) for i in range(lax.axis_size(axis))]
 
 
-def halve(x, labels, label):
-    axis, bit = label
-    dim = labels.index(label)
-    own = (lax.axis_index(axis) >> bit) & 1
-    keep = lax.dynamic_index_in_dim(x, own, dim, keepdims=False)
-    send = lax.dynamic_index_in_dim(x, 1 - own, dim, keepdims=False)
-    recv = lax.ppermute(send, axis, partner(axis, bit))
-    return keep + recv, [l for l in labels if l != label]
-
-
-def double(x, labels, label):
-    axis, bit = label
-    own = (lax.axis_index(axis) >> bit) & 1
-    recv = lax.ppermute(x, axis, partner(axis, bit))
-    low = jnp.where(own == 0, x, recv)
-    high = jnp.where(own == 0, recv, x)
-    return jnp.stack([low, high]), [label] + labels
+def portion_rows(rows, parts):
+    sizes = row_split(rows, parts)
+    return [(sum(sizes[:i]), sizes[i]) for i in range(parts)]
 
 
 def reduce_scatter(blocks, axes):
     labels, prefix, orders, suffix = plan(axes)
     n, rows, cols = blocks.shape
-    x = blocks.reshape([2] * len(labels) + [rows, cols])
-    cur = list(labels)
-    for label in prefix:
-        x, cur = halve(x, cur, label)
-    sizes = row_split(rows, len(orders))
-    starts = [sum(sizes[:i]) for i in range(len(sizes))]
-    parts = [lax.slice_in_dim(x, s, s + z, axis=x.ndim - 2) for s, z in zip(starts, sizes)]
-    curs = [list(cur) for _ in parts]
-    for step in range(len(orders[0]) + len(suffix)):
+    nb = len(labels)
+    x = blocks.reshape([2] * nb + [rows, cols])
+    steps = [prefix + order + suffix for order in orders]
+    parts = []
+    for (start, size), order in zip(portion_rows(rows, len(orders)), steps):
+        xp = lax.slice_in_dim(x, start, start + size, axis=nb)
+        xp = jnp.transpose(xp, [labels.index(l) for l in order] + [nb, nb + 1])
+        parts.append(xp.reshape(n, size, cols))
+    for k in range(nb):
         for p in range(len(parts)):
-            label = (orders[p] + suffix)[step]
-            parts[p], curs[p] = halve(parts[p], curs[p], label)
-    return jnp.concatenate(parts, axis=0)
+            axis, bit = steps[p][k]
+            own = (lax.axis_index(axis) >> bit) & 1
+            half = parts[p].shape[0] // 2
+            keep = lax.dynamic_slice_in_dim(parts[p], own * half, half, 0)
+            send = lax.dynamic_slice_in_dim(parts[p], (1 - own) * half, half, 0)
+            parts[p] = keep + lax.ppermute(send, axis, partner(axis, bit))
+    return jnp.concatenate([xp[0] for xp in parts], axis=0)
 
 
 def all_gather(block, axes):
     labels, prefix, orders, suffix = plan(axes)
     rows, cols = block.shape
-    sizes = row_split(rows, len(orders))
-    starts = [sum(sizes[:i]) for i in range(len(sizes))]
-    parts = [lax.slice_in_dim(block, s, s + z, axis=0) for s, z in zip(starts, sizes)]
-    curs = [[] for _ in parts]
-    for step in range(len(orders[0]) + len(suffix)):
+    nb = len(labels)
+    steps = [prefix + order + suffix for order in orders]
+    spans = portion_rows(rows, len(orders))
+    parts = [lax.slice_in_dim(block, start, start + size, axis=0)[None] for start, size in spans]
+    for k in reversed(range(nb)):
         for p in range(len(parts)):
-            label = list(reversed(orders[p] + suffix))[step]
-            parts[p], curs[p] = double(parts[p], curs[p], label)
-    cur = curs[0]
-    parts = [jnp.transpose(x, [c.index(l) for l in cur] + [x.ndim - 2, x.ndim - 1]) for x, c in zip(parts, curs)]
-    x = jnp.concatenate(parts, axis=-2)
-    for label in reversed(prefix):
-        x, cur = double(x, cur, label)
-    x = jnp.transpose(x, [cur.index(l) for l in labels] + [x.ndim - 2, x.ndim - 1])
-    return x.reshape(-1, rows, cols)
+            axis, bit = steps[p][k]
+            own = (lax.axis_index(axis) >> bit) & 1
+            recv = lax.ppermute(parts[p], axis, partner(axis, bit))
+            parts[p] = jnp.where(
+                own == 0, jnp.concatenate([parts[p], recv]), jnp.concatenate([recv, parts[p]])
+            )
+    out = []
+    for xp, order, (start, size) in zip(parts, steps, spans):
+        xp = xp.reshape([2] * nb + [size, cols])
+        xp = jnp.transpose(xp, [order.index(l) for l in labels] + [nb, nb + 1])
+        out.append(xp.reshape(-1, size, cols))
+    return jnp.concatenate(out, axis=1)
 
 
 def local(resid, encoder, encoder_bias, decoder, decoder_bias, topk_index, target):

time: 274 us -> 247 us (0.901)
  local copies, waits for them, and re-layouts: 93.4 us -> 61.3 us
  waiting for transfers between devices: 87.5 us -> 74 us
  starting transfers between devices: 40.7 us -> 51.5 us
  matrix products: 23.2 us -> 29.6 us
    dynamic_slice x18 -> x21, local copies, waits for them, and re-layouts: 43.3 us -> 10.6 us  [reduce_scatter(): send = lax.dynamic_slice_in_dim(parts[p], (1 - own) * half, half, 0)]
    ppermute x36 -> x42, waiting for transfers between devices: 87.5 us -> 74 us  [the longest x21 55.4 us: reduce_scatter(): parts[p] = keep + lax.ppermute(send, axis, partner(axis, bit))]
    ppermute x36 -> x42, starting transfers between devices: 40.7 us -> 51.5 us  [the longest x21 27.7 us: all_gather(): recv = lax.ppermute(parts[p], axis, partner(axis, bit))]
    transpose x0 -> x13, local copies, waits for them, and re-layouts: none -> 9.61 us  [the longest x8 9.01 us: reduce_scatter(): xp = jnp.transpose(xp, [labels.index(l) for l in order] + [nb, nb + 1])]
    select_n x0 -> x21, other arithmetic: none -> 7.6 us  [all_gather(): jnp.where(own == 0, jnp.concatenate([parts[p], recv]), jnp.concatenate([r...]
    another operation x30 -> x2, other arithmetic: 6.51 us -> 0.04 us  [double(): return (jnp.stack([low, high]), [label] + labels)]
    dot_general x1, matrix products: 7.43 us -> 13.9 us  [local(): jnp.einsum('tf,lfd->ltd', acts, decoder[0], preferred_element_type=jnp.fl...]
    slice x5 -> x1, local copies, waits for them, and re-layouts: 6.17 us -> 1.13 us  [all_gather(): lax.slice_in_dim(block, start, start + size, axis=0)[None]]
  transfers between devices with their start and end apart: 36 -> 42, of which waited for: 26 -> 24; matrix products, arithmetic and copies ran while one was open for 16% -> 14% of each run, Pallas kernels for 0% -> 0%
where the time goes in v4:
time: 247 us; the launch traced here: 246 us
  waiting for transfers between devices  74 us (30%)
  local copies, waits for them, and re-layouts  61.3 us (25%)
  starting transfers between devices  51.5 us (21%)
  matrix products  29.6 us (12%)
  other arithmetic  28.3 us (11%)
    ppermute x21, waiting for transfers between devices, reduce_scatter(): parts[p] = keep + lax.ppermute(send, axis, partner(axis, bit))  55.4 us
    ppermute x21, starting transfers between devices, all_gather(): recv = lax.ppermute(parts[p], axis, partner(axis, bit))  27.7 us
    ppermute x21, starting transfers between devices, reduce_scatter(): parts[p] = keep + lax.ppermute(send, axis, partner(axis, bit))  23.8 us
    reshape x2, local copies, waits for them, and re-layouts, local(): partial_value.reshape(layer_count, slots, slot_rows, feat_parts, cols)  18.7 us
    ppermute x21, waiting for transfers between devices, all_gather(): recv = lax.ppermute(parts[p], axis, partner(axis, bit))  18.6 us
    dot_general x1, matrix products, local(): jnp.einsum('tf,lfd->ltd', acts, decoder[0], preferred_element_type=jnp.fl...  13.9 us
    dynamic_slice x21, local copies, waits for them, and re-layouts, reduce_scatter(): send = lax.dynamic_slice_in_dim(parts[p], (1 - own) * half, half, 0)  10.6 us
    dot_general x1, matrix products, local(): jnp.einsum('ltd,lfd->tf', kept, decoder[0], preferred_element_type=jnp.fl...  10.5 us
  transfers between devices with their start and end apart: 42, of which 24 were waited for; matrix products, arithmetic and copies ran while one was open for 14% of the time, Pallas kernels for 0%

profile of v4, /device:TPU:0, one launch (start us, length us, event | category | flops | bytes accessed | tf_op | source)
XLA Modules:
  0.0 246.0 jit_solution(12801589165099372705)
XLA Ops:
  0.6 1.1 fusion.41
  1.9 3.1 %collective-permute-start = (bf16[1,64,576]{2,1,0:T(8,128)(2,1)S(1)}, bf16[1,64,576]{2,1,0:T(8,128)(2,1)S(1)}, u32[]{:S(2)}, u32[]{:S(2)}) collective-permute-start(bf16[1,64,576]{2,1,0:T(8,128)(2,1)S(1)} %copy.69), channel_id=1, source_target_pairs={{0,2},{1,3},{2,0},{3,1},{4,6},{5,7},{6,4},{7,5},{8,10},{9,11},{10,... | collective-permute-start | bytes 221192 | tf_op jit(solution)/shard_map/ppermute | solution.py:85
  5.1 1.6 collective-permute-start.3
  7.5 2.0 collective-permute-start.1
  9.9 1.2 collective-permute-start.4
  11.2 1.9 collective-permute-done.1
  13.3 2.0 collective-permute-done.4
  15.5 9.4 %compare_reduce_fusion = pred[256,1024]{1,0:T(8,128)(4,1)S(1)} fusion(s32[1024]{0:T(1024)S(1)} %iota_add_fusion, s32[256,64]{1,0:T(8,128)S(1)} %copy.51), kind=kLoop, calls=%fused_computation | loop fusion | flops 33292288 | bytes 331776 | tf_op jit(solution)/shard_map/reduce_or | solution.py:121
  26.6 3.8 %fusion.35 = bf16[256,1024,1]{1,0,2:T(8,128)(2,1)S(1)} fusion(pred[256,1024]{1,0:T(8,128)(4,1)S(1)} %compare_reduce_fusion, bf16[1,2304,1024]{2,1,0:T(8,128)(2,1)} %param.8, bf16[288,8,2,128]{3,2,1,0:T(2,128)(2,1)S(1)} %bitcast.140, f32[1024]{0:T(1024)S(1)} %bitcast.146), kind=kOutput, calls=%fused_computation.30 | convolution fusion | flops 1208745984 | bytes 6688768 | tf_op jit(solution)/shard_map/dot_general | solution.py:117
  30.4 13.9 %select_bitcast_fusion = f32[4,256,2304]{2,1,0:T(8,128)} fusion(bf16[256,1024,1]{1,0,2:T(8,128)(2,1)S(1)} %fusion.35, bf16[1,4,1024,2304]{3,2,1,0:T(8,128)(2,1)} %param.10, pred[4]{0:T(512)(128)(4,1)S(1)} %iota_compare_fusion), kind=kOutput, calls=%fused_computation.5 | convolution fusion | flops 4834197504 | bytes 28835844 | tf_op jit(solution)/shard_map/tf,lfd->ltd/dot_general | solution.py:126
  44.3 13.2 %reshape.123 = f32[4,8,32,4,576]{4,3,2,1,0:T(4,128)} reshape(f32[4,256,2304]{2,1,0:T(8,128)} %select_bitcast_fusion) | data formatting | bytes 18874368 | tf_op jit(solution)/shard_map/reshape | solution.py:129
  57.5 5.5 %copy.57 = f32[4,8,32,4,576]{4,2,0,3,1:T(8,128)S(1)} copy(f32[4,8,32,4,576]{4,3,2,1,0:T(4,128)} %reshape.123) | data formatting | bytes 18874368 | tf_op jit(solution)/shard_map/reshape | solution.py:129
  64.0 1.4 constant_dynamic-slice_fusion.15
  67.8 1.6 constant_dynamic-slice_fusion.10
  70.0 1.4 constant_dynamic-slice_fusion.20
  71.4 2.1 dynamic-slice_add_fusion.2
  73.6 1.6 collective-permute-start.12
  75.2 1.7 dynamic-slice_add_fusion.1
  77.8 1.8 dynamic-slice_add_fusion
  80.7 1.6 collective-permute-start.7
  82.3 12.0 %collective-permute-done.12 = f32[8,40,576]{2,1,0:T(8,128)S(1)} collective-permute-done((f32[8,40,576]{2,1,0:T(8,128)S(1)}, f32[8,40,576]{2,1,0:T(8,128)S(1)}, u32[]{:S(2)}, u32[]{:S(2)}) %collective-permute-start.12) | collective-permute-done | bytes 737312 | tf_op jit(solution)/shard_map/ppermute | solution.py:70
  95.2 1.2 collective-permute-start.13
  96.3 1.2 collective-permute-done.17
  99.3 1.6 collective-permute-start.18
  100.8 5.7 %collective-permute-done.13 = f32[4,40,576]{2,1,0:T(8,128)S(1)} collective-permute-done((f32[4,40,576]{2,1,0:T(8,128)}, f32[4,40,576]{2,1,0:T(8,128)S(1)}, u32[]{:S(2)}, u32[]{:S(2)}) %collective-permute-start.13) | collective-permute-done | bytes 368672 | tf_op jit(solution)/shard_map/ppermute | solution.py:70
  106.6 1.7 collective-permute-start.14
  108.3 6.1 %collective-permute-done.18 = f32[4,40,576]{2,1,0:T(8,128)} collective-permute-done((f32[4,40,576]{2,1,0:T(8,128)}, f32[4,40,576]{2,1,0:T(8,128)}, u32[]{:S(2)}, u32[]{:S(2)}) %collective-permute-start.18) | collective-permute-done | bytes 368672 | tf_op jit(solution)/shard_map/ppermute | solution.py:70
  114.4 1.2 dynamic-slice_add_fusion.9
  116.6 1.3 dynamic-slice_add_fusion.3
  118.0 1.2 collective-permute-start.8
  119.2 2.7 %collective-permute-start.15 = (f32[1,40,576]{2,1,0:T(8,128)S(1)}, f32[1,40,576]{2,1,0:T(8,128)S(1)}, u32[]{:S(2)}, u32[]{:S(2)}) collective-permute-start(f32[1,40,576]{2,1,0:T(8,128)S(1)} %constant_dynamic-slice_fusion.11), channel_id=1, source_target_pairs={{0,16},{8,24},{16,0},{24,8},{1,17},{9,25},{17,1},{25,9},{2,18},{10... | collective-permute-start | bytes 276488 | tf_op jit(solution)/shard_map/ppermute | solution.py:70
  121.9 1.8 collective-permute-done.19
  123.7 2.7 %collective-permute-start.20 = (f32[1,40,576]{2,1,0:T(8,128)S(1)}, f32[1,40,576]{2,1,0:T(8,128)S(1)}, u32[]{:S(2)}, u32[]{:S(2)}) collective-permute-start(f32[1,40,576]{2,1,0:T(8,128)S(1)} %constant_dynamic-slice_fusion.6), channel_id=1, source_target_pairs={{0,16},{8,24},{16,0},{24,8},{1,17},{9,25},{17,1},{25,9},{2,18},{10... | collective-permute-start | bytes 276488 | tf_op jit(solution)/shard_map/ppermute | solution.py:70
  126.4 5.4 %collective-permute-done.8 = f32[4,48,576]{2,1,0:T(8,128)S(1)} collective-permute-done((f32[4,48,576]{2,1,0:T(8,128)S(1)}, f32[4,48,576]{2,1,0:T(8,128)S(1)}, u32[]{:S(2)}, u32[]{:S(2)}) %collective-permute-start.8) | collective-permute-done | bytes 442400 | tf_op jit(solution)/shard_map/ppermute | solution.py:70
  132.8 5.4 %collective-permute-done.9 = f32[2,48,576]{2,1,0:T(8,128)S(1)} collective-permute-done((f32[2,48,576]{2,1,0:T(8,128)S(1)}, f32[2,48,576]{2,1,0:T(8,128)S(1)}, u32[]{:S(2)}, u32[]{:S(2)}) %collective-permute-start.9) | collective-permute-done | bytes 221216 | tf_op jit(solution)/shard_map/ppermute | solution.py:70
  138.3 2.7 %collective-permute-start.10 = (f32[1,48,576]{2,1,0:T(8,128)S(1)}, f32[1,48,576]{2,1,0:T(8,128)S(1)}, u32[]{:S(2)}, u32[]{:S(2)}) collective-permute-start(f32[1,48,576]{2,1,0:T(8,128)S(1)} %constant_dynamic-slice_fusion.16), channel_id=1, source_target_pairs={{0,16},{8,24},{16,0},{24,8},{1,17},{9,25},{17,1},{25,9},{2,18},{10... | collective-permute-start | bytes 331784 | tf_op jit(solution)/shard_map/ppermute | solution.py:70
  140.9 5.2 %collective-permute-done.10 = f32[1,48,576]{2,1,0:T(8,128)S(1)} collective-permute-done((f32[1,48,576]{2,1,0:T(8,128)S(1)}, f32[1,48,576]{2,1,0:T(8,128)S(1)}, u32[]{:S(2)}, u32[]{:S(2)}) %collective-permute-start.10) | collective-permute-done | bytes 110624 | tf_op jit(solution)/shard_map/ppermute | solution.py:70
  146.3 1.3 collective-permute-start.26
  147.6 1.7 collective-permute-start.21
  149.3 1.2 collective-permute-start.31
  151.4 4.3 %collective-permute-start.27 = (bf16[2,40,576]{2,1,0:T(8,128)(2,1)S(1)}, bf16[2,40,576]{2,1,0:T(8,128)(2,1)S(1)}, u32[]{:S(2)}, u32[]{:S(2)}) collective-permute-start(bf16[2,40,576]{2,1,0:T(8,128)(2,1)S(1)} %maximum_select_fusion.19), channel_id=1, source_target_pairs={{0,8},{8,0},{16,24},{24,16},{1,9},{9,1},{17,25},{25,17},{2,10},{10... | collective-permute-start | bytes 276488 | tf_op jit(solution)/shard_map/ppermute | solution.py:85
  158.4 1.1 collective-permute-start.28
  159.5 2.0 collective-permute-done.32
  161.6 3.6 %collective-permute-start.33 = (bf16[4,40,576]{2,1,0:T(8,128)(2,1)S(1)}, bf16[4,40,576]{2,1,0:T(8,128)(2,1)S(1)}, u32[]{:S(2)}, u32[]{:S(2)}) collective-permute-start(bf16[4,40,576]{2,1,0:T(8,128)(2,1)S(1)} %maximum_select_fusion.15), channel_id=1, source_target_pairs={{0,8},{8,0},{16,24},{24,16},{1,9},{9,1},{17,25},{25,17},{2,10},{10... | collective-permute-start | bytes 552968 | tf_op jit(solution)/shard_map/ppermute | solution.py:85
  169.9 1.7 collective-permute-done.23
  171.7 1.5 collective-permute-start.24
  173.2 2.8 %collective-permute-done.29 = bf16[8,40,576]{2,1,0:T(8,128)(2,1)S(1)} collective-permute-done((bf16[8,40,576]{2,1,0:T(8,128)(2,1)S(1)}, bf16[8,40,576]{2,1,0:T(8,128)(2,1)S(1)}, u32[]{:S(2)}, u32[]{:S(2)}) %collective-permute-start.29) | collective-permute-done | bytes 368672 | tf_op jit(solution)/shard_map/ppermute | solution.py:85
  177.4 3.2 %collective-permute-done.24 = bf16[8,48,576]{2,1,0:T(8,128)(2,1)S(1)} collective-permute-done((bf16[8,48,576]{2,1,0:T(8,128)(2,1)S(1)}, bf16[8,48,576]{2,1,0:T(8,128)(2,1)S(1)}, u32[]{:S(2)}, u32[]{:S(2)}) %collective-permute-start.24) | collective-permute-done | bytes 442400 | tf_op jit(solution)/shard_map/ppermute | solution.py:85
  181.0 1.8 maximum_select_fusion.1
  183.0 1.8 maximum_select_fusion.2
  184.9 2.1 maximum_select_fusion
  187.2 1.1 pad_maximum_fusion
  188.3 6.4 %copy.64 = bf16[4,8,32,4,576]{4,3,2,1,0:T(4,128)(2,1)} copy(bf16[4,8,32,4,576]{4,2,0,3,1:T(8,128)(2,1)S(1)} %bitcast.117) | data formatting | bytes 9437184 | tf_op jit(solution)/shard_map/transpose | solution.py:139
  194.7 9.9 %reshape.133 = bf16[4,256,2304]{2,1,0:T(8,128)(2,1)} reshape(bf16[4,8,32,4,576]{4,3,2,1,0:T(4,128)(2,1)} %copy.64) | data formatting | bytes 9437184 | tf_op jit(solution)/shard_map/reshape | solution.py:140
  204.6 10.5 %fusion.30 = bf16[256,1024]{1,0:T(8,128)(2,1)S(1)} fusion(pred[256,1024]{1,0:T(8,128)(4,1)S(1)} %copy-done.9, bf16[1,4,1024,2304]{3,2,1,0:T(8,128)(2,1)} %param.10, bf16[4,256,2304]{2,1,0:T(8,128)(2,1)} %reshape.133, pred[4]{0:T(512)(128)(4,1)S(1)} %iota_compare_fusion), kind=kOutput, calls=%fused_computation.29 | convolution fusion | flops 4834721792 | bytes 24379396 | tf_op jit(solution)/shard_map/ltd,lfd->tf/dot_general | solution.py:143
  215.2 1.4 fusion.42
  216.6 2.2 slice_bitcast_fusion.4
  218.8 2.9 %copy.65 = f32[2,2,2,64,576]{4,3,2,1,0:T(8,128)} copy(f32[2,2,2,64,576]{3,4,0,2,1:T(8,128)} %get-tuple-element.8) | data formatting | bytes 2359296 | tf_op jit(solution)/shard_map/transpose | solution.py:61
  221.7 2.0 constant_dynamic-slice_fusion.5
  224.2 1.8 copy.66
  226.0 1.2 constant_dynamic-slice_fusion.2
  227.3 1.2 dynamic-slice_add_fusion.7
  230.5 8.2 %collective-permute-done.37 = f32[2,64,576]{2,1,0:T(8,128)S(1)} collective-permute-done((f32[2,64,576]{2,1,0:T(8,128)S(1)}, f32[2,64,576]{2,1,0:T(8,128)S(1)}, u32[]{:S(2)}, u32[]{:S(2)}) %collective-permute-start.37) | collective-permute-done | bytes 294944 | tf_op jit(solution)/shard_map/ppermute | solution.py:70
  240.7 3.8 %collective-permute-done.38 = f32[1,64,576]{2,1,0:T(8,128)S(1)} collective-permute-done((f32[1,64,576]{2,1,0:T(8,128)S(1)}, f32[1,64,576]{2,1,0:T(8,128)S(1)}, u32[]{:S(2)}, u32[]{:S(2)}) %collective-permute-start.38) | collective-permute-done | bytes 147488 | tf_op jit(solution)/shard_map/ppermute | solution.py:70
  (152 shorter events, 31.2 us)
Async XLA Ops:
  0.6 6.1 %copy-start = (s32[4,256,64]{1,2,0:T(8,128)S(1)}, s32[4,256,64]{1,2,0:T(8,128)}, u32[]{:S(2)}) copy-start(s32[4,256,64]{1,2,0:T(8,128)} %param.12) | copy-start | bytes 786436
  1.9 5.5 %collective-permute-start = (bf16[1,64,576]{2,1,0:T(8,128)(2,1)S(1)}, bf16[1,64,576]{2,1,0:T(8,128)(2,1)S(1)}, u32[]{:S(2)}, u32[]{:S(2)}) collective-permute-start(bf16[1,64,576]{2,1,0:T(8,128)(2,1)S(1)} %copy.69), channel_id=1, source_target_pairs={{0,2},{1,3},{2,0},{3,1},{4,6},{5,7},{6,4},{7,5},{8,10},{9,11},{10,... | collective-permute-start | bytes 221192 | tf_op jit(solution)/shard_map/ppermute | solution.py:85
  5.1 4.7 %collective-permute-start.3 = (bf16[1,64,576]{2,1,0:T(8,128)(2,1)S(1)}, bf16[1,64,576]{2,1,0:T(8,128)(2,1)S(1)}, u32[]{:S(2)}, u32[]{:S(2)}) collective-permute-start(bf16[1,64,576]{2,1,0:T(8,128)(2,1)S(1)} %copy.70), channel_id=1, source_target_pairs={{0,4},{4,0},{1,5},{5,1},{2,6},{6,2},{3,7},{7,3},{8,12},{12,8},{9,1... | collective-permute-start | bytes 221192 | tf_op jit(solution)/shard_map/ppermute | solution.py:85
  7.5 5.7 %collective-permute-start.1 = (bf16[2,64,576]{2,1,0:T(8,128)(2,1)S(1)}, bf16[2,64,576]{2,1,0:T(8,128)(2,1)S(1)}, u32[]{:S(2)}, u32[]{:S(2)}) collective-permute-start(bf16[2,64,576]{2,1,0:T(8,128)(2,1)S(1)} %maximum_select_fusion.16), channel_id=1, source_target_pairs={{0,4},{4,0},{1,5},{5,1},{2,6},{6,2},{3,7},{7,3},{8,12},{12,8},{9,1... | collective-permute-start | bytes 442376 | tf_op jit(solution)/shard_map/ppermute | solution.py:85
  9.9 5.4 %collective-permute-start.4 = (bf16[2,64,576]{2,1,0:T(8,128)(2,1)S(1)}, bf16[2,64,576]{2,1,0:T(8,128)(2,1)S(1)}, u32[]{:S(2)}, u32[]{:S(2)}) collective-permute-start(bf16[2,64,576]{2,1,0:T(8,128)(2,1)S(1)} %maximum_select_fusion.17), channel_id=1, source_target_pairs={{0,2},{1,3},{2,0},{3,1},{4,6},{5,7},{6,4},{7,5},{8,10},{9,11},{10,... | collective-permute-start | bytes 442376 | tf_op jit(solution)/shard_map/ppermute | solution.py:85
  13.2 11.7 %collective-permute-start.2 = (bf16[4,64,576]{2,1,0:T(8,128)(2,1)S(1)}, bf16[4,64,576]{2,1,0:T(8,128)(2,1)S(1)}, u32[]{:S(2)}, u32[]{:S(2)}) collective-permute-start(bf16[4,64,576]{2,1,0:T(8,128)(2,1)S(1)} %maximum_select_fusion.11), channel_id=1, source_target_pairs={{0,1},{1,0},{2,3},{3,2},{4,5},{5,4},{6,7},{7,6},{8,9},{9,8},{10,11... | collective-permute-start | bytes 884744 | tf_op jit(solution)/shard_map/ppermute | solution.py:85
  15.4 9.8 %collective-permute-start.5 = (bf16[4,64,576]{2,1,0:T(8,128)(2,1)S(1)}, bf16[4,64,576]{2,1,0:T(8,128)(2,1)S(1)}, u32[]{:S(2)}, u32[]{:S(2)}) collective-permute-start(bf16[4,64,576]{2,1,0:T(8,128)(2,1)S(1)} %maximum_select_fusion.12), channel_id=1, source_target_pairs={{0,1},{1,0},{2,3},{3,2},{4,5},{5,4},{6,7},{7,6},{8,9},{9,8},{10,11... | collective-permute-start | bytes 884744 | tf_op jit(solution)/shard_map/ppermute | solution.py:85
  24.9 1.7 copy-start.8
  25.4 1.2 copy-start.12
  64.0 2.2 copy-start.4
  66.2 5.2 %collective-permute-start.11 = (f32[16,40,576]{2,1,0:T(8,128)}, f32[16,40,576]{2,1,0:T(8,128)}, u32[]{:S(2)}, u32[]{:S(2)}) collective-permute-start(f32[16,40,576]{2,1,0:T(8,128)} %constant_dynamic-slice_fusion.15), channel_id=1, source_target_pairs={{0,1},{1,0},{2,3},{3,2},{4,5},{5,4},{6,7},{7,6},{8,9},{9,8},{10,11... | collective-permute-start | bytes 4423688 | tf_op jit(solution)/shard_map/ppermute | solution.py:70
  67.5 2.4 copy-start.2
  69.4 5.8 %collective-permute-start.16 = (f32[16,40,576]{2,1,0:T(8,128)}, f32[16,40,576]{2,1,0:T(8,128)}, u32[]{:S(2)}, u32[]{:S(2)}) collective-permute-start(f32[16,40,576]{2,1,0:T(8,128)} %constant_dynamic-slice_fusion.10), channel_id=1, source_target_pairs={{0,1},{1,0},{2,3},{3,2},{4,5},{5,4},{6,7},{7,6},{8,9},{9,8},{10,11... | collective-permute-start | bytes 4423688 | tf_op jit(solution)/shard_map/ppermute | solution.py:70
  71.4 5.9 %collective-permute-start.6 = (f32[16,48,576]{2,1,0:T(8,128)}, f32[16,48,576]{2,1,0:T(8,128)}, u32[]{:S(2)}, u32[]{:S(2)}) collective-permute-start(f32[16,48,576]{2,1,0:T(8,128)} %constant_dynamic-slice_fusion.20), channel_id=1, source_target_pairs={{0,1},{1,0},{2,3},{3,2},{4,5},{5,4},{6,7},{7,6},{8,9},{9,8},{10,11... | collective-permute-start | bytes 5308424 | tf_op jit(solution)/shard_map/ppermute | solution.py:70
  73.6 20.7 %collective-permute-start.12 = (f32[8,40,576]{2,1,0:T(8,128)S(1)}, f32[8,40,576]{2,1,0:T(8,128)S(1)}, u32[]{:S(2)}, u32[]{:S(2)}) collective-permute-start(f32[8,40,576]{2,1,0:T(8,128)S(1)} %constant_dynamic-slice_fusion.14), channel_id=1, source_target_pairs={{0,4},{4,0},{1,5},{5,1},{2,6},{6,2},{3,7},{7,3},{8,12},{12,8},{9,1... | collective-permute-start | bytes 2211848 | tf_op jit(solution)/shard_map/ppermute | solution.py:70
  75.2 2.6 %copy-start.3 = (f32[2,2,2,2,2,48,576]{6,5,4,3,2,1,0:T(8,128)S(1)}, f32[2,2,2,2,2,48,576]{6,5,4,3,2,1,0:T(8,128)}, u32[]{:S(2)}) copy-start(f32[2,2,2,2,2,48,576]{6,5,4,3,2,1,0:T(8,128)} %copy-done.2) | copy-start | bytes 10616836
  77.1 20.4 %collective-permute-start.17 = (f32[8,40,576]{2,1,0:T(8,128)S(1)}, f32[8,40,576]{2,1,0:T(8,128)S(1)}, u32[]{:S(2)}, u32[]{:S(2)}) collective-permute-start(f32[8,40,576]{2,1,0:T(8,128)S(1)} %constant_dynamic-slice_fusion.9), channel_id=1, source_target_pairs={{0,2},{1,3},{2,0},{3,1},{4,6},{5,7},{6,4},{7,5},{8,10},{9,11},{10,... | collective-permute-start | bytes 2211848 | tf_op jit(solution)/shard_map/ppermute | solution.py:70
  80.7 35.9 %collective-permute-start.7 = (f32[8,48,576]{2,1,0:T(8,128)}, f32[8,48,576]{2,1,0:T(8,128)}, u32[]{:S(2)}, u32[]{:S(2)}) collective-permute-start(f32[8,48,576]{2,1,0:T(8,128)} %constant_dynamic-slice_fusion.19), channel_id=1, source_target_pairs={{0,8},{8,0},{16,24},{24,16},{1,9},{9,1},{17,25},{25,17},{2,10},{10... | collective-permute-start | bytes 2654216 | tf_op jit(solution)/shard_map/ppermute | solution.py:70
  95.2 11.3 %collective-permute-start.13 = (f32[4,40,576]{2,1,0:T(8,128)}, f32[4,40,576]{2,1,0:T(8,128)S(1)}, u32[]{:S(2)}, u32[]{:S(2)}) collective-permute-start(f32[4,40,576]{2,1,0:T(8,128)} %constant_dynamic-slice_fusion.13), channel_id=1, source_target_pairs={{0,2},{1,3},{2,0},{3,1},{4,6},{5,7},{6,4},{7,5},{8,10},{9,11},{10,... | collective-permute-start | bytes 1105928 | tf_op jit(solution)/shard_map/ppermute | solution.py:70
  97.6 0.9 copy-start.6
  99.3 15.2 %collective-permute-start.18 = (f32[4,40,576]{2,1,0:T(8,128)}, f32[4,40,576]{2,1,0:T(8,128)}, u32[]{:S(2)}, u32[]{:S(2)}) collective-permute-start(f32[4,40,576]{2,1,0:T(8,128)} %constant_dynamic-slice_fusion.8), channel_id=1, source_target_pairs={{0,8},{8,0},{16,24},{24,16},{1,9},{9,1},{17,25},{25,17},{2,10},{10... | collective-permute-start | bytes 1105928 | tf_op jit(solution)/shard_map/ppermute | solution.py:70
  106.6 12.6 %collective-permute-start.14 = (f32[2,40,576]{2,1,0:T(8,128)S(1)}, f32[2,40,576]{2,1,0:T(8,128)S(1)}, u32[]{:S(2)}, u32[]{:S(2)}) collective-permute-start(f32[2,40,576]{2,1,0:T(8,128)S(1)} %constant_dynamic-slice_fusion.12), channel_id=1, source_target_pairs={{0,8},{8,0},{16,24},{24,16},{1,9},{9,1},{17,25},{25,17},{2,10},{10... | collective-permute-start | bytes 552968 | tf_op jit(solution)/shard_map/ppermute | solution.py:70
  115.6 8.0 %collective-permute-start.19 = (f32[2,40,576]{2,1,0:T(8,128)S(1)}, f32[2,40,576]{2,1,0:T(8,128)S(1)}, u32[]{:S(2)}, u32[]{:S(2)}) collective-permute-start(f32[2,40,576]{2,1,0:T(8,128)S(1)} %constant_dynamic-slice_fusion.7), channel_id=1, source_target_pairs={{0,4},{4,0},{1,5},{5,1},{2,6},{6,2},{3,7},{7,3},{8,12},{12,8},{9,1... | collective-permute-start | bytes 552968 | tf_op jit(solution)/shard_map/ppermute | solution.py:70
  118.0 13.9 %collective-permute-start.8 = (f32[4,48,576]{2,1,0:T(8,128)S(1)}, f32[4,48,576]{2,1,0:T(8,128)S(1)}, u32[]{:S(2)}, u32[]{:S(2)}) collective-permute-start(f32[4,48,576]{2,1,0:T(8,128)S(1)} %constant_dynamic-slice_fusion.18), channel_id=1, source_target_pairs={{0,4},{4,0},{1,5},{5,1},{2,6},{6,2},{3,7},{7,3},{8,12},{12,8},{9,1... | collective-permute-start | bytes 1327112 | tf_op jit(solution)/shard_map/ppermute | solution.py:70
  119.2 13.5 %collective-permute-start.15 = (f32[1,40,576]{2,1,0:T(8,128)S(1)}, f32[1,40,576]{2,1,0:T(8,128)S(1)}, u32[]{:S(2)}, u32[]{:S(2)}) collective-permute-start(f32[1,40,576]{2,1,0:T(8,128)S(1)} %constant_dynamic-slice_fusion.11), channel_id=1, source_target_pairs={{0,16},{8,24},{16,0},{24,8},{1,17},{9,25},{17,1},{25,9},{2,18},{10... | collective-permute-start | bytes 276488 | tf_op jit(solution)/shard_map/ppermute | solution.py:70
  123.7 22.5 %copy-start.10 = (bf16[4,32,576]{2,1,0:T(8,128)(2,1)S(1)}, bf16[4,32,576]{2,1,0:T(8,128)(2,1)}, u32[]{:S(2)}) copy-start(bf16[4,32,576]{2,1,0:T(8,128)(2,1)} %param.13) | copy-start | bytes 442372
  123.7 22.5 %copy-start.11 = (f32[4,576]{1,0:T(4,128)S(1)}, f32[4,576]{1,0:T(4,128)}, u32[]{:S(2)}) copy-start(f32[4,576]{1,0:T(4,128)} %param.11) | copy-start | bytes 27652
  123.7 17.2 %collective-permute-start.20 = (f32[1,40,576]{2,1,0:T(8,128)S(1)}, f32[1,40,576]{2,1,0:T(8,128)S(1)}, u32[]{:S(2)}, u32[]{:S(2)}) collective-permute-start(f32[1,40,576]{2,1,0:T(8,128)S(1)} %constant_dynamic-slice_fusion.6), channel_id=1, source_target_pairs={{0,16},{8,24},{16,0},{24,8},{1,17},{9,25},{17,1},{25,9},{2,18},{10... | collective-permute-start | bytes 276488 | tf_op jit(solution)/shard_map/ppermute | solution.py:70
  131.9 6.3 %collective-permute-start.9 = (f32[2,48,576]{2,1,0:T(8,128)S(1)}, f32[2,48,576]{2,1,0:T(8,128)S(1)}, u32[]{:S(2)}, u32[]{:S(2)}) collective-permute-start(f32[2,48,576]{2,1,0:T(8,128)S(1)} %constant_dynamic-slice_fusion.17), channel_id=1, source_target_pairs={{0,2},{1,3},{2,0},{3,1},{4,6},{5,7},{6,4},{7,5},{8,10},{9,11},{10,... | collective-permute-start | bytes 663560 | tf_op jit(solution)/shard_map/ppermute | solution.py:70
  138.3 7.9 %collective-permute-start.10 = (f32[1,48,576]{2,1,0:T(8,128)S(1)}, f32[1,48,576]{2,1,0:T(8,128)S(1)}, u32[]{:S(2)}, u32[]{:S(2)}) collective-permute-start(f32[1,48,576]{2,1,0:T(8,128)S(1)} %constant_dynamic-slice_fusion.16), channel_id=1, source_target_pairs={{0,16},{8,24},{16,0},{24,8},{1,17},{9,25},{17,1},{25,9},{2,18},{10... | collective-permute-start | bytes 331784 | tf_op jit(solution)/shard_map/ppermute | solution.py:70
  146.3 19.0 %copy-start.7 = (bf16[4,32,576]{2,1,0:T(8,128)(2,1)}, bf16[4,32,576]{2,1,0:T(8,128)(2,1)S(1)}, u32[]{:S(2)}) copy-start(bf16[4,32,576]{2,1,0:T(8,128)(2,1)S(1)} %subtract_convert_fusion) | copy-start | bytes 442372
  146.3 5.1 %collective-permute-start.26 = (bf16[1,40,576]{2,1,0:T(8,128)(2,1)S(1)}, bf16[1,40,576]{2,1,0:T(8,128)(2,1)S(1)}, u32[]{:S(2)}, u32[]{:S(2)}) collective-permute-start(bf16[1,40,576]{2,1,0:T(8,128)(2,1)S(1)} %get-tuple-element.10), channel_id=1, source_target_pairs={{0,16},{8,24},{16,0},{24,8},{1,17},{9,25},{17,1},{25,9},{2,18},{10... | collective-permute-start | bytes 138248 | tf_op jit(solution)/shard_map/ppermute | solution.py:85
  147.6 9.2 %collective-permute-start.21 = (bf16[1,48,576]{2,1,0:T(8,128)(2,1)S(1)}, bf16[1,48,576]{2,1,0:T(8,128)(2,1)S(1)}, u32[]{:S(2)}, u32[]{:S(2)}) collective-permute-start(bf16[1,48,576]{2,1,0:T(8,128)(2,1)S(1)} %slice_bitcast_fusion.5), channel_id=1, source_target_pairs={{0,16},{8,24},{16,0},{24,8},{1,17},{9,25},{17,1},{25,9},{2,18},{10... | collective-permute-start | bytes 165896 | tf_op jit(solution)/shard_map/ppermute | solution.py:85
  149.3 6.4 %collective-permute-start.31 = (bf16[1,40,576]{2,1,0:T(8,128)(2,1)S(1)}, bf16[1,40,576]{2,1,0:T(8,128)(2,1)S(1)}, u32[]{:S(2)}, u32[]{:S(2)}) collective-permute-start(bf16[1,40,576]{2,1,0:T(8,128)(2,1)S(1)} %get-tuple-element.11), channel_id=1, source_target_pairs={{0,16},{8,24},{16,0},{24,8},{1,17},{9,25},{17,1},{25,9},{2,18},{10... | collective-permute-start | bytes 138248 | tf_op jit(solution)/shard_map/ppermute | solution.py:85
  151.4 6.9 %collective-permute-start.27 = (bf16[2,40,576]{2,1,0:T(8,128)(2,1)S(1)}, bf16[2,40,576]{2,1,0:T(8,128)(2,1)S(1)}, u32[]{:S(2)}, u32[]{:S(2)}) collective-permute-start(bf16[2,40,576]{2,1,0:T(8,128)(2,1)S(1)} %maximum_select_fusion.19), channel_id=1, source_target_pairs={{0,8},{8,0},{16,24},{24,16},{1,9},{9,1},{17,25},{25,17},{2,10},{10... | collective-permute-start | bytes 276488 | tf_op jit(solution)/shard_map/ppermute | solution.py:85
  155.7 5.8 %collective-permute-start.32 = (bf16[2,40,576]{2,1,0:T(8,128)(2,1)S(1)}, bf16[2,40,576]{2,1,0:T(8,128)(2,1)S(1)}, u32[]{:S(2)}, u32[]{:S(2)}) collective-permute-start(bf16[2,40,576]{2,1,0:T(8,128)(2,1)S(1)} %maximum_select_fusion.20), channel_id=1, source_target_pairs={{0,4},{4,0},{1,5},{5,1},{2,6},{6,2},{3,7},{7,3},{8,12},{12,8},{9,1... | collective-permute-start | bytes 276488 | tf_op jit(solution)/shard_map/ppermute | solution.py:85
  156.8 8.4 %collective-permute-start.22 = (bf16[2,48,576]{2,1,0:T(8,128)(2,1)S(1)}, bf16[2,48,576]{2,1,0:T(8,128)(2,1)S(1)}, u32[]{:S(2)}, u32[]{:S(2)}) collective-permute-start(bf16[2,48,576]{2,1,0:T(8,128)(2,1)S(1)} %maximum_select_fusion.18), channel_id=1, source_target_pairs={{0,2},{1,3},{2,0},{3,1},{4,6},{5,7},{6,4},{7,5},{8,10},{9,11},{10,... | collective-permute-start | bytes 331784 | tf_op jit(solution)/shard_map/ppermute | solution.py:85
  158.4 9.1 %collective-permute-start.28 = (bf16[4,40,576]{2,1,0:T(8,128)(2,1)S(1)}, bf16[4,40,576]{2,1,0:T(8,128)(2,1)S(1)}, u32[]{:S(2)}, u32[]{:S(2)}) collective-permute-start(bf16[4,40,576]{2,1,0:T(8,128)(2,1)S(1)} %maximum_select_fusion.14), channel_id=1, source_target_pairs={{0,2},{1,3},{2,0},{3,1},{4,6},{5,7},{6,4},{7,5},{8,10},{9,11},{10,... | collective-permute-start | bytes 552968 | tf_op jit(solution)/shard_map/ppermute | solution.py:85
  161.6 7.4 %collective-permute-start.33 = (bf16[4,40,576]{2,1,0:T(8,128)(2,1)S(1)}, bf16[4,40,576]{2,1,0:T(8,128)(2,1)S(1)}, u32[]{:S(2)}, u32[]{:S(2)}) collective-permute-start(bf16[4,40,576]{2,1,0:T(8,128)(2,1)S(1)} %maximum_select_fusion.15), channel_id=1, source_target_pairs={{0,8},{8,0},{16,24},{24,16},{1,9},{9,1},{17,25},{25,17},{2,10},{10... | collective-permute-start | bytes 552968 | tf_op jit(solution)/shard_map/ppermute | solution.py:85
  165.3 6.3 %collective-permute-start.23 = (bf16[4,48,576]{2,1,0:T(8,128)(2,1)S(1)}, bf16[4,48,576]{2,1,0:T(8,128)(2,1)S(1)}, u32[]{:S(2)}, u32[]{:S(2)}) collective-permute-start(bf16[4,48,576]{2,1,0:T(8,128)(2,1)S(1)} %maximum_select_fusion.13), channel_id=1, source_target_pairs={{0,4},{4,0},{1,5},{5,1},{2,6},{6,2},{3,7},{7,3},{8,12},{12,8},{9,1... | collective-permute-start | bytes 663560 | tf_op jit(solution)/shard_map/ppermute | solution.py:85
  167.6 8.4 %collective-permute-start.29 = (bf16[8,40,576]{2,1,0:T(8,128)(2,1)S(1)}, bf16[8,40,576]{2,1,0:T(8,128)(2,1)S(1)}, u32[]{:S(2)}, u32[]{:S(2)}) collective-permute-start(bf16[8,40,576]{2,1,0:T(8,128)(2,1)S(1)} %maximum_select_fusion.9), channel_id=1, source_target_pairs={{0,4},{4,0},{1,5},{5,1},{2,6},{6,2},{3,7},{7,3},{8,12},{12,8},{9,1... | collective-permute-start | bytes 1105928 | tf_op jit(solution)/shard_map/ppermute | solution.py:85
  169.1 8.0 %collective-permute-start.34 = (bf16[8,40,576]{2,1,0:T(8,128)(2,1)S(1)}, bf16[8,40,576]{2,1,0:T(8,128)(2,1)S(1)}, u32[]{:S(2)}, u32[]{:S(2)}) collective-permute-start(bf16[8,40,576]{2,1,0:T(8,128)(2,1)S(1)} %maximum_select_fusion.10), channel_id=1, source_target_pairs={{0,2},{1,3},{2,0},{3,1},{4,6},{5,7},{6,4},{7,5},{8,10},{9,11},{10,... | collective-permute-start | bytes 1105928 | tf_op jit(solution)/shard_map/ppermute | solution.py:85
  171.7 8.9 %collective-permute-start.24 = (bf16[8,48,576]{2,1,0:T(8,128)(2,1)S(1)}, bf16[8,48,576]{2,1,0:T(8,128)(2,1)S(1)}, u32[]{:S(2)}, u32[]{:S(2)}) collective-permute-start(bf16[8,48,576]{2,1,0:T(8,128)(2,1)S(1)} %maximum_select_fusion.8), channel_id=1, source_target_pairs={{0,8},{8,0},{16,24},{24,16},{1,9},{9,1},{17,25},{25,17},{2,10},{10... | collective-permute-start | bytes 1327112 | tf_op jit(solution)/shard_map/ppermute | solution.py:85
  176.2 4.8 %collective-permute-start.30 = (bf16[16,40,576]{2,1,0:T(8,128)(2,1)S(1)}, bf16[16,40,576]{2,1,0:T(8,128)(2,1)}, u32[]{:S(2)}, u32[]{:S(2)}) collective-permute-start(bf16[16,40,576]{2,1,0:T(8,128)(2,1)S(1)} %maximum_select_fusion.4), channel_id=1, source_target_pairs={{0,1},{1,0},{2,3},{3,2},{4,5},{5,4},{6,7},{7,6},{8,9},{9,8},{10,11... | collective-permute-start | bytes 2211848 | tf_op jit(solution)/shard_map/ppermute | solution.py:85
  177.3 5.6 %collective-permute-start.35 = (bf16[16,40,576]{2,1,0:T(8,128)(2,1)S(1)}, bf16[16,40,576]{2,1,0:T(8,128)(2,1)}, u32[]{:S(2)}, u32[]{:S(2)}) collective-permute-start(bf16[16,40,576]{2,1,0:T(8,128)(2,1)S(1)} %maximum_select_fusion.5), channel_id=1, source_target_pairs={{0,1},{1,0},{2,3},{3,2},{4,5},{5,4},{6,7},{7,6},{8,9},{9,8},{10,11... | collective-permute-start | bytes 2211848 | tf_op jit(solution)/shard_map/ppermute | solution.py:85
  180.9 4.0 %collective-permute-start.25 = (bf16[16,48,576]{2,1,0:T(8,128)(2,1)S(1)}, bf16[16,48,576]{2,1,0:T(8,128)(2,1)}, u32[]{:S(2)}, u32[]{:S(2)}) collective-permute-start(bf16[16,48,576]{2,1,0:T(8,128)(2,1)S(1)} %maximum_select_fusion.3), channel_id=1, source_target_pairs={{0,1},{1,0},{2,3},{3,2},{4,5},{5,4},{6,7},{7,6},{8,9},{9,8},{10,11... | collective-permute-start | bytes 2654216 | tf_op jit(solution)/shard_map/ppermute | solution.py:85
  194.7 9.9 %copy-start.9 = (pred[256,1024]{1,0:T(8,128)(4,1)S(1)}, pred[256,1024]{1,0:T(8,128)(4,1)}, u32[]{:S(2)}) copy-start(pred[256,1024]{1,0:T(8,128)(4,1)} %copy-done.8) | copy-start | bytes 786436
  194.7 20.5 %slice-start = ((s8[4718592]{0:T(1024)(128)(4,1)}), s8[524288]{0:T(1024)(128)(4,1)S(1)}, s32[]{:S(2)}) async-start(s8[4718592]{0:T(1024)(128)(4,1)} %bitcast.143), calls=%async_computation | async-start | bytes 1048576
  204.6 10.5 %slice-start.1 = ((s8[4718592]{0:T(1024)(128)(4,1)}), s8[4194304]{0:T(1024)(128)(4,1)S(1)}, s32[]{:S(2)}) async-start(s8[4718592]{0:T(1024)(128)(4,1)} %bitcast.143), calls=%async_computation.1 | async-start | bytes 8388608
  223.7 3.6 %collective-permute-start.36 = (f32[4,64,576]{2,1,0:T(8,128)}, f32[4,64,576]{2,1,0:T(8,128)S(1)}, u32[]{:S(2)}, u32[]{:S(2)}) collective-permute-start(f32[4,64,576]{2,1,0:T(8,128)} %constant_dynamic-slice_fusion.5), channel_id=1, source_target_pairs={{0,1},{1,0},{2,3},{3,2},{4,5},{5,4},{6,7},{7,6},{8,9},{9,8},{10,11... | collective-permute-start | bytes 1769480 | tf_op jit(solution)/shard_map/ppermute | solution.py:70
  226.0 3.6 %copy-start.5 = (f32[2,2,2,64,576]{4,3,2,1,0:T(8,128)S(1)}, f32[2,2,2,64,576]{4,3,2,1,0:T(8,128)}, u32[]{:S(2)}) copy-start(f32[2,2,2,64,576]{4,3,2,1,0:T(8,128)} %copy.66) | copy-start | bytes 3538948
  227.2 2.3 collective-permute-start.39
  228.5 10.2 %collective-permute-start.37 = (f32[2,64,576]{2,1,0:T(8,128)S(1)}, f32[2,64,576]{2,1,0:T(8,128)S(1)}, u32[]{:S(2)}, u32[]{:S(2)}) collective-permute-start(f32[2,64,576]{2,1,0:T(8,128)S(1)} %constant_dynamic-slice_fusion.4), channel_id=1, source_target_pairs={{0,4},{4,0},{1,5},{5,1},{2,6},{6,2},{3,7},{7,3},{8,12},{12,8},{9,1... | collective-permute-start | bytes 884744 | tf_op jit(solution)/shard_map/ppermute | solution.py:70
  229.6 16.4 %copy-start.1 = (s32[4,256,64]{1,2,0:T(8,128)S(1)}, s32[4,256,64]{1,2,0:T(8,128)}, u32[]{:S(2)}) copy-start(s32[4,256,64]{1,2,0:T(8,128)} %param.12) | copy-start | bytes 786436
  229.7 9.9 %collective-permute-start.40 = (f32[2,64,576]{2,1,0:T(8,128)S(1)}, f32[2,64,576]{2,1,0:T(8,128)S(1)}, u32[]{:S(2)}, u32[]{:S(2)}) collective-permute-start(f32[2,64,576]{2,1,0:T(8,128)S(1)} %constant_dynamic-slice_fusion.1), channel_id=1, source_target_pairs={{0,2},{1,3},{2,0},{3,1},{4,6},{5,7},{6,4},{7,5},{8,10},{9,11},{10,... | collective-permute-start | bytes 884744 | tf_op jit(solution)/shard_map/ppermute | solution.py:70
  238.7 5.8 %collective-permute-start.38 = (f32[1,64,576]{2,1,0:T(8,128)S(1)}, f32[1,64,576]{2,1,0:T(8,128)S(1)}, u32[]{:S(2)}, u32[]{:S(2)}) collective-permute-start(f32[1,64,576]{2,1,0:T(8,128)S(1)} %constant_dynamic-slice_fusion.3), channel_id=1, source_target_pairs={{0,2},{1,3},{2,0},{3,1},{4,6},{5,7},{6,4},{7,5},{8,10},{9,11},{10,... | collective-permute-start | bytes 442376 | tf_op jit(solution)/shard_map/ppermute | solution.py:70
  239.6 5.5 %collective-permute-start.41 = (f32[1,64,576]{2,1,0:T(8,128)S(1)}, f32[1,64,576]{2,1,0:T(8,128)S(1)}, u32[]{:S(2)}, u32[]{:S(2)}) collective-permute-start(f32[1,64,576]{2,1,0:T(8,128)S(1)} %constant_dynamic-slice_fusion), channel_id=1, source_target_pairs={{0,4},{4,0},{1,5},{5,1},{2,6},{6,2},{3,7},{7,3},{8,12},{12,8},{9,1... | collective-permute-start | bytes 442376 | tf_op jit(solution)/shard_map/ppermute | solution.py:70

commit v5 on v4

--- a/solution.py
+++ b/solution.py
@@ -49,7 +49,7 @@
     return [(sum(sizes[:i]), sizes[i]) for i in range(parts)]
 
 
-def reduce_scatter(blocks, axes):
+def reduce_scatter(blocks, axes, wire):
     labels, prefix, orders, suffix = plan(axes)
     n, rows, cols = blocks.shape
     nb = len(labels)
@@ -67,7 +67,8 @@
             half = parts[p].shape[0] // 2
             keep = lax.dynamic_slice_in_dim(parts[p], own * half, half, 0)
             send = lax.dynamic_slice_in_dim(parts[p], (1 - own) * half, half, 0)
-            parts[p] = keep + lax.ppermute(send, axis, partner(axis, bit))
+            recv = lax.ppermute(send.astype(wire), axis, partner(axis, bit))
+            parts[p] = keep + recv.astype(keep.dtype)
     return jnp.concatenate([xp[0] for xp in parts], axis=0)
 
 
@@ -130,7 +131,7 @@
         .transpose(1, 3, 0, 2, 4)
         .reshape(slots * feat_parts, layer_count * slot_rows, cols)
     )
-    recon = reduce_scatter(blocks, EVERY).reshape(layer_count, slot_rows, cols)
+    recon = reduce_scatter(blocks, EVERY, jnp.bfloat16).reshape(layer_count, slot_rows, cols)
     recon = recon + decoder_bias[:, None, :]
     error = (recon - target.astype(jnp.float32)).astype(jnp.bfloat16)
     pieces = all_gather(error.reshape(layer_count * slot_rows, cols), EVERY)
@@ -150,7 +151,7 @@
         .transpose(0, 2, 1, 3)
         .reshape(2 * feat_parts, half_rows, cols)
     )
-    grad_sum = reduce_scatter(grad_blocks, PLANE)
+    grad_sum = reduce_scatter(grad_blocks, PLANE, jnp.bfloat16)
     return (error, grad_sum.astype(jnp.bfloat16)[None])
 
 

time: 247 us -> 211 us (0.85)
  waiting for transfers between devices: 74 us -> 42.6 us
  local copies, waits for them, and re-layouts: 61.3 us -> 55.9 us
  starting transfers between devices: 51.5 us -> 55.7 us
  other arithmetic: 28.3 us -> 24.7 us
    ppermute x21, waiting for transfers between devices: 55.4 us -> 26 us  [reduce_scatter(): recv = lax.ppermute(send.astype(wire), axis, partner(axis, bit))]
    dynamic_slice x21 -> x0, local copies, waits for them, and re-layouts: 10.6 us -> none  [reduce_scatter(): send = lax.dynamic_slice_in_dim(parts[p], (1 - own) * half, half, 0)]
    convert_element_type x0 -> x21, local copies, waits for them, and re-layouts: none -> 6.03 us  [reduce_scatter(): recv = lax.ppermute(send.astype(wire), axis, partner(axis, bit))]
    add x16, other arithmetic: 9.8 us -> 6.28 us  [reduce_scatter(): parts[p] = keep + recv.astype(keep.dtype)]
    ppermute x21, starting transfers between devices: 23.8 us -> 26.5 us  [reduce_scatter(): recv = lax.ppermute(send.astype(wire), axis, partner(axis, bit))]
  transfers between devices with their start and end apart: 42 -> 42, of which waited for: 24 -> 21; matrix products, arithmetic and copies ran while one was open for 14% -> 14% of each run, Pallas kernels for 0% -> 0%
where the time goes in v5:
time: 211 us; the launch traced here: 210 us
  local copies, waits for them, and re-layouts  55.9 us (26%)
  starting transfers between devices  55.7 us (26%)
  waiting for transfers between devices  42.6 us (20%)
  matrix products  29.6 us (14%)
  other arithmetic  24.7 us (12%)
    ppermute x21, starting transfers between devices, all_gather(): recv = lax.ppermute(parts[p], axis, partner(axis, bit))  29.2 us
    ppermute x21, starting transfers between devices, reduce_scatter(): recv = lax.ppermute(send.astype(wire), axis, partner(axis, bit))  26.5 us
    ppermute x21, waiting for transfers between devices, reduce_scatter(): recv = lax.ppermute(send.astype(wire), axis, partner(axis, bit))  26 us
    reshape x2, local copies, waits for them, and re-layouts, local(): partial_value.reshape(layer_count, slots, slot_rows, feat_parts, cols)  18.7 us
    ppermute x21, waiting for transfers between devices, all_gather(): recv = lax.ppermute(parts[p], axis, partner(axis, bit))  16.5 us
    dot_general x1, matrix products, local(): jnp.einsum('tf,lfd->ltd', acts, decoder[0], preferred_element_type=jnp.fl...  13.9 us
    dot_general x1, matrix products, local(): jnp.einsum('ltd,lfd->tf', kept, decoder[0], preferred_element_type=jnp.fl...  10.5 us
    reshape x1, local copies, waits for them, and re-layouts, local(): piece = pieces.reshape(slots, feat_parts, layer_count, slot_rows, cols).t...  9.91 us
  transfers between devices with their start and end apart: 42, of which 21 were waited for; matrix products, arithmetic and copies ran while one was open for 14% of the time, Pallas kernels for 0%

profile of v5, /device:TPU:0, one launch (start us, length us, event | category | flops | bytes accessed | tf_op | source)
XLA Modules:
  0.0 209.8 jit_solution(4130751881605508601)
XLA Ops:
  0.6 1.1 fusion.41
  1.9 3.1 %collective-permute-start = (bf16[1,64,576]{2,1,0:T(8,128)(2,1)S(1)}, bf16[1,64,576]{2,1,0:T(8,128)(2,1)S(1)}, u32[]{:S(2)}, u32[]{:S(2)}) collective-permute-start(bf16[1,64,576]{2,1,0:T(8,128)(2,1)S(1)} %copy.69), channel_id=1, source_target_pairs={{0,2},{1,3},{2,0},{3,1},{4,6},{5,7},{6,4},{7,5},{8,10},{9,11},{10,... | collective-permute-start | bytes 221192 | tf_op jit(solution)/shard_map/ppermute | solution.py:86
  5.1 1.6 collective-permute-start.3
  7.5 2.0 collective-permute-start.1
  9.9 1.2 collective-permute-start.4
  11.2 1.9 collective-permute-done.1
  13.3 2.0 collective-permute-done.4
  15.5 9.4 %compare_reduce_fusion = pred[256,1024]{1,0:T(8,128)(4,1)S(1)} fusion(s32[1024]{0:T(1024)S(1)} %iota_add_fusion, s32[256,64]{1,0:T(8,128)S(1)} %copy.51), kind=kLoop, calls=%fused_computation | loop fusion | flops 33292288 | bytes 331776 | tf_op jit(solution)/shard_map/reduce_or | solution.py:122
  26.6 3.8 %fusion.35 = bf16[256,1024,1]{1,0,2:T(8,128)(2,1)S(1)} fusion(pred[256,1024]{1,0:T(8,128)(4,1)S(1)} %compare_reduce_fusion, bf16[1,2304,1024]{2,1,0:T(8,128)(2,1)} %param.8, bf16[288,8,2,128]{3,2,1,0:T(2,128)(2,1)S(1)} %bitcast.140, f32[1024]{0:T(1024)S(1)} %bitcast.146), kind=kOutput, calls=%fused_computation.33 | convolution fusion | flops 1208745984 | bytes 6688768 | tf_op jit(solution)/shard_map/dot_general | solution.py:118
  30.4 13.9 %select_bitcast_fusion = f32[4,256,2304]{2,1,0:T(8,128)} fusion(bf16[256,1024,1]{1,0,2:T(8,128)(2,1)S(1)} %fusion.35, bf16[1,4,1024,2304]{3,2,1,0:T(8,128)(2,1)} %param.10, pred[4]{0:T(512)(128)(4,1)S(1)} %iota_compare_fusion), kind=kOutput, calls=%fused_computation.5 | convolution fusion | flops 4834197504 | bytes 28835844 | tf_op jit(solution)/shard_map/tf,lfd->ltd/dot_general | solution.py:127
  44.3 13.2 %reshape.123 = f32[4,8,32,4,576]{4,3,2,1,0:T(4,128)} reshape(f32[4,256,2304]{2,1,0:T(8,128)} %select_bitcast_fusion) | data formatting | bytes 18874368 | tf_op jit(solution)/shard_map/reshape | solution.py:130
  57.4 5.5 %copy.57 = f32[4,8,32,4,576]{4,2,0,3,1:T(8,128)S(1)} copy(f32[4,8,32,4,576]{4,3,2,1,0:T(4,128)} %reshape.123) | data formatting | bytes 18874368 | tf_op jit(solution)/shard_map/reshape | solution.py:130
  68.3 1.9 copy-done.2
  71.3 1.8 convert_add_fusion.2
  73.2 1.6 collective-permute-start.12
  74.8 1.3 convert_add_fusion.1
  76.8 1.5 convert_add_fusion
  78.3 1.6 collective-permute-start.7
  79.9 5.2 %collective-permute-done.12 = bf16[8,40,576]{2,1,0:T(8,128)(2,1)S(1)} collective-permute-done((bf16[8,40,576]{2,1,0:T(8,128)(2,1)S(1)}, bf16[8,40,576]{2,1,0:T(8,128)(2,1)S(1)}, u32[]{:S(2)}, u32[]{:S(2)}) %collective-permute-start.12) | collective-permute-done | bytes 368672 | tf_op jit(solution)/shard_map/ppermute | solution.py:70
  85.2 1.2 collective-permute-start.13
  86.5 1.7 collective-permute-done.17
  88.2 1.5 collective-permute-start.18
  89.8 2.4 %collective-permute-done.13 = bf16[4,40,576]{2,1,0:T(8,128)(2,1)S(1)} collective-permute-done((bf16[4,40,576]{2,1,0:T(8,128)(2,1)S(1)}, bf16[4,40,576]{2,1,0:T(8,128)(2,1)S(1)}, u32[]{:S(2)}, u32[]{:S(2)}) %collective-permute-start.13) | collective-permute-done | bytes 184352 | tf_op jit(solution)/shard_map/ppermute | solution.py:70
  92.3 1.6 collective-permute-start.14
  93.9 2.8 %collective-permute-done.18 = bf16[4,40,576]{2,1,0:T(8,128)(2,1)S(1)} collective-permute-done((bf16[4,40,576]{2,1,0:T(8,128)(2,1)S(1)}, bf16[4,40,576]{2,1,0:T(8,128)(2,1)S(1)}, u32[]{:S(2)}, u32[]{:S(2)}) %collective-permute-start.18) | collective-permute-done | bytes 184352 | tf_op jit(solution)/shard_map/ppermute | solution.py:70
  96.8 1.2 collective-permute-start.19
  99.2 2.7 %collective-permute-start.15 = (bf16[1,40,576]{2,1,0:T(8,128)(2,1)S(1)}, bf16[1,40,576]{2,1,0:T(8,128)(2,1)S(1)}, u32[]{:S(2)}, u32[]{:S(2)}) collective-permute-start(bf16[1,40,576]{2,1,0:T(8,128)(2,1)S(1)} %dynamic-slice_convert_fusion.20), channel_id=1, source_target_pairs={{0,16},{8,24},{16,0},{24,8},{1,17},{9,25},{17,1},{25,9},{2,18},{10... | collective-permute-start | bytes 138248 | tf_op jit(solution)/shard_map/ppermute | solution.py:70
  102.5 2.7 %collective-permute-start.20 = (bf16[1,40,576]{2,1,0:T(8,128)(2,1)S(1)}, bf16[1,40,576]{2,1,0:T(8,128)(2,1)S(1)}, u32[]{:S(2)}, u32[]{:S(2)}) collective-permute-start(bf16[1,40,576]{2,1,0:T(8,128)(2,1)S(1)} %dynamic-slice_convert_fusion.19), channel_id=1, source_target_pairs={{0,16},{8,24},{16,0},{24,8},{1,17},{9,25},{17,1},{25,9},{2,18},{10... | collective-permute-start | bytes 138248 | tf_op jit(solution)/shard_map/ppermute | solution.py:70
  105.2 1.6 collective-permute-start.9
  106.8 3.3 %collective-permute-done.9 = bf16[2,48,576]{2,1,0:T(8,128)(2,1)S(1)} collective-permute-done((bf16[2,48,576]{2,1,0:T(8,128)(2,1)S(1)}, bf16[2,48,576]{2,1,0:T(8,128)(2,1)S(1)}, u32[]{:S(2)}, u32[]{:S(2)}) %collective-permute-start.9) | collective-permute-done | bytes 110624 | tf_op jit(solution)/shard_map/ppermute | solution.py:70
  110.2 2.6 %collective-permute-start.10 = (bf16[1,48,576]{2,1,0:T(8,128)(2,1)S(1)}, bf16[1,48,576]{2,1,0:T(8,128)(2,1)S(1)}, u32[]{:S(2)}, u32[]{:S(2)}) collective-permute-start(bf16[1,48,576]{2,1,0:T(8,128)(2,1)S(1)} %dynamic-slice_convert_fusion.18), channel_id=1, source_target_pairs={{0,16},{8,24},{16,0},{24,8},{1,17},{9,25},{17,1},{25,9},{2,18},{10... | collective-permute-start | bytes 165896 | tf_op jit(solution)/shard_map/ppermute | solution.py:70
  112.8 2.6 %collective-permute-done.10 = bf16[1,48,576]{2,1,0:T(8,128)(2,1)S(1)} collective-permute-done((bf16[1,48,576]{2,1,0:T(8,128)(2,1)S(1)}, bf16[1,48,576]{2,1,0:T(8,128)(2,1)S(1)}, u32[]{:S(2)}, u32[]{:S(2)}) %collective-permute-start.10) | collective-permute-done | bytes 55328 | tf_op jit(solution)/shard_map/ppermute | solution.py:70
  115.5 3.2 %collective-permute-start.26 = (bf16[1,40,576]{2,1,0:T(8,128)(2,1)S(1)}, bf16[1,40,576]{2,1,0:T(8,128)(2,1)S(1)}, u32[]{:S(2)}, u32[]{:S(2)}) collective-permute-start(bf16[1,40,576]{2,1,0:T(8,128)(2,1)S(1)} %get-tuple-element.10), channel_id=1, source_target_pairs={{0,16},{8,24},{16,0},{24,8},{1,17},{9,25},{17,1},{25,9},{2,18},{10... | collective-permute-start | bytes 138248 | tf_op jit(solution)/shard_map/ppermute | solution.py:86
  118.9 2.8 %collective-permute-start.31 = (bf16[1,40,576]{2,1,0:T(8,128)(2,1)S(1)}, bf16[1,40,576]{2,1,0:T(8,128)(2,1)S(1)}, u32[]{:S(2)}, u32[]{:S(2)}) collective-permute-start(bf16[1,40,576]{2,1,0:T(8,128)(2,1)S(1)} %get-tuple-element.11), channel_id=1, source_target_pairs={{0,16},{8,24},{16,0},{24,8},{1,17},{9,25},{17,1},{25,9},{2,18},{10... | collective-permute-start | bytes 138248 | tf_op jit(solution)/shard_map/ppermute | solution.py:86
  121.8 3.3 %collective-permute-start.27 = (bf16[2,40,576]{2,1,0:T(8,128)(2,1)S(1)}, bf16[2,40,576]{2,1,0:T(8,128)(2,1)S(1)}, u32[]{:S(2)}, u32[]{:S(2)}) collective-permute-start(bf16[2,40,576]{2,1,0:T(8,128)(2,1)S(1)} %maximum_select_fusion.19), channel_id=1, source_target_pairs={{0,8},{8,0},{16,24},{24,16},{1,9},{9,1},{17,25},{25,17},{2,10},{10... | collective-permute-start | bytes 276488 | tf_op jit(solution)/shard_map/ppermute | solution.py:86
  125.1 1.2 collective-permute-start.32
  126.3 1.5 collective-permute-start.22
  128.2 1.6 collective-permute-start.28
  131.0 2.7 %collective-permute-start.33 = (bf16[4,40,576]{2,1,0:T(8,128)(2,1)S(1)}, bf16[4,40,576]{2,1,0:T(8,128)(2,1)S(1)}, u32[]{:S(2)}, u32[]{:S(2)}) collective-permute-start(bf16[4,40,576]{2,1,0:T(8,128)(2,1)S(1)} %maximum_select_fusion.15), channel_id=1, source_target_pairs={{0,8},{8,0},{16,24},{24,16},{1,9},{9,1},{17,25},{25,17},{2,10},{10... | collective-permute-start | bytes 552968 | tf_op jit(solution)/shard_map/ppermute | solution.py:86
  133.7 1.2 collective-permute-start.23
  134.9 1.5 collective-permute-done.28
  137.5 1.8 collective-permute-done.33
  140.4 1.6 collective-permute-start.24
  142.0 2.6 %collective-permute-done.29 = bf16[8,40,576]{2,1,0:T(8,128)(2,1)S(1)} collective-permute-done((bf16[8,40,576]{2,1,0:T(8,128)(2,1)S(1)}, bf16[8,40,576]{2,1,0:T(8,128)(2,1)S(1)}, u32[]{:S(2)}, u32[]{:S(2)}) %collective-permute-start.29) | collective-permute-done | bytes 368672 | tf_op jit(solution)/shard_map/ppermute | solution.py:86
  144.9 2.6 %collective-permute-done.34 = bf16[8,40,576]{2,1,0:T(8,128)(2,1)S(1)} collective-permute-done((bf16[8,40,576]{2,1,0:T(8,128)(2,1)S(1)}, bf16[8,40,576]{2,1,0:T(8,128)(2,1)S(1)}, u32[]{:S(2)}, u32[]{:S(2)}) %collective-permute-start.34) | collective-permute-done | bytes 368672 | tf_op jit(solution)/shard_map/ppermute | solution.py:86
  147.8 1.5 collective-permute-done.24
  149.7 1.8 maximum_select_fusion.1
  151.6 1.8 maximum_select_fusion.2
  153.6 2.1 maximum_select_fusion
  157.0 6.4 %copy.64 = bf16[4,8,32,4,576]{4,3,2,1,0:T(4,128)(2,1)} copy(bf16[4,8,32,4,576]{4,2,0,3,1:T(8,128)(2,1)S(1)} %bitcast.117) | data formatting | bytes 9437184 | tf_op jit(solution)/shard_map/transpose | solution.py:140
  163.4 9.9 %reshape.133 = bf16[4,256,2304]{2,1,0:T(8,128)(2,1)} reshape(bf16[4,8,32,4,576]{4,3,2,1,0:T(4,128)(2,1)} %copy.64) | data formatting | bytes 9437184 | tf_op jit(solution)/shard_map/reshape | solution.py:141
  173.3 10.5 %fusion.30 = bf16[256,1024]{1,0:T(8,128)(2,1)S(1)} fusion(pred[256,1024]{1,0:T(8,128)(4,1)S(1)} %copy-done.8, bf16[1,4,1024,2304]{3,2,1,0:T(8,128)(2,1)} %param.10, bf16[4,256,2304]{2,1,0:T(8,128)(2,1)} %reshape.133, pred[4]{0:T(512)(128)(4,1)S(1)} %iota_compare_fusion), kind=kOutput, calls=%fused_computation.32 | convolution fusion | flops 4834721792 | bytes 24379396 | tf_op jit(solution)/shard_map/ltd,lfd->tf/dot_general | solution.py:144
  183.9 1.4 fusion.42
  185.3 2.2 %slice_bitcast_fusion.4 = (f32[2,2,2,64,576]{3,4,0,2,1:T(8,128)}, f32[2,2,2,64,576]{3,4,0,1,2:T(8,128)S(1)}) fusion(f32[2,2,2,128,576]{3,4,2,1,0:T(8,128)S(1)} %bitcast.124), kind=kLoop, calls=%fused_computation.15 | loop fusion | bytes 4718592 | tf_op jit(solution)/shard_map/transpose | solution.py:61
  187.5 2.9 %copy.65 = f32[2,2,2,64,576]{4,3,2,1,0:T(8,128)} copy(f32[2,2,2,64,576]{3,4,0,2,1:T(8,128)} %get-tuple-element.8) | data formatting | bytes 2359296 | tf_op jit(solution)/shard_map/transpose | solution.py:61
  190.4 1.1 dynamic-slice_convert_fusion.7
  192.0 1.8 copy.66
  193.8 1.2 dynamic-slice_convert_fusion.6
  195.2 1.1 convert_add_fusion.7
  197.5 1.4 collective-permute-start.40
  198.9 4.1 %collective-permute-done.37 = bf16[2,64,576]{2,1,0:T(8,128)(2,1)S(1)} collective-permute-done((bf16[2,64,576]{2,1,0:T(8,128)(2,1)S(1)}, bf16[2,64,576]{2,1,0:T(8,128)(2,1)S(1)}, u32[]{:S(2)}, u32[]{:S(2)}) %collective-permute-start.37) | collective-permute-done | bytes 147488 | tf_op jit(solution)/shard_map/ppermute | solution.py:70
  203.1 1.4 collective-permute-start.38
  205.6 2.0 collective-permute-done.38
  207.6 1.4 collective-permute-done.41
  (150 shorter events, 23.3 us)
Async XLA Ops:
  0.6 6.1 %copy-start = (s32[4,256,64]{1,2,0:T(8,128)S(1)}, s32[4,256,64]{1,2,0:T(8,128)}, u32[]{:S(2)}) copy-start(s32[4,256,64]{1,2,0:T(8,128)} %param.12) | copy-start | bytes 786436
  1.9 5.5 %collective-permute-start = (bf16[1,64,576]{2,1,0:T(8,128)(2,1)S(1)}, bf16[1,64,576]{2,1,0:T(8,128)(2,1)S(1)}, u32[]{:S(2)}, u32[]{:S(2)}) collective-permute-start(bf16[1,64,576]{2,1,0:T(8,128)(2,1)S(1)} %copy.69), channel_id=1, source_target_pairs={{0,2},{1,3},{2,0},{3,1},{4,6},{5,7},{6,4},{7,5},{8,10},{9,11},{10,... | collective-permute-start | bytes 221192 | tf_op jit(solution)/shard_map/ppermute | solution.py:86
  5.1 4.7 %collective-permute-start.3 = (bf16[1,64,576]{2,1,0:T(8,128)(2,1)S(1)}, bf16[1,64,576]{2,1,0:T(8,128)(2,1)S(1)}, u32[]{:S(2)}, u32[]{:S(2)}) collective-permute-start(bf16[1,64,576]{2,1,0:T(8,128)(2,1)S(1)} %copy.70), channel_id=1, source_target_pairs={{0,4},{4,0},{1,5},{5,1},{2,6},{6,2},{3,7},{7,3},{8,12},{12,8},{9,1... | collective-permute-start | bytes 221192 | tf_op jit(solution)/shard_map/ppermute | solution.py:86
  7.5 5.7 %collective-permute-start.1 = (bf16[2,64,576]{2,1,0:T(8,128)(2,1)S(1)}, bf16[2,64,576]{2,1,0:T(8,128)(2,1)S(1)}, u32[]{:S(2)}, u32[]{:S(2)}) collective-permute-start(bf16[2,64,576]{2,1,0:T(8,128)(2,1)S(1)} %maximum_select_fusion.16), channel_id=1, source_target_pairs={{0,4},{4,0},{1,5},{5,1},{2,6},{6,2},{3,7},{7,3},{8,12},{12,8},{9,1... | collective-permute-start | bytes 442376 | tf_op jit(solution)/shard_map/ppermute | solution.py:86
  9.9 5.4 %collective-permute-start.4 = (bf16[2,64,576]{2,1,0:T(8,128)(2,1)S(1)}, bf16[2,64,576]{2,1,0:T(8,128)(2,1)S(1)}, u32[]{:S(2)}, u32[]{:S(2)}) collective-permute-start(bf16[2,64,576]{2,1,0:T(8,128)(2,1)S(1)} %maximum_select_fusion.17), channel_id=1, source_target_pairs={{0,2},{1,3},{2,0},{3,1},{4,6},{5,7},{6,4},{7,5},{8,10},{9,11},{10,... | collective-permute-start | bytes 442376 | tf_op jit(solution)/shard_map/ppermute | solution.py:86
  13.2 11.7 %collective-permute-start.2 = (bf16[4,64,576]{2,1,0:T(8,128)(2,1)S(1)}, bf16[4,64,576]{2,1,0:T(8,128)(2,1)S(1)}, u32[]{:S(2)}, u32[]{:S(2)}) collective-permute-start(bf16[4,64,576]{2,1,0:T(8,128)(2,1)S(1)} %maximum_select_fusion.11), channel_id=1, source_target_pairs={{0,1},{1,0},{2,3},{3,2},{4,5},{5,4},{6,7},{7,6},{8,9},{9,8},{10,11... | collective-permute-start | bytes 884744 | tf_op jit(solution)/shard_map/ppermute | solution.py:86
  15.4 9.8 %collective-permute-start.5 = (bf16[4,64,576]{2,1,0:T(8,128)(2,1)S(1)}, bf16[4,64,576]{2,1,0:T(8,128)(2,1)S(1)}, u32[]{:S(2)}, u32[]{:S(2)}) collective-permute-start(bf16[4,64,576]{2,1,0:T(8,128)(2,1)S(1)} %maximum_select_fusion.12), channel_id=1, source_target_pairs={{0,1},{1,0},{2,3},{3,2},{4,5},{5,4},{6,7},{7,6},{8,9},{9,8},{10,11... | collective-permute-start | bytes 884744 | tf_op jit(solution)/shard_map/ppermute | solution.py:86
  24.9 1.7 copy-start.7
  25.4 1.2 copy-start.11
  64.0 2.0 copy-start.4
  65.2 6.1 %collective-permute-start.11 = (bf16[16,40,576]{2,1,0:T(8,128)(2,1)}, bf16[16,40,576]{2,1,0:T(8,128)(2,1)}, u32[]{:S(2)}, u32[]{:S(2)}) collective-permute-start(bf16[16,40,576]{2,1,0:T(8,128)(2,1)} %dynamic-slice_convert_fusion.2), channel_id=1, source_target_pairs={{0,1},{1,0},{2,3},{3,2},{4,5},{5,4},{6,7},{7,6},{8,9},{9,8},{10,11... | collective-permute-start | bytes 2211848 | tf_op jit(solution)/shard_map/ppermute | solution.py:70
  67.0 7.8 %collective-permute-start.16 = (bf16[16,40,576]{2,1,0:T(8,128)(2,1)}, bf16[16,40,576]{2,1,0:T(8,128)(2,1)}, u32[]{:S(2)}, u32[]{:S(2)}) collective-permute-start(bf16[16,40,576]{2,1,0:T(8,128)(2,1)} %dynamic-slice_convert_fusion.1), channel_id=1, source_target_pairs={{0,1},{1,0},{2,3},{3,2},{4,5},{5,4},{6,7},{7,6},{8,9},{9,8},{10,11... | collective-permute-start | bytes 2211848 | tf_op jit(solution)/shard_map/ppermute | solution.py:70
  68.3 1.9 copy-start.2
  71.3 5.5 %collective-permute-start.6 = (bf16[16,48,576]{2,1,0:T(8,128)(2,1)}, bf16[16,48,576]{2,1,0:T(8,128)(2,1)}, u32[]{:S(2)}, u32[]{:S(2)}) collective-permute-start(bf16[16,48,576]{2,1,0:T(8,128)(2,1)} %dynamic-slice_convert_fusion), channel_id=1, source_target_pairs={{0,1},{1,0},{2,3},{3,2},{4,5},{5,4},{6,7},{7,6},{8,9},{9,8},{10,11... | collective-permute-start | bytes 2654216 | tf_op jit(solution)/shard_map/ppermute | solution.py:70
  73.2 3.6 %copy-start.3 = (f32[2,2,2,2,2,48,576]{6,5,4,3,2,1,0:T(8,128)S(1)}, f32[2,2,2,2,2,48,576]{6,5,4,3,2,1,0:T(8,128)}, u32[]{:S(2)}) copy-start(f32[2,2,2,2,2,48,576]{6,5,4,3,2,1,0:T(8,128)} %copy-done.2) | copy-start | bytes 10616836
  73.2 11.9 %collective-permute-start.12 = (bf16[8,40,576]{2,1,0:T(8,128)(2,1)S(1)}, bf16[8,40,576]{2,1,0:T(8,128)(2,1)S(1)}, u32[]{:S(2)}, u32[]{:S(2)}) collective-permute-start(bf16[8,40,576]{2,1,0:T(8,128)(2,1)S(1)} %dynamic-slice_convert_fusion.5), channel_id=1, source_target_pairs={{0,4},{4,0},{1,5},{5,1},{2,6},{6,2},{3,7},{7,3},{8,12},{12,8},{9,1... | collective-permute-start | bytes 1105928 | tf_op jit(solution)/shard_map/ppermute | solution.py:70
  76.2 12.0 %collective-permute-start.17 = (bf16[8,40,576]{2,1,0:T(8,128)(2,1)S(1)}, bf16[8,40,576]{2,1,0:T(8,128)(2,1)S(1)}, u32[]{:S(2)}, u32[]{:S(2)}) collective-permute-start(bf16[8,40,576]{2,1,0:T(8,128)(2,1)S(1)} %dynamic-slice_convert_fusion.4), channel_id=1, source_target_pairs={{0,2},{1,3},{2,0},{3,1},{4,6},{5,7},{6,4},{7,5},{8,10},{9,11},{10,... | collective-permute-start | bytes 1105928 | tf_op jit(solution)/shard_map/ppermute | solution.py:70
  78.3 19.8 %collective-permute-start.7 = (bf16[8,48,576]{2,1,0:T(8,128)(2,1)S(1)}, bf16[8,48,576]{2,1,0:T(8,128)(2,1)S(1)}, u32[]{:S(2)}, u32[]{:S(2)}) collective-permute-start(bf16[8,48,576]{2,1,0:T(8,128)(2,1)S(1)} %dynamic-slice_convert_fusion.3), channel_id=1, source_target_pairs={{0,8},{8,0},{16,24},{24,16},{1,9},{9,1},{17,25},{25,17},{2,10},{10... | collective-permute-start | bytes 1327112 | tf_op jit(solution)/shard_map/ppermute | solution.py:70
  85.2 7.0 %collective-permute-start.13 = (bf16[4,40,576]{2,1,0:T(8,128)(2,1)S(1)}, bf16[4,40,576]{2,1,0:T(8,128)(2,1)S(1)}, u32[]{:S(2)}, u32[]{:S(2)}) collective-permute-start(bf16[4,40,576]{2,1,0:T(8,128)(2,1)S(1)} %dynamic-slice_convert_fusion.10), channel_id=1, source_target_pairs={{0,2},{1,3},{2,0},{3,1},{4,6},{5,7},{6,4},{7,5},{8,10},{9,11},{10,... | collective-permute-start | bytes 552968 | tf_op jit(solution)/shard_map/ppermute | solution.py:70
  88.2 8.5 %collective-permute-start.18 = (bf16[4,40,576]{2,1,0:T(8,128)(2,1)S(1)}, bf16[4,40,576]{2,1,0:T(8,128)(2,1)S(1)}, u32[]{:S(2)}, u32[]{:S(2)}) collective-permute-start(bf16[4,40,576]{2,1,0:T(8,128)(2,1)S(1)} %dynamic-slice_convert_fusion.9), channel_id=1, source_target_pairs={{0,8},{8,0},{16,24},{24,16},{1,9},{9,1},{17,25},{25,17},{2,10},{10... | collective-permute-start | bytes 552968 | tf_op jit(solution)/shard_map/ppermute | solution.py:70
  92.3 6.9 %collective-permute-start.14 = (bf16[2,40,576]{2,1,0:T(8,128)(2,1)S(1)}, bf16[2,40,576]{2,1,0:T(8,128)(2,1)S(1)}, u32[]{:S(2)}, u32[]{:S(2)}) collective-permute-start(bf16[2,40,576]{2,1,0:T(8,128)(2,1)S(1)} %dynamic-slice_convert_fusion.15), channel_id=1, source_target_pairs={{0,8},{8,0},{16,24},{24,16},{1,9},{9,1},{17,25},{25,17},{2,10},{10... | collective-permute-start | bytes 276488 | tf_op jit(solution)/shard_map/ppermute | solution.py:70
  96.8 5.6 %collective-permute-start.19 = (bf16[2,40,576]{2,1,0:T(8,128)(2,1)S(1)}, bf16[2,40,576]{2,1,0:T(8,128)(2,1)S(1)}, u32[]{:S(2)}, u32[]{:S(2)}) collective-permute-start(bf16[2,40,576]{2,1,0:T(8,128)(2,1)S(1)} %dynamic-slice_convert_fusion.14), channel_id=1, source_target_pairs={{0,4},{4,0},{1,5},{5,1},{2,6},{6,2},{3,7},{7,3},{8,12},{12,8},{9,1... | collective-permute-start | bytes 276488 | tf_op jit(solution)/shard_map/ppermute | solution.py:70
  98.2 17.2 %copy-start.9 = (bf16[4,32,576]{2,1,0:T(8,128)(2,1)S(1)}, bf16[4,32,576]{2,1,0:T(8,128)(2,1)}, u32[]{:S(2)}) copy-start(bf16[4,32,576]{2,1,0:T(8,128)(2,1)} %param.13) | copy-start | bytes 442372
  98.2 17.2 %copy-start.10 = (f32[4,576]{1,0:T(4,128)S(1)}, f32[4,576]{1,0:T(4,128)}, u32[]{:S(2)}) copy-start(f32[4,576]{1,0:T(4,128)} %param.11) | copy-start | bytes 27652
  98.3 6.9 %collective-permute-start.8 = (bf16[4,48,576]{2,1,0:T(8,128)(2,1)S(1)}, bf16[4,48,576]{2,1,0:T(8,128)(2,1)S(1)}, u32[]{:S(2)}, u32[]{:S(2)}) collective-permute-start(bf16[4,48,576]{2,1,0:T(8,128)(2,1)S(1)} %dynamic-slice_convert_fusion.8), channel_id=1, source_target_pairs={{0,4},{4,0},{1,5},{5,1},{2,6},{6,2},{3,7},{7,3},{8,12},{12,8},{9,1... | collective-permute-start | bytes 663560 | tf_op jit(solution)/shard_map/ppermute | solution.py:70
  99.2 7.6 %collective-permute-start.15 = (bf16[1,40,576]{2,1,0:T(8,128)(2,1)S(1)}, bf16[1,40,576]{2,1,0:T(8,128)(2,1)S(1)}, u32[]{:S(2)}, u32[]{:S(2)}) collective-permute-start(bf16[1,40,576]{2,1,0:T(8,128)(2,1)S(1)} %dynamic-slice_convert_fusion.20), channel_id=1, source_target_pairs={{0,16},{8,24},{16,0},{24,8},{1,17},{9,25},{17,1},{25,9},{2,18},{10... | collective-permute-start | bytes 138248 | tf_op jit(solution)/shard_map/ppermute | solution.py:70
  102.5 10.3 %collective-permute-start.20 = (bf16[1,40,576]{2,1,0:T(8,128)(2,1)S(1)}, bf16[1,40,576]{2,1,0:T(8,128)(2,1)S(1)}, u32[]{:S(2)}, u32[]{:S(2)}) collective-permute-start(bf16[1,40,576]{2,1,0:T(8,128)(2,1)S(1)} %dynamic-slice_convert_fusion.19), channel_id=1, source_target_pairs={{0,16},{8,24},{16,0},{24,8},{1,17},{9,25},{17,1},{25,9},{2,18},{10... | collective-permute-start | bytes 138248 | tf_op jit(solution)/shard_map/ppermute | solution.py:70
  105.2 4.9 %collective-permute-start.9 = (bf16[2,48,576]{2,1,0:T(8,128)(2,1)S(1)}, bf16[2,48,576]{2,1,0:T(8,128)(2,1)S(1)}, u32[]{:S(2)}, u32[]{:S(2)}) collective-permute-start(bf16[2,48,576]{2,1,0:T(8,128)(2,1)S(1)} %dynamic-slice_convert_fusion.13), channel_id=1, source_target_pairs={{0,2},{1,3},{2,0},{3,1},{4,6},{5,7},{6,4},{7,5},{8,10},{9,11},{10,... | collective-permute-start | bytes 331784 | tf_op jit(solution)/shard_map/ppermute | solution.py:70
  110.2 5.2 %collective-permute-start.10 = (bf16[1,48,576]{2,1,0:T(8,128)(2,1)S(1)}, bf16[1,48,576]{2,1,0:T(8,128)(2,1)S(1)}, u32[]{:S(2)}, u32[]{:S(2)}) collective-permute-start(bf16[1,48,576]{2,1,0:T(8,128)(2,1)S(1)} %dynamic-slice_convert_fusion.18), channel_id=1, source_target_pairs={{0,16},{8,24},{16,0},{24,8},{1,17},{9,25},{17,1},{25,9},{2,18},{10... | collective-permute-start | bytes 165896 | tf_op jit(solution)/shard_map/ppermute | solution.py:70
  115.5 24.9 %copy-start.6 = (bf16[4,32,576]{2,1,0:T(8,128)(2,1)}, bf16[4,32,576]{2,1,0:T(8,128)(2,1)S(1)}, u32[]{:S(2)}) copy-start(bf16[4,32,576]{2,1,0:T(8,128)(2,1)S(1)} %subtract_convert_fusion) | copy-start | bytes 442372
  115.5 6.2 %collective-permute-start.26 = (bf16[1,40,576]{2,1,0:T(8,128)(2,1)S(1)}, bf16[1,40,576]{2,1,0:T(8,128)(2,1)S(1)}, u32[]{:S(2)}, u32[]{:S(2)}) collective-permute-start(bf16[1,40,576]{2,1,0:T(8,128)(2,1)S(1)} %get-tuple-element.10), channel_id=1, source_target_pairs={{0,16},{8,24},{16,0},{24,8},{1,17},{9,25},{17,1},{25,9},{2,18},{10... | collective-permute-start | bytes 138248 | tf_op jit(solution)/shard_map/ppermute | solution.py:86
  118.8 7.5 %collective-permute-start.21 = (bf16[1,48,576]{2,1,0:T(8,128)(2,1)S(1)}, bf16[1,48,576]{2,1,0:T(8,128)(2,1)S(1)}, u32[]{:S(2)}, u32[]{:S(2)}) collective-permute-start(bf16[1,48,576]{2,1,0:T(8,128)(2,1)S(1)} %slice_bitcast_fusion.5), channel_id=1, source_target_pairs={{0,16},{8,24},{16,0},{24,8},{1,17},{9,25},{17,1},{25,9},{2,18},{10... | collective-permute-start | bytes 165896 | tf_op jit(solution)/shard_map/ppermute | solution.py:86
  118.9 6.2 %collective-permute-start.31 = (bf16[1,40,576]{2,1,0:T(8,128)(2,1)S(1)}, bf16[1,40,576]{2,1,0:T(8,128)(2,1)S(1)}, u32[]{:S(2)}, u32[]{:S(2)}) collective-permute-start(bf16[1,40,576]{2,1,0:T(8,128)(2,1)S(1)} %get-tuple-element.11), channel_id=1, source_target_pairs={{0,16},{8,24},{16,0},{24,8},{1,17},{9,25},{17,1},{25,9},{2,18},{10... | collective-permute-start | bytes 138248 | tf_op jit(solution)/shard_map/ppermute | solution.py:86
  121.8 6.4 %collective-permute-start.27 = (bf16[2,40,576]{2,1,0:T(8,128)(2,1)S(1)}, bf16[2,40,576]{2,1,0:T(8,128)(2,1)S(1)}, u32[]{:S(2)}, u32[]{:S(2)}) collective-permute-start(bf16[2,40,576]{2,1,0:T(8,128)(2,1)S(1)} %maximum_select_fusion.19), channel_id=1, source_target_pairs={{0,8},{8,0},{16,24},{24,16},{1,9},{9,1},{17,25},{25,17},{2,10},{10... | collective-permute-start | bytes 276488 | tf_op jit(solution)/shard_map/ppermute | solution.py:86
  125.1 5.8 %collective-permute-start.32 = (bf16[2,40,576]{2,1,0:T(8,128)(2,1)S(1)}, bf16[2,40,576]{2,1,0:T(8,128)(2,1)S(1)}, u32[]{:S(2)}, u32[]{:S(2)}) collective-permute-start(bf16[2,40,576]{2,1,0:T(8,128)(2,1)S(1)} %maximum_select_fusion.20), channel_id=1, source_target_pairs={{0,4},{4,0},{1,5},{5,1},{2,6},{6,2},{3,7},{7,3},{8,12},{12,8},{9,1... | collective-permute-start | bytes 276488 | tf_op jit(solution)/shard_map/ppermute | solution.py:86
  126.3 7.4 %collective-permute-start.22 = (bf16[2,48,576]{2,1,0:T(8,128)(2,1)S(1)}, bf16[2,48,576]{2,1,0:T(8,128)(2,1)S(1)}, u32[]{:S(2)}, u32[]{:S(2)}) collective-permute-start(bf16[2,48,576]{2,1,0:T(8,128)(2,1)S(1)} %maximum_select_fusion.18), channel_id=1, source_target_pairs={{0,2},{1,3},{2,0},{3,1},{4,6},{5,7},{6,4},{7,5},{8,10},{9,11},{10,... | collective-permute-start | bytes 331784 | tf_op jit(solution)/shard_map/ppermute | solution.py:86
  128.2 8.2 %collective-permute-start.28 = (bf16[4,40,576]{2,1,0:T(8,128)(2,1)S(1)}, bf16[4,40,576]{2,1,0:T(8,128)(2,1)S(1)}, u32[]{:S(2)}, u32[]{:S(2)}) collective-permute-start(bf16[4,40,576]{2,1,0:T(8,128)(2,1)S(1)} %maximum_select_fusion.14), channel_id=1, source_target_pairs={{0,2},{1,3},{2,0},{3,1},{4,6},{5,7},{6,4},{7,5},{8,10},{9,11},{10,... | collective-permute-start | bytes 552968 | tf_op jit(solution)/shard_map/ppermute | solution.py:86
  131.0 8.4 %collective-permute-start.33 = (bf16[4,40,576]{2,1,0:T(8,128)(2,1)S(1)}, bf16[4,40,576]{2,1,0:T(8,128)(2,1)S(1)}, u32[]{:S(2)}, u32[]{:S(2)}) collective-permute-start(bf16[4,40,576]{2,1,0:T(8,128)(2,1)S(1)} %maximum_select_fusion.15), channel_id=1, source_target_pairs={{0,8},{8,0},{16,24},{24,16},{1,9},{9,1},{17,25},{25,17},{2,10},{10... | collective-permute-start | bytes 552968 | tf_op jit(solution)/shard_map/ppermute | solution.py:86
  133.7 6.5 %collective-permute-start.23 = (bf16[4,48,576]{2,1,0:T(8,128)(2,1)S(1)}, bf16[4,48,576]{2,1,0:T(8,128)(2,1)S(1)}, u32[]{:S(2)}, u32[]{:S(2)}) collective-permute-start(bf16[4,48,576]{2,1,0:T(8,128)(2,1)S(1)} %maximum_select_fusion.13), channel_id=1, source_target_pairs={{0,4},{4,0},{1,5},{5,1},{2,6},{6,2},{3,7},{7,3},{8,12},{12,8},{9,1... | collective-permute-start | bytes 663560 | tf_op jit(solution)/shard_map/ppermute | solution.py:86
  136.6 8.0 %collective-permute-start.29 = (bf16[8,40,576]{2,1,0:T(8,128)(2,1)S(1)}, bf16[8,40,576]{2,1,0:T(8,128)(2,1)S(1)}, u32[]{:S(2)}, u32[]{:S(2)}) collective-permute-start(bf16[8,40,576]{2,1,0:T(8,128)(2,1)S(1)} %maximum_select_fusion.9), channel_id=1, source_target_pairs={{0,4},{4,0},{1,5},{5,1},{2,6},{6,2},{3,7},{7,3},{8,12},{12,8},{9,1... | collective-permute-start | bytes 1105928 | tf_op jit(solution)/shard_map/ppermute | solution.py:86
  139.5 8.0 %collective-permute-start.34 = (bf16[8,40,576]{2,1,0:T(8,128)(2,1)S(1)}, bf16[8,40,576]{2,1,0:T(8,128)(2,1)S(1)}, u32[]{:S(2)}, u32[]{:S(2)}) collective-permute-start(bf16[8,40,576]{2,1,0:T(8,128)(2,1)S(1)} %maximum_select_fusion.10), channel_id=1, source_target_pairs={{0,2},{1,3},{2,0},{3,1},{4,6},{5,7},{6,4},{7,5},{8,10},{9,11},{10,... | collective-permute-start | bytes 1105928 | tf_op jit(solution)/shard_map/ppermute | solution.py:86
  140.4 8.9 %collective-permute-start.24 = (bf16[8,48,576]{2,1,0:T(8,128)(2,1)S(1)}, bf16[8,48,576]{2,1,0:T(8,128)(2,1)S(1)}, u32[]{:S(2)}, u32[]{:S(2)}) collective-permute-start(bf16[8,48,576]{2,1,0:T(8,128)(2,1)S(1)} %maximum_select_fusion.8), channel_id=1, source_target_pairs={{0,8},{8,0},{16,24},{24,16},{1,9},{9,1},{17,25},{25,17},{2,10},{10... | collective-permute-start | bytes 1327112 | tf_op jit(solution)/shard_map/ppermute | solution.py:86
  144.8 4.8 %collective-permute-start.30 = (bf16[16,40,576]{2,1,0:T(8,128)(2,1)S(1)}, bf16[16,40,576]{2,1,0:T(8,128)(2,1)}, u32[]{:S(2)}, u32[]{:S(2)}) collective-permute-start(bf16[16,40,576]{2,1,0:T(8,128)(2,1)S(1)} %maximum_select_fusion.4), channel_id=1, source_target_pairs={{0,1},{1,0},{2,3},{3,2},{4,5},{5,4},{6,7},{7,6},{8,9},{9,8},{10,11... | collective-permute-start | bytes 2211848 | tf_op jit(solution)/shard_map/ppermute | solution.py:86
  147.7 3.9 %collective-permute-start.35 = (bf16[16,40,576]{2,1,0:T(8,128)(2,1)S(1)}, bf16[16,40,576]{2,1,0:T(8,128)(2,1)}, u32[]{:S(2)}, u32[]{:S(2)}) collective-permute-start(bf16[16,40,576]{2,1,0:T(8,128)(2,1)S(1)} %maximum_select_fusion.5), channel_id=1, source_target_pairs={{0,1},{1,0},{2,3},{3,2},{4,5},{5,4},{6,7},{7,6},{8,9},{9,8},{10,11... | collective-permute-start | bytes 2211848 | tf_op jit(solution)/shard_map/ppermute | solution.py:86
  149.6 4.0 %collective-permute-start.25 = (bf16[16,48,576]{2,1,0:T(8,128)(2,1)S(1)}, bf16[16,48,576]{2,1,0:T(8,128)(2,1)}, u32[]{:S(2)}, u32[]{:S(2)}) collective-permute-start(bf16[16,48,576]{2,1,0:T(8,128)(2,1)S(1)} %maximum_select_fusion.3), channel_id=1, source_target_pairs={{0,1},{1,0},{2,3},{3,2},{4,5},{5,4},{6,7},{7,6},{8,9},{9,8},{10,11... | collective-permute-start | bytes 2654216 | tf_op jit(solution)/shard_map/ppermute | solution.py:86
  163.4 9.9 %copy-start.8 = (pred[256,1024]{1,0:T(8,128)(4,1)S(1)}, pred[256,1024]{1,0:T(8,128)(4,1)}, u32[]{:S(2)}) copy-start(pred[256,1024]{1,0:T(8,128)(4,1)} %copy-done.7) | copy-start | bytes 786436
  163.4 20.5 %slice-start = ((s8[4718592]{0:T(1024)(128)(4,1)}), s8[524288]{0:T(1024)(128)(4,1)S(1)}, s32[]{:S(2)}) async-start(s8[4718592]{0:T(1024)(128)(4,1)} %bitcast.143), calls=%async_computation | async-start | bytes 1048576
  173.3 10.5 %slice-start.1 = ((s8[4718592]{0:T(1024)(128)(4,1)}), s8[4194304]{0:T(1024)(128)(4,1)S(1)}, s32[]{:S(2)}) async-start(s8[4718592]{0:T(1024)(128)(4,1)} %bitcast.143), calls=%async_computation.1 | async-start | bytes 8388608
  191.5 3.7 %collective-permute-start.36 = (bf16[4,64,576]{2,1,0:T(8,128)(2,1)S(1)}, bf16[4,64,576]{2,1,0:T(8,128)(2,1)S(1)}, u32[]{:S(2)}, u32[]{:S(2)}) collective-permute-start(bf16[4,64,576]{2,1,0:T(8,128)(2,1)S(1)} %dynamic-slice_convert_fusion.7), channel_id=1, source_target_pairs={{0,1},{1,0},{2,3},{3,2},{4,5},{5,4},{6,7},{7,6},{8,9},{9,8},{10,11... | collective-permute-start | bytes 884744 | tf_op jit(solution)/shard_map/ppermute | solution.py:70
  193.8 3.6 %copy-start.5 = (f32[2,2,2,64,576]{4,3,2,1,0:T(8,128)S(1)}, f32[2,2,2,64,576]{4,3,2,1,0:T(8,128)}, u32[]{:S(2)}) copy-start(f32[2,2,2,64,576]{4,3,2,1,0:T(8,128)} %copy.66) | copy-start | bytes 3538948
  195.1 2.4 %collective-permute-start.39 = (bf16[4,64,576]{2,1,0:T(8,128)(2,1)S(1)}, bf16[4,64,576]{2,1,0:T(8,128)(2,1)S(1)}, u32[]{:S(2)}, u32[]{:S(2)}) collective-permute-start(bf16[4,64,576]{2,1,0:T(8,128)(2,1)S(1)} %dynamic-slice_convert_fusion.6), channel_id=1, source_target_pairs={{0,1},{1,0},{2,3},{3,2},{4,5},{5,4},{6,7},{7,6},{8,9},{9,8},{10,11... | collective-permute-start | bytes 884744 | tf_op jit(solution)/shard_map/ppermute | solution.py:70
  196.3 13.5 %copy-start.1 = (s32[4,256,64]{1,2,0:T(8,128)S(1)}, s32[4,256,64]{1,2,0:T(8,128)}, u32[]{:S(2)}) copy-start(s32[4,256,64]{1,2,0:T(8,128)} %param.12) | copy-start | bytes 786436
  196.4 6.7 %collective-permute-start.37 = (bf16[2,64,576]{2,1,0:T(8,128)(2,1)S(1)}, bf16[2,64,576]{2,1,0:T(8,128)(2,1)S(1)}, u32[]{:S(2)}, u32[]{:S(2)}) collective-permute-start(bf16[2,64,576]{2,1,0:T(8,128)(2,1)S(1)} %dynamic-slice_convert_fusion.12), channel_id=1, source_target_pairs={{0,4},{4,0},{1,5},{5,1},{2,6},{6,2},{3,7},{7,3},{8,12},{12,8},{9,1... | collective-permute-start | bytes 442376 | tf_op jit(solution)/shard_map/ppermute | solution.py:70
  197.5 6.9 %collective-permute-start.40 = (bf16[2,64,576]{2,1,0:T(8,128)(2,1)S(1)}, bf16[2,64,576]{2,1,0:T(8,128)(2,1)S(1)}, u32[]{:S(2)}, u32[]{:S(2)}) collective-permute-start(bf16[2,64,576]{2,1,0:T(8,128)(2,1)S(1)} %dynamic-slice_convert_fusion.11), channel_id=1, source_target_pairs={{0,2},{1,3},{2,0},{3,1},{4,6},{5,7},{6,4},{7,5},{8,10},{9,11},{10,... | collective-permute-start | bytes 442376 | tf_op jit(solution)/shard_map/ppermute | solution.py:70
  203.1 4.5 %collective-permute-start.38 = (bf16[1,64,576]{2,1,0:T(8,128)(2,1)S(1)}, bf16[1,64,576]{2,1,0:T(8,128)(2,1)S(1)}, u32[]{:S(2)}, u32[]{:S(2)}) collective-permute-start(bf16[1,64,576]{2,1,0:T(8,128)(2,1)S(1)} %dynamic-slice_convert_fusion.17), channel_id=1, source_target_pairs={{0,2},{1,3},{2,0},{3,1},{4,6},{5,7},{6,4},{7,5},{8,10},{9,11},{10,... | collective-permute-start | bytes 221192 | tf_op jit(solution)/shard_map/ppermute | solution.py:70
  204.5 4.5 %collective-permute-start.41 = (bf16[1,64,576]{2,1,0:T(8,128)(2,1)S(1)}, bf16[1,64,576]{2,1,0:T(8,128)(2,1)S(1)}, u32[]{:S(2)}, u32[]{:S(2)}) collective-permute-start(bf16[1,64,576]{2,1,0:T(8,128)(2,1)S(1)} %dynamic-slice_convert_fusion.16), channel_id=1, source_target_pairs={{0,4},{4,0},{1,5},{5,1},{2,6},{6,2},{3,7},{7,3},{8,12},{12,8},{9,1... | collective-permute-start | bytes 221192 | tf_op jit(solution)/shard_map/ppermute | solution.py:70

commit v6 on v5

--- a/solution.py
+++ b/solution.py
@@ -111,11 +111,15 @@
     slot_rows = tokens // slots
     feat_total = 2 * feat_parts * feat_dev
 
+    enc_chunks = encoder[0].reshape(feat_parts, cols, feat_dev)
+    dec_chunks = decoder[0].reshape(layer_count, feat_dev, feat_parts, cols).transpose(2, 0, 1, 3)
+
     gathered = all_gather(resid[0], PLANE)
-    tokens_all = (
-        gathered.reshape(2, feat_parts, half_rows, cols).transpose(0, 2, 1, 3).reshape(tokens, width)
+    tokens_chunks = (
+        gathered.reshape(2, feat_parts, half_rows, cols).transpose(1, 0, 2, 3).reshape(feat_parts, tokens, cols)
     )
-    pre = jnp.dot(tokens_all, encoder[0], preferred_element_type=jnp.float32) + encoder_bias[0]
+    pre = jnp.einsum("cte,cef->tf", tokens_chunks, enc_chunks, preferred_element_type=jnp.float32)
+    pre = pre + encoder_bias[0]
     first_feat = half_bit * (feat_total // 2) + feat_pos * feat_dev
     feat_ids = first_feat + lax.iota(jnp.int32, feat_dev)
     layer_index = lax.dynamic_index_in_dim(topk_index, layer_id, 0, keepdims=False)
@@ -124,11 +128,11 @@
     )
     acts = (selected * pre).astype(jnp.bfloat16)
     live_layers = lax.iota(jnp.int32, layer_count) >= layer_id
-    partial_value = jnp.einsum("tf,lfd->ltd", acts, decoder[0], preferred_element_type=jnp.float32)
-    partial_value = jnp.where(live_layers[:, None, None], partial_value, 0.0)
+    partial_value = jnp.einsum("tf,clfe->clte", acts, dec_chunks, preferred_element_type=jnp.float32)
+    partial_value = jnp.where(live_layers[None, :, None, None], partial_value, 0.0)
     blocks = (
-        partial_value.reshape(layer_count, slots, slot_rows, feat_parts, cols)
-        .transpose(1, 3, 0, 2, 4)
+        partial_value.reshape(feat_parts, layer_count, slots, slot_rows, cols)
+        .transpose(2, 0, 1, 3, 4)
         .reshape(slots * feat_parts, layer_count * slot_rows, cols)
     )
     recon = reduce_scatter(blocks, EVERY, jnp.bfloat16).reshape(layer_count, slot_rows, cols)
@@ -137,18 +141,16 @@
     pieces = all_gather(error.reshape(layer_count * slot_rows, cols), EVERY)
     piece = (
         pieces.reshape(slots, feat_parts, layer_count, slot_rows, cols)
-        .transpose(2, 0, 3, 1, 4)
-        .reshape(layer_count, tokens, width)
+        .transpose(1, 2, 0, 3, 4)
+        .reshape(feat_parts, layer_count, tokens, cols)
     )
-    kept = jnp.where(live_layers[:, None, None], piece, jnp.zeros_like(piece))
-    grad_act = jnp.einsum("ltd,lfd->tf", kept, decoder[0], preferred_element_type=jnp.float32)
+    kept = jnp.where(live_layers[None, :, None, None], piece, jnp.zeros_like(piece))
+    grad_act = jnp.einsum("clte,clfe->tf", kept, dec_chunks, preferred_element_type=jnp.float32)
     grad_pre = (selected * grad_act).astype(jnp.bfloat16)
-    grad_part = lax.dot_general(
-        grad_pre, encoder[0], (((1,), (1,)), ((), ())), preferred_element_type=jnp.float32
-    )
+    grad_part = jnp.einsum("tf,cef->cte", grad_pre, enc_chunks, preferred_element_type=jnp.float32)
     grad_blocks = (
-        grad_part.reshape(2, half_rows, feat_parts, cols)
-        .transpose(0, 2, 1, 3)
+        grad_part.reshape(feat_parts, 2, half_rows, cols)
+        .transpose(1, 0, 2, 3)
         .reshape(2 * feat_parts, half_rows, cols)
     )
     grad_sum = reduce_scatter(grad_blocks, PLANE, jnp.bfloat16)

time: 211 us -> 227 us (1.076)
  local copies, waits for them, and re-layouts: 55.9 us -> 70.3 us
    unnamed x31 -> x32, local copies, waits for them, and re-layouts: 3.09 us -> 34.3 us
    reshape x3 -> x2, local copies, waits for them, and re-layouts: 28.6 us -> 3.65 us  [the longest x1 2.86 us: local(): grad_part.reshape(feat_parts, 2, half_rows, cols).transpose(1, 0, 2, 3)]
    select_n x0 -> x1, local copies, waits for them, and re-layouts: none -> 10.9 us  [local(): jnp.where(live_layers[None, :, None, None], partial_value, 0.0)]
    transpose x8 -> x5, local copies, waits for them, and re-layouts: 9.01 us -> 2.14 us  [reduce_scatter(): xp = jnp.transpose(xp, [labels.index(l) for l in order] + [nb, nb + 1])]
    transpose x1, local copies, waits for them, and re-layouts: 6.38 us -> 0.76 us  [local(): piece = pieces.reshape(slots, feat_parts, layer_count, slot_rows, cols).t...]
    transpose x1 -> x2, local copies, waits for them, and re-layouts: 1 us -> 5.99 us  [the longest x1 5 us: local(): blocks = partial_value.reshape(feat_parts, layer_count, slots, slot_rows,...]
    slice x0 -> x1, local copies, waits for them, and re-layouts: none -> 4.7 us  [reduce_scatter(): xp = lax.slice_in_dim(x, start, start + size, axis=nb)]
    dot_general x4 -> x3, matrix products: 29.6 us -> 29.8 us  [the longest x1 15.1 us: local(): jnp.einsum('tf,clfe->clte', acts, dec_chunks, preferred_element_type=jnp....]
  transfers between devices with their start and end apart: 42 -> 42, of which waited for: 21 -> 21; matrix products, arithmetic and copies ran while one was open for 14% -> 24% of each run, Pallas kernels for 0% -> 0%
where the time goes in v6:
time: 227 us; the launch traced here: 225 us
  local copies, waits for them, and re-layouts  70.3 us (31%)
  starting transfers between devices  55.6 us (24%)
  waiting for transfers between devices  42.6 us (19%)
  matrix products  29.8 us (13%)
  other arithmetic  25.4 us (11%)
    unnamed x32, local copies, waits for them, and re-layouts  34.3 us
    ppermute x21, starting transfers between devices, all_gather(): recv = lax.ppermute(parts[p], axis, partner(axis, bit))  29.2 us
    ppermute x21, starting transfers between devices, reduce_scatter(): recv = lax.ppermute(send.astype(wire), axis, partner(axis, bit))  26.5 us
    ppermute x21, waiting for transfers between devices, reduce_scatter(): recv = lax.ppermute(send.astype(wire), axis, partner(axis, bit))  26 us
    ppermute x21, waiting for transfers between devices, all_gather(): recv = lax.ppermute(parts[p], axis, partner(axis, bit))  16.5 us
    dot_general x1, matrix products, local(): jnp.einsum('tf,clfe->clte', acts, dec_chunks, preferred_element_type=jnp....  15.1 us
    select_n x1, local copies, waits for them, and re-layouts, local(): jnp.where(live_layers[None, :, None, None], partial_value, 0.0)  10.9 us
    dot_general x1, matrix products, local(): jnp.einsum('clte,clfe->tf', kept, dec_chunks, preferred_element_type=jnp....  9.48 us
  transfers between devices with their start and end apart: 42, of which 21 were waited for; matrix products, arithmetic and copies ran while one was open for 24% of the time, Pallas kernels for 0%

profile of v6, /device:TPU:0, one launch (start us, length us, event | category | flops | bytes accessed | tf_op | source)
XLA Modules:
  0.0 225.1 jit_solution(13918328413752956745)
XLA Ops:
  0.6 1.1 fusion.26
  1.9 3.1 %collective-permute-start = (bf16[1,64,576]{2,1,0:T(8,128)(2,1)S(1)}, bf16[1,64,576]{2,1,0:T(8,128)(2,1)S(1)}, u32[]{:S(2)}, u32[]{:S(2)}) collective-permute-start(bf16[1,64,576]{2,1,0:T(8,128)(2,1)S(1)} %copy.90), channel_id=1, source_target_pairs={{0,2},{1,3},{2,0},{3,1},{4,6},{5,7},{6,4},{7,5},{8,10},{9,11},{10,... | collective-permute-start | bytes 221192 | tf_op jit(solution)/shard_map/ppermute | solution.py:86
  5.1 1.6 collective-permute-start.3
  7.5 2.0 collective-permute-start.1
  9.9 1.2 collective-permute-start.4
  11.2 1.9 collective-permute-done.1
  13.3 2.0 collective-permute-done.4
  15.5 9.4 %compare_reduce_fusion = pred[256,1024]{1,0:T(8,128)(4,1)S(1)} fusion(s32[1024]{0:T(1024)S(1)} %iota_add_fusion, s32[256,64]{1,0:T(8,128)S(1)} %copy.65), kind=kLoop, calls=%fused_computation | loop fusion | flops 33292288 | bytes 331776 | tf_op jit(solution)/shard_map/reduce_or | solution.py:126
  24.9 24.5 %copy.71 = bf16[1,4,1024,2304]{2,3,1,0:T(8,128)(2,1)} copy(bf16[1,4,1024,2304]{3,2,1,0:T(8,128)(2,1)} %param.10) | data formatting | bytes 37748736 | tf_op args[3]
  51.9 15.1 %select_bitcast_fusion = f32[4,4,256,576]{2,3,1,0:T(8,128)} fusion(pred[4]{0:T(512)(128)(4,1)S(1)} %iota_compare_fusion, bf16[4,4,1024,576]{2,3,0,1:T(8,128)(2,1)} %bitcast.118, pred[256,1024]{1,0:T(8,128)(4,1)S(1)} %compare_reduce_fusion, bf16[4,256,576]{1,2,0:T(8,128)(2,1)S(1)} %reshape.121, bf16[4,576,1024]{2,1,0:T(8,128)(2,1)} %bitcast.143, ...), kind=kOutput, calls=%fused_computation.5 | convolution fusion | flops 6042943488 | bytes 34476036 | tf_op jit(solution)/shard_map/tf,clfe->clte/dot_general | solution.py:131
  67.1 10.9 %copy.73 = f32[4,4,256,576]{3,2,1,0:T(8,128)} copy(f32[4,4,256,576]{2,3,1,0:T(8,128)} %select_bitcast_fusion) | data formatting | bytes 18874368 | tf_op jit(solution)/shard_map/jit(_where)/select_n | solution.py:132
  78.0 5.0 %copy.74 = f32[8,4,4,32,576]{4,3,2,1,0:T(8,128)S(1)} copy(f32[8,4,4,32,576]{4,3,0,2,1:T(8,128)} %bitcast.115) | data formatting | bytes 18874368 | tf_op jit(solution)/shard_map/transpose | solution.py:135
  88.4 1.9 copy-done.2
  91.4 1.8 convert_add_fusion.2
  93.3 1.6 collective-permute-start.12
  95.0 1.3 convert_add_fusion.1
  96.9 1.5 convert_add_fusion
  98.4 1.6 collective-permute-start.7
  100.1 5.2 %collective-permute-done.12 = bf16[8,40,576]{2,1,0:T(8,128)(2,1)S(1)} collective-permute-done((bf16[8,40,576]{2,1,0:T(8,128)(2,1)S(1)}, bf16[8,40,576]{2,1,0:T(8,128)(2,1)S(1)}, u32[]{:S(2)}, u32[]{:S(2)}) %collective-permute-start.12) | collective-permute-done | bytes 368672 | tf_op jit(solution)/shard_map/ppermute | solution.py:70
  105.3 1.2 collective-permute-start.13
  106.6 1.7 collective-permute-done.17
  108.4 1.5 collective-permute-start.18
  109.9 2.4 %collective-permute-done.13 = bf16[4,40,576]{2,1,0:T(8,128)(2,1)S(1)} collective-permute-done((bf16[4,40,576]{2,1,0:T(8,128)(2,1)S(1)}, bf16[4,40,576]{2,1,0:T(8,128)(2,1)S(1)}, u32[]{:S(2)}, u32[]{:S(2)}) %collective-permute-start.13) | collective-permute-done | bytes 184352 | tf_op jit(solution)/shard_map/ppermute | solution.py:70
  112.4 1.6 collective-permute-start.14
  114.1 2.8 %collective-permute-done.18 = bf16[4,40,576]{2,1,0:T(8,128)(2,1)S(1)} collective-permute-done((bf16[4,40,576]{2,1,0:T(8,128)(2,1)S(1)}, bf16[4,40,576]{2,1,0:T(8,128)(2,1)S(1)}, u32[]{:S(2)}, u32[]{:S(2)}) %collective-permute-start.18) | collective-permute-done | bytes 184352 | tf_op jit(solution)/shard_map/ppermute | solution.py:70
  117.0 1.2 collective-permute-start.19
  119.3 2.7 %collective-permute-start.15 = (bf16[1,40,576]{2,1,0:T(8,128)(2,1)S(1)}, bf16[1,40,576]{2,1,0:T(8,128)(2,1)S(1)}, u32[]{:S(2)}, u32[]{:S(2)}) collective-permute-start(bf16[1,40,576]{2,1,0:T(8,128)(2,1)S(1)} %dynamic-slice_convert_fusion.20), channel_id=1, source_target_pairs={{0,16},{8,24},{16,0},{24,8},{1,17},{9,25},{17,1},{25,9},{2,18},{10... | collective-permute-start | bytes 138248 | tf_op jit(solution)/shard_map/ppermute | solution.py:70
  122.6 2.7 %collective-permute-start.20 = (bf16[1,40,576]{2,1,0:T(8,128)(2,1)S(1)}, bf16[1,40,576]{2,1,0:T(8,128)(2,1)S(1)}, u32[]{:S(2)}, u32[]{:S(2)}) collective-permute-start(bf16[1,40,576]{2,1,0:T(8,128)(2,1)S(1)} %dynamic-slice_convert_fusion.19), channel_id=1, source_target_pairs={{0,16},{8,24},{16,0},{24,8},{1,17},{9,25},{17,1},{25,9},{2,18},{10... | collective-permute-start | bytes 138248 | tf_op jit(solution)/shard_map/ppermute | solution.py:70
  125.3 1.6 collective-permute-start.9
  127.0 3.3 %collective-permute-done.9 = bf16[2,48,576]{2,1,0:T(8,128)(2,1)S(1)} collective-permute-done((bf16[2,48,576]{2,1,0:T(8,128)(2,1)S(1)}, bf16[2,48,576]{2,1,0:T(8,128)(2,1)S(1)}, u32[]{:S(2)}, u32[]{:S(2)}) %collective-permute-start.9) | collective-permute-done | bytes 110624 | tf_op jit(solution)/shard_map/ppermute | solution.py:70
  130.3 2.6 %collective-permute-start.10 = (bf16[1,48,576]{2,1,0:T(8,128)(2,1)S(1)}, bf16[1,48,576]{2,1,0:T(8,128)(2,1)S(1)}, u32[]{:S(2)}, u32[]{:S(2)}) collective-permute-start(bf16[1,48,576]{2,1,0:T(8,128)(2,1)S(1)} %dynamic-slice_convert_fusion.18), channel_id=1, source_target_pairs={{0,16},{8,24},{16,0},{24,8},{1,17},{9,25},{17,1},{25,9},{2,18},{10... | collective-permute-start | bytes 165896 | tf_op jit(solution)/shard_map/ppermute | solution.py:70
  132.9 2.6 %collective-permute-done.10 = bf16[1,48,576]{2,1,0:T(8,128)(2,1)S(1)} collective-permute-done((bf16[1,48,576]{2,1,0:T(8,128)(2,1)S(1)}, bf16[1,48,576]{2,1,0:T(8,128)(2,1)S(1)}, u32[]{:S(2)}, u32[]{:S(2)}) %collective-permute-start.10) | collective-permute-done | bytes 55328 | tf_op jit(solution)/shard_map/ppermute | solution.py:70
  135.7 3.2 %collective-permute-start.26 = (bf16[1,40,576]{2,1,0:T(8,128)(2,1)S(1)}, bf16[1,40,576]{2,1,0:T(8,128)(2,1)S(1)}, u32[]{:S(2)}, u32[]{:S(2)}) collective-permute-start(bf16[1,40,576]{2,1,0:T(8,128)(2,1)S(1)} %get-tuple-element.10), channel_id=1, source_target_pairs={{0,16},{8,24},{16,0},{24,8},{1,17},{9,25},{17,1},{25,9},{2,18},{10... | collective-permute-start | bytes 138248 | tf_op jit(solution)/shard_map/ppermute | solution.py:86
  139.0 2.8 %collective-permute-start.31 = (bf16[1,40,576]{2,1,0:T(8,128)(2,1)S(1)}, bf16[1,40,576]{2,1,0:T(8,128)(2,1)S(1)}, u32[]{:S(2)}, u32[]{:S(2)}) collective-permute-start(bf16[1,40,576]{2,1,0:T(8,128)(2,1)S(1)} %get-tuple-element.11), channel_id=1, source_target_pairs={{0,16},{8,24},{16,0},{24,8},{1,17},{9,25},{17,1},{25,9},{2,18},{10... | collective-permute-start | bytes 138248 | tf_op jit(solution)/shard_map/ppermute | solution.py:86
  141.9 3.3 %collective-permute-start.27 = (bf16[2,40,576]{2,1,0:T(8,128)(2,1)S(1)}, bf16[2,40,576]{2,1,0:T(8,128)(2,1)S(1)}, u32[]{:S(2)}, u32[]{:S(2)}) collective-permute-start(bf16[2,40,576]{2,1,0:T(8,128)(2,1)S(1)} %maximum_select_fusion.19), channel_id=1, source_target_pairs={{0,8},{8,0},{16,24},{24,16},{1,9},{9,1},{17,25},{25,17},{2,10},{10... | collective-permute-start | bytes 276488 | tf_op jit(solution)/shard_map/ppermute | solution.py:86
  145.2 1.2 collective-permute-start.32
  146.4 1.5 collective-permute-start.22
  148.3 1.6 collective-permute-start.28
  149.9 1.1 collective-permute-done.32
  151.1 2.7 %collective-permute-start.33 = (bf16[4,40,576]{2,1,0:T(8,128)(2,1)S(1)}, bf16[4,40,576]{2,1,0:T(8,128)(2,1)S(1)}, u32[]{:S(2)}, u32[]{:S(2)}) collective-permute-start(bf16[4,40,576]{2,1,0:T(8,128)(2,1)S(1)} %maximum_select_fusion.15), channel_id=1, source_target_pairs={{0,8},{8,0},{16,24},{24,16},{1,9},{9,1},{17,25},{25,17},{2,10},{10... | collective-permute-start | bytes 552968 | tf_op jit(solution)/shard_map/ppermute | solution.py:86
  153.9 1.2 collective-permute-start.23
  155.0 1.5 collective-permute-done.28
  157.6 1.8 collective-permute-done.33
  160.5 1.6 collective-permute-start.24
  162.1 2.6 %collective-permute-done.29 = bf16[8,40,576]{2,1,0:T(8,128)(2,1)S(1)} collective-permute-done((bf16[8,40,576]{2,1,0:T(8,128)(2,1)S(1)}, bf16[8,40,576]{2,1,0:T(8,128)(2,1)S(1)}, u32[]{:S(2)}, u32[]{:S(2)}) %collective-permute-start.29) | collective-permute-done | bytes 368672 | tf_op jit(solution)/shard_map/ppermute | solution.py:86
  165.0 2.6 %collective-permute-done.34 = bf16[8,40,576]{2,1,0:T(8,128)(2,1)S(1)} collective-permute-done((bf16[8,40,576]{2,1,0:T(8,128)(2,1)S(1)}, bf16[8,40,576]{2,1,0:T(8,128)(2,1)S(1)}, u32[]{:S(2)}, u32[]{:S(2)}) %collective-permute-start.34) | collective-permute-done | bytes 368672 | tf_op jit(solution)/shard_map/ppermute | solution.py:86
  167.9 1.5 collective-permute-done.24
  169.8 1.9 maximum_select_fusion.1
  171.8 1.8 maximum_select_fusion.2
  173.8 2.0 maximum_select_fusion
  178.6 9.5 %fusion.18 = bf16[256,1024,1]{1,0,2:T(8,128)(2,1)S(1)} fusion(pred[256,1024]{1,0:T(8,128)(4,1)S(1)} %copy-done.9, bf16[4,4,256,576]{3,2,1,0:T(8,128)(2,1)S(1)} %bitcast_select_fusion, bf16[4,4,1024,576]{2,3,0,1:T(8,128)(2,1)} %bitcast.119), kind=kOutput, calls=%fused_computation.29 | convolution fusion | flops 4832362496 | bytes 24379392 | tf_op jit(solution)/shard_map/clte,clfe->tf/dot_general | solution.py:148
  188.1 5.2 %convolution_bitcast_fusion = f32[4,256,576]{1,2,0:T(8,128)} fusion(bf16[256,1024,1]{1,0,2:T(8,128)(2,1)S(1)} %fusion.18, bf16[4,576,1024]{2,1,0:T(8,128)(2,1)} %bitcast.144), kind=kOutput, calls=%fused_computation.14 | convolution fusion | flops 1207959552 | bytes 7602176 | tf_op jit(solution)/shard_map/tf,cef->cte/dot_general | solution.py:150
  193.3 2.9 %reshape.133 = f32[4,2,128,576]{2,1,3,0:T(2,128)S(1)} reshape(f32[4,256,576]{1,2,0:T(8,128)} %convolution_bitcast_fusion) | data formatting | bytes 4718592 | tf_op jit(solution)/shard_map/reshape | solution.py:152
  196.1 4.7 %fusion.25 = (f32[2,2,2,64,576]{3,0,4,2,1:T(2,128)}, f32[2,2,2,64,576]{3,0,4,2,1:T(2,128)}) fusion(f32[2,2,2,128,576]{3,0,4,2,1:T(2,128)S(1)} %bitcast.116), kind=kLoop, calls=%fused_computation.97 | loop fusion | bytes 4718592 | tf_op jit(solution)/shard_map/slice | solution.py:60
  200.8 4.3 %copy.92 = f32[2,2,2,64,576]{4,3,1,0,2:T(8,128)} copy(f32[2,2,2,64,576]{3,0,4,2,1:T(2,128)} %get-tuple-element.8) | data formatting | bytes 2359296
  205.1 1.1 dynamic-slice_convert_fusion.7
  206.8 2.3 %copy.93 = f32[2,2,2,64,576]{4,3,0,1,2:T(8,128)} copy(f32[2,2,2,64,576]{3,0,4,2,1:T(2,128)S(1)} %copy-done.5) | data formatting | bytes 2359296
  209.1 1.2 dynamic-slice_convert_fusion.6
  210.4 1.1 convert_add_fusion.7
  212.8 1.4 collective-permute-start.40
  214.1 4.1 %collective-permute-done.37 = bf16[2,64,576]{2,1,0:T(8,128)(2,1)S(1)} collective-permute-done((bf16[2,64,576]{2,1,0:T(8,128)(2,1)S(1)}, bf16[2,64,576]{2,1,0:T(8,128)(2,1)S(1)}, u32[]{:S(2)}, u32[]{:S(2)}) %collective-permute-start.37) | collective-permute-done | bytes 147488 | tf_op jit(solution)/shard_map/ppermute | solution.py:70
  218.3 1.4 collective-permute-start.38
  220.8 2.0 collective-permute-done.38
  222.8 1.4 collective-permute-done.41
  (149 shorter events, 24.4 us)
Async XLA Ops:
  0.6 6.1 %copy-start = (s32[4,256,64]{1,2,0:T(8,128)S(1)}, s32[4,256,64]{1,2,0:T(8,128)}, u32[]{:S(2)}) copy-start(s32[4,256,64]{1,2,0:T(8,128)} %param.12) | copy-start | bytes 786436
  1.9 5.5 %collective-permute-start = (bf16[1,64,576]{2,1,0:T(8,128)(2,1)S(1)}, bf16[1,64,576]{2,1,0:T(8,128)(2,1)S(1)}, u32[]{:S(2)}, u32[]{:S(2)}) collective-permute-start(bf16[1,64,576]{2,1,0:T(8,128)(2,1)S(1)} %copy.90), channel_id=1, source_target_pairs={{0,2},{1,3},{2,0},{3,1},{4,6},{5,7},{6,4},{7,5},{8,10},{9,11},{10,... | collective-permute-start | bytes 221192 | tf_op jit(solution)/shard_map/ppermute | solution.py:86
  5.1 4.7 %collective-permute-start.3 = (bf16[1,64,576]{2,1,0:T(8,128)(2,1)S(1)}, bf16[1,64,576]{2,1,0:T(8,128)(2,1)S(1)}, u32[]{:S(2)}, u32[]{:S(2)}) collective-permute-start(bf16[1,64,576]{2,1,0:T(8,128)(2,1)S(1)} %copy.91), channel_id=1, source_target_pairs={{0,4},{4,0},{1,5},{5,1},{2,6},{6,2},{3,7},{7,3},{8,12},{12,8},{9,1... | collective-permute-start | bytes 221192 | tf_op jit(solution)/shard_map/ppermute | solution.py:86
  7.5 5.7 %collective-permute-start.1 = (bf16[2,64,576]{2,1,0:T(8,128)(2,1)S(1)}, bf16[2,64,576]{2,1,0:T(8,128)(2,1)S(1)}, u32[]{:S(2)}, u32[]{:S(2)}) collective-permute-start(bf16[2,64,576]{2,1,0:T(8,128)(2,1)S(1)} %maximum_select_fusion.16), channel_id=1, source_target_pairs={{0,4},{4,0},{1,5},{5,1},{2,6},{6,2},{3,7},{7,3},{8,12},{12,8},{9,1... | collective-permute-start | bytes 442376 | tf_op jit(solution)/shard_map/ppermute | solution.py:86
  9.9 5.4 %collective-permute-start.4 = (bf16[2,64,576]{2,1,0:T(8,128)(2,1)S(1)}, bf16[2,64,576]{2,1,0:T(8,128)(2,1)S(1)}, u32[]{:S(2)}, u32[]{:S(2)}) collective-permute-start(bf16[2,64,576]{2,1,0:T(8,128)(2,1)S(1)} %maximum_select_fusion.17), channel_id=1, source_target_pairs={{0,2},{1,3},{2,0},{3,1},{4,6},{5,7},{6,4},{7,5},{8,10},{9,11},{10,... | collective-permute-start | bytes 442376 | tf_op jit(solution)/shard_map/ppermute | solution.py:86
  13.2 36.2 %collective-permute-start.2 = (bf16[4,64,576]{2,1,0:T(8,128)(2,1)S(1)}, bf16[4,64,576]{2,1,0:T(8,128)(2,1)S(1)}, u32[]{:S(2)}, u32[]{:S(2)}) collective-permute-start(bf16[4,64,576]{2,1,0:T(8,128)(2,1)S(1)} %maximum_select_fusion.11), channel_id=1, source_target_pairs={{0,1},{1,0},{2,3},{3,2},{4,5},{5,4},{6,7},{7,6},{8,9},{9,8},{10,11... | collective-permute-start | bytes 884744 | tf_op jit(solution)/shard_map/ppermute | solution.py:86
  15.4 34.3 %collective-permute-start.5 = (bf16[4,64,576]{2,1,0:T(8,128)(2,1)S(1)}, bf16[4,64,576]{2,1,0:T(8,128)(2,1)S(1)}, u32[]{:S(2)}, u32[]{:S(2)}) collective-permute-start(bf16[4,64,576]{2,1,0:T(8,128)(2,1)S(1)} %maximum_select_fusion.12), channel_id=1, source_target_pairs={{0,1},{1,0},{2,3},{3,2},{4,5},{5,4},{6,7},{7,6},{8,9},{9,8},{10,11... | collective-permute-start | bytes 884744 | tf_op jit(solution)/shard_map/ppermute | solution.py:86
  24.9 27.0 %copy-start.8 = (pred[256,1024]{1,0:T(8,128)(4,1)}, pred[256,1024]{1,0:T(8,128)(4,1)S(1)}, u32[]{:S(2)}) copy-start(pred[256,1024]{1,0:T(8,128)(4,1)S(1)} %compare_reduce_fusion) | copy-start | bytes 786436
  50.1 1.8 copy-start.12
  84.1 2.0 copy-start.4
  85.2 6.2 %collective-permute-start.11 = (bf16[16,40,576]{2,1,0:T(8,128)(2,1)}, bf16[16,40,576]{2,1,0:T(8,128)(2,1)}, u32[]{:S(2)}, u32[]{:S(2)}) collective-permute-start(bf16[16,40,576]{2,1,0:T(8,128)(2,1)} %dynamic-slice_convert_fusion.2), channel_id=1, source_target_pairs={{0,1},{1,0},{2,3},{3,2},{4,5},{5,4},{6,7},{7,6},{8,9},{9,8},{10,11... | collective-permute-start | bytes 2211848 | tf_op jit(solution)/shard_map/ppermute | solution.py:70
  87.1 7.9 %collective-permute-start.16 = (bf16[16,40,576]{2,1,0:T(8,128)(2,1)}, bf16[16,40,576]{2,1,0:T(8,128)(2,1)}, u32[]{:S(2)}, u32[]{:S(2)}) collective-permute-start(bf16[16,40,576]{2,1,0:T(8,128)(2,1)} %dynamic-slice_convert_fusion.1), channel_id=1, source_target_pairs={{0,1},{1,0},{2,3},{3,2},{4,5},{5,4},{6,7},{7,6},{8,9},{9,8},{10,11... | collective-permute-start | bytes 2211848 | tf_op jit(solution)/shard_map/ppermute | solution.py:70
  88.4 1.9 copy-start.2
  91.4 5.5 %collective-permute-start.6 = (bf16[16,48,576]{2,1,0:T(8,128)(2,1)}, bf16[16,48,576]{2,1,0:T(8,128)(2,1)}, u32[]{:S(2)}, u32[]{:S(2)}) collective-permute-start(bf16[16,48,576]{2,1,0:T(8,128)(2,1)} %dynamic-slice_convert_fusion), channel_id=1, source_target_pairs={{0,1},{1,0},{2,3},{3,2},{4,5},{5,4},{6,7},{7,6},{8,9},{9,8},{10,11... | collective-permute-start | bytes 2654216 | tf_op jit(solution)/shard_map/ppermute | solution.py:70
  93.3 3.6 %copy-start.3 = (f32[2,2,2,2,2,48,576]{6,5,4,3,2,1,0:T(8,128)S(1)}, f32[2,2,2,2,2,48,576]{6,5,4,3,2,1,0:T(8,128)}, u32[]{:S(2)}) copy-start(f32[2,2,2,2,2,48,576]{6,5,4,3,2,1,0:T(8,128)} %copy-done.2) | copy-start | bytes 10616836
  93.3 11.9 %collective-permute-start.12 = (bf16[8,40,576]{2,1,0:T(8,128)(2,1)S(1)}, bf16[8,40,576]{2,1,0:T(8,128)(2,1)S(1)}, u32[]{:S(2)}, u32[]{:S(2)}) collective-permute-start(bf16[8,40,576]{2,1,0:T(8,128)(2,1)S(1)} %dynamic-slice_convert_fusion.5), channel_id=1, source_target_pairs={{0,4},{4,0},{1,5},{5,1},{2,6},{6,2},{3,7},{7,3},{8,12},{12,8},{9,1... | collective-permute-start | bytes 1105928 | tf_op jit(solution)/shard_map/ppermute | solution.py:70
  96.3 12.0 %collective-permute-start.17 = (bf16[8,40,576]{2,1,0:T(8,128)(2,1)S(1)}, bf16[8,40,576]{2,1,0:T(8,128)(2,1)S(1)}, u32[]{:S(2)}, u32[]{:S(2)}) collective-permute-start(bf16[8,40,576]{2,1,0:T(8,128)(2,1)S(1)} %dynamic-slice_convert_fusion.4), channel_id=1, source_target_pairs={{0,2},{1,3},{2,0},{3,1},{4,6},{5,7},{6,4},{7,5},{8,10},{9,11},{10,... | collective-permute-start | bytes 1105928 | tf_op jit(solution)/shard_map/ppermute | solution.py:70
  98.4 19.8 %collective-permute-start.7 = (bf16[8,48,576]{2,1,0:T(8,128)(2,1)S(1)}, bf16[8,48,576]{2,1,0:T(8,128)(2,1)S(1)}, u32[]{:S(2)}, u32[]{:S(2)}) collective-permute-start(bf16[8,48,576]{2,1,0:T(8,128)(2,1)S(1)} %dynamic-slice_convert_fusion.3), channel_id=1, source_target_pairs={{0,8},{8,0},{16,24},{24,16},{1,9},{9,1},{17,25},{25,17},{2,10},{10... | collective-permute-start | bytes 1327112 | tf_op jit(solution)/shard_map/ppermute | solution.py:70
  105.3 7.0 %collective-permute-start.13 = (bf16[4,40,576]{2,1,0:T(8,128)(2,1)S(1)}, bf16[4,40,576]{2,1,0:T(8,128)(2,1)S(1)}, u32[]{:S(2)}, u32[]{:S(2)}) collective-permute-start(bf16[4,40,576]{2,1,0:T(8,128)(2,1)S(1)} %dynamic-slice_convert_fusion.10), channel_id=1, source_target_pairs={{0,2},{1,3},{2,0},{3,1},{4,6},{5,7},{6,4},{7,5},{8,10},{9,11},{10,... | collective-permute-start | bytes 552968 | tf_op jit(solution)/shard_map/ppermute | solution.py:70
  108.4 8.5 %collective-permute-start.18 = (bf16[4,40,576]{2,1,0:T(8,128)(2,1)S(1)}, bf16[4,40,576]{2,1,0:T(8,128)(2,1)S(1)}, u32[]{:S(2)}, u32[]{:S(2)}) collective-permute-start(bf16[4,40,576]{2,1,0:T(8,128)(2,1)S(1)} %dynamic-slice_convert_fusion.9), channel_id=1, source_target_pairs={{0,8},{8,0},{16,24},{24,16},{1,9},{9,1},{17,25},{25,17},{2,10},{10... | collective-permute-start | bytes 552968 | tf_op jit(solution)/shard_map/ppermute | solution.py:70
  112.4 6.9 %collective-permute-start.14 = (bf16[2,40,576]{2,1,0:T(8,128)(2,1)S(1)}, bf16[2,40,576]{2,1,0:T(8,128)(2,1)S(1)}, u32[]{:S(2)}, u32[]{:S(2)}) collective-permute-start(bf16[2,40,576]{2,1,0:T(8,128)(2,1)S(1)} %dynamic-slice_convert_fusion.15), channel_id=1, source_target_pairs={{0,8},{8,0},{16,24},{24,16},{1,9},{9,1},{17,25},{25,17},{2,10},{10... | collective-permute-start | bytes 276488 | tf_op jit(solution)/shard_map/ppermute | solution.py:70
  117.0 5.6 %collective-permute-start.19 = (bf16[2,40,576]{2,1,0:T(8,128)(2,1)S(1)}, bf16[2,40,576]{2,1,0:T(8,128)(2,1)S(1)}, u32[]{:S(2)}, u32[]{:S(2)}) collective-permute-start(bf16[2,40,576]{2,1,0:T(8,128)(2,1)S(1)} %dynamic-slice_convert_fusion.14), channel_id=1, source_target_pairs={{0,4},{4,0},{1,5},{5,1},{2,6},{6,2},{3,7},{7,3},{8,12},{12,8},{9,1... | collective-permute-start | bytes 276488 | tf_op jit(solution)/shard_map/ppermute | solution.py:70
  118.4 17.2 %copy-start.10 = (bf16[4,32,576]{2,1,0:T(8,128)(2,1)S(1)}, bf16[4,32,576]{2,1,0:T(8,128)(2,1)}, u32[]{:S(2)}) copy-start(bf16[4,32,576]{2,1,0:T(8,128)(2,1)} %param.13) | copy-start | bytes 442372
  118.4 17.2 %copy-start.11 = (f32[4,576]{1,0:T(4,128)S(1)}, f32[4,576]{1,0:T(4,128)}, u32[]{:S(2)}) copy-start(f32[4,576]{1,0:T(4,128)} %param.11) | copy-start | bytes 27652
  118.4 6.9 %collective-permute-start.8 = (bf16[4,48,576]{2,1,0:T(8,128)(2,1)S(1)}, bf16[4,48,576]{2,1,0:T(8,128)(2,1)S(1)}, u32[]{:S(2)}, u32[]{:S(2)}) collective-permute-start(bf16[4,48,576]{2,1,0:T(8,128)(2,1)S(1)} %dynamic-slice_convert_fusion.8), channel_id=1, source_target_pairs={{0,4},{4,0},{1,5},{5,1},{2,6},{6,2},{3,7},{7,3},{8,12},{12,8},{9,1... | collective-permute-start | bytes 663560 | tf_op jit(solution)/shard_map/ppermute | solution.py:70
  119.3 7.6 %collective-permute-start.15 = (bf16[1,40,576]{2,1,0:T(8,128)(2,1)S(1)}, bf16[1,40,576]{2,1,0:T(8,128)(2,1)S(1)}, u32[]{:S(2)}, u32[]{:S(2)}) collective-permute-start(bf16[1,40,576]{2,1,0:T(8,128)(2,1)S(1)} %dynamic-slice_convert_fusion.20), channel_id=1, source_target_pairs={{0,16},{8,24},{16,0},{24,8},{1,17},{9,25},{17,1},{25,9},{2,18},{10... | collective-permute-start | bytes 138248 | tf_op jit(solution)/shard_map/ppermute | solution.py:70
  122.6 10.3 %collective-permute-start.20 = (bf16[1,40,576]{2,1,0:T(8,128)(2,1)S(1)}, bf16[1,40,576]{2,1,0:T(8,128)(2,1)S(1)}, u32[]{:S(2)}, u32[]{:S(2)}) collective-permute-start(bf16[1,40,576]{2,1,0:T(8,128)(2,1)S(1)} %dynamic-slice_convert_fusion.19), channel_id=1, source_target_pairs={{0,16},{8,24},{16,0},{24,8},{1,17},{9,25},{17,1},{25,9},{2,18},{10... | collective-permute-start | bytes 138248 | tf_op jit(solution)/shard_map/ppermute | solution.py:70
  125.3 4.9 %collective-permute-start.9 = (bf16[2,48,576]{2,1,0:T(8,128)(2,1)S(1)}, bf16[2,48,576]{2,1,0:T(8,128)(2,1)S(1)}, u32[]{:S(2)}, u32[]{:S(2)}) collective-permute-start(bf16[2,48,576]{2,1,0:T(8,128)(2,1)S(1)} %dynamic-slice_convert_fusion.13), channel_id=1, source_target_pairs={{0,2},{1,3},{2,0},{3,1},{4,6},{5,7},{6,4},{7,5},{8,10},{9,11},{10,... | collective-permute-start | bytes 331784 | tf_op jit(solution)/shard_map/ppermute | solution.py:70
  130.3 5.2 %collective-permute-start.10 = (bf16[1,48,576]{2,1,0:T(8,128)(2,1)S(1)}, bf16[1,48,576]{2,1,0:T(8,128)(2,1)S(1)}, u32[]{:S(2)}, u32[]{:S(2)}) collective-permute-start(bf16[1,48,576]{2,1,0:T(8,128)(2,1)S(1)} %dynamic-slice_convert_fusion.18), channel_id=1, source_target_pairs={{0,16},{8,24},{16,0},{24,8},{1,17},{9,25},{17,1},{25,9},{2,18},{10... | collective-permute-start | bytes 165896 | tf_op jit(solution)/shard_map/ppermute | solution.py:70
  135.6 24.9 %copy-start.7 = (bf16[4,32,576]{2,1,0:T(8,128)(2,1)}, bf16[4,32,576]{2,1,0:T(8,128)(2,1)S(1)}, u32[]{:S(2)}) copy-start(bf16[4,32,576]{2,1,0:T(8,128)(2,1)S(1)} %subtract_convert_fusion) | copy-start | bytes 442372
  135.7 6.2 %collective-permute-start.26 = (bf16[1,40,576]{2,1,0:T(8,128)(2,1)S(1)}, bf16[1,40,576]{2,1,0:T(8,128)(2,1)S(1)}, u32[]{:S(2)}, u32[]{:S(2)}) collective-permute-start(bf16[1,40,576]{2,1,0:T(8,128)(2,1)S(1)} %get-tuple-element.10), channel_id=1, source_target_pairs={{0,16},{8,24},{16,0},{24,8},{1,17},{9,25},{17,1},{25,9},{2,18},{10... | collective-permute-start | bytes 138248 | tf_op jit(solution)/shard_map/ppermute | solution.py:86
  138.9 7.5 %collective-permute-start.21 = (bf16[1,48,576]{2,1,0:T(8,128)(2,1)S(1)}, bf16[1,48,576]{2,1,0:T(8,128)(2,1)S(1)}, u32[]{:S(2)}, u32[]{:S(2)}) collective-permute-start(bf16[1,48,576]{2,1,0:T(8,128)(2,1)S(1)} %slice_bitcast_fusion.3), channel_id=1, source_target_pairs={{0,16},{8,24},{16,0},{24,8},{1,17},{9,25},{17,1},{25,9},{2,18},{10... | collective-permute-start | bytes 165896 | tf_op jit(solution)/shard_map/ppermute | solution.py:86
  139.0 6.2 %collective-permute-start.31 = (bf16[1,40,576]{2,1,0:T(8,128)(2,1)S(1)}, bf16[1,40,576]{2,1,0:T(8,128)(2,1)S(1)}, u32[]{:S(2)}, u32[]{:S(2)}) collective-permute-start(bf16[1,40,576]{2,1,0:T(8,128)(2,1)S(1)} %get-tuple-element.11), channel_id=1, source_target_pairs={{0,16},{8,24},{16,0},{24,8},{1,17},{9,25},{17,1},{25,9},{2,18},{10... | collective-permute-start | bytes 138248 | tf_op jit(solution)/shard_map/ppermute | solution.py:86
  141.9 6.4 %collective-permute-start.27 = (bf16[2,40,576]{2,1,0:T(8,128)(2,1)S(1)}, bf16[2,40,576]{2,1,0:T(8,128)(2,1)S(1)}, u32[]{:S(2)}, u32[]{:S(2)}) collective-permute-start(bf16[2,40,576]{2,1,0:T(8,128)(2,1)S(1)} %maximum_select_fusion.19), channel_id=1, source_target_pairs={{0,8},{8,0},{16,24},{24,16},{1,9},{9,1},{17,25},{25,17},{2,10},{10... | collective-permute-start | bytes 276488 | tf_op jit(solution)/shard_map/ppermute | solution.py:86
  145.2 5.8 %collective-permute-start.32 = (bf16[2,40,576]{2,1,0:T(8,128)(2,1)S(1)}, bf16[2,40,576]{2,1,0:T(8,128)(2,1)S(1)}, u32[]{:S(2)}, u32[]{:S(2)}) collective-permute-start(bf16[2,40,576]{2,1,0:T(8,128)(2,1)S(1)} %maximum_select_fusion.20), channel_id=1, source_target_pairs={{0,4},{4,0},{1,5},{5,1},{2,6},{6,2},{3,7},{7,3},{8,12},{12,8},{9,1... | collective-permute-start | bytes 276488 | tf_op jit(solution)/shard_map/ppermute | solution.py:86
  146.4 7.4 %collective-permute-start.22 = (bf16[2,48,576]{2,1,0:T(8,128)(2,1)S(1)}, bf16[2,48,576]{2,1,0:T(8,128)(2,1)S(1)}, u32[]{:S(2)}, u32[]{:S(2)}) collective-permute-start(bf16[2,48,576]{2,1,0:T(8,128)(2,1)S(1)} %maximum_select_fusion.18), channel_id=1, source_target_pairs={{0,2},{1,3},{2,0},{3,1},{4,6},{5,7},{6,4},{7,5},{8,10},{9,11},{10,... | collective-permute-start | bytes 331784 | tf_op jit(solution)/shard_map/ppermute | solution.py:86
  148.3 8.2 %collective-permute-start.28 = (bf16[4,40,576]{2,1,0:T(8,128)(2,1)S(1)}, bf16[4,40,576]{2,1,0:T(8,128)(2,1)S(1)}, u32[]{:S(2)}, u32[]{:S(2)}) collective-permute-start(bf16[4,40,576]{2,1,0:T(8,128)(2,1)S(1)} %maximum_select_fusion.14), channel_id=1, source_target_pairs={{0,2},{1,3},{2,0},{3,1},{4,6},{5,7},{6,4},{7,5},{8,10},{9,11},{10,... | collective-permute-start | bytes 552968 | tf_op jit(solution)/shard_map/ppermute | solution.py:86
  151.1 8.4 %collective-permute-start.33 = (bf16[4,40,576]{2,1,0:T(8,128)(2,1)S(1)}, bf16[4,40,576]{2,1,0:T(8,128)(2,1)S(1)}, u32[]{:S(2)}, u32[]{:S(2)}) collective-permute-start(bf16[4,40,576]{2,1,0:T(8,128)(2,1)S(1)} %maximum_select_fusion.15), channel_id=1, source_target_pairs={{0,8},{8,0},{16,24},{24,16},{1,9},{9,1},{17,25},{25,17},{2,10},{10... | collective-permute-start | bytes 552968 | tf_op jit(solution)/shard_map/ppermute | solution.py:86
  153.9 6.5 %collective-permute-start.23 = (bf16[4,48,576]{2,1,0:T(8,128)(2,1)S(1)}, bf16[4,48,576]{2,1,0:T(8,128)(2,1)S(1)}, u32[]{:S(2)}, u32[]{:S(2)}) collective-permute-start(bf16[4,48,576]{2,1,0:T(8,128)(2,1)S(1)} %maximum_select_fusion.13), channel_id=1, source_target_pairs={{0,4},{4,0},{1,5},{5,1},{2,6},{6,2},{3,7},{7,3},{8,12},{12,8},{9,1... | collective-permute-start | bytes 663560 | tf_op jit(solution)/shard_map/ppermute | solution.py:86
  156.7 8.0 %collective-permute-start.29 = (bf16[8,40,576]{2,1,0:T(8,128)(2,1)S(1)}, bf16[8,40,576]{2,1,0:T(8,128)(2,1)S(1)}, u32[]{:S(2)}, u32[]{:S(2)}) collective-permute-start(bf16[8,40,576]{2,1,0:T(8,128)(2,1)S(1)} %maximum_select_fusion.9), channel_id=1, source_target_pairs={{0,4},{4,0},{1,5},{5,1},{2,6},{6,2},{3,7},{7,3},{8,12},{12,8},{9,1... | collective-permute-start | bytes 1105928 | tf_op jit(solution)/shard_map/ppermute | solution.py:86
  159.6 8.0 %collective-permute-start.34 = (bf16[8,40,576]{2,1,0:T(8,128)(2,1)S(1)}, bf16[8,40,576]{2,1,0:T(8,128)(2,1)S(1)}, u32[]{:S(2)}, u32[]{:S(2)}) collective-permute-start(bf16[8,40,576]{2,1,0:T(8,128)(2,1)S(1)} %maximum_select_fusion.10), channel_id=1, source_target_pairs={{0,2},{1,3},{2,0},{3,1},{4,6},{5,7},{6,4},{7,5},{8,10},{9,11},{10,... | collective-permute-start | bytes 1105928 | tf_op jit(solution)/shard_map/ppermute | solution.py:86
  160.5 8.9 %collective-permute-start.24 = (bf16[8,48,576]{2,1,0:T(8,128)(2,1)S(1)}, bf16[8,48,576]{2,1,0:T(8,128)(2,1)S(1)}, u32[]{:S(2)}, u32[]{:S(2)}) collective-permute-start(bf16[8,48,576]{2,1,0:T(8,128)(2,1)S(1)} %maximum_select_fusion.8), channel_id=1, source_target_pairs={{0,8},{8,0},{16,24},{24,16},{1,9},{9,1},{17,25},{25,17},{2,10},{10... | collective-permute-start | bytes 1327112 | tf_op jit(solution)/shard_map/ppermute | solution.py:86
  164.9 4.8 %collective-permute-start.30 = (bf16[16,40,576]{2,1,0:T(8,128)(2,1)S(1)}, bf16[16,40,576]{2,1,0:T(8,128)(2,1)}, u32[]{:S(2)}, u32[]{:S(2)}) collective-permute-start(bf16[16,40,576]{2,1,0:T(8,128)(2,1)S(1)} %maximum_select_fusion.4), channel_id=1, source_target_pairs={{0,1},{1,0},{2,3},{3,2},{4,5},{5,4},{6,7},{7,6},{8,9},{9,8},{10,11... | collective-permute-start | bytes 2211848 | tf_op jit(solution)/shard_map/ppermute | solution.py:86
  167.8 4.0 %collective-permute-start.35 = (bf16[16,40,576]{2,1,0:T(8,128)(2,1)S(1)}, bf16[16,40,576]{2,1,0:T(8,128)(2,1)}, u32[]{:S(2)}, u32[]{:S(2)}) collective-permute-start(bf16[16,40,576]{2,1,0:T(8,128)(2,1)S(1)} %maximum_select_fusion.5), channel_id=1, source_target_pairs={{0,1},{1,0},{2,3},{3,2},{4,5},{5,4},{6,7},{7,6},{8,9},{9,8},{10,11... | collective-permute-start | bytes 2211848 | tf_op jit(solution)/shard_map/ppermute | solution.py:86
  169.7 4.1 %collective-permute-start.25 = (bf16[16,48,576]{2,1,0:T(8,128)(2,1)S(1)}, bf16[16,48,576]{2,1,0:T(8,128)(2,1)}, u32[]{:S(2)}, u32[]{:S(2)}) collective-permute-start(bf16[16,48,576]{2,1,0:T(8,128)(2,1)S(1)} %maximum_select_fusion.3), channel_id=1, source_target_pairs={{0,1},{1,0},{2,3},{3,2},{4,5},{5,4},{6,7},{7,6},{8,9},{9,8},{10,11... | collective-permute-start | bytes 2654216 | tf_op jit(solution)/shard_map/ppermute | solution.py:86
  177.7 1.0 copy-start.9
  200.8 5.9 %copy-start.5 = (f32[2,2,2,64,576]{3,0,4,2,1:T(2,128)S(1)}, f32[2,2,2,64,576]{3,0,4,2,1:T(2,128)}, u32[]{:S(2)}) copy-start(f32[2,2,2,64,576]{3,0,4,2,1:T(2,128)} %get-tuple-element.9) | copy-start | bytes 3538948
  206.2 4.2 %collective-permute-start.36 = (bf16[4,64,576]{2,1,0:T(8,128)(2,1)S(1)}, bf16[4,64,576]{2,1,0:T(8,128)(2,1)S(1)}, u32[]{:S(2)}, u32[]{:S(2)}) collective-permute-start(bf16[4,64,576]{2,1,0:T(8,128)(2,1)S(1)} %dynamic-slice_convert_fusion.7), channel_id=1, source_target_pairs={{0,1},{1,0},{2,3},{3,2},{4,5},{5,4},{6,7},{7,6},{8,9},{9,8},{10,11... | collective-permute-start | bytes 884744 | tf_op jit(solution)/shard_map/ppermute | solution.py:70
  209.1 3.6 %copy-start.6 = (f32[2,2,2,64,576]{4,3,0,1,2:T(8,128)S(1)}, f32[2,2,2,64,576]{4,3,0,1,2:T(8,128)}, u32[]{:S(2)}) copy-start(f32[2,2,2,64,576]{4,3,0,1,2:T(8,128)} %copy.93) | copy-start | bytes 3538948
  210.3 2.4 %collective-permute-start.39 = (bf16[4,64,576]{2,1,0:T(8,128)(2,1)S(1)}, bf16[4,64,576]{2,1,0:T(8,128)(2,1)S(1)}, u32[]{:S(2)}, u32[]{:S(2)}) collective-permute-start(bf16[4,64,576]{2,1,0:T(8,128)(2,1)S(1)} %dynamic-slice_convert_fusion.6), channel_id=1, source_target_pairs={{0,1},{1,0},{2,3},{3,2},{4,5},{5,4},{6,7},{7,6},{8,9},{9,8},{10,11... | collective-permute-start | bytes 884744 | tf_op jit(solution)/shard_map/ppermute | solution.py:70
  211.5 13.5 %copy-start.1 = (s32[4,256,64]{1,2,0:T(8,128)S(1)}, s32[4,256,64]{1,2,0:T(8,128)}, u32[]{:S(2)}) copy-start(s32[4,256,64]{1,2,0:T(8,128)} %param.12) | copy-start | bytes 786436
  211.6 6.6 %collective-permute-start.37 = (bf16[2,64,576]{2,1,0:T(8,128)(2,1)S(1)}, bf16[2,64,576]{2,1,0:T(8,128)(2,1)S(1)}, u32[]{:S(2)}, u32[]{:S(2)}) collective-permute-start(bf16[2,64,576]{2,1,0:T(8,128)(2,1)S(1)} %dynamic-slice_convert_fusion.12), channel_id=1, source_target_pairs={{0,4},{4,0},{1,5},{5,1},{2,6},{6,2},{3,7},{7,3},{8,12},{12,8},{9,1... | collective-permute-start | bytes 442376 | tf_op jit(solution)/shard_map/ppermute | solution.py:70
  212.8 6.9 %collective-permute-start.40 = (bf16[2,64,576]{2,1,0:T(8,128)(2,1)S(1)}, bf16[2,64,576]{2,1,0:T(8,128)(2,1)S(1)}, u32[]{:S(2)}, u32[]{:S(2)}) collective-permute-start(bf16[2,64,576]{2,1,0:T(8,128)(2,1)S(1)} %dynamic-slice_convert_fusion.11), channel_id=1, source_target_pairs={{0,2},{1,3},{2,0},{3,1},{4,6},{5,7},{6,4},{7,5},{8,10},{9,11},{10,... | collective-permute-start | bytes 442376 | tf_op jit(solution)/shard_map/ppermute | solution.py:70
  218.3 4.5 %collective-permute-start.38 = (bf16[1,64,576]{2,1,0:T(8,128)(2,1)S(1)}, bf16[1,64,576]{2,1,0:T(8,128)(2,1)S(1)}, u32[]{:S(2)}, u32[]{:S(2)}) collective-permute-start(bf16[1,64,576]{2,1,0:T(8,128)(2,1)S(1)} %dynamic-slice_convert_fusion.17), channel_id=1, source_target_pairs={{0,2},{1,3},{2,0},{3,1},{4,6},{5,7},{6,4},{7,5},{8,10},{9,11},{10,... | collective-permute-start | bytes 221192 | tf_op jit(solution)/shard_map/ppermute | solution.py:70
  219.7 4.5 %collective-permute-start.41 = (bf16[1,64,576]{2,1,0:T(8,128)(2,1)S(1)}, bf16[1,64,576]{2,1,0:T(8,128)(2,1)S(1)}, u32[]{:S(2)}, u32[]{:S(2)}) collective-permute-start(bf16[1,64,576]{2,1,0:T(8,128)(2,1)S(1)} %dynamic-slice_convert_fusion.16), channel_id=1, source_target_pairs={{0,4},{4,0},{1,5},{5,1},{2,6},{6,2},{3,7},{7,3},{8,12},{12,8},{9,1... | collective-permute-start | bytes 221192 | tf_op jit(solution)/shard_map/ppermute | solution.py:70

commit v7 on v5

--- a/solution.py
+++ b/solution.py
@@ -51,15 +51,11 @@
 
 def reduce_scatter(blocks, axes, wire):
     labels, prefix, orders, suffix = plan(axes)
-    n, rows, cols = blocks.shape
     nb = len(labels)
-    x = blocks.reshape([2] * nb + [rows, cols])
     steps = [prefix + order + suffix for order in orders]
     parts = []
-    for (start, size), order in zip(portion_rows(rows, len(orders)), steps):
-        xp = lax.slice_in_dim(x, start, start + size, axis=nb)
-        xp = jnp.transpose(xp, [labels.index(l) for l in order] + [nb, nb + 1])
-        parts.append(xp.reshape(n, size, cols))
+    for (start, size), order in zip(portion_rows(blocks.rows, len(orders)), steps):
+        parts.append(blocks.portion([labels.index(l) for l in order], start, size))
     for k in range(nb):
         for p in range(len(parts)):
             axis, bit = steps[p][k]
@@ -95,6 +91,20 @@
     return jnp.concatenate(out, axis=1)
 
 
+class Blocks:
+    def __init__(self, array, bit_axes, row_axes, cols):
+        self.array, self.bit_axes, self.row_axes, self.cols = array, bit_axes, row_axes, cols
+        self.rows = 1
+        for axis in row_axes:
+            self.rows *= array.shape[axis]
+
+    def portion(self, bit_order, start, size):
+        (row_axis,) = self.row_axes
+        x = lax.slice_in_dim(self.array, start, start + size, axis=row_axis)
+        order = [self.bit_axes[b] for b in bit_order] + [row_axis, self.array.ndim - 1]
+        return jnp.transpose(x, order).reshape(2 ** len(bit_order), size, self.cols)
+
+
 def local(resid, encoder, encoder_bias, decoder, decoder_bias, topk_index, target):
     planes = lax.axis_size("lz")
     feat_parts = lax.axis_size("feat")
@@ -119,18 +129,22 @@
     first_feat = half_bit * (feat_total // 2) + feat_pos * feat_dev
     feat_ids = first_feat + lax.iota(jnp.int32, feat_dev)
     layer_index = lax.dynamic_index_in_dim(topk_index, layer_id, 0, keepdims=False)
-    selected = jnp.any(layer_index[:, :, None] == feat_ids[None, None, :], axis=1).astype(
+    selected = jnp.any(layer_index.T[:, :, None] == feat_ids[None, None, :], axis=0).astype(
         jnp.float32
     )
     acts = (selected * pre).astype(jnp.bfloat16)
     live_layers = lax.iota(jnp.int32, layer_count) >= layer_id
     partial_value = jnp.einsum("tf,lfd->ltd", acts, decoder[0], preferred_element_type=jnp.float32)
     partial_value = jnp.where(live_layers[:, None, None], partial_value, 0.0)
-    blocks = (
+    slot_bits = slots.bit_length() - 1
+    feat_bits = feat_parts.bit_length() - 1
+    every_bits = slot_bits + feat_bits
+    ordered = (
         partial_value.reshape(layer_count, slots, slot_rows, feat_parts, cols)
         .transpose(1, 3, 0, 2, 4)
-        .reshape(slots * feat_parts, layer_count * slot_rows, cols)
+        .reshape([2] * every_bits + [layer_count * slot_rows, cols])
     )
+    blocks = Blocks(ordered, list(range(every_bits)), (every_bits,), cols)
     recon = reduce_scatter(blocks, EVERY, jnp.bfloat16).reshape(layer_count, slot_rows, cols)
     recon = recon + decoder_bias[:, None, :]
     error = (recon - target.astype(jnp.float32)).astype(jnp.bfloat16)
@@ -143,14 +157,10 @@
     kept = jnp.where(live_layers[:, None, None], piece, jnp.zeros_like(piece))
     grad_act = jnp.einsum("ltd,lfd->tf", kept, decoder[0], preferred_element_type=jnp.float32)
     grad_pre = (selected * grad_act).astype(jnp.bfloat16)
-    grad_part = lax.dot_general(
-        grad_pre, encoder[0], (((1,), (1,)), ((), ())), preferred_element_type=jnp.float32
-    )
-    grad_blocks = (
-        grad_part.reshape(2, half_rows, feat_parts, cols)
-        .transpose(0, 2, 1, 3)
-        .reshape(2 * feat_parts, half_rows, cols)
-    )
+    enc_chunks = encoder[0].reshape(feat_parts, cols, feat_dev)
+    grad_part = jnp.einsum("tf,cef->cte", grad_pre, enc_chunks, preferred_element_type=jnp.float32)
+    grad_shaped = grad_part.reshape([2] * feat_bits + [2, half_rows, cols])
+    grad_blocks = Blocks(grad_shaped, [feat_bits] + list(range(feat_bits)), (feat_bits + 1,), cols)
     grad_sum = reduce_scatter(grad_blocks, PLANE, jnp.bfloat16)
     return (error, grad_sum.astype(jnp.bfloat16)[None])
 

time: 211 us -> 220 us (1.043)
  local copies, waits for them, and re-layouts: 55.9 us -> 63.1 us
    transpose x8 -> x9, local copies, waits for them, and re-layouts: 9.01 us -> 13.4 us  [the longest x8 13.4 us: portion(): return jnp.transpose(x, order).reshape(2 ** len(bit_order), size, self.cols)]
    reshape x0 -> x1, local copies, waits for them, and re-layouts: none -> 2.86 us  [local(): grad_shaped = grad_part.reshape([2] * feat_bits + [2, half_rows, cols])]
  transfers between devices with their start and end apart: 42 -> 42, of which waited for: 21 -> 21; matrix products, arithmetic and copies ran while one was open for 14% -> 13% of each run, Pallas kernels for 0% -> 0%
where the time goes in v7:
time: 220 us; the launch traced here: 219 us
  local copies, waits for them, and re-layouts  63.1 us (29%)
  starting transfers between devices  55.6 us (25%)
  waiting for transfers between devices  42.7 us (19%)
  matrix products  31 us (14%)
  other arithmetic  25.4 us (12%)
    ppermute x21, starting transfers between devices, all_gather(): recv = lax.ppermute(parts[p], axis, partner(axis, bit))  29.1 us
    ppermute x21, starting transfers between devices, reduce_scatter(): recv = lax.ppermute(send.astype(wire), axis, partner(axis, bit))  26.5 us
    ppermute x21, waiting for transfers between devices, reduce_scatter(): recv = lax.ppermute(send.astype(wire), axis, partner(axis, bit))  26.1 us
    reshape x2, local copies, waits for them, and re-layouts, local(): partial_value.reshape(layer_count, slots, slot_rows, feat_parts, cols)  18.7 us
    ppermute x21, waiting for transfers between devices, all_gather(): recv = lax.ppermute(parts[p], axis, partner(axis, bit))  16.7 us
    dot_general x1, matrix products, local(): jnp.einsum('tf,lfd->ltd', acts, decoder[0], preferred_element_type=jnp.fl...  13.9 us
    transpose x8, local copies, waits for them, and re-layouts, portion(): return jnp.transpose(x, order).reshape(2 ** len(bit_order), size, self.cols)  13.4 us
    dot_general x1, matrix products, local(): jnp.einsum('ltd,lfd->tf', kept, decoder[0], preferred_element_type=jnp.fl...  10.5 us
  transfers between devices with their start and end apart: 42, of which 21 were waited for; matrix products, arithmetic and copies ran while one was open for 13% of the time, Pallas kernels for 0%

profile of v7, /device:TPU:0, one launch (start us, length us, event | category | flops | bytes accessed | tf_op | source)
XLA Modules:
  0.0 219.1 jit_solution(2139476491845120478)
XLA Ops:
  1.9 3.1 %collective-permute-start = (bf16[1,64,576]{2,1,0:T(8,128)(2,1)S(1)}, bf16[1,64,576]{2,1,0:T(8,128)(2,1)S(1)}, u32[]{:S(2)}, u32[]{:S(2)}) collective-permute-start(bf16[1,64,576]{2,1,0:T(8,128)(2,1)S(1)} %copy.64), channel_id=1, source_target_pairs={{0,2},{1,3},{2,0},{3,1},{4,6},{5,7},{6,4},{7,5},{8,10},{9,11},{10,... | collective-permute-start | bytes 221192 | tf_op jit(solution)/shard_map/ppermute | solution.py:82
  5.1 1.6 collective-permute-start.3
  7.5 2.0 collective-permute-start.1
  9.9 1.2 collective-permute-start.4
  11.1 2.0 collective-permute-done.1
  13.3 2.0 collective-permute-done.4
  15.5 10.1 %compare_reduce_fusion = pred[256,1024]{1,0:T(8,128)(4,1)S(1)} fusion(s32[1024]{0:T(1024)S(1)} %iota_add_fusion, s32[64,256]{1,0:T(8,128)S(1)} %dynamic-slice_bitcast_fusion), kind=kLoop, calls=%fused_computation | loop fusion | flops 33292288 | bytes 331776 | tf_op jit(solution)/shard_map/reduce_or | solution.py:132
  27.2 3.8 %fusion.40 = bf16[256,1024,1]{1,0,2:T(8,128)(2,1)S(1)} fusion(pred[256,1024]{1,0:T(8,128)(4,1)S(1)} %compare_reduce_fusion, bf16[1,2304,1024]{2,1,0:T(8,128)(2,1)} %param.8, bf16[288,8,2,128]{3,2,1,0:T(2,128)(2,1)S(1)} %bitcast.141, f32[1024]{0:T(1024)S(1)} %bitcast.147), kind=kOutput, calls=%fused_computation.35 | convolution fusion | flops 1208745984 | bytes 6688768 | tf_op jit(solution)/shard_map/dot_general | solution.py:128
  31.0 13.9 %select_bitcast_fusion = f32[4,256,2304]{2,1,0:T(8,128)} fusion(bf16[256,1024,1]{1,0,2:T(8,128)(2,1)S(1)} %fusion.40, bf16[1,4,1024,2304]{3,2,1,0:T(8,128)(2,1)} %param.10, pred[4]{0:T(512)(128)(4,1)S(1)} %iota_compare_fusion), kind=kOutput, calls=%fused_computation.5 | convolution fusion | flops 4834197504 | bytes 28835844 | tf_op jit(solution)/shard_map/tf,lfd->ltd/dot_general | solution.py:137
  44.9 13.2 %reshape.124 = f32[4,8,32,4,576]{4,3,2,1,0:T(4,128)} reshape(f32[4,256,2304]{2,1,0:T(8,128)} %select_bitcast_fusion) | data formatting | bytes 18874368 | tf_op jit(solution)/shard_map/reshape | solution.py:143
  58.1 5.5 %copy.53 = f32[4,8,32,4,576]{4,2,0,3,1:T(8,128)S(1)} copy(f32[4,8,32,4,576]{4,3,2,1,0:T(4,128)} %reshape.124) | data formatting | bytes 18874368 | tf_op jit(solution)/shard_map/reshape | solution.py:143
  68.9 1.9 copy-done.2
  71.9 1.8 convert_add_fusion.2
  73.8 1.7 collective-permute-start.12
  75.4 1.3 convert_add_fusion.1
  77.4 1.5 convert_add_fusion
  78.9 1.6 collective-permute-start.7
  80.5 5.2 %collective-permute-done.12 = bf16[8,40,576]{2,1,0:T(8,128)(2,1)S(1)} collective-permute-done((bf16[8,40,576]{2,1,0:T(8,128)(2,1)S(1)}, bf16[8,40,576]{2,1,0:T(8,128)(2,1)S(1)}, u32[]{:S(2)}, u32[]{:S(2)}) %collective-permute-start.12) | collective-permute-done | bytes 368672 | tf_op jit(solution)/shard_map/ppermute | solution.py:66
  85.8 1.2 collective-permute-start.13
  87.1 1.7 collective-permute-done.17
  88.9 1.5 collective-permute-start.18
  90.4 2.4 %collective-permute-done.13 = bf16[4,40,576]{2,1,0:T(8,128)(2,1)S(1)} collective-permute-done((bf16[4,40,576]{2,1,0:T(8,128)(2,1)S(1)}, bf16[4,40,576]{2,1,0:T(8,128)(2,1)S(1)}, u32[]{:S(2)}, u32[]{:S(2)}) %collective-permute-start.13) | collective-permute-done | bytes 184352 | tf_op jit(solution)/shard_map/ppermute | solution.py:66
  92.9 1.6 collective-permute-start.14
  94.5 2.8 %collective-permute-done.18 = bf16[4,40,576]{2,1,0:T(8,128)(2,1)S(1)} collective-permute-done((bf16[4,40,576]{2,1,0:T(8,128)(2,1)S(1)}, bf16[4,40,576]{2,1,0:T(8,128)(2,1)S(1)}, u32[]{:S(2)}, u32[]{:S(2)}) %collective-permute-start.18) | collective-permute-done | bytes 184352 | tf_op jit(solution)/shard_map/ppermute | solution.py:66
  97.4 1.2 collective-permute-start.19
  99.8 2.7 %collective-permute-start.15 = (bf16[1,40,576]{2,1,0:T(8,128)(2,1)S(1)}, bf16[1,40,576]{2,1,0:T(8,128)(2,1)S(1)}, u32[]{:S(2)}, u32[]{:S(2)}) collective-permute-start(bf16[1,40,576]{2,1,0:T(8,128)(2,1)S(1)} %dynamic-slice_convert_fusion.20), channel_id=1, source_target_pairs={{0,16},{8,24},{16,0},{24,8},{1,17},{9,25},{17,1},{25,9},{2,18},{10... | collective-permute-start | bytes 138248 | tf_op jit(solution)/shard_map/ppermute | solution.py:66
  103.1 2.7 %collective-permute-start.20 = (bf16[1,40,576]{2,1,0:T(8,128)(2,1)S(1)}, bf16[1,40,576]{2,1,0:T(8,128)(2,1)S(1)}, u32[]{:S(2)}, u32[]{:S(2)}) collective-permute-start(bf16[1,40,576]{2,1,0:T(8,128)(2,1)S(1)} %dynamic-slice_convert_fusion.19), channel_id=1, source_target_pairs={{0,16},{8,24},{16,0},{24,8},{1,17},{9,25},{17,1},{25,9},{2,18},{10... | collective-permute-start | bytes 138248 | tf_op jit(solution)/shard_map/ppermute | solution.py:66
  105.8 1.6 collective-permute-start.9
  107.4 3.3 %collective-permute-done.9 = bf16[2,48,576]{2,1,0:T(8,128)(2,1)S(1)} collective-permute-done((bf16[2,48,576]{2,1,0:T(8,128)(2,1)S(1)}, bf16[2,48,576]{2,1,0:T(8,128)(2,1)S(1)}, u32[]{:S(2)}, u32[]{:S(2)}) %collective-permute-start.9) | collective-permute-done | bytes 110624 | tf_op jit(solution)/shard_map/ppermute | solution.py:66
  110.8 2.6 %collective-permute-start.10 = (bf16[1,48,576]{2,1,0:T(8,128)(2,1)S(1)}, bf16[1,48,576]{2,1,0:T(8,128)(2,1)S(1)}, u32[]{:S(2)}, u32[]{:S(2)}) collective-permute-start(bf16[1,48,576]{2,1,0:T(8,128)(2,1)S(1)} %dynamic-slice_convert_fusion.18), channel_id=1, source_target_pairs={{0,16},{8,24},{16,0},{24,8},{1,17},{9,25},{17,1},{25,9},{2,18},{10... | collective-permute-start | bytes 165896 | tf_op jit(solution)/shard_map/ppermute | solution.py:66
  113.4 2.6 %collective-permute-done.10 = bf16[1,48,576]{2,1,0:T(8,128)(2,1)S(1)} collective-permute-done((bf16[1,48,576]{2,1,0:T(8,128)(2,1)S(1)}, bf16[1,48,576]{2,1,0:T(8,128)(2,1)S(1)}, u32[]{:S(2)}, u32[]{:S(2)}) %collective-permute-start.10) | collective-permute-done | bytes 55328 | tf_op jit(solution)/shard_map/ppermute | solution.py:66
  116.2 3.2 %collective-permute-start.26 = (bf16[1,40,576]{2,1,0:T(8,128)(2,1)S(1)}, bf16[1,40,576]{2,1,0:T(8,128)(2,1)S(1)}, u32[]{:S(2)}, u32[]{:S(2)}) collective-permute-start(bf16[1,40,576]{2,1,0:T(8,128)(2,1)S(1)} %get-tuple-element.10), channel_id=1, source_target_pairs={{0,16},{8,24},{16,0},{24,8},{1,17},{9,25},{17,1},{25,9},{2,18},{10... | collective-permute-start | bytes 138248 | tf_op jit(solution)/shard_map/ppermute | solution.py:82
  119.5 2.8 %collective-permute-start.31 = (bf16[1,40,576]{2,1,0:T(8,128)(2,1)S(1)}, bf16[1,40,576]{2,1,0:T(8,128)(2,1)S(1)}, u32[]{:S(2)}, u32[]{:S(2)}) collective-permute-start(bf16[1,40,576]{2,1,0:T(8,128)(2,1)S(1)} %get-tuple-element.11), channel_id=1, source_target_pairs={{0,16},{8,24},{16,0},{24,8},{1,17},{9,25},{17,1},{25,9},{2,18},{10... | collective-permute-start | bytes 138248 | tf_op jit(solution)/shard_map/ppermute | solution.py:82
  122.4 3.3 %collective-permute-start.27 = (bf16[2,40,576]{2,1,0:T(8,128)(2,1)S(1)}, bf16[2,40,576]{2,1,0:T(8,128)(2,1)S(1)}, u32[]{:S(2)}, u32[]{:S(2)}) collective-permute-start(bf16[2,40,576]{2,1,0:T(8,128)(2,1)S(1)} %maximum_select_fusion.19), channel_id=1, source_target_pairs={{0,8},{8,0},{16,24},{24,16},{1,9},{9,1},{17,25},{25,17},{2,10},{10... | collective-permute-start | bytes 276488 | tf_op jit(solution)/shard_map/ppermute | solution.py:82
  125.7 1.2 collective-permute-start.32
  126.9 1.5 collective-permute-start.22
  128.8 1.5 collective-permute-start.28
  130.4 1.1 collective-permute-done.32
  131.6 2.7 %collective-permute-start.33 = (bf16[4,40,576]{2,1,0:T(8,128)(2,1)S(1)}, bf16[4,40,576]{2,1,0:T(8,128)(2,1)S(1)}, u32[]{:S(2)}, u32[]{:S(2)}) collective-permute-start(bf16[4,40,576]{2,1,0:T(8,128)(2,1)S(1)} %maximum_select_fusion.15), channel_id=1, source_target_pairs={{0,8},{8,0},{16,24},{24,16},{1,9},{9,1},{17,25},{25,17},{2,10},{10... | collective-permute-start | bytes 552968 | tf_op jit(solution)/shard_map/ppermute | solution.py:82
  134.4 1.2 collective-permute-start.23
  135.5 1.5 collective-permute-done.28
  138.1 1.8 collective-permute-done.33
  141.0 1.6 collective-permute-start.24
  142.6 2.6 %collective-permute-done.29 = bf16[8,40,576]{2,1,0:T(8,128)(2,1)S(1)} collective-permute-done((bf16[8,40,576]{2,1,0:T(8,128)(2,1)S(1)}, bf16[8,40,576]{2,1,0:T(8,128)(2,1)S(1)}, u32[]{:S(2)}, u32[]{:S(2)}) %collective-permute-start.29) | collective-permute-done | bytes 368672 | tf_op jit(solution)/shard_map/ppermute | solution.py:82
  145.5 2.6 %collective-permute-done.34 = bf16[8,40,576]{2,1,0:T(8,128)(2,1)S(1)} collective-permute-done((bf16[8,40,576]{2,1,0:T(8,128)(2,1)S(1)}, bf16[8,40,576]{2,1,0:T(8,128)(2,1)S(1)}, u32[]{:S(2)}, u32[]{:S(2)}) %collective-permute-start.34) | collective-permute-done | bytes 368672 | tf_op jit(solution)/shard_map/ppermute | solution.py:82
  148.4 1.5 collective-permute-done.24
  150.2 1.8 maximum_select_fusion.1
  152.2 1.8 maximum_select_fusion.2
  154.2 2.1 maximum_select_fusion
  157.6 6.4 %copy.60 = bf16[4,8,32,4,576]{4,3,2,1,0:T(4,128)(2,1)} copy(bf16[4,8,32,4,576]{4,2,0,3,1:T(8,128)(2,1)S(1)} %bitcast.119) | data formatting | bytes 9437184 | tf_op jit(solution)/shard_map/transpose | solution.py:154
  164.0 9.9 %reshape.135 = bf16[4,256,2304]{2,1,0:T(8,128)(2,1)} reshape(bf16[4,8,32,4,576]{4,3,2,1,0:T(4,128)(2,1)} %copy.60) | data formatting | bytes 9437184 | tf_op jit(solution)/shard_map/reshape | solution.py:155
  173.9 10.5 %fusion.35 = bf16[256,1024,1]{1,0,2:T(8,128)(2,1)S(1)} fusion(pred[256,1024]{1,0:T(8,128)(4,1)S(1)} %copy-done.9, bf16[1,4,1024,2304]{3,2,1,0:T(8,128)(2,1)} %param.10, bf16[4,256,2304]{2,1,0:T(8,128)(2,1)} %reshape.135, pred[4]{0:T(512)(128)(4,1)S(1)} %iota_compare_fusion), kind=kOutput, calls=%fused_computation.34 | convolution fusion | flops 4834721792 | bytes 24379396 | tf_op jit(solution)/shard_map/ltd,lfd->tf/dot_general | solution.py:158
  184.4 2.8 %convolution_bitcast_fusion = f32[4,256,576]{1,2,0:T(8,128)} fusion(bf16[256,1024,1]{1,0,2:T(8,128)(2,1)S(1)} %fusion.35, bf16[4,576,1024]{2,1,0:T(8,128)(2,1)S(1)} %bitcast.146), kind=kOutput, calls=%fused_computation.20 | convolution fusion | flops 1207959552 | bytes 7602176 | tf_op jit(solution)/shard_map/tf,cef->cte/dot_general | solution.py:161
  187.3 2.9 %reshape.136 = f32[2,2,2,128,576]{3,2,4,1,0:T(2,128)S(1)} reshape(f32[4,256,576]{1,2,0:T(8,128)} %convolution_bitcast_fusion) | data formatting | bytes 4718592 | tf_op jit(solution)/shard_map/reshape | solution.py:162
  190.1 4.7 %slice_bitcast_fusion.4 = (f32[2,2,2,64,576]{3,1,4,0,2:T(2,128)}, f32[2,2,2,64,576]{3,2,4,0,1:T(2,128)}) fusion(f32[2,2,2,128,576]{3,2,4,1,0:T(2,128)S(1)} %reshape.136), kind=kLoop, calls=%fused_computation.15 | loop fusion | bytes 4718592 | tf_op jit(solution)/shard_map/transpose | solution.py:105
  194.8 4.2 %copy.61 = f32[2,2,2,64,576]{4,3,2,1,0:T(8,128)} copy(f32[2,2,2,64,576]{3,1,4,0,2:T(2,128)} %get-tuple-element.8) | data formatting | bytes 2359296 | tf_op jit(solution)/shard_map/transpose | solution.py:105
  200.8 2.3 %copy.62 = f32[2,2,2,64,576]{4,3,2,1,0:T(8,128)} copy(f32[2,2,2,64,576]{3,2,4,0,1:T(2,128)S(1)} %copy-done.5) | data formatting | bytes 2359296 | tf_op jit(solution)/shard_map/transpose | solution.py:105
  203.1 1.2 dynamic-slice_convert_fusion.6
  204.4 1.1 convert_add_fusion.7
  206.8 1.4 collective-permute-start.40
  208.2 4.1 %collective-permute-done.37 = bf16[2,64,576]{2,1,0:T(8,128)(2,1)S(1)} collective-permute-done((bf16[2,64,576]{2,1,0:T(8,128)(2,1)S(1)}, bf16[2,64,576]{2,1,0:T(8,128)(2,1)S(1)}, u32[]{:S(2)}, u32[]{:S(2)}) %collective-permute-start.37) | collective-permute-done | bytes 147488 | tf_op jit(solution)/shard_map/ppermute | solution.py:66
  212.3 1.4 collective-permute-start.38
  214.8 2.0 collective-permute-done.38
  216.8 1.4 collective-permute-done.41
  (152 shorter events, 24.4 us)
Async XLA Ops:
  0.6 6.1 %copy-start = (s32[4,256,64]{1,2,0:T(8,128)S(1)}, s32[4,256,64]{1,2,0:T(8,128)}, u32[]{:S(2)}) copy-start(s32[4,256,64]{1,2,0:T(8,128)} %param.12) | copy-start | bytes 786436
  1.9 5.5 %collective-permute-start = (bf16[1,64,576]{2,1,0:T(8,128)(2,1)S(1)}, bf16[1,64,576]{2,1,0:T(8,128)(2,1)S(1)}, u32[]{:S(2)}, u32[]{:S(2)}) collective-permute-start(bf16[1,64,576]{2,1,0:T(8,128)(2,1)S(1)} %copy.64), channel_id=1, source_target_pairs={{0,2},{1,3},{2,0},{3,1},{4,6},{5,7},{6,4},{7,5},{8,10},{9,11},{10,... | collective-permute-start | bytes 221192 | tf_op jit(solution)/shard_map/ppermute | solution.py:82
  5.1 4.7 %collective-permute-start.3 = (bf16[1,64,576]{2,1,0:T(8,128)(2,1)S(1)}, bf16[1,64,576]{2,1,0:T(8,128)(2,1)S(1)}, u32[]{:S(2)}, u32[]{:S(2)}) collective-permute-start(bf16[1,64,576]{2,1,0:T(8,128)(2,1)S(1)} %copy.65), channel_id=1, source_target_pairs={{0,4},{4,0},{1,5},{5,1},{2,6},{6,2},{3,7},{7,3},{8,12},{12,8},{9,1... | collective-permute-start | bytes 221192 | tf_op jit(solution)/shard_map/ppermute | solution.py:82
  7.5 5.7 %collective-permute-start.1 = (bf16[2,64,576]{2,1,0:T(8,128)(2,1)S(1)}, bf16[2,64,576]{2,1,0:T(8,128)(2,1)S(1)}, u32[]{:S(2)}, u32[]{:S(2)}) collective-permute-start(bf16[2,64,576]{2,1,0:T(8,128)(2,1)S(1)} %maximum_select_fusion.16), channel_id=1, source_target_pairs={{0,4},{4,0},{1,5},{5,1},{2,6},{6,2},{3,7},{7,3},{8,12},{12,8},{9,1... | collective-permute-start | bytes 442376 | tf_op jit(solution)/shard_map/ppermute | solution.py:82
  9.9 5.4 %collective-permute-start.4 = (bf16[2,64,576]{2,1,0:T(8,128)(2,1)S(1)}, bf16[2,64,576]{2,1,0:T(8,128)(2,1)S(1)}, u32[]{:S(2)}, u32[]{:S(2)}) collective-permute-start(bf16[2,64,576]{2,1,0:T(8,128)(2,1)S(1)} %maximum_select_fusion.17), channel_id=1, source_target_pairs={{0,2},{1,3},{2,0},{3,1},{4,6},{5,7},{6,4},{7,5},{8,10},{9,11},{10,... | collective-permute-start | bytes 442376 | tf_op jit(solution)/shard_map/ppermute | solution.py:82
  13.2 12.3 %collective-permute-start.2 = (bf16[4,64,576]{2,1,0:T(8,128)(2,1)S(1)}, bf16[4,64,576]{2,1,0:T(8,128)(2,1)S(1)}, u32[]{:S(2)}, u32[]{:S(2)}) collective-permute-start(bf16[4,64,576]{2,1,0:T(8,128)(2,1)S(1)} %maximum_select_fusion.11), channel_id=1, source_target_pairs={{0,1},{1,0},{2,3},{3,2},{4,5},{5,4},{6,7},{7,6},{8,9},{9,8},{10,11... | collective-permute-start | bytes 884744 | tf_op jit(solution)/shard_map/ppermute | solution.py:82
  15.4 10.4 %collective-permute-start.5 = (bf16[4,64,576]{2,1,0:T(8,128)(2,1)S(1)}, bf16[4,64,576]{2,1,0:T(8,128)(2,1)S(1)}, u32[]{:S(2)}, u32[]{:S(2)}) collective-permute-start(bf16[4,64,576]{2,1,0:T(8,128)(2,1)S(1)} %maximum_select_fusion.12), channel_id=1, source_target_pairs={{0,1},{1,0},{2,3},{3,2},{4,5},{5,4},{6,7},{7,6},{8,9},{9,8},{10,11... | collective-permute-start | bytes 884744 | tf_op jit(solution)/shard_map/ppermute | solution.py:82
  25.5 1.7 copy-start.8
  26.1 1.2 copy-start.12
  64.7 1.9 copy-start.4
  65.8 6.1 %collective-permute-start.11 = (bf16[16,40,576]{2,1,0:T(8,128)(2,1)}, bf16[16,40,576]{2,1,0:T(8,128)(2,1)}, u32[]{:S(2)}, u32[]{:S(2)}) collective-permute-start(bf16[16,40,576]{2,1,0:T(8,128)(2,1)} %dynamic-slice_convert_fusion.2), channel_id=1, source_target_pairs={{0,1},{1,0},{2,3},{3,2},{4,5},{5,4},{6,7},{7,6},{8,9},{9,8},{10,11... | collective-permute-start | bytes 2211848 | tf_op jit(solution)/shard_map/ppermute | solution.py:66
  67.6 7.8 %collective-permute-start.16 = (bf16[16,40,576]{2,1,0:T(8,128)(2,1)}, bf16[16,40,576]{2,1,0:T(8,128)(2,1)}, u32[]{:S(2)}, u32[]{:S(2)}) collective-permute-start(bf16[16,40,576]{2,1,0:T(8,128)(2,1)} %dynamic-slice_convert_fusion.1), channel_id=1, source_target_pairs={{0,1},{1,0},{2,3},{3,2},{4,5},{5,4},{6,7},{7,6},{8,9},{9,8},{10,11... | collective-permute-start | bytes 2211848 | tf_op jit(solution)/shard_map/ppermute | solution.py:66
  68.9 1.9 copy-start.2
  71.9 5.5 %collective-permute-start.6 = (bf16[16,48,576]{2,1,0:T(8,128)(2,1)}, bf16[16,48,576]{2,1,0:T(8,128)(2,1)}, u32[]{:S(2)}, u32[]{:S(2)}) collective-permute-start(bf16[16,48,576]{2,1,0:T(8,128)(2,1)} %dynamic-slice_convert_fusion), channel_id=1, source_target_pairs={{0,1},{1,0},{2,3},{3,2},{4,5},{5,4},{6,7},{7,6},{8,9},{9,8},{10,11... | collective-permute-start | bytes 2654216 | tf_op jit(solution)/shard_map/ppermute | solution.py:66
  73.8 3.6 %copy-start.3 = (f32[2,2,2,2,2,48,576]{6,5,4,3,2,1,0:T(8,128)S(1)}, f32[2,2,2,2,2,48,576]{6,5,4,3,2,1,0:T(8,128)}, u32[]{:S(2)}) copy-start(f32[2,2,2,2,2,48,576]{6,5,4,3,2,1,0:T(8,128)} %copy-done.2) | copy-start | bytes 10616836
  73.8 11.9 %collective-permute-start.12 = (bf16[8,40,576]{2,1,0:T(8,128)(2,1)S(1)}, bf16[8,40,576]{2,1,0:T(8,128)(2,1)S(1)}, u32[]{:S(2)}, u32[]{:S(2)}) collective-permute-start(bf16[8,40,576]{2,1,0:T(8,128)(2,1)S(1)} %dynamic-slice_convert_fusion.5), channel_id=1, source_target_pairs={{0,4},{4,0},{1,5},{5,1},{2,6},{6,2},{3,7},{7,3},{8,12},{12,8},{9,1... | collective-permute-start | bytes 1105928 | tf_op jit(solution)/shard_map/ppermute | solution.py:66
  76.8 12.0 %collective-permute-start.17 = (bf16[8,40,576]{2,1,0:T(8,128)(2,1)S(1)}, bf16[8,40,576]{2,1,0:T(8,128)(2,1)S(1)}, u32[]{:S(2)}, u32[]{:S(2)}) collective-permute-start(bf16[8,40,576]{2,1,0:T(8,128)(2,1)S(1)} %dynamic-slice_convert_fusion.4), channel_id=1, source_target_pairs={{0,2},{1,3},{2,0},{3,1},{4,6},{5,7},{6,4},{7,5},{8,10},{9,11},{10,... | collective-permute-start | bytes 1105928 | tf_op jit(solution)/shard_map/ppermute | solution.py:66
  78.9 19.8 %collective-permute-start.7 = (bf16[8,48,576]{2,1,0:T(8,128)(2,1)S(1)}, bf16[8,48,576]{2,1,0:T(8,128)(2,1)S(1)}, u32[]{:S(2)}, u32[]{:S(2)}) collective-permute-start(bf16[8,48,576]{2,1,0:T(8,128)(2,1)S(1)} %dynamic-slice_convert_fusion.3), channel_id=1, source_target_pairs={{0,8},{8,0},{16,24},{24,16},{1,9},{9,1},{17,25},{25,17},{2,10},{10... | collective-permute-start | bytes 1327112 | tf_op jit(solution)/shard_map/ppermute | solution.py:66
  85.8 7.0 %collective-permute-start.13 = (bf16[4,40,576]{2,1,0:T(8,128)(2,1)S(1)}, bf16[4,40,576]{2,1,0:T(8,128)(2,1)S(1)}, u32[]{:S(2)}, u32[]{:S(2)}) collective-permute-start(bf16[4,40,576]{2,1,0:T(8,128)(2,1)S(1)} %dynamic-slice_convert_fusion.10), channel_id=1, source_target_pairs={{0,2},{1,3},{2,0},{3,1},{4,6},{5,7},{6,4},{7,5},{8,10},{9,11},{10,... | collective-permute-start | bytes 552968 | tf_op jit(solution)/shard_map/ppermute | solution.py:66
  88.9 8.5 %collective-permute-start.18 = (bf16[4,40,576]{2,1,0:T(8,128)(2,1)S(1)}, bf16[4,40,576]{2,1,0:T(8,128)(2,1)S(1)}, u32[]{:S(2)}, u32[]{:S(2)}) collective-permute-start(bf16[4,40,576]{2,1,0:T(8,128)(2,1)S(1)} %dynamic-slice_convert_fusion.9), channel_id=1, source_target_pairs={{0,8},{8,0},{16,24},{24,16},{1,9},{9,1},{17,25},{25,17},{2,10},{10... | collective-permute-start | bytes 552968 | tf_op jit(solution)/shard_map/ppermute | solution.py:66
  92.9 6.9 %collective-permute-start.14 = (bf16[2,40,576]{2,1,0:T(8,128)(2,1)S(1)}, bf16[2,40,576]{2,1,0:T(8,128)(2,1)S(1)}, u32[]{:S(2)}, u32[]{:S(2)}) collective-permute-start(bf16[2,40,576]{2,1,0:T(8,128)(2,1)S(1)} %dynamic-slice_convert_fusion.15), channel_id=1, source_target_pairs={{0,8},{8,0},{16,24},{24,16},{1,9},{9,1},{17,25},{25,17},{2,10},{10... | collective-permute-start | bytes 276488 | tf_op jit(solution)/shard_map/ppermute | solution.py:66
  97.4 5.6 %collective-permute-start.19 = (bf16[2,40,576]{2,1,0:T(8,128)(2,1)S(1)}, bf16[2,40,576]{2,1,0:T(8,128)(2,1)S(1)}, u32[]{:S(2)}, u32[]{:S(2)}) collective-permute-start(bf16[2,40,576]{2,1,0:T(8,128)(2,1)S(1)} %dynamic-slice_convert_fusion.14), channel_id=1, source_target_pairs={{0,4},{4,0},{1,5},{5,1},{2,6},{6,2},{3,7},{7,3},{8,12},{12,8},{9,1... | collective-permute-start | bytes 276488 | tf_op jit(solution)/shard_map/ppermute | solution.py:66
  98.8 17.2 %copy-start.10 = (bf16[4,32,576]{2,1,0:T(8,128)(2,1)S(1)}, bf16[4,32,576]{2,1,0:T(8,128)(2,1)}, u32[]{:S(2)}) copy-start(bf16[4,32,576]{2,1,0:T(8,128)(2,1)} %param.13) | copy-start | bytes 442372
  98.9 17.2 %copy-start.11 = (f32[4,576]{1,0:T(4,128)S(1)}, f32[4,576]{1,0:T(4,128)}, u32[]{:S(2)}) copy-start(f32[4,576]{1,0:T(4,128)} %param.11) | copy-start | bytes 27652
  98.9 6.9 %collective-permute-start.8 = (bf16[4,48,576]{2,1,0:T(8,128)(2,1)S(1)}, bf16[4,48,576]{2,1,0:T(8,128)(2,1)S(1)}, u32[]{:S(2)}, u32[]{:S(2)}) collective-permute-start(bf16[4,48,576]{2,1,0:T(8,128)(2,1)S(1)} %dynamic-slice_convert_fusion.8), channel_id=1, source_target_pairs={{0,4},{4,0},{1,5},{5,1},{2,6},{6,2},{3,7},{7,3},{8,12},{12,8},{9,1... | collective-permute-start | bytes 663560 | tf_op jit(solution)/shard_map/ppermute | solution.py:66
  99.8 7.6 %collective-permute-start.15 = (bf16[1,40,576]{2,1,0:T(8,128)(2,1)S(1)}, bf16[1,40,576]{2,1,0:T(8,128)(2,1)S(1)}, u32[]{:S(2)}, u32[]{:S(2)}) collective-permute-start(bf16[1,40,576]{2,1,0:T(8,128)(2,1)S(1)} %dynamic-slice_convert_fusion.20), channel_id=1, source_target_pairs={{0,16},{8,24},{16,0},{24,8},{1,17},{9,25},{17,1},{25,9},{2,18},{10... | collective-permute-start | bytes 138248 | tf_op jit(solution)/shard_map/ppermute | solution.py:66
  103.1 10.3 %collective-permute-start.20 = (bf16[1,40,576]{2,1,0:T(8,128)(2,1)S(1)}, bf16[1,40,576]{2,1,0:T(8,128)(2,1)S(1)}, u32[]{:S(2)}, u32[]{:S(2)}) collective-permute-start(bf16[1,40,576]{2,1,0:T(8,128)(2,1)S(1)} %dynamic-slice_convert_fusion.19), channel_id=1, source_target_pairs={{0,16},{8,24},{16,0},{24,8},{1,17},{9,25},{17,1},{25,9},{2,18},{10... | collective-permute-start | bytes 138248 | tf_op jit(solution)/shard_map/ppermute | solution.py:66
  105.8 4.9 %collective-permute-start.9 = (bf16[2,48,576]{2,1,0:T(8,128)(2,1)S(1)}, bf16[2,48,576]{2,1,0:T(8,128)(2,1)S(1)}, u32[]{:S(2)}, u32[]{:S(2)}) collective-permute-start(bf16[2,48,576]{2,1,0:T(8,128)(2,1)S(1)} %dynamic-slice_convert_fusion.13), channel_id=1, source_target_pairs={{0,2},{1,3},{2,0},{3,1},{4,6},{5,7},{6,4},{7,5},{8,10},{9,11},{10,... | collective-permute-start | bytes 331784 | tf_op jit(solution)/shard_map/ppermute | solution.py:66
  110.8 5.2 %collective-permute-start.10 = (bf16[1,48,576]{2,1,0:T(8,128)(2,1)S(1)}, bf16[1,48,576]{2,1,0:T(8,128)(2,1)S(1)}, u32[]{:S(2)}, u32[]{:S(2)}) collective-permute-start(bf16[1,48,576]{2,1,0:T(8,128)(2,1)S(1)} %dynamic-slice_convert_fusion.18), channel_id=1, source_target_pairs={{0,16},{8,24},{16,0},{24,8},{1,17},{9,25},{17,1},{25,9},{2,18},{10... | collective-permute-start | bytes 165896 | tf_op jit(solution)/shard_map/ppermute | solution.py:66
  116.1 24.9 %copy-start.7 = (bf16[4,32,576]{2,1,0:T(8,128)(2,1)}, bf16[4,32,576]{2,1,0:T(8,128)(2,1)S(1)}, u32[]{:S(2)}) copy-start(bf16[4,32,576]{2,1,0:T(8,128)(2,1)S(1)} %subtract_convert_fusion) | copy-start | bytes 442372
  116.2 6.2 %collective-permute-start.26 = (bf16[1,40,576]{2,1,0:T(8,128)(2,1)S(1)}, bf16[1,40,576]{2,1,0:T(8,128)(2,1)S(1)}, u32[]{:S(2)}, u32[]{:S(2)}) collective-permute-start(bf16[1,40,576]{2,1,0:T(8,128)(2,1)S(1)} %get-tuple-element.10), channel_id=1, source_target_pairs={{0,16},{8,24},{16,0},{24,8},{1,17},{9,25},{17,1},{25,9},{2,18},{10... | collective-permute-start | bytes 138248 | tf_op jit(solution)/shard_map/ppermute | solution.py:82
  119.4 7.5 %collective-permute-start.21 = (bf16[1,48,576]{2,1,0:T(8,128)(2,1)S(1)}, bf16[1,48,576]{2,1,0:T(8,128)(2,1)S(1)}, u32[]{:S(2)}, u32[]{:S(2)}) collective-permute-start(bf16[1,48,576]{2,1,0:T(8,128)(2,1)S(1)} %slice_bitcast_fusion.5), channel_id=1, source_target_pairs={{0,16},{8,24},{16,0},{24,8},{1,17},{9,25},{17,1},{25,9},{2,18},{10... | collective-permute-start | bytes 165896 | tf_op jit(solution)/shard_map/ppermute | solution.py:82
  119.5 6.2 %collective-permute-start.31 = (bf16[1,40,576]{2,1,0:T(8,128)(2,1)S(1)}, bf16[1,40,576]{2,1,0:T(8,128)(2,1)S(1)}, u32[]{:S(2)}, u32[]{:S(2)}) collective-permute-start(bf16[1,40,576]{2,1,0:T(8,128)(2,1)S(1)} %get-tuple-element.11), channel_id=1, source_target_pairs={{0,16},{8,24},{16,0},{24,8},{1,17},{9,25},{17,1},{25,9},{2,18},{10... | collective-permute-start | bytes 138248 | tf_op jit(solution)/shard_map/ppermute | solution.py:82
  122.4 6.4 %collective-permute-start.27 = (bf16[2,40,576]{2,1,0:T(8,128)(2,1)S(1)}, bf16[2,40,576]{2,1,0:T(8,128)(2,1)S(1)}, u32[]{:S(2)}, u32[]{:S(2)}) collective-permute-start(bf16[2,40,576]{2,1,0:T(8,128)(2,1)S(1)} %maximum_select_fusion.19), channel_id=1, source_target_pairs={{0,8},{8,0},{16,24},{24,16},{1,9},{9,1},{17,25},{25,17},{2,10},{10... | collective-permute-start | bytes 276488 | tf_op jit(solution)/shard_map/ppermute | solution.py:82
  125.7 5.8 %collective-permute-start.32 = (bf16[2,40,576]{2,1,0:T(8,128)(2,1)S(1)}, bf16[2,40,576]{2,1,0:T(8,128)(2,1)S(1)}, u32[]{:S(2)}, u32[]{:S(2)}) collective-permute-start(bf16[2,40,576]{2,1,0:T(8,128)(2,1)S(1)} %maximum_select_fusion.20), channel_id=1, source_target_pairs={{0,4},{4,0},{1,5},{5,1},{2,6},{6,2},{3,7},{7,3},{8,12},{12,8},{9,1... | collective-permute-start | bytes 276488 | tf_op jit(solution)/shard_map/ppermute | solution.py:82
  126.9 7.4 %collective-permute-start.22 = (bf16[2,48,576]{2,1,0:T(8,128)(2,1)S(1)}, bf16[2,48,576]{2,1,0:T(8,128)(2,1)S(1)}, u32[]{:S(2)}, u32[]{:S(2)}) collective-permute-start(bf16[2,48,576]{2,1,0:T(8,128)(2,1)S(1)} %maximum_select_fusion.18), channel_id=1, source_target_pairs={{0,2},{1,3},{2,0},{3,1},{4,6},{5,7},{6,4},{7,5},{8,10},{9,11},{10,... | collective-permute-start | bytes 331784 | tf_op jit(solution)/shard_map/ppermute | solution.py:82
  128.8 8.2 %collective-permute-start.28 = (bf16[4,40,576]{2,1,0:T(8,128)(2,1)S(1)}, bf16[4,40,576]{2,1,0:T(8,128)(2,1)S(1)}, u32[]{:S(2)}, u32[]{:S(2)}) collective-permute-start(bf16[4,40,576]{2,1,0:T(8,128)(2,1)S(1)} %maximum_select_fusion.14), channel_id=1, source_target_pairs={{0,2},{1,3},{2,0},{3,1},{4,6},{5,7},{6,4},{7,5},{8,10},{9,11},{10,... | collective-permute-start | bytes 552968 | tf_op jit(solution)/shard_map/ppermute | solution.py:82
  131.6 8.3 %collective-permute-start.33 = (bf16[4,40,576]{2,1,0:T(8,128)(2,1)S(1)}, bf16[4,40,576]{2,1,0:T(8,128)(2,1)S(1)}, u32[]{:S(2)}, u32[]{:S(2)}) collective-permute-start(bf16[4,40,576]{2,1,0:T(8,128)(2,1)S(1)} %maximum_select_fusion.15), channel_id=1, source_target_pairs={{0,8},{8,0},{16,24},{24,16},{1,9},{9,1},{17,25},{25,17},{2,10},{10... | collective-permute-start | bytes 552968 | tf_op jit(solution)/shard_map/ppermute | solution.py:82
  134.4 6.5 %collective-permute-start.23 = (bf16[4,48,576]{2,1,0:T(8,128)(2,1)S(1)}, bf16[4,48,576]{2,1,0:T(8,128)(2,1)S(1)}, u32[]{:S(2)}, u32[]{:S(2)}) collective-permute-start(bf16[4,48,576]{2,1,0:T(8,128)(2,1)S(1)} %maximum_select_fusion.13), channel_id=1, source_target_pairs={{0,4},{4,0},{1,5},{5,1},{2,6},{6,2},{3,7},{7,3},{8,12},{12,8},{9,1... | collective-permute-start | bytes 663560 | tf_op jit(solution)/shard_map/ppermute | solution.py:82
  137.2 8.0 %collective-permute-start.29 = (bf16[8,40,576]{2,1,0:T(8,128)(2,1)S(1)}, bf16[8,40,576]{2,1,0:T(8,128)(2,1)S(1)}, u32[]{:S(2)}, u32[]{:S(2)}) collective-permute-start(bf16[8,40,576]{2,1,0:T(8,128)(2,1)S(1)} %maximum_select_fusion.9), channel_id=1, source_target_pairs={{0,4},{4,0},{1,5},{5,1},{2,6},{6,2},{3,7},{7,3},{8,12},{12,8},{9,1... | collective-permute-start | bytes 1105928 | tf_op jit(solution)/shard_map/ppermute | solution.py:82
  140.0 8.0 %collective-permute-start.34 = (bf16[8,40,576]{2,1,0:T(8,128)(2,1)S(1)}, bf16[8,40,576]{2,1,0:T(8,128)(2,1)S(1)}, u32[]{:S(2)}, u32[]{:S(2)}) collective-permute-start(bf16[8,40,576]{2,1,0:T(8,128)(2,1)S(1)} %maximum_select_fusion.10), channel_id=1, source_target_pairs={{0,2},{1,3},{2,0},{3,1},{4,6},{5,7},{6,4},{7,5},{8,10},{9,11},{10,... | collective-permute-start | bytes 1105928 | tf_op jit(solution)/shard_map/ppermute | solution.py:82
  141.0 8.9 %collective-permute-start.24 = (bf16[8,48,576]{2,1,0:T(8,128)(2,1)S(1)}, bf16[8,48,576]{2,1,0:T(8,128)(2,1)S(1)}, u32[]{:S(2)}, u32[]{:S(2)}) collective-permute-start(bf16[8,48,576]{2,1,0:T(8,128)(2,1)S(1)} %maximum_select_fusion.8), channel_id=1, source_target_pairs={{0,8},{8,0},{16,24},{24,16},{1,9},{9,1},{17,25},{25,17},{2,10},{10... | collective-permute-start | bytes 1327112 | tf_op jit(solution)/shard_map/ppermute | solution.py:82
  145.4 4.8 %collective-permute-start.30 = (bf16[16,40,576]{2,1,0:T(8,128)(2,1)S(1)}, bf16[16,40,576]{2,1,0:T(8,128)(2,1)}, u32[]{:S(2)}, u32[]{:S(2)}) collective-permute-start(bf16[16,40,576]{2,1,0:T(8,128)(2,1)S(1)} %maximum_select_fusion.4), channel_id=1, source_target_pairs={{0,1},{1,0},{2,3},{3,2},{4,5},{5,4},{6,7},{7,6},{8,9},{9,8},{10,11... | collective-permute-start | bytes 2211848 | tf_op jit(solution)/shard_map/ppermute | solution.py:82
  148.3 3.9 %collective-permute-start.35 = (bf16[16,40,576]{2,1,0:T(8,128)(2,1)S(1)}, bf16[16,40,576]{2,1,0:T(8,128)(2,1)}, u32[]{:S(2)}, u32[]{:S(2)}) collective-permute-start(bf16[16,40,576]{2,1,0:T(8,128)(2,1)S(1)} %maximum_select_fusion.5), channel_id=1, source_target_pairs={{0,1},{1,0},{2,3},{3,2},{4,5},{5,4},{6,7},{7,6},{8,9},{9,8},{10,11... | collective-permute-start | bytes 2211848 | tf_op jit(solution)/shard_map/ppermute | solution.py:82
  150.1 4.0 %collective-permute-start.25 = (bf16[16,48,576]{2,1,0:T(8,128)(2,1)S(1)}, bf16[16,48,576]{2,1,0:T(8,128)(2,1)}, u32[]{:S(2)}, u32[]{:S(2)}) collective-permute-start(bf16[16,48,576]{2,1,0:T(8,128)(2,1)S(1)} %maximum_select_fusion.3), channel_id=1, source_target_pairs={{0,1},{1,0},{2,3},{3,2},{4,5},{5,4},{6,7},{7,6},{8,9},{9,8},{10,11... | collective-permute-start | bytes 2654216 | tf_op jit(solution)/shard_map/ppermute | solution.py:82
  164.0 9.9 %copy-start.9 = (pred[256,1024]{1,0:T(8,128)(4,1)S(1)}, pred[256,1024]{1,0:T(8,128)(4,1)}, u32[]{:S(2)}) copy-start(pred[256,1024]{1,0:T(8,128)(4,1)} %copy-done.8) | copy-start | bytes 786436
  164.0 20.5 %slice-start = ((s8[4718592]{0:T(1024)(128)(4,1)}), s8[524288]{0:T(1024)(128)(4,1)S(1)}, s32[]{:S(2)}) async-start(s8[4718592]{0:T(1024)(128)(4,1)} %bitcast.144), calls=%async_computation | async-start | bytes 1048576
  173.9 10.5 %slice-start.1 = ((s8[4718592]{0:T(1024)(128)(4,1)}), s8[4194304]{0:T(1024)(128)(4,1)S(1)}, s32[]{:S(2)}) async-start(s8[4718592]{0:T(1024)(128)(4,1)} %bitcast.144), calls=%async_computation.1 | async-start | bytes 8388608
  194.8 5.9 %copy-start.5 = (f32[2,2,2,64,576]{3,2,4,0,1:T(2,128)S(1)}, f32[2,2,2,64,576]{3,2,4,0,1:T(2,128)}, u32[]{:S(2)}) copy-start(f32[2,2,2,64,576]{3,2,4,0,1:T(2,128)} %get-tuple-element.9) | copy-start | bytes 3538948
  200.2 4.2 %collective-permute-start.36 = (bf16[4,64,576]{2,1,0:T(8,128)(2,1)S(1)}, bf16[4,64,576]{2,1,0:T(8,128)(2,1)S(1)}, u32[]{:S(2)}, u32[]{:S(2)}) collective-permute-start(bf16[4,64,576]{2,1,0:T(8,128)(2,1)S(1)} %dynamic-slice_convert_fusion.7), channel_id=1, source_target_pairs={{0,1},{1,0},{2,3},{3,2},{4,5},{5,4},{6,7},{7,6},{8,9},{9,8},{10,11... | collective-permute-start | bytes 884744 | tf_op jit(solution)/shard_map/ppermute | solution.py:66
  203.1 3.6 %copy-start.6 = (f32[2,2,2,64,576]{4,3,2,1,0:T(8,128)S(1)}, f32[2,2,2,64,576]{4,3,2,1,0:T(8,128)}, u32[]{:S(2)}) copy-start(f32[2,2,2,64,576]{4,3,2,1,0:T(8,128)} %copy.62) | copy-start | bytes 3538948
  204.3 2.4 %collective-permute-start.39 = (bf16[4,64,576]{2,1,0:T(8,128)(2,1)S(1)}, bf16[4,64,576]{2,1,0:T(8,128)(2,1)S(1)}, u32[]{:S(2)}, u32[]{:S(2)}) collective-permute-start(bf16[4,64,576]{2,1,0:T(8,128)(2,1)S(1)} %dynamic-slice_convert_fusion.6), channel_id=1, source_target_pairs={{0,1},{1,0},{2,3},{3,2},{4,5},{5,4},{6,7},{7,6},{8,9},{9,8},{10,11... | collective-permute-start | bytes 884744 | tf_op jit(solution)/shard_map/ppermute | solution.py:66
  205.5 13.5 %copy-start.1 = (s32[4,256,64]{1,2,0:T(8,128)S(1)}, s32[4,256,64]{1,2,0:T(8,128)}, u32[]{:S(2)}) copy-start(s32[4,256,64]{1,2,0:T(8,128)} %param.12) | copy-start | bytes 786436
  205.6 6.6 %collective-permute-start.37 = (bf16[2,64,576]{2,1,0:T(8,128)(2,1)S(1)}, bf16[2,64,576]{2,1,0:T(8,128)(2,1)S(1)}, u32[]{:S(2)}, u32[]{:S(2)}) collective-permute-start(bf16[2,64,576]{2,1,0:T(8,128)(2,1)S(1)} %dynamic-slice_convert_fusion.12), channel_id=1, source_target_pairs={{0,4},{4,0},{1,5},{5,1},{2,6},{6,2},{3,7},{7,3},{8,12},{12,8},{9,1... | collective-permute-start | bytes 442376 | tf_op jit(solution)/shard_map/ppermute | solution.py:66
  206.8 6.9 %collective-permute-start.40 = (bf16[2,64,576]{2,1,0:T(8,128)(2,1)S(1)}, bf16[2,64,576]{2,1,0:T(8,128)(2,1)S(1)}, u32[]{:S(2)}, u32[]{:S(2)}) collective-permute-start(bf16[2,64,576]{2,1,0:T(8,128)(2,1)S(1)} %dynamic-slice_convert_fusion.11), channel_id=1, source_target_pairs={{0,2},{1,3},{2,0},{3,1},{4,6},{5,7},{6,4},{7,5},{8,10},{9,11},{10,... | collective-permute-start | bytes 442376 | tf_op jit(solution)/shard_map/ppermute | solution.py:66
  212.3 4.5 %collective-permute-start.38 = (bf16[1,64,576]{2,1,0:T(8,128)(2,1)S(1)}, bf16[1,64,576]{2,1,0:T(8,128)(2,1)S(1)}, u32[]{:S(2)}, u32[]{:S(2)}) collective-permute-start(bf16[1,64,576]{2,1,0:T(8,128)(2,1)S(1)} %dynamic-slice_convert_fusion.17), channel_id=1, source_target_pairs={{0,2},{1,3},{2,0},{3,1},{4,6},{5,7},{6,4},{7,5},{8,10},{9,11},{10,... | collective-permute-start | bytes 221192 | tf_op jit(solution)/shard_map/ppermute | solution.py:66
  213.7 4.5 %collective-permute-start.41 = (bf16[1,64,576]{2,1,0:T(8,128)(2,1)S(1)}, bf16[1,64,576]{2,1,0:T(8,128)(2,1)S(1)}, u32[]{:S(2)}, u32[]{:S(2)}) collective-permute-start(bf16[1,64,576]{2,1,0:T(8,128)(2,1)S(1)} %dynamic-slice_convert_fusion.16), channel_id=1, source_target_pairs={{0,4},{4,0},{1,5},{5,1},{2,6},{6,2},{3,7},{7,3},{8,12},{12,8},{9,1... | collective-permute-start | bytes 221192 | tf_op jit(solution)/shard_map/ppermute | solution.py:66

commit v8 on v5

--- a/solution.py
+++ b/solution.py
@@ -124,24 +124,38 @@
     )
     acts = (selected * pre).astype(jnp.bfloat16)
     live_layers = lax.iota(jnp.int32, layer_count) >= layer_id
-    partial_value = jnp.einsum("tf,lfd->ltd", acts, decoder[0], preferred_element_type=jnp.float32)
-    partial_value = jnp.where(live_layers[:, None, None], partial_value, 0.0)
-    blocks = (
-        partial_value.reshape(layer_count, slots, slot_rows, feat_parts, cols)
-        .transpose(1, 3, 0, 2, 4)
-        .reshape(slots * feat_parts, layer_count * slot_rows, cols)
-    )
-    recon = reduce_scatter(blocks, EVERY, jnp.bfloat16).reshape(layer_count, slot_rows, cols)
-    recon = recon + decoder_bias[:, None, :]
-    error = (recon - target.astype(jnp.float32)).astype(jnp.bfloat16)
-    pieces = all_gather(error.reshape(layer_count * slot_rows, cols), EVERY)
-    piece = (
-        pieces.reshape(slots, feat_parts, layer_count, slot_rows, cols)
-        .transpose(2, 0, 3, 1, 4)
-        .reshape(layer_count, tokens, width)
-    )
-    kept = jnp.where(live_layers[:, None, None], piece, jnp.zeros_like(piece))
-    grad_act = jnp.einsum("ltd,lfd->tf", kept, decoder[0], preferred_element_type=jnp.float32)
+    groups = 2 if layer_count % 2 == 0 else 1
+    per_group = layer_count // groups
+    errors = []
+    for g in range(groups):
+        chosen = slice(g * per_group, (g + 1) * per_group)
+        live = live_layers[chosen]
+        partial_value = jnp.einsum(
+            "tf,lfd->ltd", acts, decoder[0, chosen], preferred_element_type=jnp.float32
+        )
+        partial_value = jnp.where(live[:, None, None], partial_value, 0.0)
+        blocks = (
+            partial_value.reshape(per_group, slots, slot_rows, feat_parts, cols)
+            .transpose(1, 3, 0, 2, 4)
+            .reshape(slots * feat_parts, per_group * slot_rows, cols)
+        )
+        recon = reduce_scatter(blocks, EVERY, jnp.bfloat16).reshape(per_group, slot_rows, cols)
+        recon = recon + decoder_bias[chosen, None, :]
+        errors.append((recon - target[chosen].astype(jnp.float32)).astype(jnp.bfloat16))
+    grad_act = None
+    for g in range(groups):
+        chosen = slice(g * per_group, (g + 1) * per_group)
+        live = live_layers[chosen]
+        pieces = all_gather(errors[g].reshape(per_group * slot_rows, cols), EVERY)
+        piece = (
+            pieces.reshape(slots, feat_parts, per_group, slot_rows, cols)
+            .transpose(2, 0, 3, 1, 4)
+            .reshape(per_group, tokens, width)
+        )
+        kept = jnp.where(live[:, None, None], piece, jnp.zeros_like(piece))
+        term = jnp.einsum("ltd,lfd->tf", kept, decoder[0, chosen], preferred_element_type=jnp.float32)
+        grad_act = term if grad_act is None else grad_act + term
+    error = jnp.concatenate(errors, axis=0)
     grad_pre = (selected * grad_act).astype(jnp.bfloat16)
     grad_part = lax.dot_general(
         grad_pre, encoder[0], (((1,), (1,)), ((), ())), preferred_element_type=jnp.float32

time: 211 us -> 246 us (1.17); the launches traced: 210 us -> 242 us
  starting transfers between devices: 55.7 us -> 73.1 us
  matrix products: 29.6 us -> 37.9 us
  local copies, waits for them, and re-layouts: 55.9 us -> 61 us
  waiting for transfers between devices: 42.6 us -> 46.1 us
  other arithmetic: 24.7 us -> 21.4 us
    ppermute x21 -> x36, starting transfers between devices: 26.5 us -> 38.6 us  [reduce_scatter(): recv = lax.ppermute(send.astype(wire), axis, partner(axis, bit))]
    ppermute x21 -> x36, waiting for transfers between devices: 26 us -> 36.1 us  [reduce_scatter(): recv = lax.ppermute(send.astype(wire), axis, partner(axis, bit))]
    dot_general x2 -> x4, matrix products: 24.4 us -> 32.7 us  [the longest x2 17.3 us: local(): jnp.einsum('tf,lfd->ltd', acts, decoder[0, chosen], preferred_element_typ...]
    transpose x1 -> x2, local copies, waits for them, and re-layouts: 6.38 us -> 13.5 us  [local(): piece = pieces.reshape(slots, feat_parts, per_group, slot_rows, cols).tra...]
    ppermute x21 -> x36, waiting for transfers between devices: 16.5 us -> 10.1 us  [all_gather(): recv = lax.ppermute(parts[p], axis, partner(axis, bit))]
    ppermute x21 -> x36, starting transfers between devices: 29.2 us -> 34.6 us  [all_gather(): recv = lax.ppermute(parts[p], axis, partner(axis, bit))]
    add x16 -> x28, other arithmetic: 6.28 us -> 2.26 us  [reduce_scatter(): parts[p] = keep + recv.astype(keep.dtype)]
    convert_element_type x21 -> x36, local copies, waits for them, and re-layouts: 6.03 us -> 3.34 us  [reduce_scatter(): recv = lax.ppermute(send.astype(wire), axis, partner(axis, bit))]
  transfers between devices with their start and end apart: 42 -> 72, of which waited for: 21 -> 24; matrix products, arithmetic and copies ran while one was open for 14% -> 20% of each run, Pallas kernels for 0% -> 0%
where the time goes in v8:
time: 246 us; the launch traced here: 242 us
  starting transfers between devices  73.1 us (30%)
  local copies, waits for them, and re-layouts  61 us (25%)
  waiting for transfers between devices  46.1 us (19%)
  matrix products  37.9 us (15%)
  other arithmetic  21.4 us (9%)
    ppermute x36, starting transfers between devices, reduce_scatter(): recv = lax.ppermute(send.astype(wire), axis, partner(axis, bit))  38.6 us
    ppermute x36, waiting for transfers between devices, reduce_scatter(): recv = lax.ppermute(send.astype(wire), axis, partner(axis, bit))  36.1 us
    ppermute x36, starting transfers between devices, all_gather(): recv = lax.ppermute(parts[p], axis, partner(axis, bit))  34.6 us
    reshape x4, local copies, waits for them, and re-layouts, local(): partial_value.reshape(per_group, slots, slot_rows, feat_parts, cols)  21.5 us
    dot_general x2, matrix products, local(): jnp.einsum('tf,lfd->ltd', acts, decoder[0, chosen], preferred_element_typ...  17.3 us
    dot_general x2, matrix products, local(): jnp.einsum('ltd,lfd->tf', kept, decoder[0, chosen], preferred_element_typ...  15.4 us
    transpose x2, local copies, waits for them, and re-layouts, local(): piece = pieces.reshape(slots, feat_parts, per_group, slot_rows, cols).tra...  13.5 us
    transpose x13, local copies, waits for them, and re-layouts, reduce_scatter(): xp = jnp.transpose(xp, [labels.index(l) for l in order] + [nb, nb + 1])  10.3 us
  transfers between devices with their start and end apart: 72, of which 24 were waited for; matrix products, arithmetic and copies ran while one was open for 20% of the time, Pallas kernels for 0%

profile of v8, /device:TPU:0, one launch (start us, length us, event | category | flops | bytes accessed | tf_op | source)
XLA Modules:
  0.0 241.5 jit_solution(15477066800971955542)
XLA Ops:
  1.9 3.0 %collective-permute-start.3 = (bf16[1,64,576]{2,1,0:T(8,128)(2,1)S(1)}, bf16[1,64,576]{2,1,0:T(8,128)(2,1)S(1)}, u32[]{:S(2)}, u32[]{:S(2)}) collective-permute-start(bf16[1,64,576]{2,1,0:T(8,128)(2,1)S(1)} %copy.97), channel_id=1, source_target_pairs={{0,4},{4,0},{1,5},{5,1},{2,6},{6,2},{3,7},{7,3},{8,12},{12,8},{9,1... | collective-permute-start | bytes 221192 | tf_op jit(solution)/shard_map/ppermute | solution.py:86
  5.1 1.6 collective-permute-start
  6.8 9.4 %compare_reduce_fusion = pred[256,1024]{1,0:T(8,128)(4,1)S(1)} fusion(s32[1024]{0:T(1024)S(1)} %iota_add_fusion, s32[256,64]{1,0:T(8,128)S(1)} %copy.70), kind=kLoop, calls=%fused_computation | loop fusion | flops 33292288 | bytes 331776 | tf_op jit(solution)/shard_map/reduce_or | solution.py:122
  17.9 4.7 %collective-permute-done.4 = bf16[2,64,576]{2,1,0:T(8,128)(2,1)S(1)} collective-permute-done((bf16[2,64,576]{2,1,0:T(8,128)(2,1)S(1)}, bf16[2,64,576]{2,1,0:T(8,128)(2,1)S(1)}, u32[]{:S(2)}, u32[]{:S(2)}) %collective-permute-start.4) | collective-permute-done | bytes 147488 | tf_op jit(solution)/shard_map/ppermute | solution.py:86
  26.3 3.8 %fusion.56 = bf16[256,1024,1]{1,0,2:T(8,128)(2,1)S(1)} fusion(pred[256,1024]{1,0:T(8,128)(4,1)S(1)} %compare_reduce_fusion, bf16[1,2304,1024]{2,1,0:T(8,128)(2,1)} %param.8, bf16[288,8,2,128]{3,2,1,0:T(2,128)(2,1)S(1)} %bitcast.213, f32[1024]{0:T(1024)S(1)} %bitcast.223), kind=kOutput, calls=%fused_computation.40 | convolution fusion | flops 1208745984 | bytes 6688768 | tf_op jit(solution)/shard_map/dot_general | solution.py:118
  30.1 8.7 %select_bitcast_fusion.1 = f32[2,256,2304]{2,1,0:T(8,128)} fusion(bf16[256,1024,1]{1,0,2:T(8,128)(2,1)S(1)} %fusion.56, bf16[1,4,1024,2304]{3,2,1,0:T(8,128)(2,1)} %param.10, pred[2]{0:T(512)(128)(4,1)S(1)} %get-tuple-element.22), kind=kOutput, calls=%fused_computation.16 | convolution fusion | flops 2417098752 | bytes 14680066 | tf_op jit(solution)/shard_map/tf,lfd->ltd/dot_general | solution.py:133
  38.8 7.4 %reshape.170 = f32[2,8,32,4,576]{4,3,2,1,0:T(4,128)} reshape(f32[2,256,2304]{2,1,0:T(8,128)} %select_bitcast_fusion.1) | data formatting | bytes 9437184 | tf_op jit(solution)/shard_map/reshape | solution.py:138
  46.2 3.2 %copy.76 = f32[2,8,32,4,576]{4,2,0,3,1:T(8,128)S(1)} copy(f32[2,8,32,4,576]{4,3,2,1,0:T(4,128)} %reshape.170) | data formatting | bytes 9437184 | tf_op jit(solution)/shard_map/reshape | solution.py:138
  49.6 1.8 slice_bitcast_fusion.5
  51.4 8.5 %select_bitcast_fusion = f32[2,256,2304]{2,1,0:T(8,128)} fusion(bf16[256,1024,1]{1,0,2:T(8,128)(2,1)S(1)} %copy-done.13, bf16[1,4,1024,2304]{3,2,1,0:T(8,128)(2,1)} %param.10, pred[2]{0:T(512)(128)(4,1)S(1)} %get-tuple-element.23), kind=kOutput, calls=%fused_computation.15 | convolution fusion | flops 2417098752 | bytes 14680066 | tf_op jit(solution)/shard_map/tf,lfd->ltd/dot_general | solution.py:133
  59.9 7.6 %reshape.175 = f32[2,8,32,4,576]{4,3,2,1,0:T(4,128)} reshape(f32[2,256,2304]{2,1,0:T(8,128)} %select_bitcast_fusion) | data formatting | bytes 9437184 | tf_op jit(solution)/shard_map/reshape | solution.py:138
  67.6 3.2 %copy.80 = f32[2,8,32,4,576]{4,2,0,3,1:T(8,128)S(1)} copy(f32[2,8,32,4,576]{4,3,2,1,0:T(4,128)} %reshape.175) | data formatting | bytes 9437184 | tf_op jit(solution)/shard_map/reshape | solution.py:138
  76.3 1.5 collective-permute-start.17
  77.9 4.6 %collective-permute-done.17 = bf16[8,16,576]{2,1,0:T(8,128)(2,1)S(1)} collective-permute-done((bf16[8,16,576]{2,1,0:T(8,128)(2,1)S(1)}, bf16[8,16,576]{2,1,0:T(8,128)(2,1)S(1)}, u32[]{:S(2)}, u32[]{:S(2)}) %collective-permute-start.17) | collective-permute-done | bytes 147488 | tf_op jit(solution)/shard_map/ppermute | solution.py:70
  82.5 1.5 collective-permute-start.32
  84.1 1.6 collective-permute-start.18
  87.9 1.6 collective-permute-start.7
  91.0 1.6 collective-permute-start.22
  92.6 5.8 %collective-permute-done.33 = bf16[4,16,576]{2,1,0:T(8,128)(2,1)S(1)} collective-permute-done((bf16[4,16,576]{2,1,0:T(8,128)(2,1)S(1)}, bf16[4,16,576]{2,1,0:T(8,128)(2,1)S(1)}, u32[]{:S(2)}, u32[]{:S(2)}) %collective-permute-start.33) | collective-permute-done | bytes 73760 | tf_op jit(solution)/shard_map/ppermute | solution.py:70
  99.1 3.4 %collective-permute-done.19 = bf16[2,16,576]{2,1,0:T(8,128)(2,1)S(1)} collective-permute-done((bf16[2,16,576]{2,1,0:T(8,128)(2,1)S(1)}, bf16[2,16,576]{2,1,0:T(8,128)(2,1)S(1)}, u32[]{:S(2)}, u32[]{:S(2)}) %collective-permute-start.19) | collective-permute-done | bytes 36896 | tf_op jit(solution)/shard_map/ppermute | solution.py:70
  103.1 3.4 %collective-permute-done.34 = bf16[2,16,576]{2,1,0:T(8,128)(2,1)S(1)} collective-permute-done((bf16[2,16,576]{2,1,0:T(8,128)(2,1)S(1)}, bf16[2,16,576]{2,1,0:T(8,128)(2,1)S(1)}, u32[]{:S(2)}, u32[]{:S(2)}) %collective-permute-start.34) | collective-permute-done | bytes 36896 | tf_op jit(solution)/shard_map/ppermute | solution.py:70
  106.5 2.6 %collective-permute-start.20 = (bf16[1,16,576]{2,1,0:T(8,128)(2,1)S(1)}, bf16[1,16,576]{2,1,0:T(8,128)(2,1)S(1)}, u32[]{:S(2)}, u32[]{:S(2)}) collective-permute-start(bf16[1,16,576]{2,1,0:T(8,128)(2,1)S(1)} %dynamic-slice_convert_fusion.35), channel_id=1, source_target_pairs={{0,16},{8,24},{16,0},{24,8},{1,17},{9,25},{17,1},{25,9},{2,18},{10... | collective-permute-start | bytes 55304 | tf_op jit(solution)/shard_map/ppermute | solution.py:70
  109.1 2.1 collective-permute-done.20
  111.2 2.6 %collective-permute-start.35 = (bf16[1,16,576]{2,1,0:T(8,128)(2,1)S(1)}, bf16[1,16,576]{2,1,0:T(8,128)(2,1)S(1)}, u32[]{:S(2)}, u32[]{:S(2)}) collective-permute-start(bf16[1,16,576]{2,1,0:T(8,128)(2,1)S(1)} %dynamic-slice_convert_fusion.34), channel_id=1, source_target_pairs={{0,16},{8,24},{16,0},{24,8},{1,17},{9,25},{17,1},{25,9},{2,18},{10... | collective-permute-start | bytes 55304 | tf_op jit(solution)/shard_map/ppermute | solution.py:70
  113.8 2.1 collective-permute-done.35
  116.0 1.6 collective-permute-start.13
  119.0 1.6 collective-permute-start.23
  121.0 1.7 collective-permute-start.14
  122.7 1.6 collective-permute-start.9
  125.1 1.5 collective-permute-start.24
  126.6 2.9 %collective-permute-start.15 = (bf16[1,24,576]{2,1,0:T(8,128)(2,1)S(1)}, bf16[1,24,576]{2,1,0:T(8,128)(2,1)S(1)}, u32[]{:S(2)}, u32[]{:S(2)}) collective-permute-start(bf16[1,24,576]{2,1,0:T(8,128)(2,1)S(1)} %dynamic-slice_convert_fusion.32), channel_id=1, source_target_pairs={{0,16},{8,24},{16,0},{24,8},{1,17},{9,25},{17,1},{25,9},{2,18},{10... | collective-permute-start | bytes 82952 | tf_op jit(solution)/shard_map/ppermute | solution.py:70
  130.0 2.7 %collective-permute-start.30 = (bf16[1,24,576]{2,1,0:T(8,128)(2,1)S(1)}, bf16[1,24,576]{2,1,0:T(8,128)(2,1)S(1)}, u32[]{:S(2)}, u32[]{:S(2)}) collective-permute-start(bf16[1,24,576]{2,1,0:T(8,128)(2,1)S(1)} %dynamic-slice_convert_fusion.30), channel_id=1, source_target_pairs={{0,16},{8,24},{16,0},{24,8},{1,17},{9,25},{17,1},{25,9},{2,18},{10... | collective-permute-start | bytes 82952 | tf_op jit(solution)/shard_map/ppermute | solution.py:70
  133.1 2.1 collective-permute-done.10
  135.6 2.3 collective-permute-done.25
  138.2 3.0 %collective-permute-start.41 = (bf16[1,24,576]{2,1,0:T(8,128)(2,1)S(1)}, bf16[1,24,576]{2,1,0:T(8,128)(2,1)S(1)}, u32[]{:S(2)}, u32[]{:S(2)}) collective-permute-start(bf16[1,24,576]{2,1,0:T(8,128)(2,1)S(1)} %get-tuple-element.19), channel_id=1, source_target_pairs={{0,16},{8,24},{16,0},{24,8},{1,17},{9,25},{17,1},{25,9},{2,18},{10... | collective-permute-start | bytes 82952 | tf_op jit(solution)/shard_map/ppermute | solution.py:86
  141.2 2.8 %collective-permute-start.61 = (bf16[1,16,576]{2,1,0:T(8,128)(2,1)S(1)}, bf16[1,16,576]{2,1,0:T(8,128)(2,1)S(1)}, u32[]{:S(2)}, u32[]{:S(2)}) collective-permute-start(bf16[1,16,576]{2,1,0:T(8,128)(2,1)S(1)} %slice_bitcast_fusion.12), channel_id=1, source_target_pairs={{0,16},{8,24},{16,0},{24,8},{1,17},{9,25},{17,1},{25,9},{2,18},{10... | collective-permute-start | bytes 55304 | tf_op jit(solution)/shard_map/ppermute | solution.py:86
  144.2 2.8 %collective-permute-start.51 = (bf16[1,24,576]{2,1,0:T(8,128)(2,1)S(1)}, bf16[1,24,576]{2,1,0:T(8,128)(2,1)S(1)}, u32[]{:S(2)}, u32[]{:S(2)}) collective-permute-start(bf16[1,24,576]{2,1,0:T(8,128)(2,1)S(1)} %get-tuple-element.16), channel_id=1, source_target_pairs={{0,16},{8,24},{16,0},{24,8},{1,17},{9,25},{17,1},{25,9},{2,18},{10... | collective-permute-start | bytes 82952 | tf_op jit(solution)/shard_map/ppermute | solution.py:86
  147.3 1.9 collective-permute-start.62
  149.9 1.4 collective-permute-start.37
  152.1 1.5 collective-permute-start.52
  154.3 1.6 collective-permute-start.63
  156.6 1.5 collective-permute-start.38
  158.5 1.9 collective-permute-start.53
  161.1 1.5 collective-permute-start.64
  163.1 1.6 collective-permute-start.39
  165.8 1.4 collective-permute-start.54
  167.7 1.3 collective-permute-done.44
  169.9 1.8 collective-permute-done.59
  175.6 11.5 %copy.87 = bf16[2,8,32,4,576]{4,3,2,1,0:T(4,128)(2,1)S(1)} copy(bf16[2,8,32,4,576]{4,2,0,3,1:T(8,128)(2,1)S(1)} %bitcast.178) | data formatting | bytes 4718592 | tf_op jit(solution)/shard_map/transpose | solution.py:152
  187.1 3.2 %reshape.185 = bf16[2,256,2304]{2,1,0:T(8,128)(2,1)} reshape(bf16[2,8,32,4,576]{4,3,2,1,0:T(4,128)(2,1)S(1)} %copy.87) | data formatting | bytes 4718592 | tf_op jit(solution)/shard_map/reshape | solution.py:153
  190.3 8.0 %fusion.22 = f32[256,1024]{1,0:T(8,128)} fusion(bf16[1,4,1024,2304]{3,2,1,0:T(8,128)(2,1)} %param.10, bf16[2,256,2304]{2,1,0:T(8,128)(2,1)} %reshape.185, pred[2]{0:T(512)(128)(4,1)S(1)} %get-tuple-element.22), kind=kOutput, calls=%fused_computation.29 | convolution fusion | flops 2417098752 | bytes 12845058 | tf_op jit(solution)/shard_map/ltd,lfd->tf/dot_general | solution.py:156
  198.3 1.8 maximum_select_fusion.3
  200.2 1.8 maximum_select_fusion.2
  202.4 2.0 copy.91
  204.5 3.2 %reshape.191 = bf16[2,256,2304]{2,1,0:T(8,128)(2,1)} reshape(bf16[2,8,32,4,576]{4,3,2,1,0:T(4,128)(2,1)S(1)} %copy.91) | data formatting | bytes 4718592 | tf_op jit(solution)/shard_map/reshape | solution.py:153
  207.7 7.4 %fusion.51 = bf16[256,1024]{1,0:T(8,128)(2,1)S(1)} fusion(pred[256,1024]{1,0:T(8,128)(4,1)S(1)} %copy-done.9, f32[256,1024]{1,0:T(8,128)} %fusion.22, bf16[1,4,1024,2304]{3,2,1,0:T(8,128)(2,1)} %param.10, bf16[2,256,2304]{2,1,0:T(8,128)(2,1)} %reshape.191, pred[2]{0:T(512)(128)(4,1)S(1)} %get-tuple-element.23), kind=kOutput, calls=%fused_computation.39 | convolution fusion | flops 2417885184 | bytes 13631490 | tf_op jit(solution)/shard_map/ltd,lfd->tf/dot_general | solution.py:156
  215.1 1.4 fusion.68
  216.5 2.2 slice_bitcast_fusion.1
  218.7 3.0 %copy.93 = f32[2,2,2,64,576]{4,3,2,1,0:T(8,128)} copy(f32[2,2,2,64,576]{3,4,0,1,2:T(8,128)} %get-tuple-element.11) | data formatting | bytes 2359296 | tf_op jit(solution)/shard_map/transpose | solution.py:61
  224.0 1.8 copy.92
  228.4 1.3 collective-permute-start.70
  230.6 4.4 %collective-permute-done.70 = bf16[2,64,576]{2,1,0:T(8,128)(2,1)S(1)} collective-permute-done((bf16[2,64,576]{2,1,0:T(8,128)(2,1)S(1)}, bf16[2,64,576]{2,1,0:T(8,128)(2,1)S(1)}, u32[]{:S(2)}, u32[]{:S(2)}) %collective-permute-start.70) | collective-permute-done | bytes 147488 | tf_op jit(solution)/shard_map/ppermute | solution.py:70
  236.0 1.3 collective-permute-start.68
  237.3 2.3 collective-permute-done.71
  (280 shorter events, 41.3 us)
Async XLA Ops:
  1.9 15.1 %collective-permute-start.3 = (bf16[1,64,576]{2,1,0:T(8,128)(2,1)S(1)}, bf16[1,64,576]{2,1,0:T(8,128)(2,1)S(1)}, u32[]{:S(2)}, u32[]{:S(2)}) collective-permute-start(bf16[1,64,576]{2,1,0:T(8,128)(2,1)S(1)} %copy.97), channel_id=1, source_target_pairs={{0,4},{4,0},{1,5},{5,1},{2,6},{6,2},{3,7},{7,3},{8,12},{12,8},{9,1... | collective-permute-start | bytes 221192 | tf_op jit(solution)/shard_map/ppermute | solution.py:86
  5.1 12.6 %collective-permute-start = (bf16[1,64,576]{2,1,0:T(8,128)(2,1)S(1)}, bf16[1,64,576]{2,1,0:T(8,128)(2,1)S(1)}, u32[]{:S(2)}, u32[]{:S(2)}) collective-permute-start(bf16[1,64,576]{2,1,0:T(8,128)(2,1)S(1)} %copy.96), channel_id=1, source_target_pairs={{0,2},{1,3},{2,0},{3,1},{4,6},{5,7},{6,4},{7,5},{8,10},{9,11},{10,... | collective-permute-start | bytes 221192 | tf_op jit(solution)/shard_map/ppermute | solution.py:86
  17.1 5.4 %collective-permute-start.4 = (bf16[2,64,576]{2,1,0:T(8,128)(2,1)S(1)}, bf16[2,64,576]{2,1,0:T(8,128)(2,1)S(1)}, u32[]{:S(2)}, u32[]{:S(2)}) collective-permute-start(bf16[2,64,576]{2,1,0:T(8,128)(2,1)S(1)} %maximum_select_fusion.21), channel_id=1, source_target_pairs={{0,2},{1,3},{2,0},{3,1},{4,6},{5,7},{6,4},{7,5},{8,10},{9,11},{10,... | collective-permute-start | bytes 442376 | tf_op jit(solution)/shard_map/ppermute | solution.py:86
  17.7 5.4 %collective-permute-start.1 = (bf16[2,64,576]{2,1,0:T(8,128)(2,1)S(1)}, bf16[2,64,576]{2,1,0:T(8,128)(2,1)S(1)}, u32[]{:S(2)}, u32[]{:S(2)}) collective-permute-start(bf16[2,64,576]{2,1,0:T(8,128)(2,1)S(1)} %maximum_select_fusion.20), channel_id=1, source_target_pairs={{0,4},{4,0},{1,5},{5,1},{2,6},{6,2},{3,7},{7,3},{8,12},{12,8},{9,1... | collective-permute-start | bytes 442376 | tf_op jit(solution)/shard_map/ppermute | solution.py:86
  73.2 10.9 %collective-permute-start.11 = (bf16[16,24,576]{2,1,0:T(8,128)(2,1)S(1)}, bf16[16,24,576]{2,1,0:T(8,128)(2,1)S(1)}, u32[]{:S(2)}, u32[]{:S(2)}) collective-permute-start(bf16[16,24,576]{2,1,0:T(8,128)(2,1)S(1)} %dynamic-slice_convert_fusion.2), channel_id=1, source_target_pairs={{0,1},{1,0},{2,3},{3,2},{4,5},{5,4},{6,7},{7,6},{8,9},{9,8},{10,11... | collective-permute-start | bytes 1327112 | tf_op jit(solution)/shard_map/ppermute | solution.py:70
  73.6 12.3 %collective-permute-start.6 = (bf16[16,24,576]{2,1,0:T(8,128)(2,1)S(1)}, bf16[16,24,576]{2,1,0:T(8,128)(2,1)S(1)}, u32[]{:S(2)}, u32[]{:S(2)}) collective-permute-start(bf16[16,24,576]{2,1,0:T(8,128)(2,1)S(1)} %dynamic-slice_convert_fusion.3), channel_id=1, source_target_pairs={{0,1},{1,0},{2,3},{3,2},{4,5},{5,4},{6,7},{7,6},{8,9},{9,8},{10,11... | collective-permute-start | bytes 1327112 | tf_op jit(solution)/shard_map/ppermute | solution.py:70
  74.7 14.9 %collective-permute-start.26 = (bf16[16,24,576]{2,1,0:T(8,128)(2,1)S(1)}, bf16[16,24,576]{2,1,0:T(8,128)(2,1)S(1)}, u32[]{:S(2)}, u32[]{:S(2)}) collective-permute-start(bf16[16,24,576]{2,1,0:T(8,128)(2,1)S(1)} %dynamic-slice_convert_fusion), channel_id=1, source_target_pairs={{0,1},{1,0},{2,3},{3,2},{4,5},{5,4},{6,7},{7,6},{8,9},{9,8},{10,11... | collective-permute-start | bytes 1327112 | tf_op jit(solution)/shard_map/ppermute | solution.py:70
  75.3 14.9 %collective-permute-start.21 = (bf16[16,24,576]{2,1,0:T(8,128)(2,1)S(1)}, bf16[16,24,576]{2,1,0:T(8,128)(2,1)S(1)}, u32[]{:S(2)}, u32[]{:S(2)}) collective-permute-start(bf16[16,24,576]{2,1,0:T(8,128)(2,1)S(1)} %dynamic-slice_convert_fusion.1), channel_id=1, source_target_pairs={{0,1},{1,0},{2,3},{3,2},{4,5},{5,4},{6,7},{7,6},{8,9},{9,8},{10,11... | collective-permute-start | bytes 1327112 | tf_op jit(solution)/shard_map/ppermute | solution.py:70
  76.3 6.3 %collective-permute-start.17 = (bf16[8,16,576]{2,1,0:T(8,128)(2,1)S(1)}, bf16[8,16,576]{2,1,0:T(8,128)(2,1)S(1)}, u32[]{:S(2)}, u32[]{:S(2)}) collective-permute-start(bf16[8,16,576]{2,1,0:T(8,128)(2,1)S(1)} %dynamic-slice_convert_fusion.15), channel_id=1, source_target_pairs={{0,2},{1,3},{2,0},{3,1},{4,6},{5,7},{6,4},{7,5},{8,10},{9,11},{10,... | collective-permute-start | bytes 442376 | tf_op jit(solution)/shard_map/ppermute | solution.py:70
  82.5 5.4 %collective-permute-start.32 = (bf16[8,16,576]{2,1,0:T(8,128)(2,1)S(1)}, bf16[8,16,576]{2,1,0:T(8,128)(2,1)S(1)}, u32[]{:S(2)}, u32[]{:S(2)}) collective-permute-start(bf16[8,16,576]{2,1,0:T(8,128)(2,1)S(1)} %dynamic-slice_convert_fusion.14), channel_id=1, source_target_pairs={{0,2},{1,3},{2,0},{3,1},{4,6},{5,7},{6,4},{7,5},{8,10},{9,11},{10,... | collective-permute-start | bytes 442376 | tf_op jit(solution)/shard_map/ppermute | solution.py:70
  84.1 6.9 %collective-permute-start.18 = (bf16[4,16,576]{2,1,0:T(8,128)(2,1)S(1)}, bf16[4,16,576]{2,1,0:T(8,128)(2,1)S(1)}, u32[]{:S(2)}, u32[]{:S(2)}) collective-permute-start(bf16[4,16,576]{2,1,0:T(8,128)(2,1)S(1)} %dynamic-slice_convert_fusion.23), channel_id=1, source_target_pairs={{0,8},{8,0},{16,24},{24,16},{1,9},{9,1},{17,25},{25,17},{2,10},{10... | collective-permute-start | bytes 221192 | tf_op jit(solution)/shard_map/ppermute | solution.py:70
  85.9 30.0 %collective-permute-start.12 = (bf16[8,24,576]{2,1,0:T(8,128)(2,1)S(1)}, bf16[8,24,576]{2,1,0:T(8,128)(2,1)S(1)}, u32[]{:S(2)}, u32[]{:S(2)}) collective-permute-start(bf16[8,24,576]{2,1,0:T(8,128)(2,1)S(1)} %dynamic-slice_convert_fusion.10), channel_id=1, source_target_pairs={{0,4},{4,0},{1,5},{5,1},{2,6},{6,2},{3,7},{7,3},{8,12},{12,8},{9,1... | collective-permute-start | bytes 663560 | tf_op jit(solution)/shard_map/ppermute | solution.py:70
  87.9 29.6 %collective-permute-start.7 = (bf16[8,24,576]{2,1,0:T(8,128)(2,1)S(1)}, bf16[8,24,576]{2,1,0:T(8,128)(2,1)S(1)}, u32[]{:S(2)}, u32[]{:S(2)}) collective-permute-start(bf16[8,24,576]{2,1,0:T(8,128)(2,1)S(1)} %dynamic-slice_convert_fusion.11), channel_id=1, source_target_pairs={{0,8},{8,0},{16,24},{24,16},{1,9},{9,1},{17,25},{25,17},{2,10},{10... | collective-permute-start | bytes 663560 | tf_op jit(solution)/shard_map/ppermute | solution.py:70
  89.5 8.9 %collective-permute-start.33 = (bf16[4,16,576]{2,1,0:T(8,128)(2,1)S(1)}, bf16[4,16,576]{2,1,0:T(8,128)(2,1)S(1)}, u32[]{:S(2)}, u32[]{:S(2)}) collective-permute-start(bf16[4,16,576]{2,1,0:T(8,128)(2,1)S(1)} %dynamic-slice_convert_fusion.22), channel_id=1, source_target_pairs={{0,8},{8,0},{16,24},{24,16},{1,9},{9,1},{17,25},{25,17},{2,10},{10... | collective-permute-start | bytes 221192 | tf_op jit(solution)/shard_map/ppermute | solution.py:70
  90.2 28.0 %collective-permute-start.27 = (bf16[8,24,576]{2,1,0:T(8,128)(2,1)S(1)}, bf16[8,24,576]{2,1,0:T(8,128)(2,1)S(1)}, u32[]{:S(2)}, u32[]{:S(2)}) collective-permute-start(bf16[8,24,576]{2,1,0:T(8,128)(2,1)S(1)} %dynamic-slice_convert_fusion.8), channel_id=1, source_target_pairs={{0,4},{4,0},{1,5},{5,1},{2,6},{6,2},{3,7},{7,3},{8,12},{12,8},{9,1... | collective-permute-start | bytes 663560 | tf_op jit(solution)/shard_map/ppermute | solution.py:70
  91.0 27.9 %collective-permute-start.22 = (bf16[8,24,576]{2,1,0:T(8,128)(2,1)S(1)}, bf16[8,24,576]{2,1,0:T(8,128)(2,1)S(1)}, u32[]{:S(2)}, u32[]{:S(2)}) collective-permute-start(bf16[8,24,576]{2,1,0:T(8,128)(2,1)S(1)} %dynamic-slice_convert_fusion.9), channel_id=1, source_target_pairs={{0,8},{8,0},{16,24},{24,16},{1,9},{9,1},{17,25},{25,17},{2,10},{10... | collective-permute-start | bytes 663560 | tf_op jit(solution)/shard_map/ppermute | solution.py:70
  106.5 4.7 %collective-permute-start.20 = (bf16[1,16,576]{2,1,0:T(8,128)(2,1)S(1)}, bf16[1,16,576]{2,1,0:T(8,128)(2,1)S(1)}, u32[]{:S(2)}, u32[]{:S(2)}) collective-permute-start(bf16[1,16,576]{2,1,0:T(8,128)(2,1)S(1)} %dynamic-slice_convert_fusion.35), channel_id=1, source_target_pairs={{0,16},{8,24},{16,0},{24,8},{1,17},{9,25},{17,1},{25,9},{2,18},{10... | collective-permute-start | bytes 55304 | tf_op jit(solution)/shard_map/ppermute | solution.py:70
  111.2 4.7 %collective-permute-start.35 = (bf16[1,16,576]{2,1,0:T(8,128)(2,1)S(1)}, bf16[1,16,576]{2,1,0:T(8,128)(2,1)S(1)}, u32[]{:S(2)}, u32[]{:S(2)}) collective-permute-start(bf16[1,16,576]{2,1,0:T(8,128)(2,1)S(1)} %dynamic-slice_convert_fusion.34), channel_id=1, source_target_pairs={{0,16},{8,24},{16,0},{24,8},{1,17},{9,25},{17,1},{25,9},{2,18},{10... | collective-permute-start | bytes 55304 | tf_op jit(solution)/shard_map/ppermute | solution.py:70
  116.0 4.9 %collective-permute-start.13 = (bf16[4,24,576]{2,1,0:T(8,128)(2,1)S(1)}, bf16[4,24,576]{2,1,0:T(8,128)(2,1)S(1)}, u32[]{:S(2)}, u32[]{:S(2)}) collective-permute-start(bf16[4,24,576]{2,1,0:T(8,128)(2,1)S(1)} %dynamic-slice_convert_fusion.18), channel_id=1, source_target_pairs={{0,2},{1,3},{2,0},{3,1},{4,6},{5,7},{6,4},{7,5},{8,10},{9,11},{10,... | collective-permute-start | bytes 331784 | tf_op jit(solution)/shard_map/ppermute | solution.py:70
  117.6 5.0 %collective-permute-start.8 = (bf16[4,24,576]{2,1,0:T(8,128)(2,1)S(1)}, bf16[4,24,576]{2,1,0:T(8,128)(2,1)S(1)}, u32[]{:S(2)}, u32[]{:S(2)}) collective-permute-start(bf16[4,24,576]{2,1,0:T(8,128)(2,1)S(1)} %dynamic-slice_convert_fusion.19), channel_id=1, source_target_pairs={{0,4},{4,0},{1,5},{5,1},{2,6},{6,2},{3,7},{7,3},{8,12},{12,8},{9,1... | collective-permute-start | bytes 331784 | tf_op jit(solution)/shard_map/ppermute | solution.py:70
  118.3 6.0 %collective-permute-start.28 = (bf16[4,24,576]{2,1,0:T(8,128)(2,1)S(1)}, bf16[4,24,576]{2,1,0:T(8,128)(2,1)S(1)}, u32[]{:S(2)}, u32[]{:S(2)}) collective-permute-start(bf16[4,24,576]{2,1,0:T(8,128)(2,1)S(1)} %dynamic-slice_convert_fusion.16), channel_id=1, source_target_pairs={{0,2},{1,3},{2,0},{3,1},{4,6},{5,7},{6,4},{7,5},{8,10},{9,11},{10,... | collective-permute-start | bytes 331784 | tf_op jit(solution)/shard_map/ppermute | solution.py:70
  119.0 6.0 %collective-permute-start.23 = (bf16[4,24,576]{2,1,0:T(8,128)(2,1)S(1)}, bf16[4,24,576]{2,1,0:T(8,128)(2,1)S(1)}, u32[]{:S(2)}, u32[]{:S(2)}) collective-permute-start(bf16[4,24,576]{2,1,0:T(8,128)(2,1)S(1)} %dynamic-slice_convert_fusion.17), channel_id=1, source_target_pairs={{0,4},{4,0},{1,5},{5,1},{2,6},{6,2},{3,7},{7,3},{8,12},{12,8},{9,1... | collective-permute-start | bytes 331784 | tf_op jit(solution)/shard_map/ppermute | solution.py:70
  121.0 5.6 %collective-permute-start.14 = (bf16[2,24,576]{2,1,0:T(8,128)(2,1)S(1)}, bf16[2,24,576]{2,1,0:T(8,128)(2,1)S(1)}, u32[]{:S(2)}, u32[]{:S(2)}) collective-permute-start(bf16[2,24,576]{2,1,0:T(8,128)(2,1)S(1)} %dynamic-slice_convert_fusion.26), channel_id=1, source_target_pairs={{0,8},{8,0},{16,24},{24,16},{1,9},{9,1},{17,25},{25,17},{2,10},{10... | collective-permute-start | bytes 165896 | tf_op jit(solution)/shard_map/ppermute | solution.py:70
  122.7 6.8 %collective-permute-start.9 = (bf16[2,24,576]{2,1,0:T(8,128)(2,1)S(1)}, bf16[2,24,576]{2,1,0:T(8,128)(2,1)S(1)}, u32[]{:S(2)}, u32[]{:S(2)}) collective-permute-start(bf16[2,24,576]{2,1,0:T(8,128)(2,1)S(1)} %dynamic-slice_convert_fusion.27), channel_id=1, source_target_pairs={{0,2},{1,3},{2,0},{3,1},{4,6},{5,7},{6,4},{7,5},{8,10},{9,11},{10,... | collective-permute-start | bytes 165896 | tf_op jit(solution)/shard_map/ppermute | solution.py:70
  124.4 5.6 %collective-permute-start.29 = (bf16[2,24,576]{2,1,0:T(8,128)(2,1)S(1)}, bf16[2,24,576]{2,1,0:T(8,128)(2,1)S(1)}, u32[]{:S(2)}, u32[]{:S(2)}) collective-permute-start(bf16[2,24,576]{2,1,0:T(8,128)(2,1)S(1)} %dynamic-slice_convert_fusion.24), channel_id=1, source_target_pairs={{0,8},{8,0},{16,24},{24,16},{1,9},{9,1},{17,25},{25,17},{2,10},{10... | collective-permute-start | bytes 165896 | tf_op jit(solution)/shard_map/ppermute | solution.py:70
  125.1 7.6 %collective-permute-start.24 = (bf16[2,24,576]{2,1,0:T(8,128)(2,1)S(1)}, bf16[2,24,576]{2,1,0:T(8,128)(2,1)S(1)}, u32[]{:S(2)}, u32[]{:S(2)}) collective-permute-start(bf16[2,24,576]{2,1,0:T(8,128)(2,1)S(1)} %dynamic-slice_convert_fusion.25), channel_id=1, source_target_pairs={{0,2},{1,3},{2,0},{3,1},{4,6},{5,7},{6,4},{7,5},{8,10},{9,11},{10,... | collective-permute-start | bytes 165896 | tf_op jit(solution)/shard_map/ppermute | solution.py:70
  126.6 6.5 %collective-permute-start.15 = (bf16[1,24,576]{2,1,0:T(8,128)(2,1)S(1)}, bf16[1,24,576]{2,1,0:T(8,128)(2,1)S(1)}, u32[]{:S(2)}, u32[]{:S(2)}) collective-permute-start(bf16[1,24,576]{2,1,0:T(8,128)(2,1)S(1)} %dynamic-slice_convert_fusion.32), channel_id=1, source_target_pairs={{0,16},{8,24},{16,0},{24,8},{1,17},{9,25},{17,1},{25,9},{2,18},{10... | collective-permute-start | bytes 82952 | tf_op jit(solution)/shard_map/ppermute | solution.py:70
  129.6 5.6 %collective-permute-start.10 = (bf16[1,24,576]{2,1,0:T(8,128)(2,1)S(1)}, bf16[1,24,576]{2,1,0:T(8,128)(2,1)S(1)}, u32[]{:S(2)}, u32[]{:S(2)}) collective-permute-start(bf16[1,24,576]{2,1,0:T(8,128)(2,1)S(1)} %dynamic-slice_convert_fusion.33), channel_id=1, source_target_pairs={{0,16},{8,24},{16,0},{24,8},{1,17},{9,25},{17,1},{25,9},{2,18},{10... | collective-permute-start | bytes 82952 | tf_op jit(solution)/shard_map/ppermute | solution.py:70
  130.0 5.5 %collective-permute-start.30 = (bf16[1,24,576]{2,1,0:T(8,128)(2,1)S(1)}, bf16[1,24,576]{2,1,0:T(8,128)(2,1)S(1)}, u32[]{:S(2)}, u32[]{:S(2)}) collective-permute-start(bf16[1,24,576]{2,1,0:T(8,128)(2,1)S(1)} %dynamic-slice_convert_fusion.30), channel_id=1, source_target_pairs={{0,16},{8,24},{16,0},{24,8},{1,17},{9,25},{17,1},{25,9},{2,18},{10... | collective-permute-start | bytes 82952 | tf_op jit(solution)/shard_map/ppermute | solution.py:70
  132.7 5.2 %collective-permute-start.25 = (bf16[1,24,576]{2,1,0:T(8,128)(2,1)S(1)}, bf16[1,24,576]{2,1,0:T(8,128)(2,1)S(1)}, u32[]{:S(2)}, u32[]{:S(2)}) collective-permute-start(bf16[1,24,576]{2,1,0:T(8,128)(2,1)S(1)} %dynamic-slice_convert_fusion.31), channel_id=1, source_target_pairs={{0,16},{8,24},{16,0},{24,8},{1,17},{9,25},{17,1},{25,9},{2,18},{10... | collective-permute-start | bytes 82952 | tf_op jit(solution)/shard_map/ppermute | solution.py:70
  138.1 6.1 %collective-permute-start.46 = (bf16[1,16,576]{2,1,0:T(8,128)(2,1)S(1)}, bf16[1,16,576]{2,1,0:T(8,128)(2,1)S(1)}, u32[]{:S(2)}, u32[]{:S(2)}) collective-permute-start(bf16[1,16,576]{2,1,0:T(8,128)(2,1)S(1)} %slice_bitcast_fusion.13), channel_id=1, source_target_pairs={{0,16},{8,24},{16,0},{24,8},{1,17},{9,25},{17,1},{25,9},{2,18},{10... | collective-permute-start | bytes 55304 | tf_op jit(solution)/shard_map/ppermute | solution.py:86
  138.2 9.1 %collective-permute-start.41 = (bf16[1,24,576]{2,1,0:T(8,128)(2,1)S(1)}, bf16[1,24,576]{2,1,0:T(8,128)(2,1)S(1)}, u32[]{:S(2)}, u32[]{:S(2)}) collective-permute-start(bf16[1,24,576]{2,1,0:T(8,128)(2,1)S(1)} %get-tuple-element.19), channel_id=1, source_target_pairs={{0,16},{8,24},{16,0},{24,8},{1,17},{9,25},{17,1},{25,9},{2,18},{10... | collective-permute-start | bytes 82952 | tf_op jit(solution)/shard_map/ppermute | solution.py:86
  141.1 8.1 %collective-permute-start.36 = (bf16[1,24,576]{2,1,0:T(8,128)(2,1)S(1)}, bf16[1,24,576]{2,1,0:T(8,128)(2,1)S(1)}, u32[]{:S(2)}, u32[]{:S(2)}) collective-permute-start(bf16[1,24,576]{2,1,0:T(8,128)(2,1)S(1)} %get-tuple-element.18), channel_id=1, source_target_pairs={{0,16},{8,24},{16,0},{24,8},{1,17},{9,25},{17,1},{25,9},{2,18},{10... | collective-permute-start | bytes 82952 | tf_op jit(solution)/shard_map/ppermute | solution.py:86
  141.2 5.8 %collective-permute-start.61 = (bf16[1,16,576]{2,1,0:T(8,128)(2,1)S(1)}, bf16[1,16,576]{2,1,0:T(8,128)(2,1)S(1)}, u32[]{:S(2)}, u32[]{:S(2)}) collective-permute-start(bf16[1,16,576]{2,1,0:T(8,128)(2,1)S(1)} %slice_bitcast_fusion.12), channel_id=1, source_target_pairs={{0,16},{8,24},{16,0},{24,8},{1,17},{9,25},{17,1},{25,9},{2,18},{10... | collective-permute-start | bytes 55304 | tf_op jit(solution)/shard_map/ppermute | solution.py:86
  144.1 5.8 %collective-permute-start.56 = (bf16[1,24,576]{2,1,0:T(8,128)(2,1)S(1)}, bf16[1,24,576]{2,1,0:T(8,128)(2,1)S(1)}, u32[]{:S(2)}, u32[]{:S(2)}) collective-permute-start(bf16[1,24,576]{2,1,0:T(8,128)(2,1)S(1)} %get-tuple-element.17), channel_id=1, source_target_pairs={{0,16},{8,24},{16,0},{24,8},{1,17},{9,25},{17,1},{25,9},{2,18},{10... | collective-permute-start | bytes 82952 | tf_op jit(solution)/shard_map/ppermute | solution.py:86
  144.2 7.1 %collective-permute-start.51 = (bf16[1,24,576]{2,1,0:T(8,128)(2,1)S(1)}, bf16[1,24,576]{2,1,0:T(8,128)(2,1)S(1)}, u32[]{:S(2)}, u32[]{:S(2)}) collective-permute-start(bf16[1,24,576]{2,1,0:T(8,128)(2,1)S(1)} %get-tuple-element.16), channel_id=1, source_target_pairs={{0,16},{8,24},{16,0},{24,8},{1,17},{9,25},{17,1},{25,9},{2,18},{10... | collective-permute-start | bytes 82952 | tf_op jit(solution)/shard_map/ppermute | solution.py:86
  147.0 5.1 %collective-permute-start.47 = (bf16[2,16,576]{2,1,0:T(8,128)(2,1)S(1)}, bf16[2,16,576]{2,1,0:T(8,128)(2,1)S(1)}, u32[]{:S(2)}, u32[]{:S(2)}) collective-permute-start(bf16[2,16,576]{2,1,0:T(8,128)(2,1)S(1)} %maximum_select_fusion.34), channel_id=1, source_target_pairs={{0,4},{4,0},{1,5},{5,1},{2,6},{6,2},{3,7},{7,3},{8,12},{12,8},{9,1... | collective-permute-start | bytes 110600 | tf_op jit(solution)/shard_map/ppermute | solution.py:86
  147.3 6.4 %collective-permute-start.62 = (bf16[2,16,576]{2,1,0:T(8,128)(2,1)S(1)}, bf16[2,16,576]{2,1,0:T(8,128)(2,1)S(1)}, u32[]{:S(2)}, u32[]{:S(2)}) collective-permute-start(bf16[2,16,576]{2,1,0:T(8,128)(2,1)S(1)} %maximum_select_fusion.35), channel_id=1, source_target_pairs={{0,4},{4,0},{1,5},{5,1},{2,6},{6,2},{3,7},{7,3},{8,12},{12,8},{9,1... | collective-permute-start | bytes 110600 | tf_op jit(solution)/shard_map/ppermute | solution.py:86
  149.3 5.0 %collective-permute-start.42 = (bf16[2,24,576]{2,1,0:T(8,128)(2,1)S(1)}, bf16[2,24,576]{2,1,0:T(8,128)(2,1)S(1)}, u32[]{:S(2)}, u32[]{:S(2)}) collective-permute-start(bf16[2,24,576]{2,1,0:T(8,128)(2,1)S(1)} %maximum_select_fusion.31), channel_id=1, source_target_pairs={{0,8},{8,0},{16,24},{24,16},{1,9},{9,1},{17,25},{25,17},{2,10},{10... | collective-permute-start | bytes 165896 | tf_op jit(solution)/shard_map/ppermute | solution.py:86
  149.9 6.1 %collective-permute-start.37 = (bf16[2,24,576]{2,1,0:T(8,128)(2,1)S(1)}, bf16[2,24,576]{2,1,0:T(8,128)(2,1)S(1)}, u32[]{:S(2)}, u32[]{:S(2)}) collective-permute-start(bf16[2,24,576]{2,1,0:T(8,128)(2,1)S(1)} %maximum_select_fusion.30), channel_id=1, source_target_pairs={{0,2},{1,3},{2,0},{3,1},{4,6},{5,7},{6,4},{7,5},{8,10},{9,11},{10,... | collective-permute-start | bytes 165896 | tf_op jit(solution)/shard_map/ppermute | solution.py:86
  151.3 5.3 %collective-permute-start.57 = (bf16[2,24,576]{2,1,0:T(8,128)(2,1)S(1)}, bf16[2,24,576]{2,1,0:T(8,128)(2,1)S(1)}, u32[]{:S(2)}, u32[]{:S(2)}) collective-permute-start(bf16[2,24,576]{2,1,0:T(8,128)(2,1)S(1)} %maximum_select_fusion.33), channel_id=1, source_target_pairs={{0,8},{8,0},{16,24},{24,16},{1,9},{9,1},{17,25},{25,17},{2,10},{10... | collective-permute-start | bytes 165896 | tf_op jit(solution)/shard_map/ppermute | solution.py:86
  152.1 6.1 %collective-permute-start.52 = (bf16[2,24,576]{2,1,0:T(8,128)(2,1)S(1)}, bf16[2,24,576]{2,1,0:T(8,128)(2,1)S(1)}, u32[]{:S(2)}, u32[]{:S(2)}) collective-permute-start(bf16[2,24,576]{2,1,0:T(8,128)(2,1)S(1)} %maximum_select_fusion.32), channel_id=1, source_target_pairs={{0,2},{1,3},{2,0},{3,1},{4,6},{5,7},{6,4},{7,5},{8,10},{9,11},{10,... | collective-permute-start | bytes 165896 | tf_op jit(solution)/shard_map/ppermute | solution.py:86
  153.7 4.8 %collective-permute-start.48 = (bf16[4,16,576]{2,1,0:T(8,128)(2,1)S(1)}, bf16[4,16,576]{2,1,0:T(8,128)(2,1)S(1)}, u32[]{:S(2)}, u32[]{:S(2)}) collective-permute-start(bf16[4,16,576]{2,1,0:T(8,128)(2,1)S(1)} %maximum_select_fusion.28), channel_id=1, source_target_pairs={{0,8},{8,0},{16,24},{24,16},{1,9},{9,1},{17,25},{25,17},{2,10},{10... | collective-permute-start | bytes 221192 | tf_op jit(solution)/shard_map/ppermute | solution.py:86
  154.3 6.1 %collective-permute-start.63 = (bf16[4,16,576]{2,1,0:T(8,128)(2,1)S(1)}, bf16[4,16,576]{2,1,0:T(8,128)(2,1)S(1)}, u32[]{:S(2)}, u32[]{:S(2)}) collective-permute-start(bf16[4,16,576]{2,1,0:T(8,128)(2,1)S(1)} %maximum_select_fusion.29), channel_id=1, source_target_pairs={{0,8},{8,0},{16,24},{24,16},{1,9},{9,1},{17,25},{25,17},{2,10},{10... | collective-permute-start | bytes 221192 | tf_op jit(solution)/shard_map/ppermute | solution.py:86
  156.0 5.2 %collective-permute-start.43 = (bf16[4,24,576]{2,1,0:T(8,128)(2,1)S(1)}, bf16[4,24,576]{2,1,0:T(8,128)(2,1)S(1)}, u32[]{:S(2)}, u32[]{:S(2)}) collective-permute-start(bf16[4,24,576]{2,1,0:T(8,128)(2,1)S(1)} %maximum_select_fusion.25), channel_id=1, source_target_pairs={{0,2},{1,3},{2,0},{3,1},{4,6},{5,7},{6,4},{7,5},{8,10},{9,11},{10,... | collective-permute-start | bytes 331784 | tf_op jit(solution)/shard_map/ppermute | solution.py:86
  156.6 6.1 %collective-permute-start.38 = (bf16[4,24,576]{2,1,0:T(8,128)(2,1)S(1)}, bf16[4,24,576]{2,1,0:T(8,128)(2,1)S(1)}, u32[]{:S(2)}, u32[]{:S(2)}) collective-permute-start(bf16[4,24,576]{2,1,0:T(8,128)(2,1)S(1)} %maximum_select_fusion.24), channel_id=1, source_target_pairs={{0,4},{4,0},{1,5},{5,1},{2,6},{6,2},{3,7},{7,3},{8,12},{12,8},{9,1... | collective-permute-start | bytes 331784 | tf_op jit(solution)/shard_map/ppermute | solution.py:86
  158.2 4.9 %collective-permute-start.58 = (bf16[4,24,576]{2,1,0:T(8,128)(2,1)S(1)}, bf16[4,24,576]{2,1,0:T(8,128)(2,1)S(1)}, u32[]{:S(2)}, u32[]{:S(2)}) collective-permute-start(bf16[4,24,576]{2,1,0:T(8,128)(2,1)S(1)} %maximum_select_fusion.27), channel_id=1, source_target_pairs={{0,2},{1,3},{2,0},{3,1},{4,6},{5,7},{6,4},{7,5},{8,10},{9,11},{10,... | collective-permute-start | bytes 331784 | tf_op jit(solution)/shard_map/ppermute | solution.py:86
  158.5 6.3 %collective-permute-start.53 = (bf16[4,24,576]{2,1,0:T(8,128)(2,1)S(1)}, bf16[4,24,576]{2,1,0:T(8,128)(2,1)S(1)}, u32[]{:S(2)}, u32[]{:S(2)}) collective-permute-start(bf16[4,24,576]{2,1,0:T(8,128)(2,1)S(1)} %maximum_select_fusion.26), channel_id=1, source_target_pairs={{0,4},{4,0},{1,5},{5,1},{2,6},{6,2},{3,7},{7,3},{8,12},{12,8},{9,1... | collective-permute-start | bytes 331784 | tf_op jit(solution)/shard_map/ppermute | solution.py:86
  160.5 5.4 %collective-permute-start.49 = (bf16[8,16,576]{2,1,0:T(8,128)(2,1)S(1)}, bf16[8,16,576]{2,1,0:T(8,128)(2,1)S(1)}, u32[]{:S(2)}, u32[]{:S(2)}) collective-permute-start(bf16[8,16,576]{2,1,0:T(8,128)(2,1)S(1)} %maximum_select_fusion.22), channel_id=1, source_target_pairs={{0,2},{1,3},{2,0},{3,1},{4,6},{5,7},{6,4},{7,5},{8,10},{9,11},{10,... | collective-permute-start | bytes 442376 | tf_op jit(solution)/shard_map/ppermute | solution.py:86
  161.1 6.5 %collective-permute-start.64 = (bf16[8,16,576]{2,1,0:T(8,128)(2,1)S(1)}, bf16[8,16,576]{2,1,0:T(8,128)(2,1)S(1)}, u32[]{:S(2)}, u32[]{:S(2)}) collective-permute-start(bf16[8,16,576]{2,1,0:T(8,128)(2,1)S(1)} %maximum_select_fusion.23), channel_id=1, source_target_pairs={{0,2},{1,3},{2,0},{3,1},{4,6},{5,7},{6,4},{7,5},{8,10},{9,11},{10,... | collective-permute-start | bytes 442376 | tf_op jit(solution)/shard_map/ppermute | solution.py:86
  162.7 6.3 %collective-permute-start.44 = (bf16[8,24,576]{2,1,0:T(8,128)(2,1)S(1)}, bf16[8,24,576]{2,1,0:T(8,128)(2,1)S(1)}, u32[]{:S(2)}, u32[]{:S(2)}) collective-permute-start(bf16[8,24,576]{2,1,0:T(8,128)(2,1)S(1)} %maximum_select_fusion.17), channel_id=1, source_target_pairs={{0,4},{4,0},{1,5},{5,1},{2,6},{6,2},{3,7},{7,3},{8,12},{12,8},{9,1... | collective-permute-start | bytes 663560 | tf_op jit(solution)/shard_map/ppermute | solution.py:86
  163.1 6.2 %collective-permute-start.39 = (bf16[8,24,576]{2,1,0:T(8,128)(2,1)S(1)}, bf16[8,24,576]{2,1,0:T(8,128)(2,1)S(1)}, u32[]{:S(2)}, u32[]{:S(2)}) collective-permute-start(bf16[8,24,576]{2,1,0:T(8,128)(2,1)S(1)} %maximum_select_fusion.16), channel_id=1, source_target_pairs={{0,8},{8,0},{16,24},{24,16},{1,9},{9,1},{17,25},{25,17},{2,10},{10... | collective-permute-start | bytes 663560 | tf_op jit(solution)/shard_map/ppermute | solution.py:86
  164.9 6.8 %collective-permute-start.59 = (bf16[8,24,576]{2,1,0:T(8,128)(2,1)S(1)}, bf16[8,24,576]{2,1,0:T(8,128)(2,1)S(1)}, u32[]{:S(2)}, u32[]{:S(2)}) collective-permute-start(bf16[8,24,576]{2,1,0:T(8,128)(2,1)S(1)} %maximum_select_fusion.19), channel_id=1, source_target_pairs={{0,4},{4,0},{1,5},{5,1},{2,6},{6,2},{3,7},{7,3},{8,12},{12,8},{9,1... | collective-permute-start | bytes 663560 | tf_op jit(solution)/shard_map/ppermute | solution.py:86
  165.8 6.7 %collective-permute-start.54 = (bf16[8,24,576]{2,1,0:T(8,128)(2,1)S(1)}, bf16[8,24,576]{2,1,0:T(8,128)(2,1)S(1)}, u32[]{:S(2)}, u32[]{:S(2)}) collective-permute-start(bf16[8,24,576]{2,1,0:T(8,128)(2,1)S(1)} %maximum_select_fusion.18), channel_id=1, source_target_pairs={{0,8},{8,0},{16,24},{24,16},{1,9},{9,1},{17,25},{25,17},{2,10},{10... | collective-permute-start | bytes 663560 | tf_op jit(solution)/shard_map/ppermute | solution.py:86
  167.6 6.4 %collective-permute-start.50 = (bf16[16,16,576]{2,1,0:T(8,128)(2,1)S(1)}, bf16[16,16,576]{2,1,0:T(8,128)(2,1)S(1)}, u32[]{:S(2)}, u32[]{:S(2)}) collective-permute-start(bf16[16,16,576]{2,1,0:T(8,128)(2,1)S(1)} %maximum_select_fusion.14), channel_id=1, source_target_pairs={{0,1},{1,0},{2,3},{3,2},{4,5},{5,4},{6,7},{7,6},{8,9},{9,8},{10,11... | collective-permute-start | bytes 884744 | tf_op jit(solution)/shard_map/ppermute | solution.py:86
  169.0 5.2 %collective-permute-start.65 = (bf16[16,16,576]{2,1,0:T(8,128)(2,1)S(1)}, bf16[16,16,576]{2,1,0:T(8,128)(2,1)S(1)}, u32[]{:S(2)}, u32[]{:S(2)}) collective-permute-start(bf16[16,16,576]{2,1,0:T(8,128)(2,1)S(1)} %maximum_select_fusion.15), channel_id=1, source_target_pairs={{0,1},{1,0},{2,3},{3,2},{4,5},{5,4},{6,7},{7,6},{8,9},{9,8},{10,11... | collective-permute-start | bytes 884744 | tf_op jit(solution)/shard_map/ppermute | solution.py:86
  169.4 5.1 %collective-permute-start.45 = (bf16[16,24,576]{2,1,0:T(8,128)(2,1)S(1)}, bf16[16,24,576]{2,1,0:T(8,128)(2,1)S(1)}, u32[]{:S(2)}, u32[]{:S(2)}) collective-permute-start(bf16[16,24,576]{2,1,0:T(8,128)(2,1)S(1)} %maximum_select_fusion.9), channel_id=1, source_target_pairs={{0,1},{1,0},{2,3},{3,2},{4,5},{5,4},{6,7},{7,6},{8,9},{9,8},{10,11... | collective-permute-start | bytes 1327112 | tf_op jit(solution)/shard_map/ppermute | solution.py:86
  172.6 25.7 %collective-permute-start.60 = (bf16[16,24,576]{2,1,0:T(8,128)(2,1)}, bf16[16,24,576]{2,1,0:T(8,128)(2,1)}, u32[]{:S(2)}, u32[]{:S(2)}) collective-permute-start(bf16[16,24,576]{2,1,0:T(8,128)(2,1)} %maximum_select_fusion.11), channel_id=1, source_target_pairs={{0,1},{1,0},{2,3},{3,2},{4,5},{5,4},{6,7},{7,6},{8,9},{9,8},{10,11... | collective-permute-start | bytes 1327112 | tf_op jit(solution)/shard_map/ppermute | solution.py:86
  174.0 26.2 %collective-permute-start.55 = (bf16[16,24,576]{2,1,0:T(8,128)(2,1)}, bf16[16,24,576]{2,1,0:T(8,128)(2,1)}, u32[]{:S(2)}, u32[]{:S(2)}) collective-permute-start(bf16[16,24,576]{2,1,0:T(8,128)(2,1)} %maximum_select_fusion.10), channel_id=1, source_target_pairs={{0,1},{1,0},{2,3},{3,2},{4,5},{5,4},{6,7},{7,6},{8,9},{9,8},{10,11... | collective-permute-start | bytes 1327112 | tf_op jit(solution)/shard_map/ppermute | solution.py:86
  222.7 4.4 %collective-permute-start.69 = (bf16[4,64,576]{2,1,0:T(8,128)(2,1)S(1)}, bf16[4,64,576]{2,1,0:T(8,128)(2,1)S(1)}, u32[]{:S(2)}, u32[]{:S(2)}) collective-permute-start(bf16[4,64,576]{2,1,0:T(8,128)(2,1)S(1)} %dynamic-slice_convert_fusion.4), channel_id=1, source_target_pairs={{0,1},{1,0},{2,3},{3,2},{4,5},{5,4},{6,7},{7,6},{8,9},{9,8},{10,11... | collective-permute-start | bytes 884744 | tf_op jit(solution)/shard_map/ppermute | solution.py:70
  228.4 6.7 %collective-permute-start.70 = (bf16[2,64,576]{2,1,0:T(8,128)(2,1)S(1)}, bf16[2,64,576]{2,1,0:T(8,128)(2,1)S(1)}, u32[]{:S(2)}, u32[]{:S(2)}) collective-permute-start(bf16[2,64,576]{2,1,0:T(8,128)(2,1)S(1)} %dynamic-slice_convert_fusion.12), channel_id=1, source_target_pairs={{0,2},{1,3},{2,0},{3,1},{4,6},{5,7},{6,4},{7,5},{8,10},{9,11},{10,... | collective-permute-start | bytes 442376 | tf_op jit(solution)/shard_map/ppermute | solution.py:70
  229.7 6.2 %collective-permute-start.67 = (bf16[2,64,576]{2,1,0:T(8,128)(2,1)S(1)}, bf16[2,64,576]{2,1,0:T(8,128)(2,1)S(1)}, u32[]{:S(2)}, u32[]{:S(2)}) collective-permute-start(bf16[2,64,576]{2,1,0:T(8,128)(2,1)S(1)} %dynamic-slice_convert_fusion.13), channel_id=1, source_target_pairs={{0,4},{4,0},{1,5},{5,1},{2,6},{6,2},{3,7},{7,3},{8,12},{12,8},{9,1... | collective-permute-start | bytes 442376 | tf_op jit(solution)/shard_map/ppermute | solution.py:70
  235.1 4.5 %collective-permute-start.71 = (bf16[1,64,576]{2,1,0:T(8,128)(2,1)S(1)}, bf16[1,64,576]{2,1,0:T(8,128)(2,1)S(1)}, u32[]{:S(2)}, u32[]{:S(2)}) collective-permute-start(bf16[1,64,576]{2,1,0:T(8,128)(2,1)S(1)} %dynamic-slice_convert_fusion.20), channel_id=1, source_target_pairs={{0,4},{4,0},{1,5},{5,1},{2,6},{6,2},{3,7},{7,3},{8,12},{12,8},{9,1... | collective-permute-start | bytes 221192 | tf_op jit(solution)/shard_map/ppermute | solution.py:70
  236.0 4.5 %collective-permute-start.68 = (bf16[1,64,576]{2,1,0:T(8,128)(2,1)S(1)}, bf16[1,64,576]{2,1,0:T(8,128)(2,1)S(1)}, u32[]{:S(2)}, u32[]{:S(2)}) collective-permute-start(bf16[1,64,576]{2,1,0:T(8,128)(2,1)S(1)} %dynamic-slice_convert_fusion.21), channel_id=1, source_target_pairs={{0,2},{1,3},{2,0},{3,1},{4,6},{5,7},{6,4},{7,5},{8,10},{9,11},{10,... | collective-permute-start | bytes 221192 | tf_op jit(solution)/shard_map/ppermute | solution.py:70
  (24 other events, 170.4 us)

commit v9 on v5

--- a/solution.py
+++ b/solution.py
@@ -69,16 +69,22 @@
             send = lax.dynamic_slice_in_dim(parts[p], (1 - own) * half, half, 0)
             recv = lax.ppermute(send.astype(wire), axis, partner(axis, bit))
             parts[p] = keep + recv.astype(keep.dtype)
-    return jnp.concatenate([xp[0] for xp in parts], axis=0)
+    return [xp[0] for xp in parts]
 
 
-def all_gather(block, axes):
+def split_rows(block, axes):
+    _, _, orders, _ = plan(axes)
+    return [lax.slice_in_dim(block, s, s + z, axis=0) for s, z in portion_rows(block.shape[0], len(orders))]
+
+
+def all_gather(pieces, axes):
     labels, prefix, orders, suffix = plan(axes)
-    rows, cols = block.shape
+    rows = sum(p.shape[0] for p in pieces)
+    cols = pieces[0].shape[1]
     nb = len(labels)
     steps = [prefix + order + suffix for order in orders]
     spans = portion_rows(rows, len(orders))
-    parts = [lax.slice_in_dim(block, start, start + size, axis=0)[None] for start, size in spans]
+    parts = [p[None] for p in pieces]
     for k in reversed(range(nb)):
         for p in range(len(parts)):
             axis, bit = steps[p][k]
@@ -111,7 +117,7 @@
     slot_rows = tokens // slots
     feat_total = 2 * feat_parts * feat_dev
 
-    gathered = all_gather(resid[0], PLANE)
+    gathered = all_gather(split_rows(resid[0], PLANE), PLANE)
     tokens_all = (
         gathered.reshape(2, feat_parts, half_rows, cols).transpose(0, 2, 1, 3).reshape(tokens, width)
     )
@@ -131,10 +137,19 @@
         .transpose(1, 3, 0, 2, 4)
         .reshape(slots * feat_parts, layer_count * slot_rows, cols)
     )
-    recon = reduce_scatter(blocks, EVERY, jnp.bfloat16).reshape(layer_count, slot_rows, cols)
-    recon = recon + decoder_bias[:, None, :]
-    error = (recon - target.astype(jnp.float32)).astype(jnp.bfloat16)
-    pieces = all_gather(error.reshape(layer_count * slot_rows, cols), EVERY)
+    recon_parts = reduce_scatter(blocks, EVERY, jnp.float32)
+    bias_rows = jnp.broadcast_to(decoder_bias[:, None, :], target.shape).reshape(-1, cols)
+    target_rows = target.reshape(-1, cols).astype(jnp.float32)
+    error_parts = []
+    start = 0
+    for part in recon_parts:
+        size = part.shape[0]
+        bias_part = lax.slice_in_dim(bias_rows, start, start + size, axis=0)
+        target_part = lax.slice_in_dim(target_rows, start, start + size, axis=0)
+        error_parts.append((part + bias_part - target_part).astype(jnp.bfloat16))
+        start += size
+    error = jnp.concatenate(error_parts, axis=0).reshape(layer_count, slot_rows, cols)
+    pieces = all_gather(error_parts, EVERY)
     piece = (
         pieces.reshape(slots, feat_parts, layer_count, slot_rows, cols)
         .transpose(2, 0, 3, 1, 4)
@@ -151,7 +166,7 @@
         .transpose(0, 2, 1, 3)
         .reshape(2 * feat_parts, half_rows, cols)
     )
-    grad_sum = reduce_scatter(grad_blocks, PLANE, jnp.bfloat16)
+    grad_sum = jnp.concatenate(reduce_scatter(grad_blocks, PLANE, jnp.float32), axis=0)
     return (error, grad_sum.astype(jnp.bfloat16)[None])
 
 

time: 211 us -> 244 us (1.16)
  waiting for transfers between devices: 42.6 us -> 73.7 us
  starting transfers between devices: 55.7 us -> 46.3 us
  local copies, waits for them, and re-layouts: 55.9 us -> 61.9 us
  other arithmetic: 24.7 us -> 30.1 us
    ppermute x21, waiting for transfers between devices: 26 us -> 49.3 us  [reduce_scatter(): recv = lax.ppermute(send.astype(wire), axis, partner(axis, bit))]
    dynamic_slice x0 -> x21, local copies, waits for them, and re-layouts: none -> 11.6 us  [reduce_scatter(): send = lax.dynamic_slice_in_dim(parts[p], (1 - own) * half, half, 0)]
    ppermute x21, waiting for transfers between devices: 16.5 us -> 24.4 us  [all_gather(): recv = lax.ppermute(parts[p], axis, partner(axis, bit))]
    convert_element_type x21 -> x0, local copies, waits for them, and re-layouts: 6.03 us -> none  [reduce_scatter(): recv = lax.ppermute(send.astype(wire), axis, partner(axis, bit))]
    ppermute x21, starting transfers between devices: 29.2 us -> 23.3 us  [all_gather(): recv = lax.ppermute(parts[p], axis, partner(axis, bit))]
    add x16, other arithmetic: 6.28 us -> 10.8 us  [reduce_scatter(): parts[p] = keep + recv.astype(keep.dtype)]
    ppermute x21, starting transfers between devices: 26.5 us -> 23 us  [reduce_scatter(): recv = lax.ppermute(send.astype(wire), axis, partner(axis, bit))]
  transfers between devices with their start and end apart: 42 -> 42, of which waited for: 21 -> 19; matrix products, arithmetic and copies ran while one was open for 14% -> 16% of each run, Pallas kernels for 0% -> 0%
where the time goes in v9:
time: 244 us; the launch traced here: 243 us
  waiting for transfers between devices  73.7 us (30%)
  local copies, waits for them, and re-layouts  61.9 us (25%)
  starting transfers between devices  46.3 us (19%)
  other arithmetic  30.1 us (12%)
  matrix products  29.6 us (12%)
    ppermute x21, waiting for transfers between devices, reduce_scatter(): recv = lax.ppermute(send.astype(wire), axis, partner(axis, bit))  49.3 us
    ppermute x21, waiting for transfers between devices, all_gather(): recv = lax.ppermute(parts[p], axis, partner(axis, bit))  24.4 us
    ppermute x21, starting transfers between devices, all_gather(): recv = lax.ppermute(parts[p], axis, partner(axis, bit))  23.3 us
    ppermute x21, starting transfers between devices, reduce_scatter(): recv = lax.ppermute(send.astype(wire), axis, partner(axis, bit))  23 us
    reshape x2, local copies, waits for them, and re-layouts, local(): partial_value.reshape(layer_count, slots, slot_rows, feat_parts, cols)  18.6 us
    dot_general x1, matrix products, local(): jnp.einsum('tf,lfd->ltd', acts, decoder[0], preferred_element_type=jnp.fl...  13.9 us
    dynamic_slice x21, local copies, waits for them, and re-layouts, reduce_scatter(): send = lax.dynamic_slice_in_dim(parts[p], (1 - own) * half, half, 0)  11.6 us
    add x16, other arithmetic, reduce_scatter(): parts[p] = keep + recv.astype(keep.dtype)  10.8 us
  transfers between devices with their start and end apart: 42, of which 19 were waited for; matrix products, arithmetic and copies ran while one was open for 16% of the time, Pallas kernels for 0%

profile of v9, /device:TPU:0, one launch (start us, length us, event | category | flops | bytes accessed | tf_op | source)
XLA Modules:
  0.0 242.9 jit_solution(5695295567064657164)
XLA Ops:
  0.6 1.1 fusion.44
  1.9 3.1 %collective-permute-start = (bf16[1,64,576]{2,1,0:T(8,128)(2,1)S(1)}, bf16[1,64,576]{2,1,0:T(8,128)(2,1)S(1)}, u32[]{:S(2)}, u32[]{:S(2)}) collective-permute-start(bf16[1,64,576]{2,1,0:T(8,128)(2,1)S(1)} %copy.69), channel_id=1, source_target_pairs={{0,2},{1,3},{2,0},{3,1},{4,6},{5,7},{6,4},{7,5},{8,10},{9,11},{10,... | collective-permute-start | bytes 221192 | tf_op jit(solution)/shard_map/ppermute | solution.py:92
  5.1 1.6 collective-permute-start.3
  7.5 2.0 collective-permute-start.1
  9.9 1.2 collective-permute-start.4
  11.2 1.9 collective-permute-done.1
  13.3 2.0 collective-permute-done.4
  15.5 9.4 %compare_reduce_fusion = pred[256,1024]{1,0:T(8,128)(4,1)S(1)} fusion(s32[1024]{0:T(1024)S(1)} %iota_add_fusion, s32[256,64]{1,0:T(8,128)S(1)} %copy.51), kind=kLoop, calls=%fused_computation | loop fusion | flops 33292288 | bytes 331776 | tf_op jit(solution)/shard_map/reduce_or | solution.py:128
  26.6 3.8 %fusion.35 = bf16[256,1024,1]{1,0,2:T(8,128)(2,1)S(1)} fusion(pred[256,1024]{1,0:T(8,128)(4,1)S(1)} %compare_reduce_fusion, bf16[1,2304,1024]{2,1,0:T(8,128)(2,1)} %param.8, bf16[288,8,2,128]{3,2,1,0:T(2,128)(2,1)S(1)} %bitcast.141, f32[1024]{0:T(1024)S(1)} %bitcast.152), kind=kOutput, calls=%fused_computation.30 | convolution fusion | flops 1208745984 | bytes 6688768 | tf_op jit(solution)/shard_map/dot_general | solution.py:124
  30.4 13.9 %select_bitcast_fusion = f32[4,256,2304]{2,1,0:T(8,128)} fusion(bf16[256,1024,1]{1,0,2:T(8,128)(2,1)S(1)} %fusion.35, bf16[1,4,1024,2304]{3,2,1,0:T(8,128)(2,1)} %param.10, pred[4]{0:T(512)(128)(4,1)S(1)} %iota_compare_fusion), kind=kOutput, calls=%fused_computation.5 | convolution fusion | flops 4834197504 | bytes 28835844 | tf_op jit(solution)/shard_map/tf,lfd->ltd/dot_general | solution.py:133
  44.3 13.2 %reshape.126 = f32[4,8,32,4,576]{4,3,2,1,0:T(4,128)} reshape(f32[4,256,2304]{2,1,0:T(8,128)} %select_bitcast_fusion) | data formatting | bytes 18874368 | tf_op jit(solution)/shard_map/reshape | solution.py:136
  57.4 5.5 %copy.57 = f32[4,8,32,4,576]{4,2,0,3,1:T(8,128)S(1)} copy(f32[4,8,32,4,576]{4,3,2,1,0:T(4,128)} %reshape.126) | data formatting | bytes 18874368 | tf_op jit(solution)/shard_map/reshape | solution.py:136
  64.0 1.4 constant_dynamic-slice_fusion.10
  67.8 1.6 constant_dynamic-slice_fusion.15
  70.0 1.4 constant_dynamic-slice_fusion.20
  71.4 2.1 dynamic-slice_add_fusion.1
  73.5 1.2 collective-permute-start.17
  74.8 1.7 dynamic-slice_add_fusion.2
  77.4 1.8 dynamic-slice_add_fusion
  79.2 1.1 constant_dynamic-slice_fusion.19
  80.3 1.6 collective-permute-start.7
  81.9 12.4 %collective-permute-done.17 = f32[8,40,576]{2,1,0:T(8,128)S(1)} collective-permute-done((f32[8,40,576]{2,1,0:T(8,128)S(1)}, f32[8,40,576]{2,1,0:T(8,128)S(1)}, u32[]{:S(2)}, u32[]{:S(2)}) %collective-permute-start.17) | collective-permute-done | bytes 737312 | tf_op jit(solution)/shard_map/ppermute | solution.py:70
  95.1 1.7 collective-permute-start.18
  99.7 13.5 %collective-permute-done.18 = f32[4,40,576]{2,1,0:T(8,128)} collective-permute-done((f32[4,40,576]{2,1,0:T(8,128)}, f32[4,40,576]{2,1,0:T(8,128)}, u32[]{:S(2)}, u32[]{:S(2)}) %collective-permute-start.18) | collective-permute-done | bytes 368672 | tf_op jit(solution)/shard_map/ppermute | solution.py:70
  114.3 1.1 collective-permute-start.19
  115.5 1.2 dynamic-slice_add_fusion.10
  116.7 1.6 collective-permute-start.14
  118.3 1.3 dynamic-slice_add_fusion.3
  120.8 2.7 %collective-permute-start.20 = (f32[1,40,576]{2,1,0:T(8,128)S(1)}, f32[1,40,576]{2,1,0:T(8,128)S(1)}, u32[]{:S(2)}, u32[]{:S(2)}) collective-permute-start(f32[1,40,576]{2,1,0:T(8,128)S(1)} %constant_dynamic-slice_fusion.6), channel_id=1, source_target_pairs={{0,16},{8,24},{16,0},{24,8},{1,17},{9,25},{17,1},{25,9},{2,18},{10... | collective-permute-start | bytes 276488 | tf_op jit(solution)/shard_map/ppermute | solution.py:70
  123.5 2.3 collective-permute-start.15
  125.9 5.5 %collective-permute-done.8 = f32[4,48,576]{2,1,0:T(8,128)S(1)} collective-permute-done((f32[4,48,576]{2,1,0:T(8,128)S(1)}, f32[4,48,576]{2,1,0:T(8,128)S(1)}, u32[]{:S(2)}, u32[]{:S(2)}) %collective-permute-start.8) | collective-permute-done | bytes 442400 | tf_op jit(solution)/shard_map/ppermute | solution.py:70
  131.5 1.7 collective-permute-start.9
  133.3 2.7 %collective-permute-start.26 = (bf16[1,40,576]{2,1,0:T(8,128)(2,1)S(1)}, bf16[1,40,576]{2,1,0:T(8,128)(2,1)S(1)}, u32[]{:S(2)}, u32[]{:S(2)}) collective-permute-start(bf16[1,40,576]{2,1,0:T(8,128)(2,1)S(1)} %bitcast.144), channel_id=1, source_target_pairs={{0,16},{8,24},{16,0},{24,8},{1,17},{9,25},{17,1},{25,9},{2,18},{10... | collective-permute-start | bytes 138248 | tf_op jit(solution)/shard_map/ppermute | solution.py:92
  136.3 3.2 %collective-permute-done.26 = bf16[1,40,576]{2,1,0:T(8,128)(2,1)S(1)} collective-permute-done((bf16[1,40,576]{2,1,0:T(8,128)(2,1)S(1)}, bf16[1,40,576]{2,1,0:T(8,128)(2,1)S(1)}, u32[]{:S(2)}, u32[]{:S(2)}) %collective-permute-start.26) | collective-permute-done | bytes 46112 | tf_op jit(solution)/shard_map/ppermute | solution.py:92
  140.1 2.1 collective-permute-start.10
  142.3 2.2 collective-permute-start.32
  144.4 3.7 %collective-permute-done.10 = f32[1,48,576]{2,1,0:T(8,128)S(1)} collective-permute-done((f32[1,48,576]{2,1,0:T(8,128)S(1)}, f32[1,48,576]{2,1,0:T(8,128)S(1)}, u32[]{:S(2)}, u32[]{:S(2)}) %collective-permute-start.10) | collective-permute-done | bytes 110624 | tf_op jit(solution)/shard_map/ppermute | solution.py:70
  148.4 2.2 collective-permute-start.28
  150.6 3.0 %collective-permute-done.21 = bf16[1,48,576]{2,1,0:T(8,128)(2,1)S(1)} collective-permute-done((bf16[1,48,576]{2,1,0:T(8,128)(2,1)S(1)}, bf16[1,48,576]{2,1,0:T(8,128)(2,1)S(1)}, u32[]{:S(2)}, u32[]{:S(2)}) %collective-permute-start.21) | collective-permute-done | bytes 55328 | tf_op jit(solution)/shard_map/ppermute | solution.py:92
  153.7 1.2 collective-permute-start.22
  155.3 4.3 %collective-permute-done.22 = bf16[2,48,576]{2,1,0:T(8,128)(2,1)S(1)} collective-permute-done((bf16[2,48,576]{2,1,0:T(8,128)(2,1)S(1)}, bf16[2,48,576]{2,1,0:T(8,128)(2,1)S(1)}, u32[]{:S(2)}, u32[]{:S(2)}) %collective-permute-start.22) | collective-permute-done | bytes 110624 | tf_op jit(solution)/shard_map/ppermute | solution.py:92
  159.7 1.9 collective-permute-start.23
  163.2 2.8 %collective-permute-done.23 = bf16[4,48,576]{2,1,0:T(8,128)(2,1)S(1)} collective-permute-done((bf16[4,48,576]{2,1,0:T(8,128)(2,1)S(1)}, bf16[4,48,576]{2,1,0:T(8,128)(2,1)S(1)}, u32[]{:S(2)}, u32[]{:S(2)}) %collective-permute-start.23) | collective-permute-done | bytes 221216 | tf_op jit(solution)/shard_map/ppermute | solution.py:92
  166.1 1.8 collective-permute-start.24
  167.9 2.5 %collective-permute-done.29 = bf16[8,40,576]{2,1,0:T(8,128)(2,1)S(1)} collective-permute-done((bf16[8,40,576]{2,1,0:T(8,128)(2,1)S(1)}, bf16[8,40,576]{2,1,0:T(8,128)(2,1)S(1)}, u32[]{:S(2)}, u32[]{:S(2)}) %collective-permute-start.29) | collective-permute-done | bytes 368672 | tf_op jit(solution)/shard_map/ppermute | solution.py:92
  171.4 3.6 %collective-permute-done.24 = bf16[8,48,576]{2,1,0:T(8,128)(2,1)S(1)} collective-permute-done((bf16[8,48,576]{2,1,0:T(8,128)(2,1)S(1)}, bf16[8,48,576]{2,1,0:T(8,128)(2,1)S(1)}, u32[]{:S(2)}, u32[]{:S(2)}) %collective-permute-start.24) | collective-permute-done | bytes 442400 | tf_op jit(solution)/shard_map/ppermute | solution.py:92
  175.4 1.8 maximum_select_fusion.1
  177.3 1.8 maximum_select_fusion.2
  179.3 2.2 maximum_select_fusion
  181.7 1.1 pad_maximum_fusion
  182.8 6.4 %copy.64 = bf16[4,8,32,4,576]{4,3,2,1,0:T(4,128)(2,1)} copy(bf16[4,8,32,4,576]{4,2,0,3,1:T(8,128)(2,1)S(1)} %bitcast.117) | data formatting | bytes 9437184 | tf_op jit(solution)/shard_map/transpose | solution.py:155
  189.2 9.9 %reshape.136 = bf16[4,256,2304]{2,1,0:T(8,128)(2,1)} reshape(bf16[4,8,32,4,576]{4,3,2,1,0:T(4,128)(2,1)} %copy.64) | data formatting | bytes 9437184 | tf_op jit(solution)/shard_map/reshape | solution.py:156
  199.1 10.5 %fusion.30 = bf16[256,1024]{1,0:T(8,128)(2,1)S(1)} fusion(pred[256,1024]{1,0:T(8,128)(4,1)S(1)} %copy-done.15, bf16[1,4,1024,2304]{3,2,1,0:T(8,128)(2,1)} %param.10, bf16[4,256,2304]{2,1,0:T(8,128)(2,1)} %reshape.136, pred[4]{0:T(512)(128)(4,1)S(1)} %iota_compare_fusion), kind=kOutput, calls=%fused_computation.29 | convolution fusion | flops 4834721792 | bytes 24379396 | tf_op jit(solution)/shard_map/ltd,lfd->tf/dot_general | solution.py:159
  209.7 1.4 fusion.45
  211.1 2.2 slice_bitcast_fusion.4
  213.3 2.9 %copy.65 = f32[2,2,2,64,576]{4,3,2,1,0:T(8,128)} copy(f32[2,2,2,64,576]{3,4,0,2,1:T(8,128)} %get-tuple-element.8) | data formatting | bytes 2359296 | tf_op jit(solution)/shard_map/transpose | solution.py:61
  216.2 2.0 constant_dynamic-slice_fusion.5
  218.7 1.8 copy.66
  220.5 2.1 constant_dynamic-slice_fusion.2
  223.4 1.2 dynamic-slice_add_fusion.7
  224.6 1.9 collective-permute-start.37
  226.7 8.1 %collective-permute-done.37 = f32[2,64,576]{2,1,0:T(8,128)S(1)} collective-permute-done((f32[2,64,576]{2,1,0:T(8,128)S(1)}, f32[2,64,576]{2,1,0:T(8,128)S(1)}, u32[]{:S(2)}, u32[]{:S(2)}) %collective-permute-start.37) | collective-permute-done | bytes 294944 | tf_op jit(solution)/shard_map/ppermute | solution.py:70
  236.9 3.8 %collective-permute-done.38 = f32[1,64,576]{2,1,0:T(8,128)S(1)} collective-permute-done((f32[1,64,576]{2,1,0:T(8,128)S(1)}, f32[1,64,576]{2,1,0:T(8,128)S(1)}, u32[]{:S(2)}, u32[]{:S(2)}) %collective-permute-start.38) | collective-permute-done | bytes 147488 | tf_op jit(solution)/shard_map/ppermute | solution.py:70
  240.8 1.3 collective-permute-done.41
  (162 shorter events, 24.4 us)
Async XLA Ops:
  0.6 6.1 %copy-start = (s32[4,256,64]{1,2,0:T(8,128)S(1)}, s32[4,256,64]{1,2,0:T(8,128)}, u32[]{:S(2)}) copy-start(s32[4,256,64]{1,2,0:T(8,128)} %param.12) | copy-start | bytes 786436
  1.9 5.5 %collective-permute-start = (bf16[1,64,576]{2,1,0:T(8,128)(2,1)S(1)}, bf16[1,64,576]{2,1,0:T(8,128)(2,1)S(1)}, u32[]{:S(2)}, u32[]{:S(2)}) collective-permute-start(bf16[1,64,576]{2,1,0:T(8,128)(2,1)S(1)} %copy.69), channel_id=1, source_target_pairs={{0,2},{1,3},{2,0},{3,1},{4,6},{5,7},{6,4},{7,5},{8,10},{9,11},{10,... | collective-permute-start | bytes 221192 | tf_op jit(solution)/shard_map/ppermute | solution.py:92
  5.1 4.7 %collective-permute-start.3 = (bf16[1,64,576]{2,1,0:T(8,128)(2,1)S(1)}, bf16[1,64,576]{2,1,0:T(8,128)(2,1)S(1)}, u32[]{:S(2)}, u32[]{:S(2)}) collective-permute-start(bf16[1,64,576]{2,1,0:T(8,128)(2,1)S(1)} %copy.70), channel_id=1, source_target_pairs={{0,4},{4,0},{1,5},{5,1},{2,6},{6,2},{3,7},{7,3},{8,12},{12,8},{9,1... | collective-permute-start | bytes 221192 | tf_op jit(solution)/shard_map/ppermute | solution.py:92
  7.5 5.7 %collective-permute-start.1 = (bf16[2,64,576]{2,1,0:T(8,128)(2,1)S(1)}, bf16[2,64,576]{2,1,0:T(8,128)(2,1)S(1)}, u32[]{:S(2)}, u32[]{:S(2)}) collective-permute-start(bf16[2,64,576]{2,1,0:T(8,128)(2,1)S(1)} %maximum_select_fusion.16), channel_id=1, source_target_pairs={{0,4},{4,0},{1,5},{5,1},{2,6},{6,2},{3,7},{7,3},{8,12},{12,8},{9,1... | collective-permute-start | bytes 442376 | tf_op jit(solution)/shard_map/ppermute | solution.py:92
  9.9 5.4 %collective-permute-start.4 = (bf16[2,64,576]{2,1,0:T(8,128)(2,1)S(1)}, bf16[2,64,576]{2,1,0:T(8,128)(2,1)S(1)}, u32[]{:S(2)}, u32[]{:S(2)}) collective-permute-start(bf16[2,64,576]{2,1,0:T(8,128)(2,1)S(1)} %maximum_select_fusion.17), channel_id=1, source_target_pairs={{0,2},{1,3},{2,0},{3,1},{4,6},{5,7},{6,4},{7,5},{8,10},{9,11},{10,... | collective-permute-start | bytes 442376 | tf_op jit(solution)/shard_map/ppermute | solution.py:92
  13.2 11.7 %collective-permute-start.2 = (bf16[4,64,576]{2,1,0:T(8,128)(2,1)S(1)}, bf16[4,64,576]{2,1,0:T(8,128)(2,1)S(1)}, u32[]{:S(2)}, u32[]{:S(2)}) collective-permute-start(bf16[4,64,576]{2,1,0:T(8,128)(2,1)S(1)} %maximum_select_fusion.11), channel_id=1, source_target_pairs={{0,1},{1,0},{2,3},{3,2},{4,5},{5,4},{6,7},{7,6},{8,9},{9,8},{10,11... | collective-permute-start | bytes 884744 | tf_op jit(solution)/shard_map/ppermute | solution.py:92
  15.4 9.8 %collective-permute-start.5 = (bf16[4,64,576]{2,1,0:T(8,128)(2,1)S(1)}, bf16[4,64,576]{2,1,0:T(8,128)(2,1)S(1)}, u32[]{:S(2)}, u32[]{:S(2)}) collective-permute-start(bf16[4,64,576]{2,1,0:T(8,128)(2,1)S(1)} %maximum_select_fusion.12), channel_id=1, source_target_pairs={{0,1},{1,0},{2,3},{3,2},{4,5},{5,4},{6,7},{7,6},{8,9},{9,8},{10,11... | collective-permute-start | bytes 884744 | tf_op jit(solution)/shard_map/ppermute | solution.py:92
  24.9 1.7 copy-start.14
  25.4 1.2 copy-start.18
  64.0 2.2 copy-start.4
  66.2 5.2 %collective-permute-start.16 = (f32[16,40,576]{2,1,0:T(8,128)}, f32[16,40,576]{2,1,0:T(8,128)}, u32[]{:S(2)}, u32[]{:S(2)}) collective-permute-start(f32[16,40,576]{2,1,0:T(8,128)} %constant_dynamic-slice_fusion.10), channel_id=1, source_target_pairs={{0,1},{1,0},{2,3},{3,2},{4,5},{5,4},{6,7},{7,6},{8,9},{9,8},{10,11... | collective-permute-start | bytes 4423688 | tf_op jit(solution)/shard_map/ppermute | solution.py:70
  67.5 2.4 %copy-start.2 = (f32[2,2,2,2,2,48,576]{6,5,4,3,2,1,0:T(8,128)}, f32[2,2,2,2,2,48,576]{6,5,4,3,2,1,0:T(8,128)S(1)}, u32[]{:S(2)}) copy-start(f32[2,2,2,2,2,48,576]{6,5,4,3,2,1,0:T(8,128)S(1)} %copy.58) | copy-start | bytes 10616836
  69.4 5.4 %collective-permute-start.11 = (f32[16,40,576]{2,1,0:T(8,128)}, f32[16,40,576]{2,1,0:T(8,128)}, u32[]{:S(2)}, u32[]{:S(2)}) collective-permute-start(f32[16,40,576]{2,1,0:T(8,128)} %constant_dynamic-slice_fusion.15), channel_id=1, source_target_pairs={{0,1},{1,0},{2,3},{3,2},{4,5},{5,4},{6,7},{7,6},{8,9},{9,8},{10,11... | collective-permute-start | bytes 4423688 | tf_op jit(solution)/shard_map/ppermute | solution.py:70
  71.4 5.9 %collective-permute-start.6 = (f32[16,48,576]{2,1,0:T(8,128)}, f32[16,48,576]{2,1,0:T(8,128)}, u32[]{:S(2)}, u32[]{:S(2)}) collective-permute-start(f32[16,48,576]{2,1,0:T(8,128)} %constant_dynamic-slice_fusion.20), channel_id=1, source_target_pairs={{0,1},{1,0},{2,3},{3,2},{4,5},{5,4},{6,7},{7,6},{8,9},{9,8},{10,11... | collective-permute-start | bytes 5308424 | tf_op jit(solution)/shard_map/ppermute | solution.py:70
  73.5 20.7 %collective-permute-start.17 = (f32[8,40,576]{2,1,0:T(8,128)S(1)}, f32[8,40,576]{2,1,0:T(8,128)S(1)}, u32[]{:S(2)}, u32[]{:S(2)}) collective-permute-start(f32[8,40,576]{2,1,0:T(8,128)S(1)} %constant_dynamic-slice_fusion.9), channel_id=1, source_target_pairs={{0,2},{1,3},{2,0},{3,1},{4,6},{5,7},{6,4},{7,5},{8,10},{9,11},{10,... | collective-permute-start | bytes 2211848 | tf_op jit(solution)/shard_map/ppermute | solution.py:70
  74.8 2.6 %copy-start.3 = (f32[2,2,2,2,2,48,576]{6,5,4,3,2,1,0:T(8,128)S(1)}, f32[2,2,2,2,2,48,576]{6,5,4,3,2,1,0:T(8,128)}, u32[]{:S(2)}) copy-start(f32[2,2,2,2,2,48,576]{6,5,4,3,2,1,0:T(8,128)} %copy-done.2) | copy-start | bytes 10616836
  76.6 20.4 %collective-permute-start.12 = (f32[8,40,576]{2,1,0:T(8,128)S(1)}, f32[8,40,576]{2,1,0:T(8,128)S(1)}, u32[]{:S(2)}, u32[]{:S(2)}) collective-permute-start(f32[8,40,576]{2,1,0:T(8,128)S(1)} %constant_dynamic-slice_fusion.14), channel_id=1, source_target_pairs={{0,4},{4,0},{1,5},{5,1},{2,6},{6,2},{3,7},{7,3},{8,12},{12,8},{9,1... | collective-permute-start | bytes 2211848 | tf_op jit(solution)/shard_map/ppermute | solution.py:70
  80.3 38.0 %collective-permute-start.7 = (f32[8,48,576]{2,1,0:T(8,128)}, f32[8,48,576]{2,1,0:T(8,128)}, u32[]{:S(2)}, u32[]{:S(2)}) collective-permute-start(f32[8,48,576]{2,1,0:T(8,128)} %constant_dynamic-slice_fusion.19), channel_id=1, source_target_pairs={{0,8},{8,0},{16,24},{24,16},{1,9},{9,1},{17,25},{25,17},{2,10},{10... | collective-permute-start | bytes 2654216 | tf_op jit(solution)/shard_map/ppermute | solution.py:70
  94.3 5.3 %copy-start.16 = (bf16[4,32,576]{2,1,0:T(8,128)(2,1)S(1)}, bf16[4,32,576]{2,1,0:T(8,128)(2,1)}, u32[]{:S(2)}) copy-start(bf16[4,32,576]{2,1,0:T(8,128)(2,1)} %param.13) | copy-start | bytes 442372
  95.1 18.1 %collective-permute-start.18 = (f32[4,40,576]{2,1,0:T(8,128)}, f32[4,40,576]{2,1,0:T(8,128)}, u32[]{:S(2)}, u32[]{:S(2)}) collective-permute-start(f32[4,40,576]{2,1,0:T(8,128)} %constant_dynamic-slice_fusion.8), channel_id=1, source_target_pairs={{0,8},{8,0},{16,24},{24,16},{1,9},{9,1},{17,25},{25,17},{2,10},{10... | collective-permute-start | bytes 1105928 | tf_op jit(solution)/shard_map/ppermute | solution.py:70
  97.1 0.9 copy-start.7
  98.8 16.6 %collective-permute-start.13 = (f32[4,40,576]{2,1,0:T(8,128)}, f32[4,40,576]{2,1,0:T(8,128)}, u32[]{:S(2)}, u32[]{:S(2)}) collective-permute-start(f32[4,40,576]{2,1,0:T(8,128)} %constant_dynamic-slice_fusion.13), channel_id=1, source_target_pairs={{0,2},{1,3},{2,0},{3,1},{4,6},{5,7},{6,4},{7,5},{8,10},{9,11},{10,... | collective-permute-start | bytes 1105928 | tf_op jit(solution)/shard_map/ppermute | solution.py:70
  114.3 6.4 %collective-permute-start.19 = (f32[2,40,576]{2,1,0:T(8,128)S(1)}, f32[2,40,576]{2,1,0:T(8,128)S(1)}, u32[]{:S(2)}, u32[]{:S(2)}) collective-permute-start(f32[2,40,576]{2,1,0:T(8,128)S(1)} %constant_dynamic-slice_fusion.7), channel_id=1, source_target_pairs={{0,4},{4,0},{1,5},{5,1},{2,6},{6,2},{3,7},{7,3},{8,12},{12,8},{9,1... | collective-permute-start | bytes 552968 | tf_op jit(solution)/shard_map/ppermute | solution.py:70
  116.7 6.8 %collective-permute-start.14 = (f32[2,40,576]{2,1,0:T(8,128)S(1)}, f32[2,40,576]{2,1,0:T(8,128)S(1)}, u32[]{:S(2)}, u32[]{:S(2)}) collective-permute-start(f32[2,40,576]{2,1,0:T(8,128)S(1)} %constant_dynamic-slice_fusion.12), channel_id=1, source_target_pairs={{0,8},{8,0},{16,24},{24,16},{1,9},{9,1},{17,25},{25,17},{2,10},{10... | collective-permute-start | bytes 552968 | tf_op jit(solution)/shard_map/ppermute | solution.py:70
  119.7 13.6 %copy-start.17 = (f32[4,576]{1,0:T(4,128)S(1)}, f32[4,576]{1,0:T(4,128)}, u32[]{:S(2)}) copy-start(f32[4,576]{1,0:T(4,128)} %param.11) | copy-start | bytes 27652
  119.7 11.7 %collective-permute-start.8 = (f32[4,48,576]{2,1,0:T(8,128)S(1)}, f32[4,48,576]{2,1,0:T(8,128)S(1)}, u32[]{:S(2)}, u32[]{:S(2)}) collective-permute-start(f32[4,48,576]{2,1,0:T(8,128)S(1)} %constant_dynamic-slice_fusion.18), channel_id=1, source_target_pairs={{0,4},{4,0},{1,5},{5,1},{2,6},{6,2},{3,7},{7,3},{8,12},{12,8},{9,1... | collective-permute-start | bytes 1327112 | tf_op jit(solution)/shard_map/ppermute | solution.py:70
  120.8 12.4 %collective-permute-start.20 = (f32[1,40,576]{2,1,0:T(8,128)S(1)}, f32[1,40,576]{2,1,0:T(8,128)S(1)}, u32[]{:S(2)}, u32[]{:S(2)}) collective-permute-start(f32[1,40,576]{2,1,0:T(8,128)S(1)} %constant_dynamic-slice_fusion.6), channel_id=1, source_target_pairs={{0,16},{8,24},{16,0},{24,8},{1,17},{9,25},{17,1},{25,9},{2,18},{10... | collective-permute-start | bytes 276488 | tf_op jit(solution)/shard_map/ppermute | solution.py:70
  123.5 9.7 %collective-permute-start.15 = (f32[1,40,576]{2,1,0:T(8,128)S(1)}, f32[1,40,576]{2,1,0:T(8,128)S(1)}, u32[]{:S(2)}, u32[]{:S(2)}) collective-permute-start(f32[1,40,576]{2,1,0:T(8,128)S(1)} %constant_dynamic-slice_fusion.11), channel_id=1, source_target_pairs={{0,16},{8,24},{16,0},{24,8},{1,17},{9,25},{17,1},{25,9},{2,18},{10... | collective-permute-start | bytes 276488 | tf_op jit(solution)/shard_map/ppermute | solution.py:70
  131.5 8.6 %collective-permute-start.9 = (f32[2,48,576]{2,1,0:T(8,128)S(1)}, f32[2,48,576]{2,1,0:T(8,128)S(1)}, u32[]{:S(2)}, u32[]{:S(2)}) collective-permute-start(f32[2,48,576]{2,1,0:T(8,128)S(1)} %constant_dynamic-slice_fusion.17), channel_id=1, source_target_pairs={{0,2},{1,3},{2,0},{3,1},{4,6},{5,7},{6,4},{7,5},{8,10},{9,11},{10,... | collective-permute-start | bytes 663560 | tf_op jit(solution)/shard_map/ppermute | solution.py:70
  133.3 6.8 %copy-start.10 = (bf16[40,576]{1,0:T(8,128)(2,1)}, bf16[40,576]{1,0:T(8,128)(2,1)S(1)}, u32[]{:S(2)}) copy-start(bf16[40,576]{1,0:T(8,128)(2,1)S(1)} %get-tuple-element.10) | copy-start | bytes 138244
  133.3 28.4 %copy-start.12 = (bf16[40,576]{1,0:T(8,128)(2,1)}, bf16[40,576]{1,0:T(8,128)(2,1)S(1)}, u32[]{:S(2)}) copy-start(bf16[40,576]{1,0:T(8,128)(2,1)S(1)} %get-tuple-element.11) | copy-start | bytes 138244
  133.3 6.2 %collective-permute-start.26 = (bf16[1,40,576]{2,1,0:T(8,128)(2,1)S(1)}, bf16[1,40,576]{2,1,0:T(8,128)(2,1)S(1)}, u32[]{:S(2)}, u32[]{:S(2)}) collective-permute-start(bf16[1,40,576]{2,1,0:T(8,128)(2,1)S(1)} %bitcast.144), channel_id=1, source_target_pairs={{0,16},{8,24},{16,0},{24,8},{1,17},{9,25},{17,1},{25,9},{2,18},{10... | collective-permute-start | bytes 138248 | tf_op jit(solution)/shard_map/ppermute | solution.py:92
  136.0 6.2 %collective-permute-start.31 = (bf16[1,40,576]{2,1,0:T(8,128)(2,1)S(1)}, bf16[1,40,576]{2,1,0:T(8,128)(2,1)S(1)}, u32[]{:S(2)}, u32[]{:S(2)}) collective-permute-start(bf16[1,40,576]{2,1,0:T(8,128)(2,1)S(1)} %bitcast.146), channel_id=1, source_target_pairs={{0,16},{8,24},{16,0},{24,8},{1,17},{9,25},{17,1},{25,9},{2,18},{10... | collective-permute-start | bytes 138248 | tf_op jit(solution)/shard_map/ppermute | solution.py:92
  139.6 8.7 %collective-permute-start.27 = (bf16[2,40,576]{2,1,0:T(8,128)(2,1)S(1)}, bf16[2,40,576]{2,1,0:T(8,128)(2,1)S(1)}, u32[]{:S(2)}, u32[]{:S(2)}) collective-permute-start(bf16[2,40,576]{2,1,0:T(8,128)(2,1)S(1)} %maximum_select_fusion.19), channel_id=1, source_target_pairs={{0,8},{8,0},{16,24},{24,16},{1,9},{9,1},{17,25},{25,17},{2,10},{10... | collective-permute-start | bytes 276488 | tf_op jit(solution)/shard_map/ppermute | solution.py:92
  140.1 8.0 %collective-permute-start.10 = (f32[1,48,576]{2,1,0:T(8,128)S(1)}, f32[1,48,576]{2,1,0:T(8,128)S(1)}, u32[]{:S(2)}, u32[]{:S(2)}) collective-permute-start(f32[1,48,576]{2,1,0:T(8,128)S(1)} %constant_dynamic-slice_fusion.16), channel_id=1, source_target_pairs={{0,16},{8,24},{16,0},{24,8},{1,17},{9,25},{17,1},{25,9},{2,18},{10... | collective-permute-start | bytes 331784 | tf_op jit(solution)/shard_map/ppermute | solution.py:70
  142.3 12.5 %collective-permute-start.32 = (bf16[2,40,576]{2,1,0:T(8,128)(2,1)S(1)}, bf16[2,40,576]{2,1,0:T(8,128)(2,1)S(1)}, u32[]{:S(2)}, u32[]{:S(2)}) collective-permute-start(bf16[2,40,576]{2,1,0:T(8,128)(2,1)S(1)} %maximum_select_fusion.20), channel_id=1, source_target_pairs={{0,4},{4,0},{1,5},{5,1},{2,6},{6,2},{3,7},{7,3},{8,12},{12,8},{9,1... | collective-permute-start | bytes 276488 | tf_op jit(solution)/shard_map/ppermute | solution.py:92
  148.2 13.4 %copy-start.8 = (bf16[48,576]{1,0:T(8,128)(2,1)}, bf16[48,576]{1,0:T(8,128)(2,1)S(1)}, u32[]{:S(2)}) copy-start(bf16[48,576]{1,0:T(8,128)(2,1)S(1)} %fusion.40) | copy-start | bytes 165892
  148.2 5.4 %collective-permute-start.21 = (bf16[1,48,576]{2,1,0:T(8,128)(2,1)S(1)}, bf16[1,48,576]{2,1,0:T(8,128)(2,1)S(1)}, u32[]{:S(2)}, u32[]{:S(2)}) collective-permute-start(bf16[1,48,576]{2,1,0:T(8,128)(2,1)S(1)} %bitcast.142), channel_id=1, source_target_pairs={{0,16},{8,24},{16,0},{24,8},{1,17},{9,25},{17,1},{25,9},{2,18},{10... | collective-permute-start | bytes 165896 | tf_op jit(solution)/shard_map/ppermute | solution.py:92
  148.4 13.2 %collective-permute-start.28 = (bf16[4,40,576]{2,1,0:T(8,128)(2,1)S(1)}, bf16[4,40,576]{2,1,0:T(8,128)(2,1)S(1)}, u32[]{:S(2)}, u32[]{:S(2)}) collective-permute-start(bf16[4,40,576]{2,1,0:T(8,128)(2,1)S(1)} %maximum_select_fusion.14), channel_id=1, source_target_pairs={{0,2},{1,3},{2,0},{3,1},{4,6},{5,7},{6,4},{7,5},{8,10},{9,11},{10,... | collective-permute-start | bytes 552968 | tf_op jit(solution)/shard_map/ppermute | solution.py:92
  153.7 6.0 %collective-permute-start.22 = (bf16[2,48,576]{2,1,0:T(8,128)(2,1)S(1)}, bf16[2,48,576]{2,1,0:T(8,128)(2,1)S(1)}, u32[]{:S(2)}, u32[]{:S(2)}) collective-permute-start(bf16[2,48,576]{2,1,0:T(8,128)(2,1)S(1)} %maximum_select_fusion.18), channel_id=1, source_target_pairs={{0,2},{1,3},{2,0},{3,1},{4,6},{5,7},{6,4},{7,5},{8,10},{9,11},{10,... | collective-permute-start | bytes 331784 | tf_op jit(solution)/shard_map/ppermute | solution.py:92
  154.9 7.1 %collective-permute-start.33 = (bf16[4,40,576]{2,1,0:T(8,128)(2,1)S(1)}, bf16[4,40,576]{2,1,0:T(8,128)(2,1)S(1)}, u32[]{:S(2)}, u32[]{:S(2)}) collective-permute-start(bf16[4,40,576]{2,1,0:T(8,128)(2,1)S(1)} %maximum_select_fusion.15), channel_id=1, source_target_pairs={{0,8},{8,0},{16,24},{24,16},{1,9},{9,1},{17,25},{25,17},{2,10},{10... | collective-permute-start | bytes 552968 | tf_op jit(solution)/shard_map/ppermute | solution.py:92
  159.7 6.3 %collective-permute-start.23 = (bf16[4,48,576]{2,1,0:T(8,128)(2,1)S(1)}, bf16[4,48,576]{2,1,0:T(8,128)(2,1)S(1)}, u32[]{:S(2)}, u32[]{:S(2)}) collective-permute-start(bf16[4,48,576]{2,1,0:T(8,128)(2,1)S(1)} %maximum_select_fusion.13), channel_id=1, source_target_pairs={{0,4},{4,0},{1,5},{5,1},{2,6},{6,2},{3,7},{7,3},{8,12},{12,8},{9,1... | collective-permute-start | bytes 663560 | tf_op jit(solution)/shard_map/ppermute | solution.py:92
  161.7 8.7 %collective-permute-start.29 = (bf16[8,40,576]{2,1,0:T(8,128)(2,1)S(1)}, bf16[8,40,576]{2,1,0:T(8,128)(2,1)S(1)}, u32[]{:S(2)}, u32[]{:S(2)}) collective-permute-start(bf16[8,40,576]{2,1,0:T(8,128)(2,1)S(1)} %maximum_select_fusion.9), channel_id=1, source_target_pairs={{0,4},{4,0},{1,5},{5,1},{2,6},{6,2},{3,7},{7,3},{8,12},{12,8},{9,1... | collective-permute-start | bytes 1105928 | tf_op jit(solution)/shard_map/ppermute | solution.py:92
  162.1 8.5 %collective-permute-start.34 = (bf16[8,40,576]{2,1,0:T(8,128)(2,1)S(1)}, bf16[8,40,576]{2,1,0:T(8,128)(2,1)S(1)}, u32[]{:S(2)}, u32[]{:S(2)}) collective-permute-start(bf16[8,40,576]{2,1,0:T(8,128)(2,1)S(1)} %maximum_select_fusion.10), channel_id=1, source_target_pairs={{0,2},{1,3},{2,0},{3,1},{4,6},{5,7},{6,4},{7,5},{8,10},{9,11},{10,... | collective-permute-start | bytes 1105928 | tf_op jit(solution)/shard_map/ppermute | solution.py:92
  166.1 8.9 %collective-permute-start.24 = (bf16[8,48,576]{2,1,0:T(8,128)(2,1)S(1)}, bf16[8,48,576]{2,1,0:T(8,128)(2,1)S(1)}, u32[]{:S(2)}, u32[]{:S(2)}) collective-permute-start(bf16[8,48,576]{2,1,0:T(8,128)(2,1)S(1)} %maximum_select_fusion.8), channel_id=1, source_target_pairs={{0,8},{8,0},{16,24},{24,16},{1,9},{9,1},{17,25},{25,17},{2,10},{10... | collective-permute-start | bytes 1327112 | tf_op jit(solution)/shard_map/ppermute | solution.py:92
  170.6 4.8 %collective-permute-start.30 = (bf16[16,40,576]{2,1,0:T(8,128)(2,1)S(1)}, bf16[16,40,576]{2,1,0:T(8,128)(2,1)}, u32[]{:S(2)}, u32[]{:S(2)}) collective-permute-start(bf16[16,40,576]{2,1,0:T(8,128)(2,1)S(1)} %maximum_select_fusion.4), channel_id=1, source_target_pairs={{0,1},{1,0},{2,3},{3,2},{4,5},{5,4},{6,7},{7,6},{8,9},{9,8},{10,11... | collective-permute-start | bytes 2211848 | tf_op jit(solution)/shard_map/ppermute | solution.py:92
  170.9 6.4 %collective-permute-start.35 = (bf16[16,40,576]{2,1,0:T(8,128)(2,1)S(1)}, bf16[16,40,576]{2,1,0:T(8,128)(2,1)}, u32[]{:S(2)}, u32[]{:S(2)}) collective-permute-start(bf16[16,40,576]{2,1,0:T(8,128)(2,1)S(1)} %maximum_select_fusion.5), channel_id=1, source_target_pairs={{0,1},{1,0},{2,3},{3,2},{4,5},{5,4},{6,7},{7,6},{8,9},{9,8},{10,11... | collective-permute-start | bytes 2211848 | tf_op jit(solution)/shard_map/ppermute | solution.py:92
  175.3 4.1 %collective-permute-start.25 = (bf16[16,48,576]{2,1,0:T(8,128)(2,1)S(1)}, bf16[16,48,576]{2,1,0:T(8,128)(2,1)}, u32[]{:S(2)}, u32[]{:S(2)}) collective-permute-start(bf16[16,48,576]{2,1,0:T(8,128)(2,1)S(1)} %maximum_select_fusion.3), channel_id=1, source_target_pairs={{0,1},{1,0},{2,3},{3,2},{4,5},{5,4},{6,7},{7,6},{8,9},{9,8},{10,11... | collective-permute-start | bytes 2654216 | tf_op jit(solution)/shard_map/ppermute | solution.py:92
  189.2 9.9 %copy-start.15 = (pred[256,1024]{1,0:T(8,128)(4,1)S(1)}, pred[256,1024]{1,0:T(8,128)(4,1)}, u32[]{:S(2)}) copy-start(pred[256,1024]{1,0:T(8,128)(4,1)} %copy-done.14) | copy-start | bytes 786436
  189.2 20.4 %slice-start = ((s8[4718592]{0:T(1024)(128)(4,1)}), s8[524288]{0:T(1024)(128)(4,1)S(1)}, s32[]{:S(2)}) async-start(s8[4718592]{0:T(1024)(128)(4,1)} %bitcast.149), calls=%async_computation | async-start | bytes 1048576
  199.1 10.5 %slice-start.1 = ((s8[4718592]{0:T(1024)(128)(4,1)}), s8[4194304]{0:T(1024)(128)(4,1)S(1)}, s32[]{:S(2)}) async-start(s8[4718592]{0:T(1024)(128)(4,1)} %bitcast.149), calls=%async_computation.1 | async-start | bytes 8388608
  218.2 5.2 %collective-permute-start.36 = (f32[4,64,576]{2,1,0:T(8,128)}, f32[4,64,576]{2,1,0:T(8,128)}, u32[]{:S(2)}, u32[]{:S(2)}) collective-permute-start(f32[4,64,576]{2,1,0:T(8,128)} %constant_dynamic-slice_fusion.5), channel_id=1, source_target_pairs={{0,1},{1,0},{2,3},{3,2},{4,5},{5,4},{6,7},{7,6},{8,9},{9,8},{10,11... | collective-permute-start | bytes 1769480 | tf_op jit(solution)/shard_map/ppermute | solution.py:70
  218.7 4.0 %copy-start.9 = (bf16[48,576]{1,0:T(8,128)(2,1)S(1)}, bf16[48,576]{1,0:T(8,128)(2,1)}, u32[]{:S(2)}) copy-start(bf16[48,576]{1,0:T(8,128)(2,1)} %copy-done.8) | copy-start | bytes 165892
  218.7 4.0 %copy-start.11 = (bf16[40,576]{1,0:T(8,128)(2,1)S(1)}, bf16[40,576]{1,0:T(8,128)(2,1)}, u32[]{:S(2)}) copy-start(bf16[40,576]{1,0:T(8,128)(2,1)} %copy-done.10) | copy-start | bytes 138244
  218.7 4.0 %copy-start.13 = (bf16[40,576]{1,0:T(8,128)(2,1)S(1)}, bf16[40,576]{1,0:T(8,128)(2,1)}, u32[]{:S(2)}) copy-start(bf16[40,576]{1,0:T(8,128)(2,1)} %copy-done.12) | copy-start | bytes 138244
  220.5 2.9 %copy-start.6 = (f32[2,2,2,64,576]{4,3,2,1,0:T(8,128)S(1)}, f32[2,2,2,64,576]{4,3,2,1,0:T(8,128)}, u32[]{:S(2)}) copy-start(f32[2,2,2,64,576]{4,3,2,1,0:T(8,128)} %copy.65) | copy-start | bytes 3538948
  220.5 5.9 %copy-start.5 = (f32[2,2,2,64,576]{4,3,2,1,0:T(8,128)S(1)}, f32[2,2,2,64,576]{4,3,2,1,0:T(8,128)}, u32[]{:S(2)}) copy-start(f32[2,2,2,64,576]{4,3,2,1,0:T(8,128)} %copy.66) | copy-start | bytes 3538948
  222.7 3.8 %collective-permute-start.39 = (f32[4,64,576]{2,1,0:T(8,128)}, f32[4,64,576]{2,1,0:T(8,128)S(1)}, u32[]{:S(2)}, u32[]{:S(2)}) collective-permute-start(f32[4,64,576]{2,1,0:T(8,128)} %constant_dynamic-slice_fusion.2), channel_id=1, source_target_pairs={{0,1},{1,0},{2,3},{3,2},{4,5},{5,4},{6,7},{7,6},{8,9},{9,8},{10,11... | collective-permute-start | bytes 1769480 | tf_op jit(solution)/shard_map/ppermute | solution.py:70
  224.6 10.2 %collective-permute-start.37 = (f32[2,64,576]{2,1,0:T(8,128)S(1)}, f32[2,64,576]{2,1,0:T(8,128)S(1)}, u32[]{:S(2)}, u32[]{:S(2)}) collective-permute-start(f32[2,64,576]{2,1,0:T(8,128)S(1)} %constant_dynamic-slice_fusion.4), channel_id=1, source_target_pairs={{0,4},{4,0},{1,5},{5,1},{2,6},{6,2},{3,7},{7,3},{8,12},{12,8},{9,1... | collective-permute-start | bytes 884744 | tf_op jit(solution)/shard_map/ppermute | solution.py:70
  226.5 16.4 %copy-start.1 = (s32[4,256,64]{1,2,0:T(8,128)S(1)}, s32[4,256,64]{1,2,0:T(8,128)}, u32[]{:S(2)}) copy-start(s32[4,256,64]{1,2,0:T(8,128)} %param.12) | copy-start | bytes 786436
  226.6 9.9 %collective-permute-start.40 = (f32[2,64,576]{2,1,0:T(8,128)S(1)}, f32[2,64,576]{2,1,0:T(8,128)S(1)}, u32[]{:S(2)}, u32[]{:S(2)}) collective-permute-start(f32[2,64,576]{2,1,0:T(8,128)S(1)} %constant_dynamic-slice_fusion.1), channel_id=1, source_target_pairs={{0,2},{1,3},{2,0},{3,1},{4,6},{5,7},{6,4},{7,5},{8,10},{9,11},{10,... | collective-permute-start | bytes 884744 | tf_op jit(solution)/shard_map/ppermute | solution.py:70
  234.9 5.9 %collective-permute-start.38 = (f32[1,64,576]{2,1,0:T(8,128)S(1)}, f32[1,64,576]{2,1,0:T(8,128)S(1)}, u32[]{:S(2)}, u32[]{:S(2)}) collective-permute-start(f32[1,64,576]{2,1,0:T(8,128)S(1)} %constant_dynamic-slice_fusion.3), channel_id=1, source_target_pairs={{0,2},{1,3},{2,0},{3,1},{4,6},{5,7},{6,4},{7,5},{8,10},{9,11},{10,... | collective-permute-start | bytes 442376 | tf_op jit(solution)/shard_map/ppermute | solution.py:70
  236.5 5.5 %collective-permute-start.41 = (f32[1,64,576]{2,1,0:T(8,128)S(1)}, f32[1,64,576]{2,1,0:T(8,128)S(1)}, u32[]{:S(2)}, u32[]{:S(2)}) collective-permute-start(f32[1,64,576]{2,1,0:T(8,128)S(1)} %constant_dynamic-slice_fusion), channel_id=1, source_target_pairs={{0,4},{4,0},{1,5},{5,1},{2,6},{6,2},{3,7},{7,3},{8,12},{12,8},{9,1... | collective-permute-start | bytes 442376 | tf_op jit(solution)/shard_map/ppermute | solution.py:70

commit v10 on v5

--- a/solution.py
+++ b/solution.py
@@ -49,50 +49,74 @@
     return [(sum(sizes[:i]), sizes[i]) for i in range(parts)]
 
 
+def halve(x, label, wire):
+    axis, bit = label
+    own = (lax.axis_index(axis) >> bit) & 1
+    half = x.shape[0] // 2
+    keep = lax.dynamic_slice_in_dim(x, own * half, half, 0)
+    send = lax.dynamic_slice_in_dim(x, (1 - own) * half, half, 0)
+    recv = lax.ppermute(send.astype(wire), axis, partner(axis, bit))
+    return keep + recv.astype(keep.dtype)
+
+
+def double(x, label):
+    axis, bit = label
+    own = (lax.axis_index(axis) >> bit) & 1
+    recv = lax.ppermute(x, axis, partner(axis, bit))
+    return jnp.where(own == 0, jnp.concatenate([x, recv]), jnp.concatenate([recv, x]))
+
+
 def reduce_scatter(blocks, axes, wire):
     labels, prefix, orders, suffix = plan(axes)
     n, rows, cols = blocks.shape
     nb = len(labels)
+    rest = [l for l in labels if l not in prefix]
     x = blocks.reshape([2] * nb + [rows, cols])
-    steps = [prefix + order + suffix for order in orders]
+    x = jnp.transpose(x, [labels.index(l) for l in prefix + rest] + [nb, nb + 1])
+    x = x.reshape(n, rows, cols)
+    for label in prefix:
+        x = halve(x, label, wire)
+    x = x.reshape([2] * len(rest) + [rows, cols])
     parts = []
-    for (start, size), order in zip(portion_rows(rows, len(orders)), steps):
-        xp = lax.slice_in_dim(x, start, start + size, axis=nb)
-        xp = jnp.transpose(xp, [labels.index(l) for l in order] + [nb, nb + 1])
-        parts.append(xp.reshape(n, size, cols))
-    for k in range(nb):
+    for (start, size), order in zip(portion_rows(rows, len(orders)), orders):
+        xp = lax.slice_in_dim(x, start, start + size, axis=len(rest))
+        xp = jnp.transpose(xp, [rest.index(l) for l in order + suffix] + [len(rest), len(rest) + 1])
+        parts.append(xp.reshape(-1, size, cols))
+    for k in range(len(orders[0])):
         for p in range(len(parts)):
-            axis, bit = steps[p][k]
-            own = (lax.axis_index(axis) >> bit) & 1
-            half = parts[p].shape[0] // 2
-            keep = lax.dynamic_slice_in_dim(parts[p], own * half, half, 0)
-            send = lax.dynamic_slice_in_dim(parts[p], (1 - own) * half, half, 0)
-            recv = lax.ppermute(send.astype(wire), axis, partner(axis, bit))
-            parts[p] = keep + recv.astype(keep.dtype)
-    return jnp.concatenate([xp[0] for xp in parts], axis=0)
+            parts[p] = halve(parts[p], orders[p][k], wire)
+    x = jnp.concatenate(parts, axis=1)
+    for label in suffix:
+        x = halve(x, label, wire)
+    return x[0]
 
 
 def all_gather(block, axes):
     labels, prefix, orders, suffix = plan(axes)
     rows, cols = block.shape
     nb = len(labels)
-    steps = [prefix + order + suffix for order in orders]
+    rest = [l for l in labels if l not in prefix]
+    x = block[None]
+    for label in reversed(suffix):
+        x = double(x, label)
     spans = portion_rows(rows, len(orders))
-    parts = [lax.slice_in_dim(block, start, start + size, axis=0)[None] for start, size in spans]
-    for k in reversed(range(nb)):
+    parts = [lax.slice_in_dim(x, start, start + size, axis=1) for start, size in spans]
+    for k in reversed(range(len(orders[0]))):
         for p in range(len(parts)):
-            axis, bit = steps[p][k]
-            own = (lax.axis_index(axis) >> bit) & 1
-            recv = lax.ppermute(parts[p], axis, partner(axis, bit))
-            parts[p] = jnp.where(
-                own == 0, jnp.concatenate([parts[p], recv]), jnp.concatenate([recv, parts[p]])
-            )
+            parts[p] = double(parts[p], orders[p][k])
     out = []
-    for xp, order, (start, size) in zip(parts, steps, spans):
-        xp = xp.reshape([2] * nb + [size, cols])
-        xp = jnp.transpose(xp, [order.index(l) for l in labels] + [nb, nb + 1])
+    for xp, order, (start, size) in zip(parts, orders, spans):
+        xp = xp.reshape([2] * len(rest) + [size, cols])
+        have = order + suffix
+        xp = jnp.transpose(xp, [have.index(l) for l in rest] + [len(rest), len(rest) + 1])
         out.append(xp.reshape(-1, size, cols))
-    return jnp.concatenate(out, axis=1)
+    x = jnp.concatenate(out, axis=1)
+    for label in reversed(prefix):
+        x = double(x, label)
+    x = x.reshape([2] * nb + [rows, cols])
+    have = prefix + rest
+    x = jnp.transpose(x, [have.index(l) for l in labels] + [nb, nb + 1])
+    return x.reshape(-1, rows, cols)
 
 
 def local(resid, encoder, encoder_bias, decoder, decoder_bias, topk_index, target):
@@ -131,7 +155,7 @@
         .transpose(1, 3, 0, 2, 4)
         .reshape(slots * feat_parts, layer_count * slot_rows, cols)
     )
-    recon = reduce_scatter(blocks, EVERY, jnp.bfloat16).reshape(layer_count, slot_rows, cols)
+    recon = reduce_scatter(blocks, EVERY, jnp.float32).reshape(layer_count, slot_rows, cols)
     recon = recon + decoder_bias[:, None, :]
     error = (recon - target.astype(jnp.float32)).astype(jnp.bfloat16)
     pieces = all_gather(error.reshape(layer_count * slot_rows, cols), EVERY)
@@ -151,7 +175,7 @@
         .transpose(0, 2, 1, 3)
         .reshape(2 * feat_parts, half_rows, cols)
     )
-    grad_sum = reduce_scatter(grad_blocks, PLANE, jnp.bfloat16)
+    grad_sum = reduce_scatter(grad_blocks, PLANE, jnp.float32)
     return (error, grad_sum.astype(jnp.bfloat16)[None])
 
 

time: 211 us -> 288 us (1.36)
  waiting for transfers between devices: 42.6 us -> 107 us
  local copies, waits for them, and re-layouts: 55.9 us -> 94.8 us
  starting transfers between devices: 55.7 us -> 33.6 us
  matrix products: 29.6 us -> 23.2 us
    ppermute x42 -> x32, waiting for transfers between devices: 42.6 us -> 107 us  [the longest x16 66.4 us: halve(): recv = lax.ppermute(send.astype(wire), axis, partner(axis, bit))]
    transpose x13 -> x11, local copies, waits for them, and re-layouts: 9.61 us -> 34.6 us  [the longest x6 23.4 us: reduce_scatter(): jnp.transpose(xp, [rest.index(l) for l in order + suffix] + [len(rest), l...]
    ppermute x42 -> x32, starting transfers between devices: 55.7 us -> 33.6 us  [the longest x16 18.9 us: halve(): recv = lax.ppermute(send.astype(wire), axis, partner(axis, bit))]
    dynamic_slice x0 -> x16, local copies, waits for them, and re-layouts: none -> 9.6 us  [halve(): send = lax.dynamic_slice_in_dim(x, (1 - own) * half, half, 0)]
    dot_general x1, matrix products: 13.9 us -> 7.41 us  [local(): jnp.einsum('tf,lfd->ltd', acts, decoder[0], preferred_element_type=jnp.fl...]
    convert_element_type x21 -> x0, local copies, waits for them, and re-layouts: 6.03 us -> none  [reduce_scatter(): recv = lax.ppermute(send.astype(wire), axis, partner(axis, bit))]
    reshape x2, local copies, waits for them, and re-layouts: 18.7 us -> 22.5 us  [local(): partial_value.reshape(layer_count, slots, slot_rows, feat_parts, cols)]
    ppermute x0 -> x1, local copies, waits for them, and re-layouts: none -> 3.08 us  [double(): recv = lax.ppermute(x, axis, partner(axis, bit))]
  transfers between devices with their start and end apart: 42 -> 32, of which waited for: 21 -> 25; matrix products, arithmetic and copies ran while one was open for 14% -> 11% of each run, Pallas kernels for 0% -> 0%
where the time goes in v10:
time: 288 us; the launch traced here: 287 us
  waiting for transfers between devices  107 us (37%)
  local copies, waits for them, and re-layouts  94.8 us (33%)
  starting transfers between devices  33.6 us (12%)
  other arithmetic  27.2 us (9%)
  matrix products  23.2 us (8%)
    ppermute x16, waiting for transfers between devices, halve(): recv = lax.ppermute(send.astype(wire), axis, partner(axis, bit))  66.4 us
    ppermute x16, waiting for transfers between devices, double(): recv = lax.ppermute(x, axis, partner(axis, bit))  40.6 us
    transpose x6, local copies, waits for them, and re-layouts, reduce_scatter(): jnp.transpose(xp, [rest.index(l) for l in order + suffix] + [len(rest), l...  23.4 us
    reshape x2, local copies, waits for them, and re-layouts, local(): partial_value.reshape(layer_count, slots, slot_rows, feat_parts, cols)  22.5 us
    ppermute x16, starting transfers between devices, halve(): recv = lax.ppermute(send.astype(wire), axis, partner(axis, bit))  18.9 us
    ppermute x16, starting transfers between devices, double(): recv = lax.ppermute(x, axis, partner(axis, bit))  14.7 us
    transpose x1, local copies, waits for them, and re-layouts, reduce_scatter(): jnp.transpose(x, [labels.index(l) for l in prefix + rest] + [nb, nb + 1])  11 us
    dot_general x1, matrix products, local(): jnp.einsum('ltd,lfd->tf', kept, decoder[0], preferred_element_type=jnp.fl...  10.5 us
  transfers between devices with their start and end apart: 32, of which 25 were waited for; matrix products, arithmetic and copies ran while one was open for 11% of the time, Pallas kernels for 0%

profile of v10, /device:TPU:0, one launch (start us, length us, event | category | flops | bytes accessed | tf_op | source)
XLA Modules:
  0.0 287.1 jit_solution(15028729813459348220)
XLA Ops:
  0.6 1.1 fusion.43
  1.8 3.1 %collective-permute-start = (bf16[1,64,576]{1,2,0:T(8,128)(2,1)S(1)}, bf16[1,64,576]{1,2,0:T(8,128)(2,1)S(1)}, u32[]{:S(2)}, u32[]{:S(2)}) collective-permute-start(bf16[1,64,576]{1,2,0:T(8,128)(2,1)S(1)} %get-tuple-element.16), channel_id=1, source_target_pairs={{0,2},{1,3},{2,0},{3,1},{4,6},{5,7},{6,4},{7,5},{8,10},{9,11},{10,... | collective-permute-start | bytes 221192 | tf_op jit(solution)/shard_map/ppermute | solution.py:65
  4.8 1.5 collective-permute-start.2
  6.4 3.8 %collective-permute-done.2 = bf16[1,64,576]{1,2,0:T(8,128)(2,1)S(1)} collective-permute-done((bf16[1,64,576]{1,2,0:T(8,128)(2,1)S(1)}, bf16[1,64,576]{1,2,0:T(8,128)(2,1)S(1)}, u32[]{:S(2)}, u32[]{:S(2)}) %collective-permute-start.2) | collective-permute-done | bytes 73760 | tf_op jit(solution)/shard_map/ppermute | solution.py:65
  10.8 1.7 collective-permute-start.1
  12.6 5.3 %collective-permute-done.3 = bf16[2,64,576]{1,2,0:T(8,128)(2,1)S(1)} collective-permute-done((bf16[2,64,576]{1,2,0:T(8,128)(2,1)S(1)}, bf16[2,64,576]{1,2,0:T(8,128)(2,1)S(1)}, u32[]{:S(2)}, u32[]{:S(2)}) %collective-permute-start.3) | collective-permute-done | bytes 147488 | tf_op jit(solution)/shard_map/ppermute | solution.py:65
  19.2 9.4 %compare_reduce_fusion = pred[256,1024]{1,0:T(8,128)(4,1)S(1)} fusion(s32[1024]{0:T(1024)S(1)} %iota_add_fusion, s32[256,64]{1,0:T(8,128)S(1)} %copy.61), kind=kLoop, calls=%fused_computation | loop fusion | flops 33292288 | bytes 331776 | tf_op jit(solution)/shard_map/reduce_or | solution.py:146
  29.3 1.2 copy.64
  30.5 3.8 %fusion.35 = bf16[256,1024,1]{1,0,2:T(8,128)(2,1)S(1)} fusion(pred[256,1024]{1,0:T(8,128)(4,1)S(1)} %compare_reduce_fusion, bf16[1,2304,1024]{2,1,0:T(8,128)(2,1)} %param.8, bf16[288,8,2,128]{3,2,1,0:T(2,128)(2,1)S(1)} %bitcast.147, f32[1024]{0:T(1024)S(1)} %bitcast.153), kind=kOutput, calls=%fused_computation.23 | convolution fusion | flops 1208745984 | bytes 6688768 | tf_op jit(solution)/shard_map/dot_general | solution.py:142
  34.3 7.4 %select_bitcast_fusion = f32[4,256,2304]{2,1,0:T(8,128)} fusion(bf16[256,1024,1]{1,0,2:T(8,128)(2,1)S(1)} %fusion.35, bf16[1,4,1024,2304]{3,2,1,0:T(8,128)(2,1)S(1)} %copy-done.11, pred[4]{0:T(512)(128)(4,1)S(1)} %iota_compare_fusion), kind=kOutput, calls=%fused_computation.5 | convolution fusion | flops 4834197504 | bytes 28835844 | tf_op jit(solution)/shard_map/tf,lfd->ltd/dot_general | solution.py:151
  41.7 13.2 %reshape.120 = f32[4,8,32,4,576]{4,3,2,1,0:T(4,128)} reshape(f32[4,256,2304]{2,1,0:T(8,128)} %select_bitcast_fusion) | data formatting | bytes 18874368 | tf_op jit(solution)/shard_map/reshape | solution.py:154
  54.9 9.3 %copy.65 = f32[4,8,32,4,576]{4,2,0,3,1:T(8,128)} copy(f32[4,8,32,4,576]{4,3,2,1,0:T(4,128)} %reshape.120) | data formatting | bytes 18874368 | tf_op jit(solution)/shard_map/reshape | solution.py:154
  64.2 11.0 %copy.66 = f32[2,2,2,2,2,128,576]{5,6,4,3,2,1,0:T(8,128)} copy(f32[2,2,2,2,2,128,576]{6,5,0,4,3,2,1:T(8,128)} %bitcast.114) | data formatting | bytes 18874368 | tf_op jit(solution)/shard_map/transpose | solution.py:75
  75.2 4.9 %constant_dynamic-slice_fusion.16 = f32[16,128,576]{1,2,0:T(8,128)} fusion(f32[32,128,576]{1,2,0:T(8,128)} %bitcast.115, s32[]{:T(128)S(6)} %select_n.261), kind=kLoop, calls=%fused_computation.77 | loop fusion | bytes 9437188 | tf_op jit(solution)/shard_map/dynamic_slice | solution.py:57
  80.6 7.9 %collective-permute-done.5 = f32[16,128,576]{1,2,0:T(8,128)} collective-permute-done((f32[16,128,576]{1,2,0:T(8,128)}, f32[16,128,576]{1,2,0:T(8,128)}, u32[]{:S(2)}, u32[]{:S(2)}) %collective-permute-start.5) | collective-permute-done | bytes 4718624 | tf_op jit(solution)/shard_map/ppermute | solution.py:58
  88.4 4.3 %dynamic-slice_add_fusion = f32[16,128,576]{1,2,0:T(8,128)S(1)} fusion(f32[16,128,576]{1,2,0:T(8,128)} %collective-permute-done.5, f32[32,128,576]{1,2,0:T(8,128)} %bitcast.116, s32[]{:T(128)S(6)} %select_n.260), kind=kLoop, calls=%fused_computation.13 | loop fusion | flops 1179648 | bytes 14155780 | tf_op jit(solution)/shard_map/add | solution.py:59
  92.8 6.1 %slice_bitcast_fusion.1 = (f32[2,2,2,2,40,576]{4,5,1,0,2,3:T(8,128)}, f32[2,2,2,2,40,576]{4,5,0,2,1,3:T(8,128)}) fusion(f32[2,2,2,2,128,576]{4,5,3,2,1,0:T(8,128)S(1)} %bitcast.112), kind=kLoop, calls=%fused_computation.8 | loop fusion | bytes 5898240 | tf_op jit(solution)/shard_map/transpose | solution.py:83
  98.9 3.9 %copy.68 = f32[2,2,2,2,40,576]{5,4,3,2,1,0:T(8,128)S(1)} copy(f32[2,2,2,2,40,576]{4,5,1,0,2,3:T(8,128)} %get-tuple-element.8) | data formatting | bytes 2949120 | tf_op jit(solution)/shard_map/transpose | solution.py:83
  102.8 1.1 constant_dynamic-slice_fusion.12
  103.9 1.4 collective-permute-start.9
  105.2 4.1 %copy.69 = f32[2,2,2,2,40,576]{5,4,3,2,1,0:T(8,128)S(1)} copy(f32[2,2,2,2,40,576]{4,5,0,2,1,3:T(8,128)} %get-tuple-element.9) | data formatting | bytes 2949120 | tf_op jit(solution)/shard_map/transpose | solution.py:83
  110.4 1.5 collective-permute-start.12
  111.9 5.0 %slice_bitcast_fusion.2 = f32[2,2,2,2,48,576]{4,5,2,1,0,3:T(8,128)} fusion(f32[2,2,2,2,128,576]{4,5,3,2,1,0:T(8,128)} %bitcast.113), kind=kLoop, calls=%fused_computation.9 | loop fusion | bytes 3538944 | tf_op jit(solution)/shard_map/transpose | solution.py:83
  116.9 3.9 %copy.67 = f32[2,2,2,2,48,576]{5,4,3,2,1,0:T(8,128)S(1)} copy(f32[2,2,2,2,48,576]{4,5,2,1,0,3:T(8,128)} %slice_bitcast_fusion.2) | data formatting | bytes 3538944 | tf_op jit(solution)/shard_map/transpose | solution.py:83
  120.8 1.1 constant_dynamic-slice_fusion.15
  121.9 1.6 collective-permute-start.6
  123.4 1.3 collective-permute-done.9
  124.7 1.5 dynamic-slice_add_fusion.4
  126.2 1.5 collective-permute-start.10
  127.7 4.1 %collective-permute-done.12 = f32[8,40,576]{2,1,0:T(8,128)} collective-permute-done((f32[8,40,576]{2,1,0:T(8,128)}, f32[8,40,576]{2,1,0:T(8,128)}, u32[]{:S(2)}, u32[]{:S(2)}) %collective-permute-start.12) | collective-permute-done | bytes 737312 | tf_op jit(solution)/shard_map/ppermute | solution.py:58
  131.8 1.5 dynamic-slice_add_fusion.3
  133.3 1.6 collective-permute-start.13
  135.0 11.7 %collective-permute-done.6 = f32[8,48,576]{2,1,0:T(8,128)S(1)} collective-permute-done((f32[8,48,576]{2,1,0:T(8,128)}, f32[8,48,576]{2,1,0:T(8,128)S(1)}, u32[]{:S(2)}, u32[]{:S(2)}) %collective-permute-start.6) | collective-permute-done | bytes 884768 | tf_op jit(solution)/shard_map/ppermute | solution.py:58
  147.6 1.6 collective-permute-start.11
  149.2 6.3 %collective-permute-done.13 = f32[4,40,576]{2,1,0:T(8,128)S(1)} collective-permute-done((f32[4,40,576]{2,1,0:T(8,128)S(1)}, f32[4,40,576]{2,1,0:T(8,128)S(1)}, u32[]{:S(2)}, u32[]{:S(2)}) %collective-permute-start.13) | collective-permute-done | bytes 368672 | tf_op jit(solution)/shard_map/ppermute | solution.py:58
  156.2 2.6 collective-permute-done.11
  160.8 1.5 collective-permute-done.14
  162.3 3.8 %collective-permute-done.8 = f32[2,48,576]{2,1,0:T(8,128)S(1)} collective-permute-done((f32[2,48,576]{2,1,0:T(8,128)S(1)}, f32[2,48,576]{2,1,0:T(8,128)S(1)}, u32[]{:S(2)}, u32[]{:S(2)}) %collective-permute-start.8) | collective-permute-done | bytes 221216 | tf_op jit(solution)/shard_map/ppermute | solution.py:58
  166.2 2.7 collective-permute-start.15
  168.8 11.8 %collective-permute-done.15 = f32[1,128,576]{2,1,0:T(8,128)S(1)} collective-permute-done((f32[1,128,576]{2,1,0:T(8,128)S(1)}, f32[1,128,576]{2,1,0:T(8,128)S(1)}, u32[]{:S(2)}, u32[]{:S(2)}) %collective-permute-start.15) | collective-permute-done | bytes 294944 | tf_op jit(solution)/shard_map/ppermute | solution.py:58
  180.9 9.5 %collective-permute-done.16 = bf16[1,128,576]{2,1,0:T(8,128)(2,1)S(1)} collective-permute-done((bf16[1,128,576]{2,1,0:T(8,128)(2,1)S(1)}, bf16[1,128,576]{2,1,0:T(8,128)(2,1)S(1)}, u32[]{:S(2)}, u32[]{:S(2)}) %collective-permute-start.16) | collective-permute-done | bytes 147488 | tf_op jit(solution)/shard_map/ppermute | solution.py:65
  192.2 3.0 %collective-permute-done.20 = bf16[2,40,576]{2,1,0:T(8,128)(2,1)S(1)} collective-permute-done((bf16[2,40,576]{2,1,0:T(8,128)(2,1)S(1)}, bf16[2,40,576]{2,1,0:T(8,128)(2,1)S(1)}, u32[]{:S(2)}, u32[]{:S(2)}) %collective-permute-start.20) | collective-permute-done | bytes 92192 | tf_op jit(solution)/shard_map/ppermute | solution.py:65
  196.3 2.1 collective-permute-start.24
  199.1 2.0 collective-permute-done.21
  202.3 1.2 collective-permute-start.25
  203.5 3.9 %collective-permute-done.18 = bf16[4,48,576]{2,1,0:T(8,128)(2,1)S(1)} collective-permute-done((bf16[4,48,576]{2,1,0:T(8,128)(2,1)S(1)}, bf16[4,48,576]{2,1,0:T(8,128)(2,1)S(1)}, u32[]{:S(2)}, u32[]{:S(2)}) %collective-permute-start.18) | collective-permute-done | bytes 221216 | tf_op jit(solution)/shard_map/ppermute | solution.py:65
  208.0 4.0 %collective-permute-done.22 = bf16[8,40,576]{2,1,0:T(8,128)(2,1)S(1)} collective-permute-done((bf16[8,40,576]{2,1,0:T(8,128)(2,1)S(1)}, bf16[8,40,576]{2,1,0:T(8,128)(2,1)S(1)}, u32[]{:S(2)}, u32[]{:S(2)}) %collective-permute-start.22) | collective-permute-done | bytes 368672 | tf_op jit(solution)/shard_map/ppermute | solution.py:65
  212.6 3.8 %collective-permute-done.19 = bf16[8,48,576]{2,1,0:T(8,128)(2,1)S(1)} collective-permute-done((bf16[8,48,576]{2,1,0:T(8,128)(2,1)S(1)}, bf16[8,48,576]{2,1,0:T(8,128)(2,1)S(1)}, u32[]{:S(2)}, u32[]{:S(2)}) %collective-permute-start.19) | collective-permute-done | bytes 442400 | tf_op jit(solution)/shard_map/ppermute | solution.py:65
  218.1 2.6 copy.73
  220.7 4.9 %collective-permute-done.26 = bf16[16,128,576]{1,2,0:T(8,128)(2,1)} collective-permute-done((bf16[16,128,576]{1,2,0:T(8,128)(2,1)}, bf16[16,128,576]{1,2,0:T(8,128)(2,1)}, u32[]{:S(2)}, u32[]{:S(2)}) %collective-permute-start.26) | collective-permute-done | bytes 2359328 | tf_op jit(solution)/shard_map/ppermute | solution.py:65
  225.5 3.1 %copy.74 = bf16[16,128,576]{2,1,0:T(8,128)(2,1)S(1)} copy(bf16[16,128,576]{1,2,0:T(8,128)(2,1)} %collective-permute-done.26) | data formatting | bytes 4718592 | tf_op jit(solution)/shard_map/ppermute | solution.py:65
  228.6 5.3 %maximum_select_fusion = bf16[32,128,576]{2,1,0:T(8,128)(2,1)S(1)} fusion(bf16[16,128,576]{2,1,0:T(8,128)(2,1)S(1)} %copy.74, bf16[16,40,576]{2,1,0:T(8,128)(2,1)} %bitcast.129, bf16[16,40,576]{2,1,0:T(8,128)(2,1)} %bitcast.127, bf16[16,48,576]{2,1,0:T(8,128)(2,1)} %bitcast.123, pred[]{:T(512)S(6)} %eq.22), kind=kLoop, calls=%fused_computation.6 | loop fusion | flops 40108032 | bytes 9437185 | tf_op jit(solution)/shard_map/jit(_where)/select_n | solution.py:66
  234.8 6.4 %copy.77 = bf16[4,8,32,4,576]{4,3,2,1,0:T(4,128)(2,1)} copy(bf16[4,8,32,4,576]{4,2,0,3,1:T(8,128)(2,1)S(1)} %bitcast.118) | data formatting | bytes 9437184 | tf_op jit(solution)/shard_map/transpose | solution.py:164
  241.2 9.9 %reshape.129 = bf16[4,256,2304]{2,1,0:T(8,128)(2,1)} reshape(bf16[4,8,32,4,576]{4,3,2,1,0:T(4,128)(2,1)} %copy.77) | data formatting | bytes 9437184 | tf_op jit(solution)/shard_map/reshape | solution.py:165
  251.1 10.5 %fusion.30 = bf16[256,1024]{1,0:T(8,128)(2,1)S(1)} fusion(pred[256,1024]{1,0:T(8,128)(4,1)S(1)} %compare_reduce_fusion, bf16[1,4,1024,2304]{3,2,1,0:T(8,128)(2,1)} %param.10, bf16[4,256,2304]{2,1,0:T(8,128)(2,1)} %reshape.129, pred[4]{0:T(512)(128)(4,1)S(1)} %iota_compare_fusion), kind=kOutput, calls=%fused_computation.22 | convolution fusion | flops 4834721792 | bytes 24379396 | tf_op jit(solution)/shard_map/ltd,lfd->tf/dot_general | solution.py:168
  261.6 1.5 fusion.44
  263.3 1.1 constant_dynamic-slice_fusion.5
  264.6 3.1 %collective-permute-done.27 = f32[4,128,576]{1,2,0:T(8,128)} collective-permute-done((f32[4,128,576]{1,2,0:T(8,128)}, f32[4,128,576]{1,2,0:T(8,128)}, u32[]{:S(2)}, u32[]{:S(2)}) %collective-permute-start.27) | collective-permute-done | bytes 1179680 | tf_op jit(solution)/shard_map/ppermute | solution.py:58
  267.6 1.4 dynamic-slice_add_fusion.1
  270.8 1.3 collective-permute-start.30
  272.3 7.2 %collective-permute-done.28 = f32[2,64,576]{2,1,0:T(8,128)S(1)} collective-permute-done((f32[2,64,576]{2,1,0:T(8,128)S(1)}, f32[2,64,576]{2,1,0:T(8,128)S(1)}, u32[]{:S(2)}, u32[]{:S(2)}) %collective-permute-start.28) | collective-permute-done | bytes 294944 | tf_op jit(solution)/shard_map/ppermute | solution.py:58
  279.6 1.2 collective-permute-start.29
  281.9 3.1 %collective-permute-done.29 = f32[1,64,576]{2,1,0:T(8,128)S(1)} collective-permute-done((f32[1,64,576]{2,1,0:T(8,128)S(1)}, f32[1,64,576]{2,1,0:T(8,128)S(1)}, u32[]{:S(2)}, u32[]{:S(2)}) %collective-permute-start.29) | collective-permute-done | bytes 147488 | tf_op jit(solution)/shard_map/ppermute | solution.py:58
  285.1 1.2 collective-permute-done.31
  (121 shorter events, 20.7 us)
Async XLA Ops:
  0.6 5.7 %copy-start = (s32[4,256,64]{1,2,0:T(8,128)S(1)}, s32[4,256,64]{1,2,0:T(8,128)}, u32[]{:S(2)}) copy-start(s32[4,256,64]{1,2,0:T(8,128)} %param.12) | copy-start | bytes 786436
  1.8 8.9 %collective-permute-start = (bf16[1,64,576]{1,2,0:T(8,128)(2,1)S(1)}, bf16[1,64,576]{1,2,0:T(8,128)(2,1)S(1)}, u32[]{:S(2)}, u32[]{:S(2)}) collective-permute-start(bf16[1,64,576]{1,2,0:T(8,128)(2,1)S(1)} %get-tuple-element.16), channel_id=1, source_target_pairs={{0,2},{1,3},{2,0},{3,1},{4,6},{5,7},{6,4},{7,5},{8,10},{9,11},{10,... | collective-permute-start | bytes 221192 | tf_op jit(solution)/shard_map/ppermute | solution.py:65
  4.8 5.3 %collective-permute-start.2 = (bf16[1,64,576]{1,2,0:T(8,128)(2,1)S(1)}, bf16[1,64,576]{1,2,0:T(8,128)(2,1)S(1)}, u32[]{:S(2)}, u32[]{:S(2)}) collective-permute-start(bf16[1,64,576]{1,2,0:T(8,128)(2,1)S(1)} %get-tuple-element.17), channel_id=1, source_target_pairs={{0,4},{4,0},{1,5},{5,1},{2,6},{6,2},{3,7},{7,3},{8,12},{12,8},{9,1... | collective-permute-start | bytes 221192 | tf_op jit(solution)/shard_map/ppermute | solution.py:65
  10.3 7.7 %collective-permute-start.3 = (bf16[2,64,576]{1,2,0:T(8,128)(2,1)S(1)}, bf16[2,64,576]{1,2,0:T(8,128)(2,1)S(1)}, u32[]{:S(2)}, u32[]{:S(2)}) collective-permute-start(bf16[2,64,576]{1,2,0:T(8,128)(2,1)S(1)} %maximum_select_fusion.12), channel_id=1, source_target_pairs={{0,2},{1,3},{2,0},{3,1},{4,6},{5,7},{6,4},{7,5},{8,10},{9,11},{10,... | collective-permute-start | bytes 442376 | tf_op jit(solution)/shard_map/ppermute | solution.py:65
  10.8 7.7 %collective-permute-start.1 = (bf16[2,64,576]{1,2,0:T(8,128)(2,1)S(1)}, bf16[2,64,576]{1,2,0:T(8,128)(2,1)S(1)}, u32[]{:S(2)}, u32[]{:S(2)}) collective-permute-start(bf16[2,64,576]{1,2,0:T(8,128)(2,1)S(1)} %maximum_select_fusion.11), channel_id=1, source_target_pairs={{0,4},{4,0},{1,5},{5,1},{2,6},{6,2},{3,7},{7,3},{8,12},{12,8},{9,1... | collective-permute-start | bytes 442376 | tf_op jit(solution)/shard_map/ppermute | solution.py:65
  18.7 11.8 %copy-start.12 = (f32[1,1024]{1,0:T(1,128)S(1)}, f32[1,1024]{1,0:T(1,128)}, u32[]{:S(2)}) copy-start(f32[1,1024]{1,0:T(1,128)} %param.9) | copy-start | bytes 12292
  18.7 15.6 %copy-start.11 = (bf16[1,4,1024,2304]{3,2,1,0:T(8,128)(2,1)S(1)}, bf16[1,4,1024,2304]{3,2,1,0:T(8,128)(2,1)}, u32[]{:S(2)}) copy-start(bf16[1,4,1024,2304]{3,2,1,0:T(8,128)(2,1)} %param.10) | copy-start | bytes 56623108
  19.1 9.5 %collective-permute-start.4 = (bf16[4,128,576]{1,2,0:T(8,128)(2,1)S(1)}, bf16[4,128,576]{1,2,0:T(8,128)(2,1)S(1)}, u32[]{:S(2)}, u32[]{:S(2)}) collective-permute-start(bf16[4,128,576]{1,2,0:T(8,128)(2,1)S(1)} %pad_maximum_fusion.2), channel_id=1, source_target_pairs={{0,1},{1,0},{2,3},{3,2},{4,5},{5,4},{6,7},{7,6},{8,9},{9,8},{10,11... | collective-permute-start | bytes 1769480 | tf_op jit(solution)/shard_map/ppermute | solution.py:65
  80.1 8.4 %collective-permute-start.5 = (f32[16,128,576]{1,2,0:T(8,128)}, f32[16,128,576]{1,2,0:T(8,128)}, u32[]{:S(2)}, u32[]{:S(2)}) collective-permute-start(f32[16,128,576]{1,2,0:T(8,128)} %constant_dynamic-slice_fusion.16), channel_id=1, source_target_pairs={{0,1},{1,0},{2,3},{3,2},{4,5},{5,4},{6,7},{7,6},{8,9},{9,8},{10,11... | collective-permute-start | bytes 14155784 | tf_op jit(solution)/shard_map/ppermute | solution.py:58
  92.8 6.1 %copy-start.2 = (f32[16,128,576]{1,2,0:T(8,128)}, f32[16,128,576]{1,2,0:T(8,128)S(1)}, u32[]{:S(2)}) copy-start(f32[16,128,576]{1,2,0:T(8,128)S(1)} %dynamic-slice_add_fusion) | copy-start | bytes 14155780
  102.8 2.5 copy-start.7
  103.9 20.8 %collective-permute-start.9 = (f32[8,40,576]{2,1,0:T(8,128)}, f32[8,40,576]{2,1,0:T(8,128)}, u32[]{:S(2)}, u32[]{:S(2)}) collective-permute-start(f32[8,40,576]{2,1,0:T(8,128)} %constant_dynamic-slice_fusion.12), channel_id=1, source_target_pairs={{0,4},{4,0},{1,5},{5,1},{2,6},{6,2},{3,7},{7,3},{8,12},{12,8},{9,1... | collective-permute-start | bytes 2211848 | tf_op jit(solution)/shard_map/ppermute | solution.py:58
  109.3 2.6 copy-start.6
  110.4 21.4 %collective-permute-start.12 = (f32[8,40,576]{2,1,0:T(8,128)}, f32[8,40,576]{2,1,0:T(8,128)}, u32[]{:S(2)}, u32[]{:S(2)}) collective-permute-start(f32[8,40,576]{2,1,0:T(8,128)} %constant_dynamic-slice_fusion.9), channel_id=1, source_target_pairs={{0,2},{1,3},{2,0},{3,1},{4,6},{5,7},{6,4},{7,5},{8,10},{9,11},{10,... | collective-permute-start | bytes 2211848 | tf_op jit(solution)/shard_map/ppermute | solution.py:58
  121.9 24.8 %collective-permute-start.6 = (f32[8,48,576]{2,1,0:T(8,128)}, f32[8,48,576]{2,1,0:T(8,128)S(1)}, u32[]{:S(2)}, u32[]{:S(2)}) collective-permute-start(f32[8,48,576]{2,1,0:T(8,128)} %constant_dynamic-slice_fusion.15), channel_id=1, source_target_pairs={{0,8},{8,0},{16,24},{24,16},{1,9},{9,1},{17,25},{25,17},{2,10},{10... | collective-permute-start | bytes 2654216 | tf_op jit(solution)/shard_map/ppermute | solution.py:58
  126.2 21.2 %collective-permute-start.10 = (f32[4,40,576]{2,1,0:T(8,128)S(1)}, f32[4,40,576]{2,1,0:T(8,128)S(1)}, u32[]{:S(2)}, u32[]{:S(2)}) collective-permute-start(f32[4,40,576]{2,1,0:T(8,128)S(1)} %constant_dynamic-slice_fusion.11), channel_id=1, source_target_pairs={{0,2},{1,3},{2,0},{3,1},{4,6},{5,7},{6,4},{7,5},{8,10},{9,11},{10,... | collective-permute-start | bytes 1105928 | tf_op jit(solution)/shard_map/ppermute | solution.py:58
  133.3 22.2 %collective-permute-start.13 = (f32[4,40,576]{2,1,0:T(8,128)S(1)}, f32[4,40,576]{2,1,0:T(8,128)S(1)}, u32[]{:S(2)}, u32[]{:S(2)}) collective-permute-start(f32[4,40,576]{2,1,0:T(8,128)S(1)} %constant_dynamic-slice_fusion.8), channel_id=1, source_target_pairs={{0,8},{8,0},{16,24},{24,16},{1,9},{9,1},{17,25},{25,17},{2,10},{10... | collective-permute-start | bytes 1105928 | tf_op jit(solution)/shard_map/ppermute | solution.py:58
  146.9 12.8 %collective-permute-start.7 = (f32[4,48,576]{2,1,0:T(8,128)S(1)}, f32[4,48,576]{2,1,0:T(8,128)S(1)}, u32[]{:S(2)}, u32[]{:S(2)}) collective-permute-start(f32[4,48,576]{2,1,0:T(8,128)S(1)} %constant_dynamic-slice_fusion.14), channel_id=1, source_target_pairs={{0,4},{4,0},{1,5},{5,1},{2,6},{6,2},{3,7},{7,3},{8,12},{12,8},{9,1... | collective-permute-start | bytes 1327112 | tf_op jit(solution)/shard_map/ppermute | solution.py:58
  147.5 33.2 %copy-start.9 = (bf16[4,32,576]{2,1,0:T(8,128)(2,1)S(1)}, bf16[4,32,576]{2,1,0:T(8,128)(2,1)}, u32[]{:S(2)}) copy-start(bf16[4,32,576]{2,1,0:T(8,128)(2,1)} %param.13) | copy-start | bytes 442372
  147.5 33.2 %copy-start.10 = (f32[4,576]{1,0:T(4,128)S(1)}, f32[4,576]{1,0:T(4,128)}, u32[]{:S(2)}) copy-start(f32[4,576]{1,0:T(4,128)} %param.11) | copy-start | bytes 27652
  147.6 11.1 %collective-permute-start.11 = (f32[2,40,576]{2,1,0:T(8,128)S(1)}, f32[2,40,576]{2,1,0:T(8,128)S(1)}, u32[]{:S(2)}, u32[]{:S(2)}) collective-permute-start(f32[2,40,576]{2,1,0:T(8,128)S(1)} %constant_dynamic-slice_fusion.10), channel_id=1, source_target_pairs={{0,8},{8,0},{16,24},{24,16},{1,9},{9,1},{17,25},{25,17},{2,10},{10... | collective-permute-start | bytes 552968 | tf_op jit(solution)/shard_map/ppermute | solution.py:58
  155.6 6.7 %collective-permute-start.14 = (f32[2,40,576]{2,1,0:T(8,128)S(1)}, f32[2,40,576]{2,1,0:T(8,128)S(1)}, u32[]{:S(2)}, u32[]{:S(2)}) collective-permute-start(f32[2,40,576]{2,1,0:T(8,128)S(1)} %constant_dynamic-slice_fusion.7), channel_id=1, source_target_pairs={{0,4},{4,0},{1,5},{5,1},{2,6},{6,2},{3,7},{7,3},{8,12},{12,8},{9,1... | collective-permute-start | bytes 552968 | tf_op jit(solution)/shard_map/ppermute | solution.py:58
  159.8 6.3 %collective-permute-start.8 = (f32[2,48,576]{2,1,0:T(8,128)S(1)}, f32[2,48,576]{2,1,0:T(8,128)S(1)}, u32[]{:S(2)}, u32[]{:S(2)}) collective-permute-start(f32[2,48,576]{2,1,0:T(8,128)S(1)} %constant_dynamic-slice_fusion.13), channel_id=1, source_target_pairs={{0,2},{1,3},{2,0},{3,1},{4,6},{5,7},{6,4},{7,5},{8,10},{9,11},{10,... | collective-permute-start | bytes 663560 | tf_op jit(solution)/shard_map/ppermute | solution.py:58
  166.2 14.5 %collective-permute-start.15 = (f32[1,128,576]{2,1,0:T(8,128)S(1)}, f32[1,128,576]{2,1,0:T(8,128)S(1)}, u32[]{:S(2)}, u32[]{:S(2)}) collective-permute-start(f32[1,128,576]{2,1,0:T(8,128)S(1)} %constant_dynamic-slice_fusion.6), channel_id=1, source_target_pairs={{0,16},{8,24},{16,0},{24,8},{1,17},{9,25},{17,1},{25,9},{2,18},{10... | collective-permute-start | bytes 884744 | tf_op jit(solution)/shard_map/ppermute | solution.py:58
  180.8 31.7 %copy-start.8 = (bf16[4,32,576]{2,1,0:T(8,128)(2,1)}, bf16[4,32,576]{2,1,0:T(8,128)(2,1)S(1)}, u32[]{:S(2)}) copy-start(bf16[4,32,576]{2,1,0:T(8,128)(2,1)S(1)} %subtract_convert_fusion) | copy-start | bytes 442372
  180.8 9.6 %collective-permute-start.16 = (bf16[1,128,576]{2,1,0:T(8,128)(2,1)S(1)}, bf16[1,128,576]{2,1,0:T(8,128)(2,1)S(1)}, u32[]{:S(2)}, u32[]{:S(2)}) collective-permute-start(bf16[1,128,576]{2,1,0:T(8,128)(2,1)S(1)} %bitcast.148), channel_id=1, source_target_pairs={{0,16},{8,24},{16,0},{24,8},{1,17},{9,25},{17,1},{25,9},{2,18},{10... | collective-permute-start | bytes 442376 | tf_op jit(solution)/shard_map/ppermute | solution.py:65
  190.5 4.7 %collective-permute-start.20 = (bf16[2,40,576]{2,1,0:T(8,128)(2,1)S(1)}, bf16[2,40,576]{2,1,0:T(8,128)(2,1)S(1)}, u32[]{:S(2)}, u32[]{:S(2)}) collective-permute-start(bf16[2,40,576]{2,1,0:T(8,128)(2,1)S(1)} %get-tuple-element.14), channel_id=1, source_target_pairs={{0,8},{8,0},{16,24},{24,16},{1,9},{9,1},{17,25},{25,17},{2,10},{10... | collective-permute-start | bytes 276488 | tf_op jit(solution)/shard_map/ppermute | solution.py:65
  190.6 7.8 %collective-permute-start.17 = (bf16[2,48,576]{2,1,0:T(8,128)(2,1)S(1)}, bf16[2,48,576]{2,1,0:T(8,128)(2,1)S(1)}, u32[]{:S(2)}, u32[]{:S(2)}) collective-permute-start(bf16[2,48,576]{2,1,0:T(8,128)(2,1)S(1)} %slice.43), channel_id=1, source_target_pairs={{0,2},{1,3},{2,0},{3,1},{4,6},{5,7},{6,4},{7,5},{8,10},{9,11},{10,... | collective-permute-start | bytes 331784 | tf_op jit(solution)/shard_map/ppermute | solution.py:65
  191.6 4.7 %collective-permute-start.23 = (bf16[2,40,576]{2,1,0:T(8,128)(2,1)S(1)}, bf16[2,40,576]{2,1,0:T(8,128)(2,1)S(1)}, u32[]{:S(2)}, u32[]{:S(2)}) collective-permute-start(bf16[2,40,576]{2,1,0:T(8,128)(2,1)S(1)} %get-tuple-element.15), channel_id=1, source_target_pairs={{0,4},{4,0},{1,5},{5,1},{2,6},{6,2},{3,7},{7,3},{8,12},{12,8},{9,1... | collective-permute-start | bytes 276488 | tf_op jit(solution)/shard_map/ppermute | solution.py:65
  195.3 5.8 %collective-permute-start.21 = (bf16[4,40,576]{2,1,0:T(8,128)(2,1)S(1)}, bf16[4,40,576]{2,1,0:T(8,128)(2,1)S(1)}, u32[]{:S(2)}, u32[]{:S(2)}) collective-permute-start(bf16[4,40,576]{2,1,0:T(8,128)(2,1)S(1)} %maximum_select_fusion.14), channel_id=1, source_target_pairs={{0,2},{1,3},{2,0},{3,1},{4,6},{5,7},{6,4},{7,5},{8,10},{9,11},{10,... | collective-permute-start | bytes 552968 | tf_op jit(solution)/shard_map/ppermute | solution.py:65
  196.3 5.8 %collective-permute-start.24 = (bf16[4,40,576]{2,1,0:T(8,128)(2,1)S(1)}, bf16[4,40,576]{2,1,0:T(8,128)(2,1)S(1)}, u32[]{:S(2)}, u32[]{:S(2)}) collective-permute-start(bf16[4,40,576]{2,1,0:T(8,128)(2,1)S(1)} %maximum_select_fusion.15), channel_id=1, source_target_pairs={{0,8},{8,0},{16,24},{24,16},{1,9},{9,1},{17,25},{25,17},{2,10},{10... | collective-permute-start | bytes 552968 | tf_op jit(solution)/shard_map/ppermute | solution.py:65
  198.5 8.9 %collective-permute-start.18 = (bf16[4,48,576]{2,1,0:T(8,128)(2,1)S(1)}, bf16[4,48,576]{2,1,0:T(8,128)(2,1)S(1)}, u32[]{:S(2)}, u32[]{:S(2)}) collective-permute-start(bf16[4,48,576]{2,1,0:T(8,128)(2,1)S(1)} %maximum_select_fusion.13), channel_id=1, source_target_pairs={{0,4},{4,0},{1,5},{5,1},{2,6},{6,2},{3,7},{7,3},{8,12},{12,8},{9,1... | collective-permute-start | bytes 663560 | tf_op jit(solution)/shard_map/ppermute | solution.py:65
  201.2 10.7 %collective-permute-start.22 = (bf16[8,40,576]{2,1,0:T(8,128)(2,1)S(1)}, bf16[8,40,576]{2,1,0:T(8,128)(2,1)S(1)}, u32[]{:S(2)}, u32[]{:S(2)}) collective-permute-start(bf16[8,40,576]{2,1,0:T(8,128)(2,1)S(1)} %maximum_select_fusion.8), channel_id=1, source_target_pairs={{0,4},{4,0},{1,5},{5,1},{2,6},{6,2},{3,7},{7,3},{8,12},{12,8},{9,1... | collective-permute-start | bytes 1105928 | tf_op jit(solution)/shard_map/ppermute | solution.py:65
  202.3 10.0 %collective-permute-start.25 = (bf16[8,40,576]{2,1,0:T(8,128)(2,1)S(1)}, bf16[8,40,576]{2,1,0:T(8,128)(2,1)S(1)}, u32[]{:S(2)}, u32[]{:S(2)}) collective-permute-start(bf16[8,40,576]{2,1,0:T(8,128)(2,1)S(1)} %maximum_select_fusion.9), channel_id=1, source_target_pairs={{0,2},{1,3},{2,0},{3,1},{4,6},{5,7},{6,4},{7,5},{8,10},{9,11},{10,... | collective-permute-start | bytes 1105928 | tf_op jit(solution)/shard_map/ppermute | solution.py:65
  207.5 8.9 %collective-permute-start.19 = (bf16[8,48,576]{2,1,0:T(8,128)(2,1)S(1)}, bf16[8,48,576]{2,1,0:T(8,128)(2,1)S(1)}, u32[]{:S(2)}, u32[]{:S(2)}) collective-permute-start(bf16[8,48,576]{2,1,0:T(8,128)(2,1)S(1)} %maximum_select_fusion.7), channel_id=1, source_target_pairs={{0,8},{8,0},{16,24},{24,16},{1,9},{9,1},{17,25},{25,17},{2,10},{10... | collective-permute-start | bytes 1327112 | tf_op jit(solution)/shard_map/ppermute | solution.py:65
  212.2 4.5 %copy-start.4 = (bf16[2,2,2,2,40,576]{5,4,3,2,1,0:T(8,128)(2,1)}, bf16[2,2,2,2,40,576]{5,4,3,2,1,0:T(8,128)(2,1)S(1)}, u32[]{:S(2)}) copy-start(bf16[2,2,2,2,40,576]{5,4,3,2,1,0:T(8,128)(2,1)S(1)} %copy.71) | copy-start | bytes 2211844
  212.6 4.2 %copy-start.5 = (bf16[2,2,2,2,40,576]{5,4,3,2,1,0:T(8,128)(2,1)}, bf16[2,2,2,2,40,576]{5,4,3,2,1,0:T(8,128)(2,1)S(1)}, u32[]{:S(2)}) copy-start(bf16[2,2,2,2,40,576]{5,4,3,2,1,0:T(8,128)(2,1)S(1)} %copy.72) | copy-start | bytes 2211844
  216.8 1.0 copy-start.3
  220.7 4.9 %collective-permute-start.26 = (bf16[16,128,576]{1,2,0:T(8,128)(2,1)}, bf16[16,128,576]{1,2,0:T(8,128)(2,1)}, u32[]{:S(2)}, u32[]{:S(2)}) collective-permute-start(bf16[16,128,576]{1,2,0:T(8,128)(2,1)} %copy.73), channel_id=1, source_target_pairs={{0,1},{1,0},{2,3},{3,2},{4,5},{5,4},{6,7},{7,6},{8,9},{9,8},{10,11... | collective-permute-start | bytes 7077896 | tf_op jit(solution)/shard_map/ppermute | solution.py:65
  241.2 20.4 %slice-start = ((s8[4718592]{0:T(1024)(128)(4,1)}), s8[524288]{0:T(1024)(128)(4,1)S(1)}, s32[]{:S(2)}) async-start(s8[4718592]{0:T(1024)(128)(4,1)} %bitcast.150), calls=%async_computation | async-start | bytes 1048576
  251.1 10.5 %slice-start.1 = ((s8[4718592]{0:T(1024)(128)(4,1)}), s8[4194304]{0:T(1024)(128)(4,1)S(1)}, s32[]{:S(2)}) async-start(s8[4718592]{0:T(1024)(128)(4,1)} %bitcast.150), calls=%async_computation.1 | async-start | bytes 8388608
  264.4 3.2 %collective-permute-start.27 = (f32[4,128,576]{1,2,0:T(8,128)}, f32[4,128,576]{1,2,0:T(8,128)}, u32[]{:S(2)}, u32[]{:S(2)}) collective-permute-start(f32[4,128,576]{1,2,0:T(8,128)} %constant_dynamic-slice_fusion.5), channel_id=1, source_target_pairs={{0,1},{1,0},{2,3},{3,2},{4,5},{5,4},{6,7},{7,6},{8,9},{9,8},{10,11... | collective-permute-start | bytes 3538952 | tf_op jit(solution)/shard_map/ppermute | solution.py:58
  269.4 17.7 %copy-start.1 = (s32[4,256,64]{1,2,0:T(8,128)S(1)}, s32[4,256,64]{1,2,0:T(8,128)}, u32[]{:S(2)}) copy-start(s32[4,256,64]{1,2,0:T(8,128)} %param.12) | copy-start | bytes 786436
  269.7 9.8 %collective-permute-start.28 = (f32[2,64,576]{2,1,0:T(8,128)S(1)}, f32[2,64,576]{2,1,0:T(8,128)S(1)}, u32[]{:S(2)}, u32[]{:S(2)}) collective-permute-start(f32[2,64,576]{2,1,0:T(8,128)S(1)} %copy.85), channel_id=1, source_target_pairs={{0,4},{4,0},{1,5},{5,1},{2,6},{6,2},{3,7},{7,3},{8,12},{12,8},{9,1... | collective-permute-start | bytes 884744 | tf_op jit(solution)/shard_map/ppermute | solution.py:58
  270.8 10.0 %collective-permute-start.30 = (f32[2,64,576]{2,1,0:T(8,128)S(1)}, f32[2,64,576]{2,1,0:T(8,128)S(1)}, u32[]{:S(2)}, u32[]{:S(2)}) collective-permute-start(f32[2,64,576]{2,1,0:T(8,128)S(1)} %constant_dynamic-slice_fusion.1), channel_id=1, source_target_pairs={{0,2},{1,3},{2,0},{3,1},{4,6},{5,7},{6,4},{7,5},{8,10},{9,11},{10,... | collective-permute-start | bytes 884744 | tf_op jit(solution)/shard_map/ppermute | solution.py:58
  279.6 5.5 %collective-permute-start.29 = (f32[1,64,576]{2,1,0:T(8,128)S(1)}, f32[1,64,576]{2,1,0:T(8,128)S(1)}, u32[]{:S(2)}, u32[]{:S(2)}) collective-permute-start(f32[1,64,576]{2,1,0:T(8,128)S(1)} %constant_dynamic-slice_fusion.2), channel_id=1, source_target_pairs={{0,2},{1,3},{2,0},{3,1},{4,6},{5,7},{6,4},{7,5},{8,10},{9,11},{10,... | collective-permute-start | bytes 442376 | tf_op jit(solution)/shard_map/ppermute | solution.py:58
  280.9 5.4 %collective-permute-start.31 = (f32[1,64,576]{2,1,0:T(8,128)S(1)}, f32[1,64,576]{2,1,0:T(8,128)S(1)}, u32[]{:S(2)}, u32[]{:S(2)}) collective-permute-start(f32[1,64,576]{2,1,0:T(8,128)S(1)} %constant_dynamic-slice_fusion), channel_id=1, source_target_pairs={{0,4},{4,0},{1,5},{5,1},{2,6},{6,2},{3,7},{7,3},{8,12},{12,8},{9,1... | collective-permute-start | bytes 442376 | tf_op jit(solution)/shard_map/ppermute | solution.py:58

commit v11 on v9

--- a/solution.py
+++ b/solution.py
@@ -77,7 +77,7 @@
     return [lax.slice_in_dim(block, s, s + z, axis=0) for s, z in portion_rows(block.shape[0], len(orders))]
 
 
-def all_gather(pieces, axes):
+def all_gather(pieces, axes, companion=None):
     labels, prefix, orders, suffix = plan(axes)
     rows = sum(p.shape[0] for p in pieces)
     cols = pieces[0].shape[1]
@@ -93,12 +93,15 @@
             parts[p] = jnp.where(
                 own == 0, jnp.concatenate([parts[p], recv]), jnp.concatenate([recv, parts[p]])
             )
+        if companion is not None and k == nb - 1:
+            parts, companion = lax.optimization_barrier((parts, companion))
     out = []
     for xp, order, (start, size) in zip(parts, steps, spans):
         xp = xp.reshape([2] * nb + [size, cols])
         xp = jnp.transpose(xp, [order.index(l) for l in labels] + [nb, nb + 1])
         out.append(xp.reshape(-1, size, cols))
-    return jnp.concatenate(out, axis=1)
+    gathered = jnp.concatenate(out, axis=1)
+    return gathered if companion is None else (gathered, companion)
 
 
 def local(resid, encoder, encoder_bias, decoder, decoder_bias, topk_index, target):
@@ -117,17 +120,17 @@
     slot_rows = tokens // slots
     feat_total = 2 * feat_parts * feat_dev
 
-    gathered = all_gather(split_rows(resid[0], PLANE), PLANE)
-    tokens_all = (
-        gathered.reshape(2, feat_parts, half_rows, cols).transpose(0, 2, 1, 3).reshape(tokens, width)
-    )
-    pre = jnp.dot(tokens_all, encoder[0], preferred_element_type=jnp.float32) + encoder_bias[0]
     first_feat = half_bit * (feat_total // 2) + feat_pos * feat_dev
     feat_ids = first_feat + lax.iota(jnp.int32, feat_dev)
     layer_index = lax.dynamic_index_in_dim(topk_index, layer_id, 0, keepdims=False)
     selected = jnp.any(layer_index[:, :, None] == feat_ids[None, None, :], axis=1).astype(
         jnp.float32
     )
+    gathered, selected = all_gather(split_rows(resid[0], PLANE), PLANE, selected)
+    tokens_all = (
+        gathered.reshape(2, feat_parts, half_rows, cols).transpose(0, 2, 1, 3).reshape(tokens, width)
+    )
+    pre = jnp.dot(tokens_all, encoder[0], preferred_element_type=jnp.float32) + encoder_bias[0]
     acts = (selected * pre).astype(jnp.bfloat16)
     live_layers = lax.iota(jnp.int32, layer_count) >= layer_id
     partial_value = jnp.einsum("tf,lfd->ltd", acts, decoder[0], preferred_element_type=jnp.float32)

time: 244 us -> 245 us (level)
    ppermute x21, starting transfers between devices: 23.3 us -> 20.8 us  [all_gather(): recv = lax.ppermute(parts[p], axis, partner(axis, bit))]
  transfers between devices with their start and end apart: 42 -> 42, of which waited for: 19 -> 18; matrix products, arithmetic and copies ran while one was open for 16% -> 16% of each run, Pallas kernels for 0% -> 0%
where the time goes in v11:
time: 245 us; the launch traced here: 244 us
  waiting for transfers between devices  72.8 us (30%)
  local copies, waits for them, and re-layouts  61.7 us (25%)
  starting transfers between devices  45.4 us (19%)
  matrix products  31.6 us (13%)
  other arithmetic  31 us (13%)
    ppermute x21, waiting for transfers between devices, reduce_scatter(): recv = lax.ppermute(send.astype(wire), axis, partner(axis, bit))  48 us
    ppermute x21, waiting for transfers between devices, all_gather(): recv = lax.ppermute(parts[p], axis, partner(axis, bit))  24.8 us
    ppermute x21, starting transfers between devices, reduce_scatter(): recv = lax.ppermute(send.astype(wire), axis, partner(axis, bit))  24.6 us
    ppermute x21, starting transfers between devices, all_gather(): recv = lax.ppermute(parts[p], axis, partner(axis, bit))  20.8 us
    reshape x2, local copies, waits for them, and re-layouts, local(): partial_value.reshape(layer_count, slots, slot_rows, feat_parts, cols)  18.7 us
    dot_general x1, matrix products, local(): jnp.einsum('tf,lfd->ltd', acts, decoder[0], preferred_element_type=jnp.fl...  13.9 us
    dynamic_slice x21, local copies, waits for them, and re-layouts, reduce_scatter(): send = lax.dynamic_slice_in_dim(parts[p], (1 - own) * half, half, 0)  11.5 us
    add x16, other arithmetic, reduce_scatter(): parts[p] = keep + recv.astype(keep.dtype)  10.8 us
  transfers between devices with their start and end apart: 42, of which 18 were waited for; matrix products, arithmetic and copies ran while one was open for 16% of the time, Pallas kernels for 0%

profile of v11, /device:TPU:0, one launch (start us, length us, event | category | flops | bytes accessed | tf_op | source)
XLA Modules:
  0.0 243.9 jit_solution(10275029418673101465)
XLA Ops:
  0.6 1.1 fusion.44
  1.9 3.1 %collective-permute-start = (bf16[1,64,576]{2,1,0:T(8,128)(2,1)S(1)}, bf16[1,64,576]{2,1,0:T(8,128)(2,1)S(1)}, u32[]{:S(2)}, u32[]{:S(2)}) collective-permute-start(bf16[1,64,576]{2,1,0:T(8,128)(2,1)S(1)} %copy.69), channel_id=1, source_target_pairs={{0,2},{1,3},{2,0},{3,1},{4,6},{5,7},{6,4},{7,5},{8,10},{9,11},{10,... | collective-permute-start | bytes 221192 | tf_op jit(solution)/shard_map/ppermute | solution.py:92
  5.1 1.6 collective-permute-start.1
  6.8 9.4 %compare_reduce_fusion = pred[256,1024]{1,0:T(8,128)(4,1)S(1)} fusion(s32[1024]{0:T(1024)S(1)} %iota_add_fusion, s32[256,64]{1,0:T(8,128)S(1)} %copy.53), kind=kLoop, calls=%fused_computation | loop fusion | flops 33292288 | bytes 331776 | tf_op jit(solution)/shard_map/reduce_or | solution.py:126
  16.2 1.1 convert_element_type.32
  18.1 4.8 %collective-permute-done.4 = bf16[2,64,576]{2,1,0:T(8,128)(2,1)S(1)} collective-permute-done((bf16[2,64,576]{2,1,0:T(8,128)(2,1)S(1)}, bf16[2,64,576]{2,1,0:T(8,128)(2,1)S(1)}, u32[]{:S(2)}, u32[]{:S(2)}) %collective-permute-start.4) | collective-permute-done | bytes 147488 | tf_op jit(solution)/shard_map/ppermute | solution.py:92
  26.5 4.1 %fusion.35 = bf16[256,1024,1]{1,0,2:T(8,128)(2,1)S(1)} fusion(f32[256,1024]{1,0:T(8,128)} %convert_element_type.32, bf16[1,2304,1024]{2,1,0:T(8,128)(2,1)} %param.8, bf16[288,8,2,128]{3,2,1,0:T(2,128)(2,1)S(1)} %bitcast.141, f32[1024]{0:T(1024)S(1)} %bitcast.150), kind=kOutput, calls=%fused_computation.30 | convolution fusion | flops 1208745984 | bytes 7475200 | tf_op jit(solution)/shard_map/dot_general | solution.py:133
  30.6 13.9 %select_bitcast_fusion = f32[4,256,2304]{2,1,0:T(8,128)} fusion(bf16[256,1024,1]{1,0,2:T(8,128)(2,1)S(1)} %fusion.35, bf16[1,4,1024,2304]{3,2,1,0:T(8,128)(2,1)} %param.10, pred[4]{0:T(512)(128)(4,1)S(1)} %iota_compare_fusion), kind=kOutput, calls=%fused_computation.5 | convolution fusion | flops 4834197504 | bytes 28835844 | tf_op jit(solution)/shard_map/tf,lfd->ltd/dot_general | solution.py:136
  44.5 13.2 %reshape.126 = f32[4,8,32,4,576]{4,3,2,1,0:T(4,128)} reshape(f32[4,256,2304]{2,1,0:T(8,128)} %select_bitcast_fusion) | data formatting | bytes 18874368 | tf_op jit(solution)/shard_map/reshape | solution.py:139
  57.7 5.5 %copy.57 = f32[4,8,32,4,576]{4,2,0,3,1:T(8,128)S(1)} copy(f32[4,8,32,4,576]{4,3,2,1,0:T(4,128)} %reshape.126) | data formatting | bytes 18874368 | tf_op jit(solution)/shard_map/reshape | solution.py:139
  64.3 1.4 constant_dynamic-slice_fusion.10
  67.7 1.6 constant_dynamic-slice_fusion.15
  69.9 1.4 constant_dynamic-slice_fusion.20
  71.6 2.1 dynamic-slice_add_fusion.1
  73.8 1.6 collective-permute-start.17
  75.3 1.7 dynamic-slice_add_fusion.2
  78.0 1.8 dynamic-slice_add_fusion
  79.8 1.1 constant_dynamic-slice_fusion.19
  80.8 1.6 collective-permute-start.7
  82.4 11.8 %collective-permute-done.17 = f32[8,40,576]{2,1,0:T(8,128)S(1)} collective-permute-done((f32[8,40,576]{2,1,0:T(8,128)S(1)}, f32[8,40,576]{2,1,0:T(8,128)S(1)}, u32[]{:S(2)}, u32[]{:S(2)}) %collective-permute-start.17) | collective-permute-done | bytes 737312 | tf_op jit(solution)/shard_map/ppermute | solution.py:70
  95.1 1.6 collective-permute-start.18
  99.9 13.5 %collective-permute-done.18 = f32[4,40,576]{2,1,0:T(8,128)} collective-permute-done((f32[4,40,576]{2,1,0:T(8,128)}, f32[4,40,576]{2,1,0:T(8,128)}, u32[]{:S(2)}, u32[]{:S(2)}) %collective-permute-start.18) | collective-permute-done | bytes 368672 | tf_op jit(solution)/shard_map/ppermute | solution.py:70
  114.5 1.1 collective-permute-start.19
  115.6 1.2 dynamic-slice_add_fusion.10
  116.8 1.6 collective-permute-start.14
  118.5 1.3 dynamic-slice_add_fusion.3
  121.0 2.7 %collective-permute-start.20 = (f32[1,40,576]{2,1,0:T(8,128)S(1)}, f32[1,40,576]{2,1,0:T(8,128)S(1)}, u32[]{:S(2)}, u32[]{:S(2)}) collective-permute-start(f32[1,40,576]{2,1,0:T(8,128)S(1)} %constant_dynamic-slice_fusion.6), channel_id=1, source_target_pairs={{0,16},{8,24},{16,0},{24,8},{1,17},{9,25},{17,1},{25,9},{2,18},{10... | collective-permute-start | bytes 276488 | tf_op jit(solution)/shard_map/ppermute | solution.py:70
  123.7 2.8 %collective-permute-start.15 = (f32[1,40,576]{2,1,0:T(8,128)S(1)}, f32[1,40,576]{2,1,0:T(8,128)S(1)}, u32[]{:S(2)}, u32[]{:S(2)}) collective-permute-start(f32[1,40,576]{2,1,0:T(8,128)S(1)} %constant_dynamic-slice_fusion.11), channel_id=1, source_target_pairs={{0,16},{8,24},{16,0},{24,8},{1,17},{9,25},{17,1},{25,9},{2,18},{10... | collective-permute-start | bytes 276488 | tf_op jit(solution)/shard_map/ppermute | solution.py:70
  126.5 4.7 %collective-permute-done.8 = f32[4,48,576]{2,1,0:T(8,128)S(1)} collective-permute-done((f32[4,48,576]{2,1,0:T(8,128)S(1)}, f32[4,48,576]{2,1,0:T(8,128)S(1)}, u32[]{:S(2)}, u32[]{:S(2)}) %collective-permute-start.8) | collective-permute-done | bytes 442400 | tf_op jit(solution)/shard_map/ppermute | solution.py:70
  132.1 2.7 %collective-permute-start.26 = (bf16[1,40,576]{2,1,0:T(8,128)(2,1)S(1)}, bf16[1,40,576]{2,1,0:T(8,128)(2,1)S(1)}, u32[]{:S(2)}, u32[]{:S(2)}) collective-permute-start(bf16[1,40,576]{2,1,0:T(8,128)(2,1)S(1)} %bitcast.144), channel_id=1, source_target_pairs={{0,16},{8,24},{16,0},{24,8},{1,17},{9,25},{17,1},{25,9},{2,18},{10... | collective-permute-start | bytes 138248 | tf_op jit(solution)/shard_map/ppermute | solution.py:92
  135.1 2.1 collective-permute-done.26
  137.3 1.8 collective-permute-start.27
  139.1 3.2 %collective-permute-start.10 = (f32[1,48,576]{2,1,0:T(8,128)S(1)}, f32[1,48,576]{2,1,0:T(8,128)S(1)}, u32[]{:S(2)}, u32[]{:S(2)}) collective-permute-start(f32[1,48,576]{2,1,0:T(8,128)S(1)} %constant_dynamic-slice_fusion.16), channel_id=1, source_target_pairs={{0,16},{8,24},{16,0},{24,8},{1,17},{9,25},{17,1},{25,9},{2,18},{10... | collective-permute-start | bytes 331784 | tf_op jit(solution)/shard_map/ppermute | solution.py:70
  142.3 1.2 collective-permute-start.32
  143.6 4.2 %collective-permute-done.10 = f32[1,48,576]{2,1,0:T(8,128)S(1)} collective-permute-done((f32[1,48,576]{2,1,0:T(8,128)S(1)}, f32[1,48,576]{2,1,0:T(8,128)S(1)}, u32[]{:S(2)}, u32[]{:S(2)}) %collective-permute-start.10) | collective-permute-done | bytes 110624 | tf_op jit(solution)/shard_map/ppermute | solution.py:70
  147.8 1.1 collective-permute-start.21
  149.0 1.2 collective-permute-start.28
  150.2 2.9 %collective-permute-done.21 = bf16[1,48,576]{2,1,0:T(8,128)(2,1)S(1)} collective-permute-done((bf16[1,48,576]{2,1,0:T(8,128)(2,1)S(1)}, bf16[1,48,576]{2,1,0:T(8,128)(2,1)S(1)}, u32[]{:S(2)}, u32[]{:S(2)}) %collective-permute-start.21) | collective-permute-done | bytes 55328 | tf_op jit(solution)/shard_map/ppermute | solution.py:92
  153.1 1.4 collective-permute-start.22
  155.2 3.8 %collective-permute-done.22 = bf16[2,48,576]{2,1,0:T(8,128)(2,1)S(1)} collective-permute-done((bf16[2,48,576]{2,1,0:T(8,128)(2,1)S(1)}, bf16[2,48,576]{2,1,0:T(8,128)(2,1)S(1)}, u32[]{:S(2)}, u32[]{:S(2)}) %collective-permute-start.22) | collective-permute-done | bytes 110624 | tf_op jit(solution)/shard_map/ppermute | solution.py:92
  159.4 2.1 collective-permute-start.29
  161.6 1.6 collective-permute-start.34
  163.2 2.2 collective-permute-done.23
  165.8 4.0 %collective-permute-done.29 = bf16[8,40,576]{2,1,0:T(8,128)(2,1)S(1)} collective-permute-done((bf16[8,40,576]{2,1,0:T(8,128)(2,1)S(1)}, bf16[8,40,576]{2,1,0:T(8,128)(2,1)S(1)}, u32[]{:S(2)}, u32[]{:S(2)}) %collective-permute-start.29) | collective-permute-done | bytes 368672 | tf_op jit(solution)/shard_map/ppermute | solution.py:92
  170.9 3.6 %collective-permute-done.24 = bf16[8,48,576]{2,1,0:T(8,128)(2,1)S(1)} collective-permute-done((bf16[8,48,576]{2,1,0:T(8,128)(2,1)S(1)}, bf16[8,48,576]{2,1,0:T(8,128)(2,1)S(1)}, u32[]{:S(2)}, u32[]{:S(2)}) %collective-permute-start.24) | collective-permute-done | bytes 442400 | tf_op jit(solution)/shard_map/ppermute | solution.py:92
  174.8 1.8 maximum_select_fusion.1
  176.8 1.8 maximum_select_fusion.2
  178.7 2.0 maximum_select_fusion
  181.0 1.1 pad_maximum_fusion
  182.1 6.4 %copy.64 = bf16[4,8,32,4,576]{4,3,2,1,0:T(4,128)(2,1)} copy(bf16[4,8,32,4,576]{4,2,0,3,1:T(8,128)(2,1)S(1)} %bitcast.117) | data formatting | bytes 9437184 | tf_op jit(solution)/shard_map/transpose | solution.py:158
  188.5 9.9 %reshape.136 = bf16[4,256,2304]{2,1,0:T(8,128)(2,1)} reshape(bf16[4,8,32,4,576]{4,3,2,1,0:T(4,128)(2,1)} %copy.64) | data formatting | bytes 9437184 | tf_op jit(solution)/shard_map/reshape | solution.py:159
  198.4 10.4 %fusion.30 = bf16[256,1024]{1,0:T(8,128)(2,1)S(1)} fusion(f32[256,1024]{1,0:T(8,128)S(1)} %copy-done.8, bf16[1,4,1024,2304]{3,2,1,0:T(8,128)(2,1)} %param.10, bf16[4,256,2304]{2,1,0:T(8,128)(2,1)} %reshape.136, pred[4]{0:T(512)(128)(4,1)S(1)} %iota_compare_fusion), kind=kOutput, calls=%fused_computation.29 | convolution fusion | flops 4834721792 | bytes 25165828 | tf_op jit(solution)/shard_map/ltd,lfd->tf/dot_general | solution.py:162
  208.8 3.4 %fusion.45 = f32[2,128,4,576]{1,3,2,0:T(8,128)S(1)} fusion(bf16[2,128,1024,1]{2,1,3,0:T(8,128)(2,1)S(1)} %bitcast.151, bf16[4,576,1024,1]{2,1,0,3:T(8,128)(2,1)} %bitcast.149), kind=kOutput, calls=%fused_computation.104 | convolution fusion | flops 1207959552 | bytes 7602176 | tf_op jit(solution)/shard_map/dot_general | solution.py:164
  212.1 2.2 slice_bitcast_fusion.4
  214.3 2.9 %copy.65 = f32[2,2,2,64,576]{4,3,2,1,0:T(8,128)} copy(f32[2,2,2,64,576]{3,4,0,2,1:T(8,128)} %get-tuple-element.14) | data formatting | bytes 2359296 | tf_op jit(solution)/shard_map/transpose | solution.py:61
  217.2 2.0 constant_dynamic-slice_fusion.5
  219.7 1.8 copy.66
  221.5 2.1 constant_dynamic-slice_fusion.2
  224.4 1.2 dynamic-slice_add_fusion.7
  226.1 1.6 collective-permute-start.40
  227.7 8.0 %collective-permute-done.37 = f32[2,64,576]{2,1,0:T(8,128)S(1)} collective-permute-done((f32[2,64,576]{2,1,0:T(8,128)S(1)}, f32[2,64,576]{2,1,0:T(8,128)S(1)}, u32[]{:S(2)}, u32[]{:S(2)}) %collective-permute-start.37) | collective-permute-done | bytes 294944 | tf_op jit(solution)/shard_map/ppermute | solution.py:70
  235.8 1.6 collective-permute-start.38
  237.9 3.7 %collective-permute-done.38 = f32[1,64,576]{2,1,0:T(8,128)S(1)} collective-permute-done((f32[1,64,576]{2,1,0:T(8,128)S(1)}, f32[1,64,576]{2,1,0:T(8,128)S(1)}, u32[]{:S(2)}, u32[]{:S(2)}) %collective-permute-start.38) | collective-permute-done | bytes 147488 | tf_op jit(solution)/shard_map/ppermute | solution.py:70
  241.6 1.4 collective-permute-done.41
  (156 shorter events, 24.0 us)
Async XLA Ops:
  0.6 6.1 %copy-start = (s32[4,256,64]{1,2,0:T(8,128)S(1)}, s32[4,256,64]{1,2,0:T(8,128)}, u32[]{:S(2)}) copy-start(s32[4,256,64]{1,2,0:T(8,128)} %param.12) | copy-start | bytes 786436
  1.9 15.4 %collective-permute-start = (bf16[1,64,576]{2,1,0:T(8,128)(2,1)S(1)}, bf16[1,64,576]{2,1,0:T(8,128)(2,1)S(1)}, u32[]{:S(2)}, u32[]{:S(2)}) collective-permute-start(bf16[1,64,576]{2,1,0:T(8,128)(2,1)S(1)} %copy.69), channel_id=1, source_target_pairs={{0,2},{1,3},{2,0},{3,1},{4,6},{5,7},{6,4},{7,5},{8,10},{9,11},{10,... | collective-permute-start | bytes 221192 | tf_op jit(solution)/shard_map/ppermute | solution.py:92
  5.1 12.3 %collective-permute-start.1 = (bf16[1,64,576]{2,1,0:T(8,128)(2,1)S(1)}, bf16[1,64,576]{2,1,0:T(8,128)(2,1)S(1)}, u32[]{:S(2)}, u32[]{:S(2)}) collective-permute-start(bf16[1,64,576]{2,1,0:T(8,128)(2,1)S(1)} %copy.70), channel_id=1, source_target_pairs={{0,4},{4,0},{1,5},{5,1},{2,6},{6,2},{3,7},{7,3},{8,12},{12,8},{9,1... | collective-permute-start | bytes 221192 | tf_op jit(solution)/shard_map/ppermute | solution.py:92
  17.4 5.4 %collective-permute-start.4 = (bf16[2,64,576]{2,1,0:T(8,128)(2,1)S(1)}, bf16[2,64,576]{2,1,0:T(8,128)(2,1)S(1)}, u32[]{:S(2)}, u32[]{:S(2)}) collective-permute-start(bf16[2,64,576]{2,1,0:T(8,128)(2,1)S(1)} %maximum_select_fusion.17), channel_id=1, source_target_pairs={{0,2},{1,3},{2,0},{3,1},{4,6},{5,7},{6,4},{7,5},{8,10},{9,11},{10,... | collective-permute-start | bytes 442376 | tf_op jit(solution)/shard_map/ppermute | solution.py:92
  18.0 5.3 %collective-permute-start.2 = (bf16[2,64,576]{2,1,0:T(8,128)(2,1)S(1)}, bf16[2,64,576]{2,1,0:T(8,128)(2,1)S(1)}, u32[]{:S(2)}, u32[]{:S(2)}) collective-permute-start(bf16[2,64,576]{2,1,0:T(8,128)(2,1)S(1)} %maximum_select_fusion.16), channel_id=1, source_target_pairs={{0,4},{4,0},{1,5},{5,1},{2,6},{6,2},{3,7},{7,3},{8,12},{12,8},{9,1... | collective-permute-start | bytes 442376 | tf_op jit(solution)/shard_map/ppermute | solution.py:92
  23.0 1.7 collective-permute-start.5
  23.4 1.7 collective-permute-start.3
  25.4 1.2 copy-start.17
  64.2 2.2 copy-start.4
  66.4 5.2 %collective-permute-start.16 = (f32[16,40,576]{2,1,0:T(8,128)}, f32[16,40,576]{2,1,0:T(8,128)}, u32[]{:S(2)}, u32[]{:S(2)}) collective-permute-start(f32[16,40,576]{2,1,0:T(8,128)} %constant_dynamic-slice_fusion.10), channel_id=1, source_target_pairs={{0,1},{1,0},{2,3},{3,2},{4,5},{5,4},{6,7},{7,6},{8,9},{9,8},{10,11... | collective-permute-start | bytes 4423688 | tf_op jit(solution)/shard_map/ppermute | solution.py:70
  67.5 2.4 %copy-start.2 = (f32[2,2,2,2,2,48,576]{6,5,4,3,2,1,0:T(8,128)}, f32[2,2,2,2,2,48,576]{6,5,4,3,2,1,0:T(8,128)S(1)}, u32[]{:S(2)}) copy-start(f32[2,2,2,2,2,48,576]{6,5,4,3,2,1,0:T(8,128)S(1)} %copy.58) | copy-start | bytes 10616836
  69.3 6.0 %collective-permute-start.11 = (f32[16,40,576]{2,1,0:T(8,128)}, f32[16,40,576]{2,1,0:T(8,128)}, u32[]{:S(2)}, u32[]{:S(2)}) collective-permute-start(f32[16,40,576]{2,1,0:T(8,128)} %constant_dynamic-slice_fusion.15), channel_id=1, source_target_pairs={{0,1},{1,0},{2,3},{3,2},{4,5},{5,4},{6,7},{7,6},{8,9},{9,8},{10,11... | collective-permute-start | bytes 4423688 | tf_op jit(solution)/shard_map/ppermute | solution.py:70
  71.3 6.5 %collective-permute-start.6 = (f32[16,48,576]{2,1,0:T(8,128)}, f32[16,48,576]{2,1,0:T(8,128)}, u32[]{:S(2)}, u32[]{:S(2)}) collective-permute-start(f32[16,48,576]{2,1,0:T(8,128)} %constant_dynamic-slice_fusion.20), channel_id=1, source_target_pairs={{0,1},{1,0},{2,3},{3,2},{4,5},{5,4},{6,7},{7,6},{8,9},{9,8},{10,11... | collective-permute-start | bytes 5308424 | tf_op jit(solution)/shard_map/ppermute | solution.py:70
  73.8 20.4 %collective-permute-start.17 = (f32[8,40,576]{2,1,0:T(8,128)S(1)}, f32[8,40,576]{2,1,0:T(8,128)S(1)}, u32[]{:S(2)}, u32[]{:S(2)}) collective-permute-start(f32[8,40,576]{2,1,0:T(8,128)S(1)} %constant_dynamic-slice_fusion.9), channel_id=1, source_target_pairs={{0,2},{1,3},{2,0},{3,1},{4,6},{5,7},{6,4},{7,5},{8,10},{9,11},{10,... | collective-permute-start | bytes 2211848 | tf_op jit(solution)/shard_map/ppermute | solution.py:70
  75.3 2.6 %copy-start.3 = (f32[2,2,2,2,2,48,576]{6,5,4,3,2,1,0:T(8,128)S(1)}, f32[2,2,2,2,2,48,576]{6,5,4,3,2,1,0:T(8,128)}, u32[]{:S(2)}) copy-start(f32[2,2,2,2,2,48,576]{6,5,4,3,2,1,0:T(8,128)} %copy-done.2) | copy-start | bytes 10616836
  77.2 20.1 %collective-permute-start.12 = (f32[8,40,576]{2,1,0:T(8,128)S(1)}, f32[8,40,576]{2,1,0:T(8,128)S(1)}, u32[]{:S(2)}, u32[]{:S(2)}) collective-permute-start(f32[8,40,576]{2,1,0:T(8,128)S(1)} %constant_dynamic-slice_fusion.14), channel_id=1, source_target_pairs={{0,4},{4,0},{1,5},{5,1},{2,6},{6,2},{3,7},{7,3},{8,12},{12,8},{9,1... | collective-permute-start | bytes 2211848 | tf_op jit(solution)/shard_map/ppermute | solution.py:70
  80.8 37.6 %collective-permute-start.7 = (f32[8,48,576]{2,1,0:T(8,128)}, f32[8,48,576]{2,1,0:T(8,128)}, u32[]{:S(2)}, u32[]{:S(2)}) collective-permute-start(f32[8,48,576]{2,1,0:T(8,128)} %constant_dynamic-slice_fusion.19), channel_id=1, source_target_pairs={{0,8},{8,0},{16,24},{24,16},{1,9},{9,1},{17,25},{25,17},{2,10},{10... | collective-permute-start | bytes 2654216 | tf_op jit(solution)/shard_map/ppermute | solution.py:70
  94.3 5.6 %copy-start.15 = (bf16[4,32,576]{2,1,0:T(8,128)(2,1)S(1)}, bf16[4,32,576]{2,1,0:T(8,128)(2,1)}, u32[]{:S(2)}) copy-start(bf16[4,32,576]{2,1,0:T(8,128)(2,1)} %param.13) | copy-start | bytes 442372
  95.1 18.4 %collective-permute-start.18 = (f32[4,40,576]{2,1,0:T(8,128)}, f32[4,40,576]{2,1,0:T(8,128)}, u32[]{:S(2)}, u32[]{:S(2)}) collective-permute-start(f32[4,40,576]{2,1,0:T(8,128)} %constant_dynamic-slice_fusion.8), channel_id=1, source_target_pairs={{0,8},{8,0},{16,24},{24,16},{1,9},{9,1},{17,25},{25,17},{2,10},{10... | collective-permute-start | bytes 1105928 | tf_op jit(solution)/shard_map/ppermute | solution.py:70
  97.3 0.9 copy-start.7
  99.0 16.6 %collective-permute-start.13 = (f32[4,40,576]{2,1,0:T(8,128)}, f32[4,40,576]{2,1,0:T(8,128)}, u32[]{:S(2)}, u32[]{:S(2)}) collective-permute-start(f32[4,40,576]{2,1,0:T(8,128)} %constant_dynamic-slice_fusion.13), channel_id=1, source_target_pairs={{0,2},{1,3},{2,0},{3,1},{4,6},{5,7},{6,4},{7,5},{8,10},{9,11},{10,... | collective-permute-start | bytes 1105928 | tf_op jit(solution)/shard_map/ppermute | solution.py:70
  114.5 6.4 %collective-permute-start.19 = (f32[2,40,576]{2,1,0:T(8,128)S(1)}, f32[2,40,576]{2,1,0:T(8,128)S(1)}, u32[]{:S(2)}, u32[]{:S(2)}) collective-permute-start(f32[2,40,576]{2,1,0:T(8,128)S(1)} %constant_dynamic-slice_fusion.7), channel_id=1, source_target_pairs={{0,4},{4,0},{1,5},{5,1},{2,6},{6,2},{3,7},{7,3},{8,12},{12,8},{9,1... | collective-permute-start | bytes 552968 | tf_op jit(solution)/shard_map/ppermute | solution.py:70
  116.8 6.8 %collective-permute-start.14 = (f32[2,40,576]{2,1,0:T(8,128)S(1)}, f32[2,40,576]{2,1,0:T(8,128)S(1)}, u32[]{:S(2)}, u32[]{:S(2)}) collective-permute-start(f32[2,40,576]{2,1,0:T(8,128)S(1)} %constant_dynamic-slice_fusion.12), channel_id=1, source_target_pairs={{0,8},{8,0},{16,24},{24,16},{1,9},{9,1},{17,25},{25,17},{2,10},{10... | collective-permute-start | bytes 552968 | tf_op jit(solution)/shard_map/ppermute | solution.py:70
  119.8 12.2 %copy-start.16 = (f32[4,576]{1,0:T(4,128)S(1)}, f32[4,576]{1,0:T(4,128)}, u32[]{:S(2)}) copy-start(f32[4,576]{1,0:T(4,128)} %param.11) | copy-start | bytes 27652
  119.9 11.4 %collective-permute-start.8 = (f32[4,48,576]{2,1,0:T(8,128)S(1)}, f32[4,48,576]{2,1,0:T(8,128)S(1)}, u32[]{:S(2)}, u32[]{:S(2)}) collective-permute-start(f32[4,48,576]{2,1,0:T(8,128)S(1)} %constant_dynamic-slice_fusion.18), channel_id=1, source_target_pairs={{0,4},{4,0},{1,5},{5,1},{2,6},{6,2},{3,7},{7,3},{8,12},{12,8},{9,1... | collective-permute-start | bytes 1327112 | tf_op jit(solution)/shard_map/ppermute | solution.py:70
  121.0 11.1 %collective-permute-start.20 = (f32[1,40,576]{2,1,0:T(8,128)S(1)}, f32[1,40,576]{2,1,0:T(8,128)S(1)}, u32[]{:S(2)}, u32[]{:S(2)}) collective-permute-start(f32[1,40,576]{2,1,0:T(8,128)S(1)} %constant_dynamic-slice_fusion.6), channel_id=1, source_target_pairs={{0,16},{8,24},{16,0},{24,8},{1,17},{9,25},{17,1},{25,9},{2,18},{10... | collective-permute-start | bytes 276488 | tf_op jit(solution)/shard_map/ppermute | solution.py:70
  123.7 8.3 %collective-permute-start.15 = (f32[1,40,576]{2,1,0:T(8,128)S(1)}, f32[1,40,576]{2,1,0:T(8,128)S(1)}, u32[]{:S(2)}, u32[]{:S(2)}) collective-permute-start(f32[1,40,576]{2,1,0:T(8,128)S(1)} %constant_dynamic-slice_fusion.11), channel_id=1, source_target_pairs={{0,16},{8,24},{16,0},{24,8},{1,17},{9,25},{17,1},{25,9},{2,18},{10... | collective-permute-start | bytes 276488 | tf_op jit(solution)/shard_map/ppermute | solution.py:70
  131.3 7.8 %collective-permute-start.9 = (f32[2,48,576]{2,1,0:T(8,128)S(1)}, f32[2,48,576]{2,1,0:T(8,128)S(1)}, u32[]{:S(2)}, u32[]{:S(2)}) collective-permute-start(f32[2,48,576]{2,1,0:T(8,128)S(1)} %constant_dynamic-slice_fusion.17), channel_id=1, source_target_pairs={{0,2},{1,3},{2,0},{3,1},{4,6},{5,7},{6,4},{7,5},{8,10},{9,11},{10,... | collective-permute-start | bytes 663560 | tf_op jit(solution)/shard_map/ppermute | solution.py:70
  132.1 6.9 %copy-start.11 = (bf16[40,576]{1,0:T(8,128)(2,1)}, bf16[40,576]{1,0:T(8,128)(2,1)S(1)}, u32[]{:S(2)}) copy-start(bf16[40,576]{1,0:T(8,128)(2,1)S(1)} %get-tuple-element.16) | copy-start | bytes 138244
  132.1 27.2 %copy-start.13 = (bf16[40,576]{1,0:T(8,128)(2,1)}, bf16[40,576]{1,0:T(8,128)(2,1)S(1)}, u32[]{:S(2)}) copy-start(bf16[40,576]{1,0:T(8,128)(2,1)S(1)} %get-tuple-element.17) | copy-start | bytes 138244
  132.1 5.1 %collective-permute-start.26 = (bf16[1,40,576]{2,1,0:T(8,128)(2,1)S(1)}, bf16[1,40,576]{2,1,0:T(8,128)(2,1)S(1)}, u32[]{:S(2)}, u32[]{:S(2)}) collective-permute-start(bf16[1,40,576]{2,1,0:T(8,128)(2,1)S(1)} %bitcast.144), channel_id=1, source_target_pairs={{0,16},{8,24},{16,0},{24,8},{1,17},{9,25},{17,1},{25,9},{2,18},{10... | collective-permute-start | bytes 138248 | tf_op jit(solution)/shard_map/ppermute | solution.py:92
  134.8 7.5 %collective-permute-start.31 = (bf16[1,40,576]{2,1,0:T(8,128)(2,1)S(1)}, bf16[1,40,576]{2,1,0:T(8,128)(2,1)S(1)}, u32[]{:S(2)}, u32[]{:S(2)}) collective-permute-start(bf16[1,40,576]{2,1,0:T(8,128)(2,1)S(1)} %bitcast.146), channel_id=1, source_target_pairs={{0,16},{8,24},{16,0},{24,8},{1,17},{9,25},{17,1},{25,9},{2,18},{10... | collective-permute-start | bytes 138248 | tf_op jit(solution)/shard_map/ppermute | solution.py:92
  137.3 11.6 %collective-permute-start.27 = (bf16[2,40,576]{2,1,0:T(8,128)(2,1)S(1)}, bf16[2,40,576]{2,1,0:T(8,128)(2,1)S(1)}, u32[]{:S(2)}, u32[]{:S(2)}) collective-permute-start(bf16[2,40,576]{2,1,0:T(8,128)(2,1)S(1)} %maximum_select_fusion.19), channel_id=1, source_target_pairs={{0,8},{8,0},{16,24},{24,16},{1,9},{9,1},{17,25},{25,17},{2,10},{10... | collective-permute-start | bytes 276488 | tf_op jit(solution)/shard_map/ppermute | solution.py:92
  139.1 8.6 %collective-permute-start.10 = (f32[1,48,576]{2,1,0:T(8,128)S(1)}, f32[1,48,576]{2,1,0:T(8,128)S(1)}, u32[]{:S(2)}, u32[]{:S(2)}) collective-permute-start(f32[1,48,576]{2,1,0:T(8,128)S(1)} %constant_dynamic-slice_fusion.16), channel_id=1, source_target_pairs={{0,16},{8,24},{16,0},{24,8},{1,17},{9,25},{17,1},{25,9},{2,18},{10... | collective-permute-start | bytes 331784 | tf_op jit(solution)/shard_map/ppermute | solution.py:70
  142.3 12.2 %collective-permute-start.32 = (bf16[2,40,576]{2,1,0:T(8,128)(2,1)S(1)}, bf16[2,40,576]{2,1,0:T(8,128)(2,1)S(1)}, u32[]{:S(2)}, u32[]{:S(2)}) collective-permute-start(bf16[2,40,576]{2,1,0:T(8,128)(2,1)S(1)} %maximum_select_fusion.20), channel_id=1, source_target_pairs={{0,4},{4,0},{1,5},{5,1},{2,6},{6,2},{3,7},{7,3},{8,12},{12,8},{9,1... | collective-permute-start | bytes 276488 | tf_op jit(solution)/shard_map/ppermute | solution.py:92
  147.8 11.4 %copy-start.9 = (bf16[48,576]{1,0:T(8,128)(2,1)}, bf16[48,576]{1,0:T(8,128)(2,1)S(1)}, u32[]{:S(2)}) copy-start(bf16[48,576]{1,0:T(8,128)(2,1)S(1)} %fusion.40) | copy-start | bytes 165892
  147.8 5.3 %collective-permute-start.21 = (bf16[1,48,576]{2,1,0:T(8,128)(2,1)S(1)}, bf16[1,48,576]{2,1,0:T(8,128)(2,1)S(1)}, u32[]{:S(2)}, u32[]{:S(2)}) collective-permute-start(bf16[1,48,576]{2,1,0:T(8,128)(2,1)S(1)} %bitcast.142), channel_id=1, source_target_pairs={{0,16},{8,24},{16,0},{24,8},{1,17},{9,25},{17,1},{25,9},{2,18},{10... | collective-permute-start | bytes 165896 | tf_op jit(solution)/shard_map/ppermute | solution.py:92
  149.0 10.2 %collective-permute-start.28 = (bf16[4,40,576]{2,1,0:T(8,128)(2,1)S(1)}, bf16[4,40,576]{2,1,0:T(8,128)(2,1)S(1)}, u32[]{:S(2)}, u32[]{:S(2)}) collective-permute-start(bf16[4,40,576]{2,1,0:T(8,128)(2,1)S(1)} %maximum_select_fusion.14), channel_id=1, source_target_pairs={{0,2},{1,3},{2,0},{3,1},{4,6},{5,7},{6,4},{7,5},{8,10},{9,11},{10,... | collective-permute-start | bytes 552968 | tf_op jit(solution)/shard_map/ppermute | solution.py:92
  153.1 6.0 %collective-permute-start.22 = (bf16[2,48,576]{2,1,0:T(8,128)(2,1)S(1)}, bf16[2,48,576]{2,1,0:T(8,128)(2,1)S(1)}, u32[]{:S(2)}, u32[]{:S(2)}) collective-permute-start(bf16[2,48,576]{2,1,0:T(8,128)(2,1)S(1)} %maximum_select_fusion.18), channel_id=1, source_target_pairs={{0,2},{1,3},{2,0},{3,1},{4,6},{5,7},{6,4},{7,5},{8,10},{9,11},{10,... | collective-permute-start | bytes 331784 | tf_op jit(solution)/shard_map/ppermute | solution.py:92
  154.6 6.8 %collective-permute-start.33 = (bf16[4,40,576]{2,1,0:T(8,128)(2,1)S(1)}, bf16[4,40,576]{2,1,0:T(8,128)(2,1)S(1)}, u32[]{:S(2)}, u32[]{:S(2)}) collective-permute-start(bf16[4,40,576]{2,1,0:T(8,128)(2,1)S(1)} %maximum_select_fusion.15), channel_id=1, source_target_pairs={{0,8},{8,0},{16,24},{24,16},{1,9},{9,1},{17,25},{25,17},{2,10},{10... | collective-permute-start | bytes 552968 | tf_op jit(solution)/shard_map/ppermute | solution.py:92
  159.1 6.3 %collective-permute-start.23 = (bf16[4,48,576]{2,1,0:T(8,128)(2,1)S(1)}, bf16[4,48,576]{2,1,0:T(8,128)(2,1)S(1)}, u32[]{:S(2)}, u32[]{:S(2)}) collective-permute-start(bf16[4,48,576]{2,1,0:T(8,128)(2,1)S(1)} %maximum_select_fusion.13), channel_id=1, source_target_pairs={{0,4},{4,0},{1,5},{5,1},{2,6},{6,2},{3,7},{7,3},{8,12},{12,8},{9,1... | collective-permute-start | bytes 663560 | tf_op jit(solution)/shard_map/ppermute | solution.py:92
  159.4 10.4 %collective-permute-start.29 = (bf16[8,40,576]{2,1,0:T(8,128)(2,1)S(1)}, bf16[8,40,576]{2,1,0:T(8,128)(2,1)S(1)}, u32[]{:S(2)}, u32[]{:S(2)}) collective-permute-start(bf16[8,40,576]{2,1,0:T(8,128)(2,1)S(1)} %maximum_select_fusion.9), channel_id=1, source_target_pairs={{0,4},{4,0},{1,5},{5,1},{2,6},{6,2},{3,7},{7,3},{8,12},{12,8},{9,1... | collective-permute-start | bytes 1105928 | tf_op jit(solution)/shard_map/ppermute | solution.py:92
  161.6 8.5 %collective-permute-start.34 = (bf16[8,40,576]{2,1,0:T(8,128)(2,1)S(1)}, bf16[8,40,576]{2,1,0:T(8,128)(2,1)S(1)}, u32[]{:S(2)}, u32[]{:S(2)}) collective-permute-start(bf16[8,40,576]{2,1,0:T(8,128)(2,1)S(1)} %maximum_select_fusion.10), channel_id=1, source_target_pairs={{0,2},{1,3},{2,0},{3,1},{4,6},{5,7},{6,4},{7,5},{8,10},{9,11},{10,... | collective-permute-start | bytes 1105928 | tf_op jit(solution)/shard_map/ppermute | solution.py:92
  165.5 8.9 %collective-permute-start.24 = (bf16[8,48,576]{2,1,0:T(8,128)(2,1)S(1)}, bf16[8,48,576]{2,1,0:T(8,128)(2,1)S(1)}, u32[]{:S(2)}, u32[]{:S(2)}) collective-permute-start(bf16[8,48,576]{2,1,0:T(8,128)(2,1)S(1)} %maximum_select_fusion.8), channel_id=1, source_target_pairs={{0,8},{8,0},{16,24},{24,16},{1,9},{9,1},{17,25},{25,17},{2,10},{10... | collective-permute-start | bytes 1327112 | tf_op jit(solution)/shard_map/ppermute | solution.py:92
  170.0 4.8 %collective-permute-start.30 = (bf16[16,40,576]{2,1,0:T(8,128)(2,1)S(1)}, bf16[16,40,576]{2,1,0:T(8,128)(2,1)}, u32[]{:S(2)}, u32[]{:S(2)}) collective-permute-start(bf16[16,40,576]{2,1,0:T(8,128)(2,1)S(1)} %maximum_select_fusion.4), channel_id=1, source_target_pairs={{0,1},{1,0},{2,3},{3,2},{4,5},{5,4},{6,7},{7,6},{8,9},{9,8},{10,11... | collective-permute-start | bytes 2211848 | tf_op jit(solution)/shard_map/ppermute | solution.py:92
  170.3 6.4 %collective-permute-start.35 = (bf16[16,40,576]{2,1,0:T(8,128)(2,1)S(1)}, bf16[16,40,576]{2,1,0:T(8,128)(2,1)}, u32[]{:S(2)}, u32[]{:S(2)}) collective-permute-start(bf16[16,40,576]{2,1,0:T(8,128)(2,1)S(1)} %maximum_select_fusion.5), channel_id=1, source_target_pairs={{0,1},{1,0},{2,3},{3,2},{4,5},{5,4},{6,7},{7,6},{8,9},{9,8},{10,11... | collective-permute-start | bytes 2211848 | tf_op jit(solution)/shard_map/ppermute | solution.py:92
  174.7 4.0 %collective-permute-start.25 = (bf16[16,48,576]{2,1,0:T(8,128)(2,1)S(1)}, bf16[16,48,576]{2,1,0:T(8,128)(2,1)}, u32[]{:S(2)}, u32[]{:S(2)}) collective-permute-start(bf16[16,48,576]{2,1,0:T(8,128)(2,1)S(1)} %maximum_select_fusion.3), channel_id=1, source_target_pairs={{0,1},{1,0},{2,3},{3,2},{4,5},{5,4},{6,7},{7,6},{8,9},{9,8},{10,11... | collective-permute-start | bytes 2654216 | tf_op jit(solution)/shard_map/ppermute | solution.py:92
  188.5 9.9 %copy-start.8 = (f32[256,1024]{1,0:T(8,128)S(1)}, f32[256,1024]{1,0:T(8,128)}, u32[]{:S(2)}) copy-start(f32[256,1024]{1,0:T(8,128)} %convert_element_type.32) | copy-start | bytes 3145732
  219.2 5.1 %collective-permute-start.36 = (f32[4,64,576]{2,1,0:T(8,128)}, f32[4,64,576]{2,1,0:T(8,128)}, u32[]{:S(2)}, u32[]{:S(2)}) collective-permute-start(f32[4,64,576]{2,1,0:T(8,128)} %constant_dynamic-slice_fusion.5), channel_id=1, source_target_pairs={{0,1},{1,0},{2,3},{3,2},{4,5},{5,4},{6,7},{7,6},{8,9},{9,8},{10,11... | collective-permute-start | bytes 1769480 | tf_op jit(solution)/shard_map/ppermute | solution.py:70
  219.7 4.0 %copy-start.10 = (bf16[48,576]{1,0:T(8,128)(2,1)S(1)}, bf16[48,576]{1,0:T(8,128)(2,1)}, u32[]{:S(2)}) copy-start(bf16[48,576]{1,0:T(8,128)(2,1)} %copy-done.9) | copy-start | bytes 165892
  219.7 4.0 %copy-start.12 = (bf16[40,576]{1,0:T(8,128)(2,1)S(1)}, bf16[40,576]{1,0:T(8,128)(2,1)}, u32[]{:S(2)}) copy-start(bf16[40,576]{1,0:T(8,128)(2,1)} %copy-done.11) | copy-start | bytes 138244
  219.7 4.0 %copy-start.14 = (bf16[40,576]{1,0:T(8,128)(2,1)S(1)}, bf16[40,576]{1,0:T(8,128)(2,1)}, u32[]{:S(2)}) copy-start(bf16[40,576]{1,0:T(8,128)(2,1)} %copy-done.13) | copy-start | bytes 138244
  221.5 2.9 %copy-start.6 = (f32[2,2,2,64,576]{4,3,2,1,0:T(8,128)S(1)}, f32[2,2,2,64,576]{4,3,2,1,0:T(8,128)}, u32[]{:S(2)}) copy-start(f32[2,2,2,64,576]{4,3,2,1,0:T(8,128)} %copy.65) | copy-start | bytes 3538948
  221.5 4.5 %copy-start.5 = (f32[2,2,2,64,576]{4,3,2,1,0:T(8,128)S(1)}, f32[2,2,2,64,576]{4,3,2,1,0:T(8,128)}, u32[]{:S(2)}) copy-start(f32[2,2,2,64,576]{4,3,2,1,0:T(8,128)} %copy.66) | copy-start | bytes 3538948
  223.7 2.3 collective-permute-start.39
  225.6 10.2 %collective-permute-start.37 = (f32[2,64,576]{2,1,0:T(8,128)S(1)}, f32[2,64,576]{2,1,0:T(8,128)S(1)}, u32[]{:S(2)}, u32[]{:S(2)}) collective-permute-start(f32[2,64,576]{2,1,0:T(8,128)S(1)} %constant_dynamic-slice_fusion.4), channel_id=1, source_target_pairs={{0,4},{4,0},{1,5},{5,1},{2,6},{6,2},{3,7},{7,3},{8,12},{12,8},{9,1... | collective-permute-start | bytes 884744 | tf_op jit(solution)/shard_map/ppermute | solution.py:70
  226.1 17.8 %copy-start.1 = (s32[4,256,64]{1,2,0:T(8,128)S(1)}, s32[4,256,64]{1,2,0:T(8,128)}, u32[]{:S(2)}) copy-start(s32[4,256,64]{1,2,0:T(8,128)} %param.12) | copy-start | bytes 786436
  226.1 11.3 %collective-permute-start.40 = (f32[2,64,576]{2,1,0:T(8,128)S(1)}, f32[2,64,576]{2,1,0:T(8,128)S(1)}, u32[]{:S(2)}, u32[]{:S(2)}) collective-permute-start(f32[2,64,576]{2,1,0:T(8,128)S(1)} %constant_dynamic-slice_fusion.1), channel_id=1, source_target_pairs={{0,2},{1,3},{2,0},{3,1},{4,6},{5,7},{6,4},{7,5},{8,10},{9,11},{10,... | collective-permute-start | bytes 884744 | tf_op jit(solution)/shard_map/ppermute | solution.py:70
  235.8 5.8 %collective-permute-start.38 = (f32[1,64,576]{2,1,0:T(8,128)S(1)}, f32[1,64,576]{2,1,0:T(8,128)S(1)}, u32[]{:S(2)}, u32[]{:S(2)}) collective-permute-start(f32[1,64,576]{2,1,0:T(8,128)S(1)} %constant_dynamic-slice_fusion.3), channel_id=1, source_target_pairs={{0,2},{1,3},{2,0},{3,1},{4,6},{5,7},{6,4},{7,5},{8,10},{9,11},{10,... | collective-permute-start | bytes 442376 | tf_op jit(solution)/shard_map/ppermute | solution.py:70
  237.5 5.5 %collective-permute-start.41 = (f32[1,64,576]{2,1,0:T(8,128)S(1)}, f32[1,64,576]{2,1,0:T(8,128)S(1)}, u32[]{:S(2)}, u32[]{:S(2)}) collective-permute-start(f32[1,64,576]{2,1,0:T(8,128)S(1)} %constant_dynamic-slice_fusion), channel_id=1, source_target_pairs={{0,4},{4,0},{1,5},{5,1},{2,6},{6,2},{3,7},{7,3},{8,12},{12,8},{9,1... | collective-permute-start | bytes 442376 | tf_op jit(solution)/shard_map/ppermute | solution.py:70

commit v12 on v9

--- a/solution.py
+++ b/solution.py
@@ -23,7 +23,7 @@
     prefix = [("feat", 0)]
     suffix = [("lz", lax.axis_size("lz").bit_length() - 2)] if "lz" in axes else []
     rotation = [label for label in labels if label not in prefix + suffix]
-    orders = [rotation[p:] + rotation[:p] for p in range(len(rotation))]
+    orders = [rotation[p:] + rotation[:p] for p in range(min(2, len(rotation)))]
     return labels, prefix, orders, suffix
 
 

time: 244 us -> 259 us (1.061)
  waiting for transfers between devices: 73.7 us -> 99.6 us
  starting transfers between devices: 46.3 us -> 34.5 us
  local copies, waits for them, and re-layouts: 61.9 us -> 66.3 us
  other arithmetic: 30.1 us -> 26.3 us
    ppermute x21 -> x16, waiting for transfers between devices: 49.3 us -> 70 us  [reduce_scatter(): recv = lax.ppermute(send.astype(wire), axis, partner(axis, bit))]
    ppermute x21 -> x16, starting transfers between devices: 23.3 us -> 13.8 us  [all_gather(): recv = lax.ppermute(parts[p], axis, partner(axis, bit))]
    transpose x8 -> x6, local copies, waits for them, and re-layouts: 9.04 us -> 15.1 us  [reduce_scatter(): xp = jnp.transpose(xp, [labels.index(l) for l in order] + [nb, nb + 1])]
    ppermute x21 -> x16, waiting for transfers between devices: 24.4 us -> 29.7 us  [all_gather(): recv = lax.ppermute(parts[p], axis, partner(axis, bit))]
    ppermute x21 -> x16, starting transfers between devices: 23 us -> 20.7 us  [reduce_scatter(): recv = lax.ppermute(send.astype(wire), axis, partner(axis, bit))]
    dynamic_slice x21 -> x16, local copies, waits for them, and re-layouts: 11.6 us -> 9.38 us  [reduce_scatter(): send = lax.dynamic_slice_in_dim(parts[p], (1 - own) * half, half, 0)]
    add x16 -> x12, other arithmetic: 10.8 us -> 9.12 us  [reduce_scatter(): parts[p] = keep + recv.astype(keep.dtype)]
    select_n x21 -> x16, other arithmetic: 7.74 us -> 6.22 us  [all_gather(): jnp.where(own == 0, jnp.concatenate([parts[p], recv]), jnp.concatenate([r...]
  transfers between devices with their start and end apart: 42 -> 32, of which waited for: 19 -> 25; matrix products, arithmetic and copies ran while one was open for 16% -> 12% of each run, Pallas kernels for 0% -> 0%
where the time goes in v12:
time: 259 us; the launch traced here: 258 us
  waiting for transfers between devices  99.6 us (38%)
  local copies, waits for them, and re-layouts  66.3 us (26%)
  starting transfers between devices  34.5 us (13%)
  matrix products  29.6 us (11%)
  other arithmetic  26.3 us (10%)
    ppermute x16, waiting for transfers between devices, reduce_scatter(): recv = lax.ppermute(send.astype(wire), axis, partner(axis, bit))  70 us
    ppermute x16, waiting for transfers between devices, all_gather(): recv = lax.ppermute(parts[p], axis, partner(axis, bit))  29.7 us
    ppermute x16, starting transfers between devices, reduce_scatter(): recv = lax.ppermute(send.astype(wire), axis, partner(axis, bit))  20.7 us
    reshape x2, local copies, waits for them, and re-layouts, local(): partial_value.reshape(layer_count, slots, slot_rows, feat_parts, cols)  18.6 us
    transpose x6, local copies, waits for them, and re-layouts, reduce_scatter(): xp = jnp.transpose(xp, [labels.index(l) for l in order] + [nb, nb + 1])  15.1 us
    dot_general x1, matrix products, local(): jnp.einsum('tf,lfd->ltd', acts, decoder[0], preferred_element_type=jnp.fl...  13.9 us
    ppermute x16, starting transfers between devices, all_gather(): recv = lax.ppermute(parts[p], axis, partner(axis, bit))  13.8 us
    dot_general x1, matrix products, local(): jnp.einsum('ltd,lfd->tf', kept, decoder[0], preferred_element_type=jnp.fl...  10.5 us
  transfers between devices with their start and end apart: 32, of which 25 were waited for; matrix products, arithmetic and copies ran while one was open for 12% of the time, Pallas kernels for 0%

profile of v12, /device:TPU:0, one launch (start us, length us, event | category | flops | bytes accessed | tf_op | source)
XLA Modules:
  0.0 257.5 jit_solution(14804332006950384994)
XLA Ops:
  1.9 3.1 %collective-permute-start = (bf16[1,64,576]{2,1,0:T(8,128)(2,1)S(1)}, bf16[1,64,576]{2,1,0:T(8,128)(2,1)S(1)}, u32[]{:S(2)}, u32[]{:S(2)}) collective-permute-start(bf16[1,64,576]{2,1,0:T(8,128)(2,1)S(1)} %copy.71), channel_id=1, source_target_pairs={{0,2},{1,3},{2,0},{3,1},{4,6},{5,7},{6,4},{7,5},{8,10},{9,11},{10,... | collective-permute-start | bytes 221192 | tf_op jit(solution)/shard_map/ppermute | solution.py:92
  5.1 1.6 collective-permute-start.3
  7.5 2.0 collective-permute-start.1
  9.9 1.2 collective-permute-start.4
  11.2 1.9 collective-permute-done.1
  13.3 2.0 collective-permute-done.4
  15.5 9.4 %compare_reduce_fusion = pred[256,1024]{1,0:T(8,128)(4,1)S(1)} fusion(s32[1024]{0:T(1024)S(1)} %iota_add_fusion, s32[256,64]{1,0:T(8,128)S(1)} %copy.55), kind=kLoop, calls=%fused_computation | loop fusion | flops 33292288 | bytes 331776 | tf_op jit(solution)/shard_map/reduce_or | solution.py:128
  26.6 3.8 %fusion.35 = bf16[256,1024,1]{1,0,2:T(8,128)(2,1)S(1)} fusion(pred[256,1024]{1,0:T(8,128)(4,1)S(1)} %compare_reduce_fusion, bf16[1,2304,1024]{2,1,0:T(8,128)(2,1)} %param.8, bf16[288,8,2,128]{3,2,1,0:T(2,128)(2,1)S(1)} %bitcast.138, f32[1024]{0:T(1024)S(1)} %bitcast.147), kind=kOutput, calls=%fused_computation.31 | convolution fusion | flops 1208745984 | bytes 6688768 | tf_op jit(solution)/shard_map/dot_general | solution.py:124
  30.4 13.9 %select_bitcast_fusion = f32[4,256,2304]{2,1,0:T(8,128)} fusion(bf16[256,1024,1]{1,0,2:T(8,128)(2,1)S(1)} %fusion.35, bf16[1,4,1024,2304]{3,2,1,0:T(8,128)(2,1)} %param.10, pred[4]{0:T(512)(128)(4,1)S(1)} %iota_compare_fusion), kind=kOutput, calls=%fused_computation.5 | convolution fusion | flops 4834197504 | bytes 28835844 | tf_op jit(solution)/shard_map/tf,lfd->ltd/dot_general | solution.py:133
  44.3 13.2 %reshape.116 = f32[4,8,32,4,576]{4,3,2,1,0:T(4,128)} reshape(f32[4,256,2304]{2,1,0:T(8,128)} %select_bitcast_fusion) | data formatting | bytes 18874368 | tf_op jit(solution)/shard_map/reshape | solution.py:136
  57.4 5.5 %copy.61 = f32[4,8,32,4,576]{4,2,0,3,1:T(8,128)S(1)} copy(f32[4,8,32,4,576]{4,3,2,1,0:T(4,128)} %reshape.116) | data formatting | bytes 18874368 | tf_op jit(solution)/shard_map/reshape | solution.py:136
  62.9 4.7 %slice_bitcast_fusion.1 = (f32[2,2,2,2,2,64,576]{6,5,0,3,2,1,4:T(8,128)}, f32[2,2,2,2,2,64,576]{6,5,0,2,1,3,4:T(8,128)}) fusion(f32[2,2,2,2,2,128,576]{6,5,4,3,2,1,0:T(8,128)S(1)} %bitcast.117), kind=kLoop, calls=%fused_computation.7 | loop fusion | bytes 18874368 | tf_op jit(solution)/shard_map/transpose | solution.py:61
  67.6 3.0 %copy.62 = f32[2,2,2,2,2,64,576]{6,5,4,3,2,1,0:T(8,128)S(1)} copy(f32[2,2,2,2,2,64,576]{6,5,0,3,2,1,4:T(8,128)} %get-tuple-element.6) | data formatting | bytes 9437184 | tf_op jit(solution)/shard_map/transpose | solution.py:61
  70.6 1.7 constant_dynamic-slice_fusion.15
  72.3 1.5 copy-done.4
  74.8 1.8 constant_dynamic-slice_fusion.10
  76.7 1.4 copy-done.2
  79.0 2.2 dynamic-slice_add_fusion.1
  82.3 1.7 collective-permute-start.7
  84.0 2.1 dynamic-slice_add_fusion
  86.1 1.2 constant_dynamic-slice_fusion.9
  87.3 1.5 collective-permute-start.12
  88.8 24.9 %collective-permute-done.7 = f32[8,64,576]{2,1,0:T(8,128)} collective-permute-done((f32[8,64,576]{2,1,0:T(8,128)}, f32[8,64,576]{2,1,0:T(8,128)}, u32[]{:S(2)}, u32[]{:S(2)}) %collective-permute-start.7) | collective-permute-done | bytes 1179680 | tf_op jit(solution)/shard_map/ppermute | solution.py:70
  113.7 1.8 dynamic-slice_add_fusion.3
  115.6 1.7 collective-permute-start.8
  117.3 1.6 collective-permute-done.12
  118.9 1.5 dynamic-slice_add_fusion.2
  121.5 10.9 %collective-permute-done.8 = f32[4,64,576]{2,1,0:T(8,128)S(1)} collective-permute-done((f32[4,64,576]{2,1,0:T(8,128)S(1)}, f32[4,64,576]{2,1,0:T(8,128)S(1)}, u32[]{:S(2)}, u32[]{:S(2)}) %collective-permute-start.8) | collective-permute-done | bytes 589856 | tf_op jit(solution)/shard_map/ppermute | solution.py:70
  133.6 3.8 %collective-permute-done.13 = f32[4,64,576]{2,1,0:T(8,128)S(1)} collective-permute-done((f32[4,64,576]{2,1,0:T(8,128)S(1)}, f32[4,64,576]{2,1,0:T(8,128)S(1)}, u32[]{:S(2)}, u32[]{:S(2)}) %collective-permute-start.13) | collective-permute-done | bytes 589856 | tf_op jit(solution)/shard_map/ppermute | solution.py:70
  137.6 1.2 collective-permute-start.14
  138.8 4.1 %collective-permute-done.9 = f32[2,64,576]{2,1,0:T(8,128)S(1)} collective-permute-done((f32[2,64,576]{2,1,0:T(8,128)S(1)}, f32[2,64,576]{2,1,0:T(8,128)S(1)}, u32[]{:S(2)}, u32[]{:S(2)}) %collective-permute-start.9) | collective-permute-done | bytes 294944 | tf_op jit(solution)/shard_map/ppermute | solution.py:70
  143.0 2.7 %collective-permute-start.10 = (f32[1,64,576]{2,1,0:T(8,128)S(1)}, f32[1,64,576]{2,1,0:T(8,128)S(1)}, u32[]{:S(2)}, u32[]{:S(2)}) collective-permute-start(f32[1,64,576]{2,1,0:T(8,128)S(1)} %constant_dynamic-slice_fusion.11), channel_id=1, source_target_pairs={{0,16},{8,24},{16,0},{24,8},{1,17},{9,25},{17,1},{25,9},{2,18},{10... | collective-permute-start | bytes 442376 | tf_op jit(solution)/shard_map/ppermute | solution.py:70
  145.7 3.3 %collective-permute-start.15 = (f32[1,64,576]{2,1,0:T(8,128)S(1)}, f32[1,64,576]{2,1,0:T(8,128)S(1)}, u32[]{:S(2)}, u32[]{:S(2)}) collective-permute-start(f32[1,64,576]{2,1,0:T(8,128)S(1)} %constant_dynamic-slice_fusion.6), channel_id=1, source_target_pairs={{0,16},{8,24},{16,0},{24,8},{1,17},{9,25},{17,1},{25,9},{2,18},{10... | collective-permute-start | bytes 442376 | tf_op jit(solution)/shard_map/ppermute | solution.py:70
  149.0 8.0 %collective-permute-done.10 = f32[1,64,576]{2,1,0:T(8,128)S(1)} collective-permute-done((f32[1,64,576]{2,1,0:T(8,128)S(1)}, f32[1,64,576]{2,1,0:T(8,128)S(1)}, u32[]{:S(2)}, u32[]{:S(2)}) %collective-permute-start.10) | collective-permute-done | bytes 147488 | tf_op jit(solution)/shard_map/ppermute | solution.py:70
  157.1 4.7 %collective-permute-done.15 = f32[1,64,576]{2,1,0:T(8,128)S(1)} collective-permute-done((f32[1,64,576]{2,1,0:T(8,128)S(1)}, f32[1,64,576]{2,1,0:T(8,128)S(1)}, u32[]{:S(2)}, u32[]{:S(2)}) %collective-permute-start.15) | collective-permute-done | bytes 147488 | tf_op jit(solution)/shard_map/ppermute | solution.py:70
  161.9 2.5 collective-permute-done.16
  164.4 1.5 collective-permute-start.17
  165.9 2.3 collective-permute-done.21
  168.5 1.3 collective-permute-done.17
  169.9 1.9 collective-permute-start.18
  171.8 1.8 collective-permute-done.22
  173.8 3.2 %collective-permute-done.18 = bf16[4,64,576]{2,1,0:T(8,128)(2,1)S(1)} collective-permute-done((bf16[4,64,576]{2,1,0:T(8,128)(2,1)S(1)}, bf16[4,64,576]{2,1,0:T(8,128)(2,1)S(1)}, u32[]{:S(2)}, u32[]{:S(2)}) %collective-permute-start.18) | collective-permute-done | bytes 294944 | tf_op jit(solution)/shard_map/ppermute | solution.py:92
  177.2 1.6 collective-permute-start.19
  178.8 2.0 collective-permute-done.23
  181.1 8.0 %collective-permute-done.19 = bf16[8,64,576]{2,1,0:T(8,128)(2,1)S(1)} collective-permute-done((bf16[8,64,576]{2,1,0:T(8,128)(2,1)S(1)}, bf16[8,64,576]{2,1,0:T(8,128)(2,1)S(1)}, u32[]{:S(2)}, u32[]{:S(2)}) %collective-permute-start.19) | collective-permute-done | bytes 589856 | tf_op jit(solution)/shard_map/ppermute | solution.py:92
  189.5 2.8 %collective-permute-done.24 = bf16[8,64,576]{2,1,0:T(8,128)(2,1)S(1)} collective-permute-done((bf16[8,64,576]{2,1,0:T(8,128)(2,1)S(1)}, bf16[8,64,576]{2,1,0:T(8,128)(2,1)S(1)}, u32[]{:S(2)}, u32[]{:S(2)}) %collective-permute-start.24) | collective-permute-done | bytes 589856 | tf_op jit(solution)/shard_map/ppermute | solution.py:92
  192.7 2.1 maximum_select_fusion
  195.9 2.3 maximum_select_fusion.1
  199.1 6.4 %copy.66 = bf16[4,8,32,4,576]{4,3,2,1,0:T(4,128)(2,1)} copy(bf16[4,8,32,4,576]{4,2,0,3,1:T(8,128)(2,1)S(1)} %bitcast.124) | data formatting | bytes 9437184 | tf_op jit(solution)/shard_map/transpose | solution.py:155
  205.5 9.9 %reshape.123 = bf16[4,256,2304]{2,1,0:T(8,128)(2,1)} reshape(bf16[4,8,32,4,576]{4,3,2,1,0:T(4,128)(2,1)} %copy.66) | data formatting | bytes 9437184 | tf_op jit(solution)/shard_map/reshape | solution.py:156
  215.4 10.5 %fusion.30 = bf16[256,1024]{1,0:T(8,128)(2,1)S(1)} fusion(pred[256,1024]{1,0:T(8,128)(4,1)S(1)} %compare_reduce_fusion, bf16[1,4,1024,2304]{3,2,1,0:T(8,128)(2,1)} %param.10, bf16[4,256,2304]{2,1,0:T(8,128)(2,1)} %reshape.123, pred[4]{0:T(512)(128)(4,1)S(1)} %iota_compare_fusion), kind=kOutput, calls=%fused_computation.30 | convolution fusion | flops 4834721792 | bytes 24379396 | tf_op jit(solution)/shard_map/ltd,lfd->tf/dot_general | solution.py:159
  225.9 1.4 fusion.46
  227.3 2.2 slice_bitcast_fusion.3
  229.5 2.9 %copy.67 = f32[2,2,2,64,576]{4,3,2,1,0:T(8,128)} copy(f32[2,2,2,64,576]{3,4,0,2,1:T(8,128)} %get-tuple-element.8) | data formatting | bytes 2359296 | tf_op jit(solution)/shard_map/transpose | solution.py:61
  232.4 2.0 constant_dynamic-slice_fusion.5
  234.6 1.8 copy.68
  236.4 1.2 constant_dynamic-slice_fusion.2
  239.9 1.7 collective-permute-start.27
  241.7 1.2 collective-permute-start.30
  242.9 6.9 %collective-permute-done.27 = f32[2,64,576]{2,1,0:T(8,128)S(1)} collective-permute-done((f32[2,64,576]{2,1,0:T(8,128)S(1)}, f32[2,64,576]{2,1,0:T(8,128)S(1)}, u32[]{:S(2)}, u32[]{:S(2)}) %collective-permute-start.27) | collective-permute-done | bytes 294944 | tf_op jit(solution)/shard_map/ppermute | solution.py:70
  249.8 1.2 collective-permute-start.28
  251.3 1.4 collective-permute-start.31
  252.7 2.5 collective-permute-done.28
  255.3 1.4 collective-permute-done.31
  (112 shorter events, 18.3 us)
Async XLA Ops:
  0.6 6.1 %copy-start = (s32[4,256,64]{1,2,0:T(8,128)S(1)}, s32[4,256,64]{1,2,0:T(8,128)}, u32[]{:S(2)}) copy-start(s32[4,256,64]{1,2,0:T(8,128)} %param.12) | copy-start | bytes 786436
  1.9 5.5 %collective-permute-start = (bf16[1,64,576]{2,1,0:T(8,128)(2,1)S(1)}, bf16[1,64,576]{2,1,0:T(8,128)(2,1)S(1)}, u32[]{:S(2)}, u32[]{:S(2)}) collective-permute-start(bf16[1,64,576]{2,1,0:T(8,128)(2,1)S(1)} %copy.71), channel_id=1, source_target_pairs={{0,2},{1,3},{2,0},{3,1},{4,6},{5,7},{6,4},{7,5},{8,10},{9,11},{10,... | collective-permute-start | bytes 221192 | tf_op jit(solution)/shard_map/ppermute | solution.py:92
  5.1 4.7 %collective-permute-start.3 = (bf16[1,64,576]{2,1,0:T(8,128)(2,1)S(1)}, bf16[1,64,576]{2,1,0:T(8,128)(2,1)S(1)}, u32[]{:S(2)}, u32[]{:S(2)}) collective-permute-start(bf16[1,64,576]{2,1,0:T(8,128)(2,1)S(1)} %copy.72), channel_id=1, source_target_pairs={{0,4},{4,0},{1,5},{5,1},{2,6},{6,2},{3,7},{7,3},{8,12},{12,8},{9,1... | collective-permute-start | bytes 221192 | tf_op jit(solution)/shard_map/ppermute | solution.py:92
  7.5 5.7 %collective-permute-start.1 = (bf16[2,64,576]{2,1,0:T(8,128)(2,1)S(1)}, bf16[2,64,576]{2,1,0:T(8,128)(2,1)S(1)}, u32[]{:S(2)}, u32[]{:S(2)}) collective-permute-start(bf16[2,64,576]{2,1,0:T(8,128)(2,1)S(1)} %maximum_select_fusion.12), channel_id=1, source_target_pairs={{0,4},{4,0},{1,5},{5,1},{2,6},{6,2},{3,7},{7,3},{8,12},{12,8},{9,1... | collective-permute-start | bytes 442376 | tf_op jit(solution)/shard_map/ppermute | solution.py:92
  9.9 5.4 %collective-permute-start.4 = (bf16[2,64,576]{2,1,0:T(8,128)(2,1)S(1)}, bf16[2,64,576]{2,1,0:T(8,128)(2,1)S(1)}, u32[]{:S(2)}, u32[]{:S(2)}) collective-permute-start(bf16[2,64,576]{2,1,0:T(8,128)(2,1)S(1)} %maximum_select_fusion.13), channel_id=1, source_target_pairs={{0,2},{1,3},{2,0},{3,1},{4,6},{5,7},{6,4},{7,5},{8,10},{9,11},{10,... | collective-permute-start | bytes 442376 | tf_op jit(solution)/shard_map/ppermute | solution.py:92
  13.2 11.7 %collective-permute-start.2 = (bf16[4,64,576]{2,1,0:T(8,128)(2,1)S(1)}, bf16[4,64,576]{2,1,0:T(8,128)(2,1)S(1)}, u32[]{:S(2)}, u32[]{:S(2)}) collective-permute-start(bf16[4,64,576]{2,1,0:T(8,128)(2,1)S(1)} %maximum_select_fusion.8), channel_id=1, source_target_pairs={{0,1},{1,0},{2,3},{3,2},{4,5},{5,4},{6,7},{7,6},{8,9},{9,8},{10,11... | collective-permute-start | bytes 884744 | tf_op jit(solution)/shard_map/ppermute | solution.py:92
  15.4 9.8 %collective-permute-start.5 = (bf16[4,64,576]{2,1,0:T(8,128)(2,1)S(1)}, bf16[4,64,576]{2,1,0:T(8,128)(2,1)S(1)}, u32[]{:S(2)}, u32[]{:S(2)}) collective-permute-start(bf16[4,64,576]{2,1,0:T(8,128)(2,1)S(1)} %maximum_select_fusion.9), channel_id=1, source_target_pairs={{0,1},{1,0},{2,3},{3,2},{4,5},{5,4},{6,7},{7,6},{8,9},{9,8},{10,11... | collective-permute-start | bytes 884744 | tf_op jit(solution)/shard_map/ppermute | solution.py:92
  25.4 1.2 copy-start.9
  67.6 6.7 %slice-start = ((s8[5242880]{0:T(1024)(128)(4,1)}), s8[4194304]{0:T(1024)(128)(4,1)S(1)}, s32[]{:S(2)}) async-start(s8[5242880]{0:T(1024)(128)(4,1)} %bitcast.118), calls=%async_computation | async-start | bytes 8388608
  67.6 6.7 %slice-start.1 = ((s8[5242880]{0:T(1024)(128)(4,1)}), s8[1048576]{0:T(1024)(128)(4,1)S(1)}, s32[]{:S(2)}) async-start(s8[5242880]{0:T(1024)(128)(4,1)} %bitcast.118), calls=%async_computation.1 | async-start | bytes 2097152
  70.6 3.2 %copy-start.4 = (f32[2,2,2,2,2,64,576]{6,5,4,3,2,1,0:T(8,128)}, f32[2,2,2,2,2,64,576]{6,5,4,3,2,1,0:T(8,128)S(1)}, u32[]{:S(2)}) copy-start(f32[2,2,2,2,2,64,576]{6,5,4,3,2,1,0:T(8,128)S(1)} %copy.62) | copy-start | bytes 14155780
  73.8 5.2 %collective-permute-start.6 = (f32[16,64,576]{2,1,0:T(8,128)}, f32[16,64,576]{2,1,0:T(8,128)S(1)}, u32[]{:S(2)}, u32[]{:S(2)}) collective-permute-start(f32[16,64,576]{2,1,0:T(8,128)} %constant_dynamic-slice_fusion.15), channel_id=1, source_target_pairs={{0,1},{1,0},{2,3},{3,2},{4,5},{5,4},{6,7},{7,6},{8,9},{9,8},{10,11... | collective-permute-start | bytes 7077896 | tf_op jit(solution)/shard_map/ppermute | solution.py:70
  74.8 3.2 %copy-start.2 = (f32[2,2,2,2,2,64,576]{6,5,4,3,2,1,0:T(8,128)}, f32[2,2,2,2,2,64,576]{6,5,4,3,2,1,0:T(8,128)S(1)}, u32[]{:S(2)}) copy-start(f32[2,2,2,2,2,64,576]{6,5,4,3,2,1,0:T(8,128)S(1)} %copy.63) | copy-start | bytes 14155780
  78.0 6.0 %collective-permute-start.11 = (f32[16,64,576]{2,1,0:T(8,128)}, f32[16,64,576]{2,1,0:T(8,128)}, u32[]{:S(2)}, u32[]{:S(2)}) collective-permute-start(f32[16,64,576]{2,1,0:T(8,128)} %constant_dynamic-slice_fusion.10), channel_id=1, source_target_pairs={{0,1},{1,0},{2,3},{3,2},{4,5},{5,4},{6,7},{7,6},{8,9},{9,8},{10,11... | collective-permute-start | bytes 7077896 | tf_op jit(solution)/shard_map/ppermute | solution.py:70
  79.0 5.0 %copy-start.3 = (f32[2,2,2,2,2,64,576]{6,5,4,3,2,1,0:T(8,128)S(1)}, f32[2,2,2,2,2,64,576]{6,5,4,3,2,1,0:T(8,128)}, u32[]{:S(2)}) copy-start(f32[2,2,2,2,2,64,576]{6,5,4,3,2,1,0:T(8,128)} %copy-done.2) | copy-start | bytes 14155780
  81.2 5.0 %copy-start.5 = (f32[16,64,576]{2,1,0:T(8,128)}, f32[16,64,576]{2,1,0:T(8,128)S(1)}, u32[]{:S(2)}) copy-start(f32[16,64,576]{2,1,0:T(8,128)S(1)} %dynamic-slice_add_fusion.1) | copy-start | bytes 7077892
  82.3 31.4 %collective-permute-start.7 = (f32[8,64,576]{2,1,0:T(8,128)}, f32[8,64,576]{2,1,0:T(8,128)}, u32[]{:S(2)}, u32[]{:S(2)}) collective-permute-start(f32[8,64,576]{2,1,0:T(8,128)} %constant_dynamic-slice_fusion.14), channel_id=1, source_target_pairs={{0,8},{8,0},{16,24},{24,16},{1,9},{9,1},{17,25},{25,17},{2,10},{10... | collective-permute-start | bytes 3538952 | tf_op jit(solution)/shard_map/ppermute | solution.py:70
  87.3 31.6 %collective-permute-start.12 = (f32[8,64,576]{2,1,0:T(8,128)}, f32[8,64,576]{2,1,0:T(8,128)}, u32[]{:S(2)}, u32[]{:S(2)}) collective-permute-start(f32[8,64,576]{2,1,0:T(8,128)} %constant_dynamic-slice_fusion.9), channel_id=1, source_target_pairs={{0,4},{4,0},{1,5},{5,1},{2,6},{6,2},{3,7},{7,3},{8,12},{12,8},{9,1... | collective-permute-start | bytes 3538952 | tf_op jit(solution)/shard_map/ppermute | solution.py:70
  115.6 5.8 %copy-start.7 = (bf16[4,32,576]{2,1,0:T(8,128)(2,1)S(1)}, bf16[4,32,576]{2,1,0:T(8,128)(2,1)}, u32[]{:S(2)}) copy-start(bf16[4,32,576]{2,1,0:T(8,128)(2,1)} %param.13) | copy-start | bytes 442372
  115.6 16.7 %collective-permute-start.8 = (f32[4,64,576]{2,1,0:T(8,128)S(1)}, f32[4,64,576]{2,1,0:T(8,128)S(1)}, u32[]{:S(2)}, u32[]{:S(2)}) collective-permute-start(f32[4,64,576]{2,1,0:T(8,128)S(1)} %constant_dynamic-slice_fusion.13), channel_id=1, source_target_pairs={{0,4},{4,0},{1,5},{5,1},{2,6},{6,2},{3,7},{7,3},{8,12},{12,8},{9,1... | collective-permute-start | bytes 1769480 | tf_op jit(solution)/shard_map/ppermute | solution.py:70
  120.4 17.0 %collective-permute-start.13 = (f32[4,64,576]{2,1,0:T(8,128)S(1)}, f32[4,64,576]{2,1,0:T(8,128)S(1)}, u32[]{:S(2)}, u32[]{:S(2)}) collective-permute-start(f32[4,64,576]{2,1,0:T(8,128)S(1)} %constant_dynamic-slice_fusion.8), channel_id=1, source_target_pairs={{0,2},{1,3},{2,0},{3,1},{4,6},{5,7},{6,4},{7,5},{8,10},{9,11},{10,... | collective-permute-start | bytes 1769480 | tf_op jit(solution)/shard_map/ppermute | solution.py:70
  132.5 16.5 %copy-start.8 = (f32[4,576]{1,0:T(4,128)S(1)}, f32[4,576]{1,0:T(4,128)}, u32[]{:S(2)}) copy-start(f32[4,576]{1,0:T(4,128)} %param.11) | copy-start | bytes 27652
  132.5 10.4 %collective-permute-start.9 = (f32[2,64,576]{2,1,0:T(8,128)S(1)}, f32[2,64,576]{2,1,0:T(8,128)S(1)}, u32[]{:S(2)}, u32[]{:S(2)}) collective-permute-start(f32[2,64,576]{2,1,0:T(8,128)S(1)} %constant_dynamic-slice_fusion.12), channel_id=1, source_target_pairs={{0,2},{1,3},{2,0},{3,1},{4,6},{5,7},{6,4},{7,5},{8,10},{9,11},{10,... | collective-permute-start | bytes 884744 | tf_op jit(solution)/shard_map/ppermute | solution.py:70
  137.6 8.0 %collective-permute-start.14 = (f32[2,64,576]{2,1,0:T(8,128)S(1)}, f32[2,64,576]{2,1,0:T(8,128)S(1)}, u32[]{:S(2)}, u32[]{:S(2)}) collective-permute-start(f32[2,64,576]{2,1,0:T(8,128)S(1)} %constant_dynamic-slice_fusion.7), channel_id=1, source_target_pairs={{0,8},{8,0},{16,24},{24,16},{1,9},{9,1},{17,25},{25,17},{2,10},{10... | collective-permute-start | bytes 884744 | tf_op jit(solution)/shard_map/ppermute | solution.py:70
  143.0 14.0 %collective-permute-start.10 = (f32[1,64,576]{2,1,0:T(8,128)S(1)}, f32[1,64,576]{2,1,0:T(8,128)S(1)}, u32[]{:S(2)}, u32[]{:S(2)}) collective-permute-start(f32[1,64,576]{2,1,0:T(8,128)S(1)} %constant_dynamic-slice_fusion.11), channel_id=1, source_target_pairs={{0,16},{8,24},{16,0},{24,8},{1,17},{9,25},{17,1},{25,9},{2,18},{10... | collective-permute-start | bytes 442376 | tf_op jit(solution)/shard_map/ppermute | solution.py:70
  145.7 16.1 %collective-permute-start.15 = (f32[1,64,576]{2,1,0:T(8,128)S(1)}, f32[1,64,576]{2,1,0:T(8,128)S(1)}, u32[]{:S(2)}, u32[]{:S(2)}) collective-permute-start(f32[1,64,576]{2,1,0:T(8,128)S(1)} %constant_dynamic-slice_fusion.6), channel_id=1, source_target_pairs={{0,16},{8,24},{16,0},{24,8},{1,17},{9,25},{17,1},{25,9},{2,18},{10... | collective-permute-start | bytes 442376 | tf_op jit(solution)/shard_map/ppermute | solution.py:70
  157.0 7.4 %collective-permute-start.16 = (bf16[1,64,576]{2,1,0:T(8,128)(2,1)S(1)}, bf16[1,64,576]{2,1,0:T(8,128)(2,1)S(1)}, u32[]{:S(2)}, u32[]{:S(2)}) collective-permute-start(bf16[1,64,576]{2,1,0:T(8,128)(2,1)S(1)} %bitcast.139), channel_id=1, source_target_pairs={{0,16},{8,24},{16,0},{24,8},{1,17},{9,25},{17,1},{25,9},{2,18},{10... | collective-permute-start | bytes 221192 | tf_op jit(solution)/shard_map/ppermute | solution.py:92
  161.8 6.4 %collective-permute-start.21 = (bf16[1,64,576]{2,1,0:T(8,128)(2,1)S(1)}, bf16[1,64,576]{2,1,0:T(8,128)(2,1)S(1)}, u32[]{:S(2)}, u32[]{:S(2)}) collective-permute-start(bf16[1,64,576]{2,1,0:T(8,128)(2,1)S(1)} %bitcast.141), channel_id=1, source_target_pairs={{0,16},{8,24},{16,0},{24,8},{1,17},{9,25},{17,1},{25,9},{2,18},{10... | collective-permute-start | bytes 221192 | tf_op jit(solution)/shard_map/ppermute | solution.py:92
  164.4 5.4 %collective-permute-start.17 = (bf16[2,64,576]{2,1,0:T(8,128)(2,1)S(1)}, bf16[2,64,576]{2,1,0:T(8,128)(2,1)S(1)}, u32[]{:S(2)}, u32[]{:S(2)}) collective-permute-start(bf16[2,64,576]{2,1,0:T(8,128)(2,1)S(1)} %maximum_select_fusion.14), channel_id=1, source_target_pairs={{0,2},{1,3},{2,0},{3,1},{4,6},{5,7},{6,4},{7,5},{8,10},{9,11},{10,... | collective-permute-start | bytes 442376 | tf_op jit(solution)/shard_map/ppermute | solution.py:92
  168.2 5.4 %collective-permute-start.22 = (bf16[2,64,576]{2,1,0:T(8,128)(2,1)S(1)}, bf16[2,64,576]{2,1,0:T(8,128)(2,1)S(1)}, u32[]{:S(2)}, u32[]{:S(2)}) collective-permute-start(bf16[2,64,576]{2,1,0:T(8,128)(2,1)S(1)} %maximum_select_fusion.15), channel_id=1, source_target_pairs={{0,8},{8,0},{16,24},{24,16},{1,9},{9,1},{17,25},{25,17},{2,10},{10... | collective-permute-start | bytes 442376 | tf_op jit(solution)/shard_map/ppermute | solution.py:92
  169.9 7.1 %collective-permute-start.18 = (bf16[4,64,576]{2,1,0:T(8,128)(2,1)S(1)}, bf16[4,64,576]{2,1,0:T(8,128)(2,1)S(1)}, u32[]{:S(2)}, u32[]{:S(2)}) collective-permute-start(bf16[4,64,576]{2,1,0:T(8,128)(2,1)S(1)} %maximum_select_fusion.10), channel_id=1, source_target_pairs={{0,4},{4,0},{1,5},{5,1},{2,6},{6,2},{3,7},{7,3},{8,12},{12,8},{9,1... | collective-permute-start | bytes 884744 | tf_op jit(solution)/shard_map/ppermute | solution.py:92
  173.7 7.1 %collective-permute-start.23 = (bf16[4,64,576]{2,1,0:T(8,128)(2,1)S(1)}, bf16[4,64,576]{2,1,0:T(8,128)(2,1)S(1)}, u32[]{:S(2)}, u32[]{:S(2)}) collective-permute-start(bf16[4,64,576]{2,1,0:T(8,128)(2,1)S(1)} %maximum_select_fusion.11), channel_id=1, source_target_pairs={{0,2},{1,3},{2,0},{3,1},{4,6},{5,7},{6,4},{7,5},{8,10},{9,11},{10,... | collective-permute-start | bytes 884744 | tf_op jit(solution)/shard_map/ppermute | solution.py:92
  177.2 11.9 %collective-permute-start.19 = (bf16[8,64,576]{2,1,0:T(8,128)(2,1)S(1)}, bf16[8,64,576]{2,1,0:T(8,128)(2,1)S(1)}, u32[]{:S(2)}, u32[]{:S(2)}) collective-permute-start(bf16[8,64,576]{2,1,0:T(8,128)(2,1)S(1)} %maximum_select_fusion.6), channel_id=1, source_target_pairs={{0,8},{8,0},{16,24},{24,16},{1,9},{9,1},{17,25},{25,17},{2,10},{10... | collective-permute-start | bytes 1769480 | tf_op jit(solution)/shard_map/ppermute | solution.py:92
  181.0 11.3 %collective-permute-start.24 = (bf16[8,64,576]{2,1,0:T(8,128)(2,1)S(1)}, bf16[8,64,576]{2,1,0:T(8,128)(2,1)S(1)}, u32[]{:S(2)}, u32[]{:S(2)}) collective-permute-start(bf16[8,64,576]{2,1,0:T(8,128)(2,1)S(1)} %maximum_select_fusion.7), channel_id=1, source_target_pairs={{0,4},{4,0},{1,5},{5,1},{2,6},{6,2},{3,7},{7,3},{8,12},{12,8},{9,1... | collective-permute-start | bytes 1769480 | tf_op jit(solution)/shard_map/ppermute | solution.py:92
  189.4 3.3 %collective-permute-start.20 = (bf16[16,64,576]{2,1,0:T(8,128)(2,1)S(1)}, bf16[16,64,576]{2,1,0:T(8,128)(2,1)}, u32[]{:S(2)}, u32[]{:S(2)}) collective-permute-start(bf16[16,64,576]{2,1,0:T(8,128)(2,1)S(1)} %maximum_select_fusion.2), channel_id=1, source_target_pairs={{0,1},{1,0},{2,3},{3,2},{4,5},{5,4},{6,7},{7,6},{8,9},{9,8},{10,11... | collective-permute-start | bytes 3538952 | tf_op jit(solution)/shard_map/ppermute | solution.py:92
  192.6 3.2 %collective-permute-start.25 = (bf16[16,64,576]{2,1,0:T(8,128)(2,1)S(1)}, bf16[16,64,576]{2,1,0:T(8,128)(2,1)}, u32[]{:S(2)}, u32[]{:S(2)}) collective-permute-start(bf16[16,64,576]{2,1,0:T(8,128)(2,1)S(1)} %maximum_select_fusion.3), channel_id=1, source_target_pairs={{0,1},{1,0},{2,3},{3,2},{4,5},{5,4},{6,7},{7,6},{8,9},{9,8},{10,11... | collective-permute-start | bytes 3538952 | tf_op jit(solution)/shard_map/ppermute | solution.py:92
  205.5 20.4 %slice-start.2 = ((s8[4718592]{0:T(1024)(128)(4,1)}), s8[524288]{0:T(1024)(128)(4,1)S(1)}, s32[]{:S(2)}) async-start(s8[4718592]{0:T(1024)(128)(4,1)} %bitcast.144), calls=%async_computation.2 | async-start | bytes 1048576
  215.4 10.5 %slice-start.3 = ((s8[4718592]{0:T(1024)(128)(4,1)}), s8[4194304]{0:T(1024)(128)(4,1)S(1)}, s32[]{:S(2)}) async-start(s8[4718592]{0:T(1024)(128)(4,1)} %bitcast.144), calls=%async_computation.3 | async-start | bytes 8388608
  234.4 4.3 %collective-permute-start.26 = (f32[4,64,576]{2,1,0:T(8,128)}, f32[4,64,576]{2,1,0:T(8,128)S(1)}, u32[]{:S(2)}, u32[]{:S(2)}) collective-permute-start(f32[4,64,576]{2,1,0:T(8,128)} %constant_dynamic-slice_fusion.5), channel_id=1, source_target_pairs={{0,1},{1,0},{2,3},{3,2},{4,5},{5,4},{6,7},{7,6},{8,9},{9,8},{10,11... | collective-permute-start | bytes 1769480 | tf_op jit(solution)/shard_map/ppermute | solution.py:70
  236.4 5.2 %copy-start.6 = (f32[2,2,2,64,576]{4,3,2,1,0:T(8,128)S(1)}, f32[2,2,2,64,576]{4,3,2,1,0:T(8,128)}, u32[]{:S(2)}) copy-start(f32[2,2,2,64,576]{4,3,2,1,0:T(8,128)} %copy.68) | copy-start | bytes 3538948
  237.6 4.0 %collective-permute-start.29 = (f32[4,64,576]{2,1,0:T(8,128)S(1)}, f32[4,64,576]{2,1,0:T(8,128)S(1)}, u32[]{:S(2)}, u32[]{:S(2)}) collective-permute-start(f32[4,64,576]{2,1,0:T(8,128)S(1)} %constant_dynamic-slice_fusion.2), channel_id=1, source_target_pairs={{0,1},{1,0},{2,3},{3,2},{4,5},{5,4},{6,7},{7,6},{8,9},{9,8},{10,11... | collective-permute-start | bytes 1769480 | tf_op jit(solution)/shard_map/ppermute | solution.py:70
  239.9 9.8 %collective-permute-start.27 = (f32[2,64,576]{2,1,0:T(8,128)S(1)}, f32[2,64,576]{2,1,0:T(8,128)S(1)}, u32[]{:S(2)}, u32[]{:S(2)}) collective-permute-start(f32[2,64,576]{2,1,0:T(8,128)S(1)} %constant_dynamic-slice_fusion.4), channel_id=1, source_target_pairs={{0,4},{4,0},{1,5},{5,1},{2,6},{6,2},{3,7},{7,3},{8,12},{12,8},{9,1... | collective-permute-start | bytes 884744 | tf_op jit(solution)/shard_map/ppermute | solution.py:70
  241.6 16.0 %copy-start.1 = (s32[4,256,64]{1,2,0:T(8,128)S(1)}, s32[4,256,64]{1,2,0:T(8,128)}, u32[]{:S(2)}) copy-start(s32[4,256,64]{1,2,0:T(8,128)} %param.12) | copy-start | bytes 786436
  241.7 9.5 %collective-permute-start.30 = (f32[2,64,576]{2,1,0:T(8,128)S(1)}, f32[2,64,576]{2,1,0:T(8,128)S(1)}, u32[]{:S(2)}, u32[]{:S(2)}) collective-permute-start(f32[2,64,576]{2,1,0:T(8,128)S(1)} %constant_dynamic-slice_fusion.1), channel_id=1, source_target_pairs={{0,2},{1,3},{2,0},{3,1},{4,6},{5,7},{6,4},{7,5},{8,10},{9,11},{10,... | collective-permute-start | bytes 884744 | tf_op jit(solution)/shard_map/ppermute | solution.py:70
  249.8 5.5 %collective-permute-start.28 = (f32[1,64,576]{2,1,0:T(8,128)S(1)}, f32[1,64,576]{2,1,0:T(8,128)S(1)}, u32[]{:S(2)}, u32[]{:S(2)}) collective-permute-start(f32[1,64,576]{2,1,0:T(8,128)S(1)} %constant_dynamic-slice_fusion.3), channel_id=1, source_target_pairs={{0,2},{1,3},{2,0},{3,1},{4,6},{5,7},{6,4},{7,5},{8,10},{9,11},{10,... | collective-permute-start | bytes 442376 | tf_op jit(solution)/shard_map/ppermute | solution.py:70
  251.3 5.4 %collective-permute-start.31 = (f32[1,64,576]{2,1,0:T(8,128)S(1)}, f32[1,64,576]{2,1,0:T(8,128)S(1)}, u32[]{:S(2)}, u32[]{:S(2)}) collective-permute-start(f32[1,64,576]{2,1,0:T(8,128)S(1)} %constant_dynamic-slice_fusion), channel_id=1, source_target_pairs={{0,4},{4,0},{1,5},{5,1},{2,6},{6,2},{3,7},{7,3},{8,12},{12,8},{9,1... | collective-permute-start | bytes 442376 | tf_op jit(solution)/shard_map/ppermute | solution.py:70

commit v13 on v9

--- a/solution.py
+++ b/solution.py
@@ -123,11 +123,14 @@
     )
     pre = jnp.dot(tokens_all, encoder[0], preferred_element_type=jnp.float32) + encoder_bias[0]
     first_feat = half_bit * (feat_total // 2) + feat_pos * feat_dev
-    feat_ids = first_feat + lax.iota(jnp.int32, feat_dev)
     layer_index = lax.dynamic_index_in_dim(topk_index, layer_id, 0, keepdims=False)
-    selected = jnp.any(layer_index[:, :, None] == feat_ids[None, None, :], axis=1).astype(
-        jnp.float32
-    )
+    local_ids = layer_index - first_feat
+    low_bits = (feat_dev.bit_length() - 1) // 2
+    side = 1 << low_bits
+    high_hot = ((local_ids >> low_bits)[:, :, None] == lax.iota(jnp.int32, feat_dev // side)).astype(jnp.bfloat16)
+    low_hot = ((local_ids & (side - 1))[:, :, None] == lax.iota(jnp.int32, side)).astype(jnp.bfloat16)
+    selected = jnp.einsum("tka,tkb->tab", high_hot, low_hot, preferred_element_type=jnp.float32)
+    selected = selected.reshape(tokens, feat_dev)
     acts = (selected * pre).astype(jnp.bfloat16)
     live_layers = lax.iota(jnp.int32, layer_count) >= layer_id
     partial_value = jnp.einsum("tf,lfd->ltd", acts, decoder[0], preferred_element_type=jnp.float32)

time: 244 us -> 240 us (0.984)
  waiting for transfers between devices: 73.7 us -> 59.9 us
  starting transfers between devices: 46.3 us -> 59.1 us
  other arithmetic: 30.1 us -> 18.8 us
  matrix products: 29.6 us -> 34.9 us
  local copies, waits for them, and re-layouts: 61.9 us -> 64.7 us
    reduce_or x1 -> x0, other arithmetic: 9.43 us -> none  [local(): jnp.any(layer_index[:, :, None] == feat_ids[None, None, :], axis=1)]
    ppermute x21, starting transfers between devices: 23.3 us -> 31.5 us  [all_gather(): recv = lax.ppermute(parts[p], axis, partner(axis, bit))]
    ppermute x21, waiting for transfers between devices: 24.4 us -> 16.8 us  [all_gather(): recv = lax.ppermute(parts[p], axis, partner(axis, bit))]
    ppermute x21, waiting for transfers between devices: 49.3 us -> 43.1 us  [reduce_scatter(): recv = lax.ppermute(send.astype(wire), axis, partner(axis, bit))]
    ppermute x21, starting transfers between devices: 23 us -> 27.6 us  [reduce_scatter(): recv = lax.ppermute(send.astype(wire), axis, partner(axis, bit))]
    dot_general x0 -> x1, matrix products: none -> 3.54 us  [local(): jnp.einsum('tka,tkb->tab', high_hot, low_hot, preferred_element_type=jnp....]
    dot_general x0 -> x1, local copies, waits for them, and re-layouts: none -> 3.51 us  [local(): jnp.einsum('tka,tkb->tab', high_hot, low_hot, preferred_element_type=jnp....]
  transfers between devices with their start and end apart: 42 -> 42, of which waited for: 19 -> 20; matrix products, arithmetic and copies ran while one was open for 16% -> 14% of each run, Pallas kernels for 0% -> 0%
where the time goes in v13:
time: 240 us; the launch traced here: 239 us
  local copies, waits for them, and re-layouts  64.7 us (27%)
  waiting for transfers between devices  59.9 us (25%)
  starting transfers between devices  59.1 us (25%)
  matrix products  34.9 us (15%)
  other arithmetic  18.8 us (8%)
    ppermute x21, waiting for transfers between devices, reduce_scatter(): recv = lax.ppermute(send.astype(wire), axis, partner(axis, bit))  43.1 us
    ppermute x21, starting transfers between devices, all_gather(): recv = lax.ppermute(parts[p], axis, partner(axis, bit))  31.5 us
    ppermute x21, starting transfers between devices, reduce_scatter(): recv = lax.ppermute(send.astype(wire), axis, partner(axis, bit))  27.6 us
    reshape x2, local copies, waits for them, and re-layouts, local(): partial_value.reshape(layer_count, slots, slot_rows, feat_parts, cols)  18.7 us
    ppermute x21, waiting for transfers between devices, all_gather(): recv = lax.ppermute(parts[p], axis, partner(axis, bit))  16.8 us
    dot_general x1, matrix products, local(): jnp.einsum('tf,lfd->ltd', acts, decoder[0], preferred_element_type=jnp.fl...  13.9 us
    dynamic_slice x21, local copies, waits for them, and re-layouts, reduce_scatter(): send = lax.dynamic_slice_in_dim(parts[p], (1 - own) * half, half, 0)  10.6 us
    dot_general x1, matrix products, local(): jnp.einsum('ltd,lfd->tf', kept, decoder[0], preferred_element_type=jnp.fl...  10.4 us
  transfers between devices with their start and end apart: 42, of which 20 were waited for; matrix products, arithmetic and copies ran while one was open for 14% of the time, Pallas kernels for 0%

profile of v13, /device:TPU:0, one launch (start us, length us, event | category | flops | bytes accessed | tf_op | source)
XLA Modules:
  0.0 238.7 jit_solution(524393904229668351)
XLA Ops:
  0.6 1.1 fusion.47
  1.9 3.1 %collective-permute-start = (bf16[1,64,576]{2,1,0:T(8,128)(2,1)S(1)}, bf16[1,64,576]{2,1,0:T(8,128)(2,1)S(1)}, u32[]{:S(2)}, u32[]{:S(2)}) collective-permute-start(bf16[1,64,576]{2,1,0:T(8,128)(2,1)S(1)} %copy.66), channel_id=1, source_target_pairs={{0,2},{1,3},{2,0},{3,1},{4,6},{5,7},{6,4},{7,5},{8,10},{9,11},{10,... | collective-permute-start | bytes 221192 | tf_op jit(solution)/shard_map/ppermute | solution.py:92
  5.1 1.6 collective-permute-start.3
  7.4 2.0 collective-permute-start.1
  9.9 1.2 collective-permute-start.4
  13.3 2.0 collective-permute-done.4
  15.4 3.5 %fusion.10 = f32[256,32,32]{2,1,0:T(8,128)} fusion(s32[256,64]{1,0:T(8,128)S(1)} %copy.45, s32[256,64]{1,0:T(8,128)S(1)} %copy.44), kind=kOutput, calls=%fused_computation.12 | convolution fusion | flops 34603008 | bytes 1179648 | tf_op jit(solution)/shard_map/tka,tkb->tab/dot_general | solution.py:132
  18.9 3.5 %copy.46 = f32[256,32,32]{0,2,1:T(8,128)S(1)} copy(f32[256,32,32]{2,1,0:T(8,128)} %fusion.10) | data formatting | bytes 2097152 | tf_op jit(solution)/shard_map/tka,tkb->tab/dot_general | solution.py:132
  24.5 3.8 %fusion.38 = bf16[256,1024,1]{1,0,2:T(8,128)(2,1)S(1)} fusion(f32[256,1024]{1,0:T(8,128)S(1)} %copy.52, bf16[1,2304,1024]{2,1,0:T(8,128)(2,1)} %param.8, bf16[288,8,2,128]{3,2,1,0:T(2,128)(2,1)S(1)} %bitcast.145, f32[1024]{0:T(1024)S(1)} %bitcast.154), kind=kOutput, calls=%fused_computation.34 | convolution fusion | flops 1208745984 | bytes 7475200 | tf_op jit(solution)/shard_map/dot_general | solution.py:124
  28.3 13.9 %select_bitcast_fusion = f32[4,256,2304]{2,1,0:T(8,128)} fusion(bf16[256,1024,1]{1,0,2:T(8,128)(2,1)S(1)} %fusion.38, bf16[1,4,1024,2304]{3,2,1,0:T(8,128)(2,1)} %param.10, pred[4]{0:T(512)(128)(4,1)S(1)} %iota_compare_fusion.4), kind=kOutput, calls=%fused_computation.4 | convolution fusion | flops 4834197504 | bytes 28835844 | tf_op jit(solution)/shard_map/tf,lfd->ltd/dot_general | solution.py:136
  42.2 13.2 %reshape.140 = f32[4,8,32,4,576]{4,3,2,1,0:T(4,128)} reshape(f32[4,256,2304]{2,1,0:T(8,128)} %select_bitcast_fusion) | data formatting | bytes 18874368 | tf_op jit(solution)/shard_map/reshape | solution.py:139
  55.3 5.5 %copy.53 = f32[4,8,32,4,576]{4,2,0,3,1:T(8,128)S(1)} copy(f32[4,8,32,4,576]{4,3,2,1,0:T(4,128)} %reshape.140) | data formatting | bytes 18874368 | tf_op jit(solution)/shard_map/reshape | solution.py:139
  61.9 1.4 constant_dynamic-slice_fusion.10
  65.7 1.6 constant_dynamic-slice_fusion.15
  67.9 1.4 constant_dynamic-slice_fusion.20
  69.3 2.1 dynamic-slice_add_fusion.1
  71.5 1.2 collective-permute-start.17
  72.7 1.6 dynamic-slice_add_fusion.2
  75.2 1.8 dynamic-slice_add_fusion
  77.0 1.0 constant_dynamic-slice_fusion.19
  78.1 1.6 collective-permute-start.7
  79.7 12.5 %collective-permute-done.17 = f32[8,40,576]{2,1,0:T(8,128)S(1)} collective-permute-done((f32[8,40,576]{2,1,0:T(8,128)S(1)}, f32[8,40,576]{2,1,0:T(8,128)S(1)}, u32[]{:S(2)}, u32[]{:S(2)}) %collective-permute-start.17) | collective-permute-done | bytes 737312 | tf_op jit(solution)/shard_map/ppermute | solution.py:70
  93.1 1.7 collective-permute-start.18
  97.8 13.0 %collective-permute-done.18 = f32[4,40,576]{2,1,0:T(8,128)S(1)} collective-permute-done((f32[4,40,576]{2,1,0:T(8,128)}, f32[4,40,576]{2,1,0:T(8,128)S(1)}, u32[]{:S(2)}, u32[]{:S(2)}) %collective-permute-start.18) | collective-permute-done | bytes 368672 | tf_op jit(solution)/shard_map/ppermute | solution.py:70
  110.9 1.4 collective-permute-start.19
  112.3 1.2 dynamic-slice_add_fusion.10
  113.5 1.7 collective-permute-start.14
  115.3 1.3 dynamic-slice_add_fusion.3
  117.3 2.7 %collective-permute-start.20 = (f32[1,40,576]{2,1,0:T(8,128)S(1)}, f32[1,40,576]{2,1,0:T(8,128)S(1)}, u32[]{:S(2)}, u32[]{:S(2)}) collective-permute-start(f32[1,40,576]{2,1,0:T(8,128)S(1)} %constant_dynamic-slice_fusion.6), channel_id=1, source_target_pairs={{0,16},{8,24},{16,0},{24,8},{1,17},{9,25},{17,1},{25,9},{2,18},{10... | collective-permute-start | bytes 276488 | tf_op jit(solution)/shard_map/ppermute | solution.py:70
  120.7 3.1 %collective-permute-start.15 = (f32[1,40,576]{2,1,0:T(8,128)S(1)}, f32[1,40,576]{2,1,0:T(8,128)S(1)}, u32[]{:S(2)}, u32[]{:S(2)}) collective-permute-start(f32[1,40,576]{2,1,0:T(8,128)S(1)} %constant_dynamic-slice_fusion.11), channel_id=1, source_target_pairs={{0,16},{8,24},{16,0},{24,8},{1,17},{9,25},{17,1},{25,9},{2,18},{10... | collective-permute-start | bytes 276488 | tf_op jit(solution)/shard_map/ppermute | solution.py:70
  123.8 4.8 %collective-permute-done.8 = f32[4,48,576]{2,1,0:T(8,128)S(1)} collective-permute-done((f32[4,48,576]{2,1,0:T(8,128)S(1)}, f32[4,48,576]{2,1,0:T(8,128)S(1)}, u32[]{:S(2)}, u32[]{:S(2)}) %collective-permute-start.8) | collective-permute-done | bytes 442400 | tf_op jit(solution)/shard_map/ppermute | solution.py:70
  129.9 2.7 %collective-permute-start.26 = (bf16[1,40,576]{2,1,0:T(8,128)(2,1)S(1)}, bf16[1,40,576]{2,1,0:T(8,128)(2,1)S(1)}, u32[]{:S(2)}, u32[]{:S(2)}) collective-permute-start(bf16[1,40,576]{2,1,0:T(8,128)(2,1)S(1)} %bitcast.148), channel_id=1, source_target_pairs={{0,16},{8,24},{16,0},{24,8},{1,17},{9,25},{17,1},{25,9},{2,18},{10... | collective-permute-start | bytes 138248 | tf_op jit(solution)/shard_map/ppermute | solution.py:92
  132.8 3.2 %collective-permute-done.26 = bf16[1,40,576]{2,1,0:T(8,128)(2,1)S(1)} collective-permute-done((bf16[1,40,576]{2,1,0:T(8,128)(2,1)S(1)}, bf16[1,40,576]{2,1,0:T(8,128)(2,1)S(1)}, u32[]{:S(2)}, u32[]{:S(2)}) %collective-permute-start.26) | collective-permute-done | bytes 46112 | tf_op jit(solution)/shard_map/ppermute | solution.py:92
  136.5 2.7 %collective-permute-start.10 = (f32[1,48,576]{2,1,0:T(8,128)S(1)}, f32[1,48,576]{2,1,0:T(8,128)S(1)}, u32[]{:S(2)}, u32[]{:S(2)}) collective-permute-start(f32[1,48,576]{2,1,0:T(8,128)S(1)} %constant_dynamic-slice_fusion.16), channel_id=1, source_target_pairs={{0,16},{8,24},{16,0},{24,8},{1,17},{9,25},{17,1},{25,9},{2,18},{10... | collective-permute-start | bytes 331784 | tf_op jit(solution)/shard_map/ppermute | solution.py:70
  139.2 1.6 collective-permute-start.32
  140.8 1.5 collective-permute-done.10
  142.4 2.8 %collective-permute-start.21 = (bf16[1,48,576]{2,1,0:T(8,128)(2,1)S(1)}, bf16[1,48,576]{2,1,0:T(8,128)(2,1)S(1)}, u32[]{:S(2)}, u32[]{:S(2)}) collective-permute-start(bf16[1,48,576]{2,1,0:T(8,128)(2,1)S(1)} %bitcast.146), channel_id=1, source_target_pairs={{0,16},{8,24},{16,0},{24,8},{1,17},{9,25},{17,1},{25,9},{2,18},{10... | collective-permute-start | bytes 165896 | tf_op jit(solution)/shard_map/ppermute | solution.py:92
  145.6 2.0 collective-permute-done.21
  148.6 3.5 %collective-permute-start.33 = (bf16[4,40,576]{2,1,0:T(8,128)(2,1)S(1)}, bf16[4,40,576]{2,1,0:T(8,128)(2,1)S(1)}, u32[]{:S(2)}, u32[]{:S(2)}) collective-permute-start(bf16[4,40,576]{2,1,0:T(8,128)(2,1)S(1)} %maximum_select_fusion.15), channel_id=1, source_target_pairs={{0,8},{8,0},{16,24},{24,16},{1,9},{9,1},{17,25},{25,17},{2,10},{10... | collective-permute-start | bytes 552968 | tf_op jit(solution)/shard_map/ppermute | solution.py:92
  152.6 4.3 %collective-permute-start.23 = (bf16[4,48,576]{2,1,0:T(8,128)(2,1)S(1)}, bf16[4,48,576]{2,1,0:T(8,128)(2,1)S(1)}, u32[]{:S(2)}, u32[]{:S(2)}) collective-permute-start(bf16[4,48,576]{2,1,0:T(8,128)(2,1)S(1)} %maximum_select_fusion.13), channel_id=1, source_target_pairs={{0,4},{4,0},{1,5},{5,1},{2,6},{6,2},{3,7},{7,3},{8,12},{12,8},{9,1... | collective-permute-start | bytes 663560 | tf_op jit(solution)/shard_map/ppermute | solution.py:92
  157.3 2.5 %collective-permute-start.34 = (bf16[8,40,576]{2,1,0:T(8,128)(2,1)S(1)}, bf16[8,40,576]{2,1,0:T(8,128)(2,1)S(1)}, u32[]{:S(2)}, u32[]{:S(2)}) collective-permute-start(bf16[8,40,576]{2,1,0:T(8,128)(2,1)S(1)} %maximum_select_fusion.10), channel_id=1, source_target_pairs={{0,2},{1,3},{2,0},{3,1},{4,6},{5,7},{6,4},{7,5},{8,10},{9,11},{10,... | collective-permute-start | bytes 1105928 | tf_op jit(solution)/shard_map/ppermute | solution.py:92
  159.8 1.3 collective-permute-done.23
  161.2 3.2 %collective-permute-start.24 = (bf16[8,48,576]{2,1,0:T(8,128)(2,1)S(1)}, bf16[8,48,576]{2,1,0:T(8,128)(2,1)S(1)}, u32[]{:S(2)}, u32[]{:S(2)}) collective-permute-start(bf16[8,48,576]{2,1,0:T(8,128)(2,1)S(1)} %maximum_select_fusion.8), channel_id=1, source_target_pairs={{0,8},{8,0},{16,24},{24,16},{1,9},{9,1},{17,25},{25,17},{2,10},{10... | collective-permute-start | bytes 1327112 | tf_op jit(solution)/shard_map/ppermute | solution.py:92
  164.5 1.0 collective-permute-done.29
  166.6 4.7 %collective-permute-done.24 = bf16[8,48,576]{2,1,0:T(8,128)(2,1)S(1)} collective-permute-done((bf16[8,48,576]{2,1,0:T(8,128)(2,1)S(1)}, bf16[8,48,576]{2,1,0:T(8,128)(2,1)S(1)}, u32[]{:S(2)}, u32[]{:S(2)}) %collective-permute-start.24) | collective-permute-done | bytes 442400 | tf_op jit(solution)/shard_map/ppermute | solution.py:92
  172.2 1.8 maximum_select_fusion.2
  174.3 2.1 maximum_select_fusion
  176.6 1.1 pad_maximum_fusion
  177.7 6.4 %copy.60 = bf16[4,8,32,4,576]{4,3,2,1,0:T(4,128)(2,1)} copy(bf16[4,8,32,4,576]{4,2,0,3,1:T(8,128)(2,1)S(1)} %bitcast.120) | data formatting | bytes 9437184 | tf_op jit(solution)/shard_map/transpose | solution.py:158
  184.1 9.9 %reshape.150 = bf16[4,256,2304]{2,1,0:T(8,128)(2,1)} reshape(bf16[4,8,32,4,576]{4,3,2,1,0:T(4,128)(2,1)} %copy.60) | data formatting | bytes 9437184 | tf_op jit(solution)/shard_map/reshape | solution.py:159
  194.0 10.4 %fusion.33 = bf16[256,1024]{1,0:T(8,128)(2,1)S(1)} fusion(f32[256,1024]{1,0:T(8,128)S(1)} %copy-done.6, bf16[1,4,1024,2304]{3,2,1,0:T(8,128)(2,1)} %param.10, bf16[4,256,2304]{2,1,0:T(8,128)(2,1)} %reshape.150, pred[4]{0:T(512)(128)(4,1)S(1)} %copy-done.13), kind=kOutput, calls=%fused_computation.33 | convolution fusion | flops 4834721792 | bytes 25165828 | tf_op jit(solution)/shard_map/ltd,lfd->tf/dot_general | solution.py:162
  204.4 3.3 %fusion.48 = f32[2,128,4,576]{1,3,2,0:T(8,128)S(1)} fusion(bf16[2,128,1024,1]{2,1,3,0:T(8,128)(2,1)S(1)} %bitcast.155, bf16[4,576,1024,1]{2,1,0,3:T(8,128)(2,1)} %bitcast.153), kind=kOutput, calls=%fused_computation.109 | convolution fusion | flops 1207959552 | bytes 7602176 | tf_op jit(solution)/shard_map/dot_general | solution.py:164
  207.8 2.2 slice_bitcast_fusion.4
  209.9 2.9 %copy.62 = f32[2,2,2,64,576]{4,3,2,1,0:T(8,128)} copy(f32[2,2,2,64,576]{3,4,0,2,1:T(8,128)} %get-tuple-element.6) | data formatting | bytes 2359296 | tf_op jit(solution)/shard_map/transpose | solution.py:61
  212.8 2.0 constant_dynamic-slice_fusion.5
  215.2 1.8 copy.63
  217.0 1.2 constant_dynamic-slice_fusion.2
  219.1 1.2 dynamic-slice_add_fusion.7
  221.4 2.6 %collective-permute-start.40 = (f32[2,64,576]{2,1,0:T(8,128)S(1)}, f32[2,64,576]{2,1,0:T(8,128)S(1)}, u32[]{:S(2)}, u32[]{:S(2)}) collective-permute-start(f32[2,64,576]{2,1,0:T(8,128)S(1)} %constant_dynamic-slice_fusion.1), channel_id=1, source_target_pairs={{0,2},{1,3},{2,0},{3,1},{4,6},{5,7},{6,4},{7,5},{8,10},{9,11},{10,... | collective-permute-start | bytes 884744 | tf_op jit(solution)/shard_map/ppermute | solution.py:70
  223.9 6.4 %collective-permute-done.37 = f32[2,64,576]{2,1,0:T(8,128)S(1)} collective-permute-done((f32[2,64,576]{2,1,0:T(8,128)S(1)}, f32[2,64,576]{2,1,0:T(8,128)S(1)}, u32[]{:S(2)}, u32[]{:S(2)}) %collective-permute-start.37) | collective-permute-done | bytes 294944 | tf_op jit(solution)/shard_map/ppermute | solution.py:70
  230.4 1.7 collective-permute-start.38
  232.2 1.8 collective-permute-start.41
  234.0 2.3 collective-permute-done.38
  236.3 1.6 collective-permute-done.41
  (149 shorter events, 26.3 us)
Async XLA Ops:
  1.9 5.5 %collective-permute-start = (bf16[1,64,576]{2,1,0:T(8,128)(2,1)S(1)}, bf16[1,64,576]{2,1,0:T(8,128)(2,1)S(1)}, u32[]{:S(2)}, u32[]{:S(2)}) collective-permute-start(bf16[1,64,576]{2,1,0:T(8,128)(2,1)S(1)} %copy.66), channel_id=1, source_target_pairs={{0,2},{1,3},{2,0},{3,1},{4,6},{5,7},{6,4},{7,5},{8,10},{9,11},{10,... | collective-permute-start | bytes 221192 | tf_op jit(solution)/shard_map/ppermute | solution.py:92
  5.1 4.7 %collective-permute-start.3 = (bf16[1,64,576]{2,1,0:T(8,128)(2,1)S(1)}, bf16[1,64,576]{2,1,0:T(8,128)(2,1)S(1)}, u32[]{:S(2)}, u32[]{:S(2)}) collective-permute-start(bf16[1,64,576]{2,1,0:T(8,128)(2,1)S(1)} %copy.67), channel_id=1, source_target_pairs={{0,4},{4,0},{1,5},{5,1},{2,6},{6,2},{3,7},{7,3},{8,12},{12,8},{9,1... | collective-permute-start | bytes 221192 | tf_op jit(solution)/shard_map/ppermute | solution.py:92
  7.4 5.7 %collective-permute-start.1 = (bf16[2,64,576]{2,1,0:T(8,128)(2,1)S(1)}, bf16[2,64,576]{2,1,0:T(8,128)(2,1)S(1)}, u32[]{:S(2)}, u32[]{:S(2)}) collective-permute-start(bf16[2,64,576]{2,1,0:T(8,128)(2,1)S(1)} %maximum_select_fusion.16), channel_id=1, source_target_pairs={{0,4},{4,0},{1,5},{5,1},{2,6},{6,2},{3,7},{7,3},{8,12},{12,8},{9,1... | collective-permute-start | bytes 442376 | tf_op jit(solution)/shard_map/ppermute | solution.py:92
  9.9 5.4 %collective-permute-start.4 = (bf16[2,64,576]{2,1,0:T(8,128)(2,1)S(1)}, bf16[2,64,576]{2,1,0:T(8,128)(2,1)S(1)}, u32[]{:S(2)}, u32[]{:S(2)}) collective-permute-start(bf16[2,64,576]{2,1,0:T(8,128)(2,1)S(1)} %maximum_select_fusion.17), channel_id=1, source_target_pairs={{0,2},{1,3},{2,0},{3,1},{4,6},{5,7},{6,4},{7,5},{8,10},{9,11},{10,... | collective-permute-start | bytes 442376 | tf_op jit(solution)/shard_map/ppermute | solution.py:92
  13.2 9.7 %collective-permute-start.2 = (bf16[4,64,576]{2,1,0:T(8,128)(2,1)S(1)}, bf16[4,64,576]{2,1,0:T(8,128)(2,1)S(1)}, u32[]{:S(2)}, u32[]{:S(2)}) collective-permute-start(bf16[4,64,576]{2,1,0:T(8,128)(2,1)S(1)} %maximum_select_fusion.11), channel_id=1, source_target_pairs={{0,1},{1,0},{2,3},{3,2},{4,5},{5,4},{6,7},{7,6},{8,9},{9,8},{10,11... | collective-permute-start | bytes 884744 | tf_op jit(solution)/shard_map/ppermute | solution.py:92
  15.3 7.8 %collective-permute-start.5 = (bf16[4,64,576]{2,1,0:T(8,128)(2,1)S(1)}, bf16[4,64,576]{2,1,0:T(8,128)(2,1)S(1)}, u32[]{:S(2)}, u32[]{:S(2)}) collective-permute-start(bf16[4,64,576]{2,1,0:T(8,128)(2,1)S(1)} %maximum_select_fusion.12), channel_id=1, source_target_pairs={{0,1},{1,0},{2,3},{3,2},{4,5},{5,4},{6,7},{7,6},{8,9},{9,8},{10,11... | collective-permute-start | bytes 884744 | tf_op jit(solution)/shard_map/ppermute | solution.py:92
  22.8 1.7 copy-start.5
  22.8 5.5 %copy-start.12 = (pred[4]{0:T(512)(128)(4,1)}, pred[4]{0:T(512)(128)(4,1)S(1)}, u32[]{:S(2)}) copy-start(pred[4]{0:T(512)(128)(4,1)S(1)} %iota_compare_fusion.4) | copy-start | bytes 16
  23.3 1.2 copy-start.11
  61.9 2.2 copy-start.2
  64.1 5.2 %collective-permute-start.16 = (f32[16,40,576]{2,1,0:T(8,128)}, f32[16,40,576]{2,1,0:T(8,128)}, u32[]{:S(2)}, u32[]{:S(2)}) collective-permute-start(f32[16,40,576]{2,1,0:T(8,128)} %constant_dynamic-slice_fusion.10), channel_id=1, source_target_pairs={{0,1},{1,0},{2,3},{3,2},{4,5},{5,4},{6,7},{7,6},{8,9},{9,8},{10,11... | collective-permute-start | bytes 4423688 | tf_op jit(solution)/shard_map/ppermute | solution.py:70
  65.4 2.4 %copy-start = (f32[2,2,2,2,2,48,576]{6,5,4,3,2,1,0:T(8,128)}, f32[2,2,2,2,2,48,576]{6,5,4,3,2,1,0:T(8,128)S(1)}, u32[]{:S(2)}) copy-start(f32[2,2,2,2,2,48,576]{6,5,4,3,2,1,0:T(8,128)S(1)} %copy.54) | copy-start | bytes 10616836
  67.3 5.4 %collective-permute-start.11 = (f32[16,40,576]{2,1,0:T(8,128)}, f32[16,40,576]{2,1,0:T(8,128)}, u32[]{:S(2)}, u32[]{:S(2)}) collective-permute-start(f32[16,40,576]{2,1,0:T(8,128)} %constant_dynamic-slice_fusion.15), channel_id=1, source_target_pairs={{0,1},{1,0},{2,3},{3,2},{4,5},{5,4},{6,7},{7,6},{8,9},{9,8},{10,11... | collective-permute-start | bytes 4423688 | tf_op jit(solution)/shard_map/ppermute | solution.py:70
  69.3 5.9 %collective-permute-start.6 = (f32[16,48,576]{2,1,0:T(8,128)}, f32[16,48,576]{2,1,0:T(8,128)}, u32[]{:S(2)}, u32[]{:S(2)}) collective-permute-start(f32[16,48,576]{2,1,0:T(8,128)} %constant_dynamic-slice_fusion.20), channel_id=1, source_target_pairs={{0,1},{1,0},{2,3},{3,2},{4,5},{5,4},{6,7},{7,6},{8,9},{9,8},{10,11... | collective-permute-start | bytes 5308424 | tf_op jit(solution)/shard_map/ppermute | solution.py:70
  71.5 3.7 %copy-start.1 = (f32[2,2,2,2,2,48,576]{6,5,4,3,2,1,0:T(8,128)S(1)}, f32[2,2,2,2,2,48,576]{6,5,4,3,2,1,0:T(8,128)}, u32[]{:S(2)}) copy-start(f32[2,2,2,2,2,48,576]{6,5,4,3,2,1,0:T(8,128)} %copy-done) | copy-start | bytes 10616836
  71.5 20.7 %collective-permute-start.17 = (f32[8,40,576]{2,1,0:T(8,128)S(1)}, f32[8,40,576]{2,1,0:T(8,128)S(1)}, u32[]{:S(2)}, u32[]{:S(2)}) collective-permute-start(f32[8,40,576]{2,1,0:T(8,128)S(1)} %constant_dynamic-slice_fusion.9), channel_id=1, source_target_pairs={{0,2},{1,3},{2,0},{3,1},{4,6},{5,7},{6,4},{7,5},{8,10},{9,11},{10,... | collective-permute-start | bytes 2211848 | tf_op jit(solution)/shard_map/ppermute | solution.py:70
  74.4 20.6 %collective-permute-start.12 = (f32[8,40,576]{2,1,0:T(8,128)S(1)}, f32[8,40,576]{2,1,0:T(8,128)S(1)}, u32[]{:S(2)}, u32[]{:S(2)}) collective-permute-start(f32[8,40,576]{2,1,0:T(8,128)S(1)} %constant_dynamic-slice_fusion.14), channel_id=1, source_target_pairs={{0,4},{4,0},{1,5},{5,1},{2,6},{6,2},{3,7},{7,3},{8,12},{12,8},{9,1... | collective-permute-start | bytes 2211848 | tf_op jit(solution)/shard_map/ppermute | solution.py:70
  78.1 37.2 %collective-permute-start.7 = (f32[8,48,576]{2,1,0:T(8,128)}, f32[8,48,576]{2,1,0:T(8,128)}, u32[]{:S(2)}, u32[]{:S(2)}) collective-permute-start(f32[8,48,576]{2,1,0:T(8,128)} %constant_dynamic-slice_fusion.19), channel_id=1, source_target_pairs={{0,8},{8,0},{16,24},{24,16},{1,9},{9,1},{17,25},{25,17},{2,10},{10... | collective-permute-start | bytes 2654216 | tf_op jit(solution)/shard_map/ppermute | solution.py:70
  92.3 5.5 %copy-start.9 = (bf16[4,32,576]{2,1,0:T(8,128)(2,1)S(1)}, bf16[4,32,576]{2,1,0:T(8,128)(2,1)}, u32[]{:S(2)}) copy-start(bf16[4,32,576]{2,1,0:T(8,128)(2,1)} %param.13) | copy-start | bytes 442372
  93.1 17.7 %collective-permute-start.18 = (f32[4,40,576]{2,1,0:T(8,128)}, f32[4,40,576]{2,1,0:T(8,128)S(1)}, u32[]{:S(2)}, u32[]{:S(2)}) collective-permute-start(f32[4,40,576]{2,1,0:T(8,128)} %constant_dynamic-slice_fusion.8), channel_id=1, source_target_pairs={{0,8},{8,0},{16,24},{24,16},{1,9},{9,1},{17,25},{25,17},{2,10},{10... | collective-permute-start | bytes 1105928 | tf_op jit(solution)/shard_map/ppermute | solution.py:70
  95.1 0.9 copy-start.4
  96.8 15.5 %collective-permute-start.13 = (f32[4,40,576]{2,1,0:T(8,128)}, f32[4,40,576]{2,1,0:T(8,128)}, u32[]{:S(2)}, u32[]{:S(2)}) collective-permute-start(f32[4,40,576]{2,1,0:T(8,128)} %constant_dynamic-slice_fusion.13), channel_id=1, source_target_pairs={{0,2},{1,3},{2,0},{3,1},{4,6},{5,7},{6,4},{7,5},{8,10},{9,11},{10,... | collective-permute-start | bytes 1105928 | tf_op jit(solution)/shard_map/ppermute | solution.py:70
  110.9 6.4 %collective-permute-start.19 = (f32[2,40,576]{2,1,0:T(8,128)S(1)}, f32[2,40,576]{2,1,0:T(8,128)S(1)}, u32[]{:S(2)}, u32[]{:S(2)}) collective-permute-start(f32[2,40,576]{2,1,0:T(8,128)S(1)} %constant_dynamic-slice_fusion.7), channel_id=1, source_target_pairs={{0,4},{4,0},{1,5},{5,1},{2,6},{6,2},{3,7},{7,3},{8,12},{12,8},{9,1... | collective-permute-start | bytes 552968 | tf_op jit(solution)/shard_map/ppermute | solution.py:70
  113.5 7.2 %collective-permute-start.14 = (f32[2,40,576]{2,1,0:T(8,128)S(1)}, f32[2,40,576]{2,1,0:T(8,128)S(1)}, u32[]{:S(2)}, u32[]{:S(2)}) collective-permute-start(f32[2,40,576]{2,1,0:T(8,128)S(1)} %constant_dynamic-slice_fusion.12), channel_id=1, source_target_pairs={{0,8},{8,0},{16,24},{24,16},{1,9},{9,1},{17,25},{25,17},{2,10},{10... | collective-permute-start | bytes 552968 | tf_op jit(solution)/shard_map/ppermute | solution.py:70
  116.6 13.2 %copy-start.10 = (f32[4,576]{1,0:T(4,128)S(1)}, f32[4,576]{1,0:T(4,128)}, u32[]{:S(2)}) copy-start(f32[4,576]{1,0:T(4,128)} %param.11) | copy-start | bytes 27652
  116.6 12.0 %collective-permute-start.8 = (f32[4,48,576]{2,1,0:T(8,128)S(1)}, f32[4,48,576]{2,1,0:T(8,128)S(1)}, u32[]{:S(2)}, u32[]{:S(2)}) collective-permute-start(f32[4,48,576]{2,1,0:T(8,128)S(1)} %constant_dynamic-slice_fusion.18), channel_id=1, source_target_pairs={{0,4},{4,0},{1,5},{5,1},{2,6},{6,2},{3,7},{7,3},{8,12},{12,8},{9,1... | collective-permute-start | bytes 1327112 | tf_op jit(solution)/shard_map/ppermute | solution.py:70
  117.3 12.4 %collective-permute-start.20 = (f32[1,40,576]{2,1,0:T(8,128)S(1)}, f32[1,40,576]{2,1,0:T(8,128)S(1)}, u32[]{:S(2)}, u32[]{:S(2)}) collective-permute-start(f32[1,40,576]{2,1,0:T(8,128)S(1)} %constant_dynamic-slice_fusion.6), channel_id=1, source_target_pairs={{0,16},{8,24},{16,0},{24,8},{1,17},{9,25},{17,1},{25,9},{2,18},{10... | collective-permute-start | bytes 276488 | tf_op jit(solution)/shard_map/ppermute | solution.py:70
  120.7 9.0 %collective-permute-start.15 = (f32[1,40,576]{2,1,0:T(8,128)S(1)}, f32[1,40,576]{2,1,0:T(8,128)S(1)}, u32[]{:S(2)}, u32[]{:S(2)}) collective-permute-start(f32[1,40,576]{2,1,0:T(8,128)S(1)} %constant_dynamic-slice_fusion.11), channel_id=1, source_target_pairs={{0,16},{8,24},{16,0},{24,8},{1,17},{9,25},{17,1},{25,9},{2,18},{10... | collective-permute-start | bytes 276488 | tf_op jit(solution)/shard_map/ppermute | solution.py:70
  128.7 7.7 %collective-permute-start.9 = (f32[2,48,576]{2,1,0:T(8,128)S(1)}, f32[2,48,576]{2,1,0:T(8,128)S(1)}, u32[]{:S(2)}, u32[]{:S(2)}) collective-permute-start(f32[2,48,576]{2,1,0:T(8,128)S(1)} %constant_dynamic-slice_fusion.17), channel_id=1, source_target_pairs={{0,2},{1,3},{2,0},{3,1},{4,6},{5,7},{6,4},{7,5},{8,10},{9,11},{10,... | collective-permute-start | bytes 663560 | tf_op jit(solution)/shard_map/ppermute | solution.py:70
  129.8 27.4 %copy-start.7 = (bf16[40,576]{1,0:T(8,128)(2,1)}, bf16[40,576]{1,0:T(8,128)(2,1)S(1)}, u32[]{:S(2)}) copy-start(bf16[40,576]{1,0:T(8,128)(2,1)S(1)} %get-tuple-element.9) | copy-start | bytes 138244
  129.9 6.2 %collective-permute-start.26 = (bf16[1,40,576]{2,1,0:T(8,128)(2,1)S(1)}, bf16[1,40,576]{2,1,0:T(8,128)(2,1)S(1)}, u32[]{:S(2)}, u32[]{:S(2)}) collective-permute-start(bf16[1,40,576]{2,1,0:T(8,128)(2,1)S(1)} %bitcast.148), channel_id=1, source_target_pairs={{0,16},{8,24},{16,0},{24,8},{1,17},{9,25},{17,1},{25,9},{2,18},{10... | collective-permute-start | bytes 138248 | tf_op jit(solution)/shard_map/ppermute | solution.py:92
  132.5 6.6 %collective-permute-start.31 = (bf16[1,40,576]{2,1,0:T(8,128)(2,1)S(1)}, bf16[1,40,576]{2,1,0:T(8,128)(2,1)S(1)}, u32[]{:S(2)}, u32[]{:S(2)}) collective-permute-start(bf16[1,40,576]{2,1,0:T(8,128)(2,1)S(1)} %bitcast.150), channel_id=1, source_target_pairs={{0,16},{8,24},{16,0},{24,8},{1,17},{9,25},{17,1},{25,9},{2,18},{10... | collective-permute-start | bytes 138248 | tf_op jit(solution)/shard_map/ppermute | solution.py:92
  136.1 9.1 %collective-permute-start.27 = (bf16[2,40,576]{2,1,0:T(8,128)(2,1)S(1)}, bf16[2,40,576]{2,1,0:T(8,128)(2,1)S(1)}, u32[]{:S(2)}, u32[]{:S(2)}) collective-permute-start(bf16[2,40,576]{2,1,0:T(8,128)(2,1)S(1)} %maximum_select_fusion.19), channel_id=1, source_target_pairs={{0,8},{8,0},{16,24},{24,16},{1,9},{9,1},{17,25},{25,17},{2,10},{10... | collective-permute-start | bytes 276488 | tf_op jit(solution)/shard_map/ppermute | solution.py:92
  136.5 5.9 %collective-permute-start.10 = (f32[1,48,576]{2,1,0:T(8,128)S(1)}, f32[1,48,576]{2,1,0:T(8,128)S(1)}, u32[]{:S(2)}, u32[]{:S(2)}) collective-permute-start(f32[1,48,576]{2,1,0:T(8,128)S(1)} %constant_dynamic-slice_fusion.16), channel_id=1, source_target_pairs={{0,16},{8,24},{16,0},{24,8},{1,17},{9,25},{17,1},{25,9},{2,18},{10... | collective-permute-start | bytes 331784 | tf_op jit(solution)/shard_map/ppermute | solution.py:70
  139.2 9.4 %collective-permute-start.32 = (bf16[2,40,576]{2,1,0:T(8,128)(2,1)S(1)}, bf16[2,40,576]{2,1,0:T(8,128)(2,1)S(1)}, u32[]{:S(2)}, u32[]{:S(2)}) collective-permute-start(bf16[2,40,576]{2,1,0:T(8,128)(2,1)S(1)} %maximum_select_fusion.20), channel_id=1, source_target_pairs={{0,4},{4,0},{1,5},{5,1},{2,6},{6,2},{3,7},{7,3},{8,12},{12,8},{9,1... | collective-permute-start | bytes 276488 | tf_op jit(solution)/shard_map/ppermute | solution.py:92
  142.4 5.2 %collective-permute-start.21 = (bf16[1,48,576]{2,1,0:T(8,128)(2,1)S(1)}, bf16[1,48,576]{2,1,0:T(8,128)(2,1)S(1)}, u32[]{:S(2)}, u32[]{:S(2)}) collective-permute-start(bf16[1,48,576]{2,1,0:T(8,128)(2,1)S(1)} %bitcast.146), channel_id=1, source_target_pairs={{0,16},{8,24},{16,0},{24,8},{1,17},{9,25},{17,1},{25,9},{2,18},{10... | collective-permute-start | bytes 165896 | tf_op jit(solution)/shard_map/ppermute | solution.py:92
  145.2 11.8 %collective-permute-start.28 = (bf16[4,40,576]{2,1,0:T(8,128)(2,1)S(1)}, bf16[4,40,576]{2,1,0:T(8,128)(2,1)S(1)}, u32[]{:S(2)}, u32[]{:S(2)}) collective-permute-start(bf16[4,40,576]{2,1,0:T(8,128)(2,1)S(1)} %maximum_select_fusion.14), channel_id=1, source_target_pairs={{0,2},{1,3},{2,0},{3,1},{4,6},{5,7},{6,4},{7,5},{8,10},{9,11},{10,... | collective-permute-start | bytes 552968 | tf_op jit(solution)/shard_map/ppermute | solution.py:92
  147.6 4.9 %collective-permute-start.22 = (bf16[2,48,576]{2,1,0:T(8,128)(2,1)S(1)}, bf16[2,48,576]{2,1,0:T(8,128)(2,1)S(1)}, u32[]{:S(2)}, u32[]{:S(2)}) collective-permute-start(bf16[2,48,576]{2,1,0:T(8,128)(2,1)S(1)} %maximum_select_fusion.18), channel_id=1, source_target_pairs={{0,2},{1,3},{2,0},{3,1},{4,6},{5,7},{6,4},{7,5},{8,10},{9,11},{10,... | collective-permute-start | bytes 331784 | tf_op jit(solution)/shard_map/ppermute | solution.py:92
  148.6 8.5 %collective-permute-start.33 = (bf16[4,40,576]{2,1,0:T(8,128)(2,1)S(1)}, bf16[4,40,576]{2,1,0:T(8,128)(2,1)S(1)}, u32[]{:S(2)}, u32[]{:S(2)}) collective-permute-start(bf16[4,40,576]{2,1,0:T(8,128)(2,1)S(1)} %maximum_select_fusion.15), channel_id=1, source_target_pairs={{0,8},{8,0},{16,24},{24,16},{1,9},{9,1},{17,25},{25,17},{2,10},{10... | collective-permute-start | bytes 552968 | tf_op jit(solution)/shard_map/ppermute | solution.py:92
  152.6 8.5 %collective-permute-start.23 = (bf16[4,48,576]{2,1,0:T(8,128)(2,1)S(1)}, bf16[4,48,576]{2,1,0:T(8,128)(2,1)S(1)}, u32[]{:S(2)}, u32[]{:S(2)}) collective-permute-start(bf16[4,48,576]{2,1,0:T(8,128)(2,1)S(1)} %maximum_select_fusion.13), channel_id=1, source_target_pairs={{0,4},{4,0},{1,5},{5,1},{2,6},{6,2},{3,7},{7,3},{8,12},{12,8},{9,1... | collective-permute-start | bytes 663560 | tf_op jit(solution)/shard_map/ppermute | solution.py:92
  157.0 8.4 %collective-permute-start.29 = (bf16[8,40,576]{2,1,0:T(8,128)(2,1)S(1)}, bf16[8,40,576]{2,1,0:T(8,128)(2,1)S(1)}, u32[]{:S(2)}, u32[]{:S(2)}) collective-permute-start(bf16[8,40,576]{2,1,0:T(8,128)(2,1)S(1)} %maximum_select_fusion.9), channel_id=1, source_target_pairs={{0,4},{4,0},{1,5},{5,1},{2,6},{6,2},{3,7},{7,3},{8,12},{12,8},{9,1... | collective-permute-start | bytes 1105928 | tf_op jit(solution)/shard_map/ppermute | solution.py:92
  157.3 8.5 %collective-permute-start.34 = (bf16[8,40,576]{2,1,0:T(8,128)(2,1)S(1)}, bf16[8,40,576]{2,1,0:T(8,128)(2,1)S(1)}, u32[]{:S(2)}, u32[]{:S(2)}) collective-permute-start(bf16[8,40,576]{2,1,0:T(8,128)(2,1)S(1)} %maximum_select_fusion.10), channel_id=1, source_target_pairs={{0,2},{1,3},{2,0},{3,1},{4,6},{5,7},{6,4},{7,5},{8,10},{9,11},{10,... | collective-permute-start | bytes 1105928 | tf_op jit(solution)/shard_map/ppermute | solution.py:92
  161.2 10.0 %collective-permute-start.24 = (bf16[8,48,576]{2,1,0:T(8,128)(2,1)S(1)}, bf16[8,48,576]{2,1,0:T(8,128)(2,1)S(1)}, u32[]{:S(2)}, u32[]{:S(2)}) collective-permute-start(bf16[8,48,576]{2,1,0:T(8,128)(2,1)S(1)} %maximum_select_fusion.8), channel_id=1, source_target_pairs={{0,8},{8,0},{16,24},{24,16},{1,9},{9,1},{17,25},{25,17},{2,10},{10... | collective-permute-start | bytes 1327112 | tf_op jit(solution)/shard_map/ppermute | solution.py:92
  165.7 5.9 %collective-permute-start.30 = (bf16[16,40,576]{2,1,0:T(8,128)(2,1)S(1)}, bf16[16,40,576]{2,1,0:T(8,128)(2,1)S(1)}, u32[]{:S(2)}, u32[]{:S(2)}) collective-permute-start(bf16[16,40,576]{2,1,0:T(8,128)(2,1)S(1)} %maximum_select_fusion.4), channel_id=1, source_target_pairs={{0,1},{1,0},{2,3},{3,2},{4,5},{5,4},{6,7},{7,6},{8,9},{9,8},{10,11... | collective-permute-start | bytes 2211848 | tf_op jit(solution)/shard_map/ppermute | solution.py:92
  166.0 6.2 %collective-permute-start.35 = (bf16[16,40,576]{2,1,0:T(8,128)(2,1)S(1)}, bf16[16,40,576]{2,1,0:T(8,128)(2,1)}, u32[]{:S(2)}, u32[]{:S(2)}) collective-permute-start(bf16[16,40,576]{2,1,0:T(8,128)(2,1)S(1)} %maximum_select_fusion.5), channel_id=1, source_target_pairs={{0,1},{1,0},{2,3},{3,2},{4,5},{5,4},{6,7},{7,6},{8,9},{9,8},{10,11... | collective-permute-start | bytes 2211848 | tf_op jit(solution)/shard_map/ppermute | solution.py:92
  171.5 2.8 %collective-permute-start.25 = (bf16[16,48,576]{2,1,0:T(8,128)(2,1)S(1)}, bf16[16,48,576]{2,1,0:T(8,128)(2,1)}, u32[]{:S(2)}, u32[]{:S(2)}) collective-permute-start(bf16[16,48,576]{2,1,0:T(8,128)(2,1)S(1)} %maximum_select_fusion.3), channel_id=1, source_target_pairs={{0,1},{1,0},{2,3},{3,2},{4,5},{5,4},{6,7},{7,6},{8,9},{9,8},{10,11... | collective-permute-start | bytes 2654216 | tf_op jit(solution)/shard_map/ppermute | solution.py:92
  184.1 9.9 %copy-start.6 = (f32[256,1024]{1,0:T(8,128)S(1)}, f32[256,1024]{1,0:T(8,128)}, u32[]{:S(2)}) copy-start(f32[256,1024]{1,0:T(8,128)} %copy-done.5) | copy-start | bytes 3145732
  184.1 9.9 %copy-start.13 = (pred[4]{0:T(512)(128)(4,1)S(1)}, pred[4]{0:T(512)(128)(4,1)}, u32[]{:S(2)}) copy-start(pred[4]{0:T(512)(128)(4,1)} %copy-done.12) | copy-start | bytes 16
  214.8 4.3 %collective-permute-start.36 = (f32[4,64,576]{2,1,0:T(8,128)}, f32[4,64,576]{2,1,0:T(8,128)S(1)}, u32[]{:S(2)}, u32[]{:S(2)}) collective-permute-start(f32[4,64,576]{2,1,0:T(8,128)} %constant_dynamic-slice_fusion.5), channel_id=1, source_target_pairs={{0,1},{1,0},{2,3},{3,2},{4,5},{5,4},{6,7},{7,6},{8,9},{9,8},{10,11... | collective-permute-start | bytes 1769480 | tf_op jit(solution)/shard_map/ppermute | solution.py:70
  215.2 3.3 %copy-start.8 = (bf16[40,576]{1,0:T(8,128)(2,1)S(1)}, bf16[40,576]{1,0:T(8,128)(2,1)}, u32[]{:S(2)}) copy-start(bf16[40,576]{1,0:T(8,128)(2,1)} %copy-done.7) | copy-start | bytes 138244
  217.0 4.3 %copy-start.3 = (f32[2,2,2,64,576]{4,3,2,1,0:T(8,128)S(1)}, f32[2,2,2,64,576]{4,3,2,1,0:T(8,128)}, u32[]{:S(2)}) copy-start(f32[2,2,2,64,576]{4,3,2,1,0:T(8,128)} %copy.63) | copy-start | bytes 3538948
  218.2 3.0 %collective-permute-start.39 = (f32[4,64,576]{2,1,0:T(8,128)S(1)}, f32[4,64,576]{2,1,0:T(8,128)S(1)}, u32[]{:S(2)}, u32[]{:S(2)}) collective-permute-start(f32[4,64,576]{2,1,0:T(8,128)S(1)} %constant_dynamic-slice_fusion.2), channel_id=1, source_target_pairs={{0,1},{1,0},{2,3},{3,2},{4,5},{5,4},{6,7},{7,6},{8,9},{9,8},{10,11... | collective-permute-start | bytes 1769480 | tf_op jit(solution)/shard_map/ppermute | solution.py:70
  220.3 10.0 %collective-permute-start.37 = (f32[2,64,576]{2,1,0:T(8,128)S(1)}, f32[2,64,576]{2,1,0:T(8,128)S(1)}, u32[]{:S(2)}, u32[]{:S(2)}) collective-permute-start(f32[2,64,576]{2,1,0:T(8,128)S(1)} %constant_dynamic-slice_fusion.4), channel_id=1, source_target_pairs={{0,4},{4,0},{1,5},{5,1},{2,6},{6,2},{3,7},{7,3},{8,12},{12,8},{9,1... | collective-permute-start | bytes 884744 | tf_op jit(solution)/shard_map/ppermute | solution.py:70
  221.4 10.8 %collective-permute-start.40 = (f32[2,64,576]{2,1,0:T(8,128)S(1)}, f32[2,64,576]{2,1,0:T(8,128)S(1)}, u32[]{:S(2)}, u32[]{:S(2)}) collective-permute-start(f32[2,64,576]{2,1,0:T(8,128)S(1)} %constant_dynamic-slice_fusion.1), channel_id=1, source_target_pairs={{0,2},{1,3},{2,0},{3,1},{4,6},{5,7},{6,4},{7,5},{8,10},{9,11},{10,... | collective-permute-start | bytes 884744 | tf_op jit(solution)/shard_map/ppermute | solution.py:70
  230.4 5.9 %collective-permute-start.38 = (f32[1,64,576]{2,1,0:T(8,128)S(1)}, f32[1,64,576]{2,1,0:T(8,128)S(1)}, u32[]{:S(2)}, u32[]{:S(2)}) collective-permute-start(f32[1,64,576]{2,1,0:T(8,128)S(1)} %constant_dynamic-slice_fusion.3), channel_id=1, source_target_pairs={{0,2},{1,3},{2,0},{3,1},{4,6},{5,7},{6,4},{7,5},{8,10},{9,11},{10,... | collective-permute-start | bytes 442376 | tf_op jit(solution)/shard_map/ppermute | solution.py:70
  232.2 5.7 %collective-permute-start.41 = (f32[1,64,576]{2,1,0:T(8,128)S(1)}, f32[1,64,576]{2,1,0:T(8,128)S(1)}, u32[]{:S(2)}, u32[]{:S(2)}) collective-permute-start(f32[1,64,576]{2,1,0:T(8,128)S(1)} %constant_dynamic-slice_fusion), channel_id=1, source_target_pairs={{0,4},{4,0},{1,5},{5,1},{2,6},{6,2},{3,7},{7,3},{8,12},{12,8},{9,1... | collective-permute-start | bytes 442376 | tf_op jit(solution)/shard_map/ppermute | solution.py:70

commit v14 on v13

--- a/solution.py
+++ b/solution.py
@@ -125,7 +125,7 @@
     first_feat = half_bit * (feat_total // 2) + feat_pos * feat_dev
     layer_index = lax.dynamic_index_in_dim(topk_index, layer_id, 0, keepdims=False)
     local_ids = layer_index - first_feat
-    low_bits = (feat_dev.bit_length() - 1) // 2
+    low_bits = min(7, feat_dev.bit_length() - 1)
     side = 1 << low_bits
     high_hot = ((local_ids >> low_bits)[:, :, None] == lax.iota(jnp.int32, feat_dev // side)).astype(jnp.bfloat16)
     low_hot = ((local_ids & (side - 1))[:, :, None] == lax.iota(jnp.int32, side)).astype(jnp.bfloat16)

time: 240 us -> 237 us (0.988)
  starting transfers between devices: 59.1 us -> 45 us
  waiting for transfers between devices: 59.9 us -> 73.6 us
  local copies, waits for them, and re-layouts: 64.7 us -> 61.9 us
    ppermute x21, starting transfers between devices: 31.5 us -> 22.3 us  [all_gather(): recv = lax.ppermute(parts[p], axis, partner(axis, bit))]
    ppermute x21, waiting for transfers between devices: 16.8 us -> 24.6 us  [all_gather(): recv = lax.ppermute(parts[p], axis, partner(axis, bit))]
    ppermute x21, waiting for transfers between devices: 43.1 us -> 49 us  [reduce_scatter(): recv = lax.ppermute(send.astype(wire), axis, partner(axis, bit))]
    ppermute x21, starting transfers between devices: 27.6 us -> 22.7 us  [reduce_scatter(): recv = lax.ppermute(send.astype(wire), axis, partner(axis, bit))]
    dot_general x1 -> x0, local copies, waits for them, and re-layouts: 3.51 us -> none  [local(): jnp.einsum('tka,tkb->tab', high_hot, low_hot, preferred_element_type=jnp....]
where the time goes in v14:
time: 237 us; the launch traced here: 236 us
  waiting for transfers between devices  73.6 us (31%)
  local copies, waits for them, and re-layouts  61.9 us (26%)
  starting transfers between devices  45 us (19%)
  matrix products  34.9 us (15%)
  other arithmetic  19 us (8%)
    ppermute x21, waiting for transfers between devices, reduce_scatter(): recv = lax.ppermute(send.astype(wire), axis, partner(axis, bit))  49 us
    ppermute x21, waiting for transfers between devices, all_gather(): recv = lax.ppermute(parts[p], axis, partner(axis, bit))  24.6 us
    ppermute x21, starting transfers between devices, reduce_scatter(): recv = lax.ppermute(send.astype(wire), axis, partner(axis, bit))  22.7 us
    ppermute x21, starting transfers between devices, all_gather(): recv = lax.ppermute(parts[p], axis, partner(axis, bit))  22.3 us
    reshape x2, local copies, waits for them, and re-layouts, local(): partial_value.reshape(layer_count, slots, slot_rows, feat_parts, cols)  18.7 us
    dot_general x1, matrix products, local(): jnp.einsum('tf,lfd->ltd', acts, decoder[0], preferred_element_type=jnp.fl...  13.9 us
    dynamic_slice x21, local copies, waits for them, and re-layouts, reduce_scatter(): send = lax.dynamic_slice_in_dim(parts[p], (1 - own) * half, half, 0)  11.6 us
    dot_general x1, matrix products, local(): jnp.einsum('ltd,lfd->tf', kept, decoder[0], preferred_element_type=jnp.fl...  10.6 us
  transfers between devices with their start and end apart: 42, of which 20 were waited for; matrix products, arithmetic and copies ran while one was open for 14% of the time, Pallas kernels for 0%

profile of v14, /device:TPU:0, one launch (start us, length us, event | category | flops | bytes accessed | tf_op | source)
XLA Modules:
  0.0 235.9 jit_solution(18359639245222827050)
XLA Ops:
  0.6 1.1 fusion.47
  1.9 3.1 %collective-permute-start = (bf16[1,64,576]{2,1,0:T(8,128)(2,1)S(1)}, bf16[1,64,576]{2,1,0:T(8,128)(2,1)S(1)}, u32[]{:S(2)}, u32[]{:S(2)}) collective-permute-start(bf16[1,64,576]{2,1,0:T(8,128)(2,1)S(1)} %copy.57), channel_id=1, source_target_pairs={{0,2},{1,3},{2,0},{3,1},{4,6},{5,7},{6,4},{7,5},{8,10},{9,11},{10,... | collective-permute-start | bytes 221192 | tf_op jit(solution)/shard_map/ppermute | solution.py:92
  5.1 1.6 collective-permute-start.3
  7.4 2.0 collective-permute-start.1
  9.9 1.2 collective-permute-start.4
  12.1 0.9 collective-permute-done.1
  13.3 2.0 collective-permute-done.4
  15.4 5.2 %fusion.4 = f32[256,8,128]{2,1,0:T(8,128)S(1)} fusion(s32[256,64]{1,0:T(8,128)S(1)} %copy.39, s32[256,64]{1,0:T(8,128)S(1)} %copy.38), kind=kOutput, calls=%fused_computation.6 | convolution fusion | flops 35782656 | bytes 1179648 | tf_op jit(solution)/shard_map/tka,tkb->tab/dot_general | solution.py:132
  21.3 1.0 copy.44
  22.4 3.8 %fusion.37 = bf16[256,1024,1]{1,0,2:T(8,128)(2,1)S(1)} fusion(bf16[1,2304,1024]{2,1,0:T(8,128)(2,1)} %param.8, bf16[288,8,2,128]{3,2,1,0:T(2,128)(2,1)S(1)} %bitcast.147, f32[32,8,8,128]{3,2,1,0:T(8,128)S(1)} %bitcast.159, f32[1024]{0:T(1024)S(1)} %bitcast.158), kind=kOutput, calls=%fused_computation.32 | convolution fusion | flops 1208745984 | bytes 7475200 | tf_op jit(solution)/shard_map/dot_general | solution.py:124
  26.2 13.9 %select_bitcast_fusion = f32[4,256,2304]{2,1,0:T(8,128)} fusion(bf16[256,1024,1]{1,0,2:T(8,128)(2,1)S(1)} %fusion.37, bf16[1,4,1024,2304]{3,2,1,0:T(8,128)(2,1)} %param.10, pred[4]{0:T(512)(128)(4,1)S(1)} %iota_compare_fusion.4), kind=kOutput, calls=%fused_computation.4 | convolution fusion | flops 4834197504 | bytes 28835844 | tf_op jit(solution)/shard_map/tf,lfd->ltd/dot_general | solution.py:136
  40.0 13.2 %reshape.140 = f32[4,8,32,4,576]{4,3,2,1,0:T(4,128)} reshape(f32[4,256,2304]{2,1,0:T(8,128)} %select_bitcast_fusion) | data formatting | bytes 18874368 | tf_op jit(solution)/shard_map/reshape | solution.py:139
  53.2 5.5 %copy.45 = f32[4,8,32,4,576]{4,2,0,3,1:T(8,128)S(1)} copy(f32[4,8,32,4,576]{4,3,2,1,0:T(4,128)} %reshape.140) | data formatting | bytes 18874368 | tf_op jit(solution)/shard_map/reshape | solution.py:139
  59.8 1.4 constant_dynamic-slice_fusion.10
  63.5 1.6 constant_dynamic-slice_fusion.15
  65.6 1.4 constant_dynamic-slice_fusion.20
  67.1 2.1 dynamic-slice_add_fusion.1
  69.3 1.2 collective-permute-start.17
  70.5 1.7 dynamic-slice_add_fusion.2
  73.1 1.8 dynamic-slice_add_fusion
  75.0 1.1 constant_dynamic-slice_fusion.19
  76.0 1.6 collective-permute-start.7
  77.6 12.3 %collective-permute-done.17 = f32[8,40,576]{2,1,0:T(8,128)S(1)} collective-permute-done((f32[8,40,576]{2,1,0:T(8,128)S(1)}, f32[8,40,576]{2,1,0:T(8,128)S(1)}, u32[]{:S(2)}, u32[]{:S(2)}) %collective-permute-start.17) | collective-permute-done | bytes 737312 | tf_op jit(solution)/shard_map/ppermute | solution.py:70
  90.8 1.7 collective-permute-start.18
  95.4 13.4 %collective-permute-done.18 = f32[4,40,576]{2,1,0:T(8,128)S(1)} collective-permute-done((f32[4,40,576]{2,1,0:T(8,128)}, f32[4,40,576]{2,1,0:T(8,128)S(1)}, u32[]{:S(2)}, u32[]{:S(2)}) %collective-permute-start.18) | collective-permute-done | bytes 368672 | tf_op jit(solution)/shard_map/ppermute | solution.py:70
  108.9 1.1 collective-permute-start.19
  110.0 1.2 dynamic-slice_add_fusion.10
  111.2 1.6 collective-permute-start.14
  112.9 1.3 dynamic-slice_add_fusion.3
  114.2 1.1 collective-permute-start.8
  115.4 2.7 %collective-permute-start.20 = (f32[1,40,576]{2,1,0:T(8,128)S(1)}, f32[1,40,576]{2,1,0:T(8,128)S(1)}, u32[]{:S(2)}, u32[]{:S(2)}) collective-permute-start(f32[1,40,576]{2,1,0:T(8,128)S(1)} %constant_dynamic-slice_fusion.6), channel_id=1, source_target_pairs={{0,16},{8,24},{16,0},{24,8},{1,17},{9,25},{17,1},{25,9},{2,18},{10... | collective-permute-start | bytes 276488 | tf_op jit(solution)/shard_map/ppermute | solution.py:70
  118.1 2.4 %collective-permute-start.15 = (f32[1,40,576]{2,1,0:T(8,128)S(1)}, f32[1,40,576]{2,1,0:T(8,128)S(1)}, u32[]{:S(2)}, u32[]{:S(2)}) collective-permute-start(f32[1,40,576]{2,1,0:T(8,128)S(1)} %constant_dynamic-slice_fusion.11), channel_id=1, source_target_pairs={{0,16},{8,24},{16,0},{24,8},{1,17},{9,25},{17,1},{25,9},{2,18},{10... | collective-permute-start | bytes 276488 | tf_op jit(solution)/shard_map/ppermute | solution.py:70
  120.5 5.4 %collective-permute-done.8 = f32[4,48,576]{2,1,0:T(8,128)S(1)} collective-permute-done((f32[4,48,576]{2,1,0:T(8,128)S(1)}, f32[4,48,576]{2,1,0:T(8,128)S(1)}, u32[]{:S(2)}, u32[]{:S(2)}) %collective-permute-start.8) | collective-permute-done | bytes 442400 | tf_op jit(solution)/shard_map/ppermute | solution.py:70
  126.0 1.7 collective-permute-start.9
  127.9 2.7 %collective-permute-start.26 = (bf16[1,40,576]{2,1,0:T(8,128)(2,1)S(1)}, bf16[1,40,576]{2,1,0:T(8,128)(2,1)S(1)}, u32[]{:S(2)}, u32[]{:S(2)}) collective-permute-start(bf16[1,40,576]{2,1,0:T(8,128)(2,1)S(1)} %bitcast.150), channel_id=1, source_target_pairs={{0,16},{8,24},{16,0},{24,8},{1,17},{9,25},{17,1},{25,9},{2,18},{10... | collective-permute-start | bytes 138248 | tf_op jit(solution)/shard_map/ppermute | solution.py:92
  130.9 3.2 %collective-permute-done.26 = bf16[1,40,576]{2,1,0:T(8,128)(2,1)S(1)} collective-permute-done((bf16[1,40,576]{2,1,0:T(8,128)(2,1)S(1)}, bf16[1,40,576]{2,1,0:T(8,128)(2,1)S(1)}, u32[]{:S(2)}, u32[]{:S(2)}) %collective-permute-start.26) | collective-permute-done | bytes 46112 | tf_op jit(solution)/shard_map/ppermute | solution.py:92
  134.7 2.0 collective-permute-start.10
  136.8 2.1 collective-permute-start.32
  138.9 3.9 %collective-permute-done.10 = f32[1,48,576]{2,1,0:T(8,128)S(1)} collective-permute-done((f32[1,48,576]{2,1,0:T(8,128)S(1)}, f32[1,48,576]{2,1,0:T(8,128)S(1)}, u32[]{:S(2)}, u32[]{:S(2)}) %collective-permute-start.10) | collective-permute-done | bytes 110624 | tf_op jit(solution)/shard_map/ppermute | solution.py:70
  143.0 2.1 collective-permute-start.28
  145.0 3.3 %collective-permute-done.21 = bf16[1,48,576]{2,1,0:T(8,128)(2,1)S(1)} collective-permute-done((bf16[1,48,576]{2,1,0:T(8,128)(2,1)S(1)}, bf16[1,48,576]{2,1,0:T(8,128)(2,1)S(1)}, u32[]{:S(2)}, u32[]{:S(2)}) %collective-permute-start.21) | collective-permute-done | bytes 55328 | tf_op jit(solution)/shard_map/ppermute | solution.py:92
  149.8 4.6 %collective-permute-done.22 = bf16[2,48,576]{2,1,0:T(8,128)(2,1)S(1)} collective-permute-done((bf16[2,48,576]{2,1,0:T(8,128)(2,1)S(1)}, bf16[2,48,576]{2,1,0:T(8,128)(2,1)S(1)}, u32[]{:S(2)}, u32[]{:S(2)}) %collective-permute-start.22) | collective-permute-done | bytes 110624 | tf_op jit(solution)/shard_map/ppermute | solution.py:92
  154.4 1.6 collective-permute-start.23
  157.5 3.2 %collective-permute-done.23 = bf16[4,48,576]{2,1,0:T(8,128)(2,1)S(1)} collective-permute-done((bf16[4,48,576]{2,1,0:T(8,128)(2,1)S(1)}, bf16[4,48,576]{2,1,0:T(8,128)(2,1)S(1)}, u32[]{:S(2)}, u32[]{:S(2)}) %collective-permute-start.23) | collective-permute-done | bytes 221216 | tf_op jit(solution)/shard_map/ppermute | solution.py:92
  160.8 1.6 collective-permute-start.24
  162.4 2.7 %collective-permute-done.29 = bf16[8,40,576]{2,1,0:T(8,128)(2,1)S(1)} collective-permute-done((bf16[8,40,576]{2,1,0:T(8,128)(2,1)S(1)}, bf16[8,40,576]{2,1,0:T(8,128)(2,1)S(1)}, u32[]{:S(2)}, u32[]{:S(2)}) %collective-permute-start.29) | collective-permute-done | bytes 368672 | tf_op jit(solution)/shard_map/ppermute | solution.py:92
  166.2 3.6 %collective-permute-done.24 = bf16[8,48,576]{2,1,0:T(8,128)(2,1)S(1)} collective-permute-done((bf16[8,48,576]{2,1,0:T(8,128)(2,1)S(1)}, bf16[8,48,576]{2,1,0:T(8,128)(2,1)S(1)}, u32[]{:S(2)}, u32[]{:S(2)}) %collective-permute-start.24) | collective-permute-done | bytes 442400 | tf_op jit(solution)/shard_map/ppermute | solution.py:92
  170.7 1.8 maximum_select_fusion.2
  172.8 2.1 maximum_select_fusion
  175.1 1.1 pad_maximum_fusion
  176.2 6.4 %copy.52 = bf16[4,8,32,4,576]{4,3,2,1,0:T(4,128)(2,1)} copy(bf16[4,8,32,4,576]{4,2,0,3,1:T(8,128)(2,1)S(1)} %bitcast.123) | data formatting | bytes 9437184 | tf_op jit(solution)/shard_map/transpose | solution.py:158
  182.6 10.0 %reshape.150 = bf16[4,256,2304]{2,1,0:T(8,128)(2,1)} reshape(bf16[4,8,32,4,576]{4,3,2,1,0:T(4,128)(2,1)} %copy.52) | data formatting | bytes 9437184 | tf_op jit(solution)/shard_map/reshape | solution.py:159
  192.5 10.6 %fusion.32 = bf16[256,1024]{1,0:T(8,128)(2,1)S(1)} fusion(bf16[1,4,1024,2304]{3,2,1,0:T(8,128)(2,1)} %param.10, bf16[4,256,2304]{2,1,0:T(8,128)(2,1)} %reshape.150, pred[4]{0:T(512)(128)(4,1)S(1)} %copy-done.14, f32[32,8,8,128]{3,2,1,0:T(8,128)S(1)} %bitcast.160), kind=kOutput, calls=%fused_computation.31 | convolution fusion | flops 4834721792 | bytes 25165828 | tf_op jit(solution)/shard_map/ltd,lfd->tf/dot_general | solution.py:162
  203.2 1.5 fusion.48
  204.7 2.2 slice_bitcast_fusion.4
  206.9 2.9 %copy.53 = f32[2,2,2,64,576]{4,3,2,1,0:T(8,128)} copy(f32[2,2,2,64,576]{3,4,0,2,1:T(8,128)} %get-tuple-element.6) | data formatting | bytes 2359296 | tf_op jit(solution)/shard_map/transpose | solution.py:61
  209.8 2.0 constant_dynamic-slice_fusion.5
  212.2 1.8 copy.54
  214.0 2.1 constant_dynamic-slice_fusion.2
  216.9 1.2 dynamic-slice_add_fusion.7
  218.1 1.6 collective-permute-start.37
  219.9 8.3 %collective-permute-done.37 = f32[2,64,576]{2,1,0:T(8,128)S(1)} collective-permute-done((f32[2,64,576]{2,1,0:T(8,128)S(1)}, f32[2,64,576]{2,1,0:T(8,128)S(1)}, u32[]{:S(2)}, u32[]{:S(2)}) %collective-permute-start.37) | collective-permute-done | bytes 294944 | tf_op jit(solution)/shard_map/ppermute | solution.py:70
  230.3 3.7 %collective-permute-done.38 = f32[1,64,576]{2,1,0:T(8,128)S(1)} collective-permute-done((f32[1,64,576]{2,1,0:T(8,128)S(1)}, f32[1,64,576]{2,1,0:T(8,128)S(1)}, u32[]{:S(2)}, u32[]{:S(2)}) %collective-permute-start.38) | collective-permute-done | bytes 147488 | tf_op jit(solution)/shard_map/ppermute | solution.py:70
  234.0 1.1 collective-permute-done.41
  (154 shorter events, 23.7 us)
Async XLA Ops:
  1.9 5.5 %collective-permute-start = (bf16[1,64,576]{2,1,0:T(8,128)(2,1)S(1)}, bf16[1,64,576]{2,1,0:T(8,128)(2,1)S(1)}, u32[]{:S(2)}, u32[]{:S(2)}) collective-permute-start(bf16[1,64,576]{2,1,0:T(8,128)(2,1)S(1)} %copy.57), channel_id=1, source_target_pairs={{0,2},{1,3},{2,0},{3,1},{4,6},{5,7},{6,4},{7,5},{8,10},{9,11},{10,... | collective-permute-start | bytes 221192 | tf_op jit(solution)/shard_map/ppermute | solution.py:92
  5.1 4.7 %collective-permute-start.3 = (bf16[1,64,576]{2,1,0:T(8,128)(2,1)S(1)}, bf16[1,64,576]{2,1,0:T(8,128)(2,1)S(1)}, u32[]{:S(2)}, u32[]{:S(2)}) collective-permute-start(bf16[1,64,576]{2,1,0:T(8,128)(2,1)S(1)} %copy.58), channel_id=1, source_target_pairs={{0,4},{4,0},{1,5},{5,1},{2,6},{6,2},{3,7},{7,3},{8,12},{12,8},{9,1... | collective-permute-start | bytes 221192 | tf_op jit(solution)/shard_map/ppermute | solution.py:92
  7.4 5.7 %collective-permute-start.1 = (bf16[2,64,576]{2,1,0:T(8,128)(2,1)S(1)}, bf16[2,64,576]{2,1,0:T(8,128)(2,1)S(1)}, u32[]{:S(2)}, u32[]{:S(2)}) collective-permute-start(bf16[2,64,576]{2,1,0:T(8,128)(2,1)S(1)} %maximum_select_fusion.16), channel_id=1, source_target_pairs={{0,4},{4,0},{1,5},{5,1},{2,6},{6,2},{3,7},{7,3},{8,12},{12,8},{9,1... | collective-permute-start | bytes 442376 | tf_op jit(solution)/shard_map/ppermute | solution.py:92
  9.9 5.4 %collective-permute-start.4 = (bf16[2,64,576]{2,1,0:T(8,128)(2,1)S(1)}, bf16[2,64,576]{2,1,0:T(8,128)(2,1)S(1)}, u32[]{:S(2)}, u32[]{:S(2)}) collective-permute-start(bf16[2,64,576]{2,1,0:T(8,128)(2,1)S(1)} %maximum_select_fusion.17), channel_id=1, source_target_pairs={{0,2},{1,3},{2,0},{3,1},{4,6},{5,7},{6,4},{7,5},{8,10},{9,11},{10,... | collective-permute-start | bytes 442376 | tf_op jit(solution)/shard_map/ppermute | solution.py:92
  13.2 7.5 %collective-permute-start.2 = (bf16[4,64,576]{2,1,0:T(8,128)(2,1)S(1)}, bf16[4,64,576]{2,1,0:T(8,128)(2,1)S(1)}, u32[]{:S(2)}, u32[]{:S(2)}) collective-permute-start(bf16[4,64,576]{2,1,0:T(8,128)(2,1)S(1)} %maximum_select_fusion.11), channel_id=1, source_target_pairs={{0,1},{1,0},{2,3},{3,2},{4,5},{5,4},{6,7},{7,6},{8,9},{9,8},{10,11... | collective-permute-start | bytes 884744 | tf_op jit(solution)/shard_map/ppermute | solution.py:92
  15.3 5.6 %collective-permute-start.5 = (bf16[4,64,576]{2,1,0:T(8,128)(2,1)S(1)}, bf16[4,64,576]{2,1,0:T(8,128)(2,1)S(1)}, u32[]{:S(2)}, u32[]{:S(2)}) collective-permute-start(bf16[4,64,576]{2,1,0:T(8,128)(2,1)S(1)} %maximum_select_fusion.12), channel_id=1, source_target_pairs={{0,1},{1,0},{2,3},{3,2},{4,5},{5,4},{6,7},{7,6},{8,9},{9,8},{10,11... | collective-permute-start | bytes 884744 | tf_op jit(solution)/shard_map/ppermute | solution.py:92
  20.6 1.7 copy-start.11
  20.7 5.5 %copy-start.13 = (pred[4]{0:T(512)(128)(4,1)}, pred[4]{0:T(512)(128)(4,1)S(1)}, u32[]{:S(2)}) copy-start(pred[4]{0:T(512)(128)(4,1)S(1)} %iota_compare_fusion.4) | copy-start | bytes 16
  21.2 1.2 copy-start.10
  59.8 2.2 copy-start.2
  62.0 5.2 %collective-permute-start.16 = (f32[16,40,576]{2,1,0:T(8,128)}, f32[16,40,576]{2,1,0:T(8,128)}, u32[]{:S(2)}, u32[]{:S(2)}) collective-permute-start(f32[16,40,576]{2,1,0:T(8,128)} %constant_dynamic-slice_fusion.10), channel_id=1, source_target_pairs={{0,1},{1,0},{2,3},{3,2},{4,5},{5,4},{6,7},{7,6},{8,9},{9,8},{10,11... | collective-permute-start | bytes 4423688 | tf_op jit(solution)/shard_map/ppermute | solution.py:70
  63.2 2.4 %copy-start = (f32[2,2,2,2,2,48,576]{6,5,4,3,2,1,0:T(8,128)}, f32[2,2,2,2,2,48,576]{6,5,4,3,2,1,0:T(8,128)S(1)}, u32[]{:S(2)}) copy-start(f32[2,2,2,2,2,48,576]{6,5,4,3,2,1,0:T(8,128)S(1)} %copy.46) | copy-start | bytes 10616836
  65.1 5.4 %collective-permute-start.11 = (f32[16,40,576]{2,1,0:T(8,128)}, f32[16,40,576]{2,1,0:T(8,128)}, u32[]{:S(2)}, u32[]{:S(2)}) collective-permute-start(f32[16,40,576]{2,1,0:T(8,128)} %constant_dynamic-slice_fusion.15), channel_id=1, source_target_pairs={{0,1},{1,0},{2,3},{3,2},{4,5},{5,4},{6,7},{7,6},{8,9},{9,8},{10,11... | collective-permute-start | bytes 4423688 | tf_op jit(solution)/shard_map/ppermute | solution.py:70
  67.0 6.0 %collective-permute-start.6 = (f32[16,48,576]{2,1,0:T(8,128)}, f32[16,48,576]{2,1,0:T(8,128)}, u32[]{:S(2)}, u32[]{:S(2)}) collective-permute-start(f32[16,48,576]{2,1,0:T(8,128)} %constant_dynamic-slice_fusion.20), channel_id=1, source_target_pairs={{0,1},{1,0},{2,3},{3,2},{4,5},{5,4},{6,7},{7,6},{8,9},{9,8},{10,11... | collective-permute-start | bytes 5308424 | tf_op jit(solution)/shard_map/ppermute | solution.py:70
  69.3 20.6 %collective-permute-start.17 = (f32[8,40,576]{2,1,0:T(8,128)S(1)}, f32[8,40,576]{2,1,0:T(8,128)S(1)}, u32[]{:S(2)}, u32[]{:S(2)}) collective-permute-start(f32[8,40,576]{2,1,0:T(8,128)S(1)} %constant_dynamic-slice_fusion.9), channel_id=1, source_target_pairs={{0,2},{1,3},{2,0},{3,1},{4,6},{5,7},{6,4},{7,5},{8,10},{9,11},{10,... | collective-permute-start | bytes 2211848 | tf_op jit(solution)/shard_map/ppermute | solution.py:70
  70.5 2.6 %copy-start.1 = (f32[2,2,2,2,2,48,576]{6,5,4,3,2,1,0:T(8,128)S(1)}, f32[2,2,2,2,2,48,576]{6,5,4,3,2,1,0:T(8,128)}, u32[]{:S(2)}) copy-start(f32[2,2,2,2,2,48,576]{6,5,4,3,2,1,0:T(8,128)} %copy-done) | copy-start | bytes 10616836
  72.4 20.4 %collective-permute-start.12 = (f32[8,40,576]{2,1,0:T(8,128)S(1)}, f32[8,40,576]{2,1,0:T(8,128)S(1)}, u32[]{:S(2)}, u32[]{:S(2)}) collective-permute-start(f32[8,40,576]{2,1,0:T(8,128)S(1)} %constant_dynamic-slice_fusion.14), channel_id=1, source_target_pairs={{0,4},{4,0},{1,5},{5,1},{2,6},{6,2},{3,7},{7,3},{8,12},{12,8},{9,1... | collective-permute-start | bytes 2211848 | tf_op jit(solution)/shard_map/ppermute | solution.py:70
  76.0 36.8 %collective-permute-start.7 = (f32[8,48,576]{2,1,0:T(8,128)}, f32[8,48,576]{2,1,0:T(8,128)}, u32[]{:S(2)}, u32[]{:S(2)}) collective-permute-start(f32[8,48,576]{2,1,0:T(8,128)} %constant_dynamic-slice_fusion.19), channel_id=1, source_target_pairs={{0,8},{8,0},{16,24},{24,16},{1,9},{9,1},{17,25},{25,17},{2,10},{10... | collective-permute-start | bytes 2654216 | tf_op jit(solution)/shard_map/ppermute | solution.py:70
  90.0 5.4 %copy-start.8 = (bf16[4,32,576]{2,1,0:T(8,128)(2,1)S(1)}, bf16[4,32,576]{2,1,0:T(8,128)(2,1)}, u32[]{:S(2)}) copy-start(bf16[4,32,576]{2,1,0:T(8,128)(2,1)} %param.13) | copy-start | bytes 442372
  90.8 18.0 %collective-permute-start.18 = (f32[4,40,576]{2,1,0:T(8,128)}, f32[4,40,576]{2,1,0:T(8,128)S(1)}, u32[]{:S(2)}, u32[]{:S(2)}) collective-permute-start(f32[4,40,576]{2,1,0:T(8,128)} %constant_dynamic-slice_fusion.8), channel_id=1, source_target_pairs={{0,8},{8,0},{16,24},{24,16},{1,9},{9,1},{17,25},{25,17},{2,10},{10... | collective-permute-start | bytes 1105928 | tf_op jit(solution)/shard_map/ppermute | solution.py:70
  92.8 0.9 copy-start.5
  94.5 15.5 %collective-permute-start.13 = (f32[4,40,576]{2,1,0:T(8,128)}, f32[4,40,576]{2,1,0:T(8,128)}, u32[]{:S(2)}, u32[]{:S(2)}) collective-permute-start(f32[4,40,576]{2,1,0:T(8,128)} %constant_dynamic-slice_fusion.13), channel_id=1, source_target_pairs={{0,2},{1,3},{2,0},{3,1},{4,6},{5,7},{6,4},{7,5},{8,10},{9,11},{10,... | collective-permute-start | bytes 1105928 | tf_op jit(solution)/shard_map/ppermute | solution.py:70
  108.9 6.4 %collective-permute-start.19 = (f32[2,40,576]{2,1,0:T(8,128)S(1)}, f32[2,40,576]{2,1,0:T(8,128)S(1)}, u32[]{:S(2)}, u32[]{:S(2)}) collective-permute-start(f32[2,40,576]{2,1,0:T(8,128)S(1)} %constant_dynamic-slice_fusion.7), channel_id=1, source_target_pairs={{0,4},{4,0},{1,5},{5,1},{2,6},{6,2},{3,7},{7,3},{8,12},{12,8},{9,1... | collective-permute-start | bytes 552968 | tf_op jit(solution)/shard_map/ppermute | solution.py:70
  111.2 6.8 %collective-permute-start.14 = (f32[2,40,576]{2,1,0:T(8,128)S(1)}, f32[2,40,576]{2,1,0:T(8,128)S(1)}, u32[]{:S(2)}, u32[]{:S(2)}) collective-permute-start(f32[2,40,576]{2,1,0:T(8,128)S(1)} %constant_dynamic-slice_fusion.12), channel_id=1, source_target_pairs={{0,8},{8,0},{16,24},{24,16},{1,9},{9,1},{17,25},{25,17},{2,10},{10... | collective-permute-start | bytes 552968 | tf_op jit(solution)/shard_map/ppermute | solution.py:70
  114.2 13.5 %copy-start.9 = (f32[4,576]{1,0:T(4,128)S(1)}, f32[4,576]{1,0:T(4,128)}, u32[]{:S(2)}) copy-start(f32[4,576]{1,0:T(4,128)} %param.11) | copy-start | bytes 27652
  114.2 11.6 %collective-permute-start.8 = (f32[4,48,576]{2,1,0:T(8,128)S(1)}, f32[4,48,576]{2,1,0:T(8,128)S(1)}, u32[]{:S(2)}, u32[]{:S(2)}) collective-permute-start(f32[4,48,576]{2,1,0:T(8,128)S(1)} %constant_dynamic-slice_fusion.18), channel_id=1, source_target_pairs={{0,4},{4,0},{1,5},{5,1},{2,6},{6,2},{3,7},{7,3},{8,12},{12,8},{9,1... | collective-permute-start | bytes 1327112 | tf_op jit(solution)/shard_map/ppermute | solution.py:70
  115.4 12.4 %collective-permute-start.20 = (f32[1,40,576]{2,1,0:T(8,128)S(1)}, f32[1,40,576]{2,1,0:T(8,128)S(1)}, u32[]{:S(2)}, u32[]{:S(2)}) collective-permute-start(f32[1,40,576]{2,1,0:T(8,128)S(1)} %constant_dynamic-slice_fusion.6), channel_id=1, source_target_pairs={{0,16},{8,24},{16,0},{24,8},{1,17},{9,25},{17,1},{25,9},{2,18},{10... | collective-permute-start | bytes 276488 | tf_op jit(solution)/shard_map/ppermute | solution.py:70
  118.1 9.7 %collective-permute-start.15 = (f32[1,40,576]{2,1,0:T(8,128)S(1)}, f32[1,40,576]{2,1,0:T(8,128)S(1)}, u32[]{:S(2)}, u32[]{:S(2)}) collective-permute-start(f32[1,40,576]{2,1,0:T(8,128)S(1)} %constant_dynamic-slice_fusion.11), channel_id=1, source_target_pairs={{0,16},{8,24},{16,0},{24,8},{1,17},{9,25},{17,1},{25,9},{2,18},{10... | collective-permute-start | bytes 276488 | tf_op jit(solution)/shard_map/ppermute | solution.py:70
  126.0 8.7 %collective-permute-start.9 = (f32[2,48,576]{2,1,0:T(8,128)S(1)}, f32[2,48,576]{2,1,0:T(8,128)S(1)}, u32[]{:S(2)}, u32[]{:S(2)}) collective-permute-start(f32[2,48,576]{2,1,0:T(8,128)S(1)} %constant_dynamic-slice_fusion.17), channel_id=1, source_target_pairs={{0,2},{1,3},{2,0},{3,1},{4,6},{5,7},{6,4},{7,5},{8,10},{9,11},{10,... | collective-permute-start | bytes 663560 | tf_op jit(solution)/shard_map/ppermute | solution.py:70
  127.9 28.3 %copy-start.6 = (bf16[40,576]{1,0:T(8,128)(2,1)}, bf16[40,576]{1,0:T(8,128)(2,1)S(1)}, u32[]{:S(2)}) copy-start(bf16[40,576]{1,0:T(8,128)(2,1)S(1)} %get-tuple-element.9) | copy-start | bytes 138244
  127.9 6.2 %collective-permute-start.26 = (bf16[1,40,576]{2,1,0:T(8,128)(2,1)S(1)}, bf16[1,40,576]{2,1,0:T(8,128)(2,1)S(1)}, u32[]{:S(2)}, u32[]{:S(2)}) collective-permute-start(bf16[1,40,576]{2,1,0:T(8,128)(2,1)S(1)} %bitcast.150), channel_id=1, source_target_pairs={{0,16},{8,24},{16,0},{24,8},{1,17},{9,25},{17,1},{25,9},{2,18},{10... | collective-permute-start | bytes 138248 | tf_op jit(solution)/shard_map/ppermute | solution.py:92
  130.5 6.2 %collective-permute-start.31 = (bf16[1,40,576]{2,1,0:T(8,128)(2,1)S(1)}, bf16[1,40,576]{2,1,0:T(8,128)(2,1)S(1)}, u32[]{:S(2)}, u32[]{:S(2)}) collective-permute-start(bf16[1,40,576]{2,1,0:T(8,128)(2,1)S(1)} %bitcast.152), channel_id=1, source_target_pairs={{0,16},{8,24},{16,0},{24,8},{1,17},{9,25},{17,1},{25,9},{2,18},{10... | collective-permute-start | bytes 138248 | tf_op jit(solution)/shard_map/ppermute | solution.py:92
  134.1 8.8 %collective-permute-start.27 = (bf16[2,40,576]{2,1,0:T(8,128)(2,1)S(1)}, bf16[2,40,576]{2,1,0:T(8,128)(2,1)S(1)}, u32[]{:S(2)}, u32[]{:S(2)}) collective-permute-start(bf16[2,40,576]{2,1,0:T(8,128)(2,1)S(1)} %maximum_select_fusion.19), channel_id=1, source_target_pairs={{0,8},{8,0},{16,24},{24,16},{1,9},{9,1},{17,25},{25,17},{2,10},{10... | collective-permute-start | bytes 276488 | tf_op jit(solution)/shard_map/ppermute | solution.py:92
  134.7 8.1 %collective-permute-start.10 = (f32[1,48,576]{2,1,0:T(8,128)S(1)}, f32[1,48,576]{2,1,0:T(8,128)S(1)}, u32[]{:S(2)}, u32[]{:S(2)}) collective-permute-start(f32[1,48,576]{2,1,0:T(8,128)S(1)} %constant_dynamic-slice_fusion.16), channel_id=1, source_target_pairs={{0,16},{8,24},{16,0},{24,8},{1,17},{9,25},{17,1},{25,9},{2,18},{10... | collective-permute-start | bytes 331784 | tf_op jit(solution)/shard_map/ppermute | solution.py:70
  136.8 12.5 %collective-permute-start.32 = (bf16[2,40,576]{2,1,0:T(8,128)(2,1)S(1)}, bf16[2,40,576]{2,1,0:T(8,128)(2,1)S(1)}, u32[]{:S(2)}, u32[]{:S(2)}) collective-permute-start(bf16[2,40,576]{2,1,0:T(8,128)(2,1)S(1)} %maximum_select_fusion.20), channel_id=1, source_target_pairs={{0,4},{4,0},{1,5},{5,1},{2,6},{6,2},{3,7},{7,3},{8,12},{12,8},{9,1... | collective-permute-start | bytes 276488 | tf_op jit(solution)/shard_map/ppermute | solution.py:92
  142.8 5.5 %collective-permute-start.21 = (bf16[1,48,576]{2,1,0:T(8,128)(2,1)S(1)}, bf16[1,48,576]{2,1,0:T(8,128)(2,1)S(1)}, u32[]{:S(2)}, u32[]{:S(2)}) collective-permute-start(bf16[1,48,576]{2,1,0:T(8,128)(2,1)S(1)} %bitcast.148), channel_id=1, source_target_pairs={{0,16},{8,24},{16,0},{24,8},{1,17},{9,25},{17,1},{25,9},{2,18},{10... | collective-permute-start | bytes 165896 | tf_op jit(solution)/shard_map/ppermute | solution.py:92
  143.0 13.1 %collective-permute-start.28 = (bf16[4,40,576]{2,1,0:T(8,128)(2,1)S(1)}, bf16[4,40,576]{2,1,0:T(8,128)(2,1)S(1)}, u32[]{:S(2)}, u32[]{:S(2)}) collective-permute-start(bf16[4,40,576]{2,1,0:T(8,128)(2,1)S(1)} %maximum_select_fusion.14), channel_id=1, source_target_pairs={{0,2},{1,3},{2,0},{3,1},{4,6},{5,7},{6,4},{7,5},{8,10},{9,11},{10,... | collective-permute-start | bytes 552968 | tf_op jit(solution)/shard_map/ppermute | solution.py:92
  148.3 6.1 %collective-permute-start.22 = (bf16[2,48,576]{2,1,0:T(8,128)(2,1)S(1)}, bf16[2,48,576]{2,1,0:T(8,128)(2,1)S(1)}, u32[]{:S(2)}, u32[]{:S(2)}) collective-permute-start(bf16[2,48,576]{2,1,0:T(8,128)(2,1)S(1)} %maximum_select_fusion.18), channel_id=1, source_target_pairs={{0,2},{1,3},{2,0},{3,1},{4,6},{5,7},{6,4},{7,5},{8,10},{9,11},{10,... | collective-permute-start | bytes 331784 | tf_op jit(solution)/shard_map/ppermute | solution.py:92
  149.3 7.4 %collective-permute-start.33 = (bf16[4,40,576]{2,1,0:T(8,128)(2,1)S(1)}, bf16[4,40,576]{2,1,0:T(8,128)(2,1)S(1)}, u32[]{:S(2)}, u32[]{:S(2)}) collective-permute-start(bf16[4,40,576]{2,1,0:T(8,128)(2,1)S(1)} %maximum_select_fusion.15), channel_id=1, source_target_pairs={{0,8},{8,0},{16,24},{24,16},{1,9},{9,1},{17,25},{25,17},{2,10},{10... | collective-permute-start | bytes 552968 | tf_op jit(solution)/shard_map/ppermute | solution.py:92
  154.4 6.3 %collective-permute-start.23 = (bf16[4,48,576]{2,1,0:T(8,128)(2,1)S(1)}, bf16[4,48,576]{2,1,0:T(8,128)(2,1)S(1)}, u32[]{:S(2)}, u32[]{:S(2)}) collective-permute-start(bf16[4,48,576]{2,1,0:T(8,128)(2,1)S(1)} %maximum_select_fusion.13), channel_id=1, source_target_pairs={{0,4},{4,0},{1,5},{5,1},{2,6},{6,2},{3,7},{7,3},{8,12},{12,8},{9,1... | collective-permute-start | bytes 663560 | tf_op jit(solution)/shard_map/ppermute | solution.py:92
  156.1 9.0 %collective-permute-start.29 = (bf16[8,40,576]{2,1,0:T(8,128)(2,1)S(1)}, bf16[8,40,576]{2,1,0:T(8,128)(2,1)S(1)}, u32[]{:S(2)}, u32[]{:S(2)}) collective-permute-start(bf16[8,40,576]{2,1,0:T(8,128)(2,1)S(1)} %maximum_select_fusion.9), channel_id=1, source_target_pairs={{0,4},{4,0},{1,5},{5,1},{2,6},{6,2},{3,7},{7,3},{8,12},{12,8},{9,1... | collective-permute-start | bytes 1105928 | tf_op jit(solution)/shard_map/ppermute | solution.py:92
  156.9 8.6 %collective-permute-start.34 = (bf16[8,40,576]{2,1,0:T(8,128)(2,1)S(1)}, bf16[8,40,576]{2,1,0:T(8,128)(2,1)S(1)}, u32[]{:S(2)}, u32[]{:S(2)}) collective-permute-start(bf16[8,40,576]{2,1,0:T(8,128)(2,1)S(1)} %maximum_select_fusion.10), channel_id=1, source_target_pairs={{0,2},{1,3},{2,0},{3,1},{4,6},{5,7},{6,4},{7,5},{8,10},{9,11},{10,... | collective-permute-start | bytes 1105928 | tf_op jit(solution)/shard_map/ppermute | solution.py:92
  160.8 8.9 %collective-permute-start.24 = (bf16[8,48,576]{2,1,0:T(8,128)(2,1)S(1)}, bf16[8,48,576]{2,1,0:T(8,128)(2,1)S(1)}, u32[]{:S(2)}, u32[]{:S(2)}) collective-permute-start(bf16[8,48,576]{2,1,0:T(8,128)(2,1)S(1)} %maximum_select_fusion.8), channel_id=1, source_target_pairs={{0,8},{8,0},{16,24},{24,16},{1,9},{9,1},{17,25},{25,17},{2,10},{10... | collective-permute-start | bytes 1327112 | tf_op jit(solution)/shard_map/ppermute | solution.py:92
  165.3 4.8 %collective-permute-start.30 = (bf16[16,40,576]{2,1,0:T(8,128)(2,1)S(1)}, bf16[16,40,576]{2,1,0:T(8,128)(2,1)S(1)}, u32[]{:S(2)}, u32[]{:S(2)}) collective-permute-start(bf16[16,40,576]{2,1,0:T(8,128)(2,1)S(1)} %maximum_select_fusion.4), channel_id=1, source_target_pairs={{0,1},{1,0},{2,3},{3,2},{4,5},{5,4},{6,7},{7,6},{8,9},{9,8},{10,11... | collective-permute-start | bytes 2211848 | tf_op jit(solution)/shard_map/ppermute | solution.py:92
  165.6 5.0 %collective-permute-start.35 = (bf16[16,40,576]{2,1,0:T(8,128)(2,1)S(1)}, bf16[16,40,576]{2,1,0:T(8,128)(2,1)}, u32[]{:S(2)}, u32[]{:S(2)}) collective-permute-start(bf16[16,40,576]{2,1,0:T(8,128)(2,1)S(1)} %maximum_select_fusion.5), channel_id=1, source_target_pairs={{0,1},{1,0},{2,3},{3,2},{4,5},{5,4},{6,7},{7,6},{8,9},{9,8},{10,11... | collective-permute-start | bytes 2211848 | tf_op jit(solution)/shard_map/ppermute | solution.py:92
  170.0 2.8 %collective-permute-start.25 = (bf16[16,48,576]{2,1,0:T(8,128)(2,1)S(1)}, bf16[16,48,576]{2,1,0:T(8,128)(2,1)}, u32[]{:S(2)}, u32[]{:S(2)}) collective-permute-start(bf16[16,48,576]{2,1,0:T(8,128)(2,1)S(1)} %maximum_select_fusion.3), channel_id=1, source_target_pairs={{0,1},{1,0},{2,3},{3,2},{4,5},{5,4},{6,7},{7,6},{8,9},{9,8},{10,11... | collective-permute-start | bytes 2654216 | tf_op jit(solution)/shard_map/ppermute | solution.py:92
  182.6 10.0 %copy-start.12 = (f32[256,8,128]{2,1,0:T(8,128)S(1)}, f32[256,8,128]{2,1,0:T(8,128)}, u32[]{:S(2)}) copy-start(f32[256,8,128]{2,1,0:T(8,128)} %copy-done.11) | copy-start | bytes 3145732
  182.6 10.0 %copy-start.14 = (pred[4]{0:T(512)(128)(4,1)S(1)}, pred[4]{0:T(512)(128)(4,1)}, u32[]{:S(2)}) copy-start(pred[4]{0:T(512)(128)(4,1)} %copy-done.13) | copy-start | bytes 16
  182.6 20.6 %slice-start = ((s8[4718592]{0:T(1024)(128)(4,1)}), s8[524288]{0:T(1024)(128)(4,1)S(1)}, s32[]{:S(2)}) async-start(s8[4718592]{0:T(1024)(128)(4,1)} %bitcast.155), calls=%async_computation | async-start | bytes 1048576
  192.5 10.6 %slice-start.1 = ((s8[4718592]{0:T(1024)(128)(4,1)}), s8[4194304]{0:T(1024)(128)(4,1)S(1)}, s32[]{:S(2)}) async-start(s8[4718592]{0:T(1024)(128)(4,1)} %bitcast.155), calls=%async_computation.1 | async-start | bytes 8388608
  211.8 5.1 %collective-permute-start.36 = (f32[4,64,576]{2,1,0:T(8,128)}, f32[4,64,576]{2,1,0:T(8,128)}, u32[]{:S(2)}, u32[]{:S(2)}) collective-permute-start(f32[4,64,576]{2,1,0:T(8,128)} %constant_dynamic-slice_fusion.5), channel_id=1, source_target_pairs={{0,1},{1,0},{2,3},{3,2},{4,5},{5,4},{6,7},{7,6},{8,9},{9,8},{10,11... | collective-permute-start | bytes 1769480 | tf_op jit(solution)/shard_map/ppermute | solution.py:70
  212.2 4.1 %copy-start.7 = (bf16[40,576]{1,0:T(8,128)(2,1)S(1)}, bf16[40,576]{1,0:T(8,128)(2,1)}, u32[]{:S(2)}) copy-start(bf16[40,576]{1,0:T(8,128)(2,1)} %copy-done.6) | copy-start | bytes 138244
  214.0 3.0 %copy-start.4 = (f32[2,2,2,64,576]{4,3,2,1,0:T(8,128)S(1)}, f32[2,2,2,64,576]{4,3,2,1,0:T(8,128)}, u32[]{:S(2)}) copy-start(f32[2,2,2,64,576]{4,3,2,1,0:T(8,128)} %copy.53) | copy-start | bytes 3538948
  214.0 5.7 %copy-start.3 = (f32[2,2,2,64,576]{4,3,2,1,0:T(8,128)S(1)}, f32[2,2,2,64,576]{4,3,2,1,0:T(8,128)}, u32[]{:S(2)}) copy-start(f32[2,2,2,64,576]{4,3,2,1,0:T(8,128)} %copy.54) | copy-start | bytes 3538948
  216.1 3.6 %collective-permute-start.39 = (f32[4,64,576]{2,1,0:T(8,128)}, f32[4,64,576]{2,1,0:T(8,128)S(1)}, u32[]{:S(2)}, u32[]{:S(2)}) collective-permute-start(f32[4,64,576]{2,1,0:T(8,128)} %constant_dynamic-slice_fusion.2), channel_id=1, source_target_pairs={{0,1},{1,0},{2,3},{3,2},{4,5},{5,4},{6,7},{7,6},{8,9},{9,8},{10,11... | collective-permute-start | bytes 1769480 | tf_op jit(solution)/shard_map/ppermute | solution.py:70
  218.1 10.1 %collective-permute-start.37 = (f32[2,64,576]{2,1,0:T(8,128)S(1)}, f32[2,64,576]{2,1,0:T(8,128)S(1)}, u32[]{:S(2)}, u32[]{:S(2)}) collective-permute-start(f32[2,64,576]{2,1,0:T(8,128)S(1)} %constant_dynamic-slice_fusion.4), channel_id=1, source_target_pairs={{0,4},{4,0},{1,5},{5,1},{2,6},{6,2},{3,7},{7,3},{8,12},{12,8},{9,1... | collective-permute-start | bytes 884744 | tf_op jit(solution)/shard_map/ppermute | solution.py:70
  219.8 9.8 %collective-permute-start.40 = (f32[2,64,576]{2,1,0:T(8,128)S(1)}, f32[2,64,576]{2,1,0:T(8,128)S(1)}, u32[]{:S(2)}, u32[]{:S(2)}) collective-permute-start(f32[2,64,576]{2,1,0:T(8,128)S(1)} %constant_dynamic-slice_fusion.1), channel_id=1, source_target_pairs={{0,2},{1,3},{2,0},{3,1},{4,6},{5,7},{6,4},{7,5},{8,10},{9,11},{10,... | collective-permute-start | bytes 884744 | tf_op jit(solution)/shard_map/ppermute | solution.py:70
  228.3 5.7 %collective-permute-start.38 = (f32[1,64,576]{2,1,0:T(8,128)S(1)}, f32[1,64,576]{2,1,0:T(8,128)S(1)}, u32[]{:S(2)}, u32[]{:S(2)}) collective-permute-start(f32[1,64,576]{2,1,0:T(8,128)S(1)} %constant_dynamic-slice_fusion.3), channel_id=1, source_target_pairs={{0,2},{1,3},{2,0},{3,1},{4,6},{5,7},{6,4},{7,5},{8,10},{9,11},{10,... | collective-permute-start | bytes 442376 | tf_op jit(solution)/shard_map/ppermute | solution.py:70
  229.7 5.4 %collective-permute-start.41 = (f32[1,64,576]{2,1,0:T(8,128)S(1)}, f32[1,64,576]{2,1,0:T(8,128)S(1)}, u32[]{:S(2)}, u32[]{:S(2)}) collective-permute-start(f32[1,64,576]{2,1,0:T(8,128)S(1)} %constant_dynamic-slice_fusion), channel_id=1, source_target_pairs={{0,4},{4,0},{1,5},{5,1},{2,6},{6,2},{3,7},{7,3},{8,12},{12,8},{9,1... | collective-permute-start | bytes 442376 | tf_op jit(solution)/shard_map/ppermute | solution.py:70

commit v15 on v14

--- a/solution.py
+++ b/solution.py
@@ -130,8 +130,9 @@
     high_hot = ((local_ids >> low_bits)[:, :, None] == lax.iota(jnp.int32, feat_dev // side)).astype(jnp.bfloat16)
     low_hot = ((local_ids & (side - 1))[:, :, None] == lax.iota(jnp.int32, side)).astype(jnp.bfloat16)
     selected = jnp.einsum("tka,tkb->tab", high_hot, low_hot, preferred_element_type=jnp.float32)
+    selected = selected.astype(jnp.bfloat16)
     selected = selected.reshape(tokens, feat_dev)
-    acts = (selected * pre).astype(jnp.bfloat16)
+    acts = (selected.astype(jnp.float32) * pre).astype(jnp.bfloat16)
     live_layers = lax.iota(jnp.int32, layer_count) >= layer_id
     partial_value = jnp.einsum("tf,lfd->ltd", acts, decoder[0], preferred_element_type=jnp.float32)
     partial_value = jnp.where(live_layers[:, None, None], partial_value, 0.0)
@@ -160,7 +161,7 @@
     )
     kept = jnp.where(live_layers[:, None, None], piece, jnp.zeros_like(piece))
     grad_act = jnp.einsum("ltd,lfd->tf", kept, decoder[0], preferred_element_type=jnp.float32)
-    grad_pre = (selected * grad_act).astype(jnp.bfloat16)
+    grad_pre = (selected.astype(jnp.float32) * grad_act).astype(jnp.bfloat16)
     grad_part = lax.dot_general(
         grad_pre, encoder[0], (((1,), (1,)), ((), ())), preferred_element_type=jnp.float32
     )

time: 237 us -> 237 us (level)
  no operation moved by 1% of the time
where the time goes in v15:
time: 237 us; the launch traced here: 236 us
  waiting for transfers between devices  73.6 us (31%)
  local copies, waits for them, and re-layouts  61.9 us (26%)
  starting transfers between devices  45 us (19%)
  matrix products  34.9 us (15%)
  other arithmetic  19 us (8%)
    ppermute x21, waiting for transfers between devices, reduce_scatter(): recv = lax.ppermute(send.astype(wire), axis, partner(axis, bit))  49 us
    ppermute x21, waiting for transfers between devices, all_gather(): recv = lax.ppermute(parts[p], axis, partner(axis, bit))  24.6 us
    ppermute x21, starting transfers between devices, reduce_scatter(): recv = lax.ppermute(send.astype(wire), axis, partner(axis, bit))  22.7 us
    ppermute x21, starting transfers between devices, all_gather(): recv = lax.ppermute(parts[p], axis, partner(axis, bit))  22.3 us
    reshape x2, local copies, waits for them, and re-layouts, local(): partial_value.reshape(layer_count, slots, slot_rows, feat_parts, cols)  18.7 us
    dot_general x1, matrix products, local(): jnp.einsum('tf,lfd->ltd', acts, decoder[0], preferred_element_type=jnp.fl...  13.9 us
    dynamic_slice x21, local copies, waits for them, and re-layouts, reduce_scatter(): send = lax.dynamic_slice_in_dim(parts[p], (1 - own) * half, half, 0)  11.6 us
    dot_general x1, matrix products, local(): jnp.einsum('ltd,lfd->tf', kept, decoder[0], preferred_element_type=jnp.fl...  10.6 us
  transfers between devices with their start and end apart: 42, of which 20 were waited for; matrix products, arithmetic and copies ran while one was open for 14% of the time, Pallas kernels for 0%

profile of v15, /device:TPU:0, one launch (start us, length us, event | category | flops | bytes accessed | tf_op | source)
XLA Modules:
  0.0 235.9 jit_solution(18359639245222827050)
XLA Ops:
  0.6 1.1 fusion.49
  1.9 3.1 %collective-permute-start = (bf16[1,64,576]{2,1,0:T(8,128)(2,1)S(1)}, bf16[1,64,576]{2,1,0:T(8,128)(2,1)S(1)}, u32[]{:S(2)}, u32[]{:S(2)}) collective-permute-start(bf16[1,64,576]{2,1,0:T(8,128)(2,1)S(1)} %copy.57), channel_id=1, source_target_pairs={{0,2},{1,3},{2,0},{3,1},{4,6},{5,7},{6,4},{7,5},{8,10},{9,11},{10,... | collective-permute-start | bytes 221192 | tf_op jit(solution)/shard_map/ppermute | solution.py:92
  5.1 1.6 collective-permute-start.3
  7.4 2.0 collective-permute-start.1
  9.9 1.2 collective-permute-start.4
  12.1 0.9 collective-permute-done.1
  13.3 2.0 collective-permute-done.4
  15.4 5.2 %fusion.33 = f32[256,8,128]{2,1,0:T(8,128)S(1)} fusion(s32[256,64]{1,0:T(8,128)S(1)} %copy.39, s32[256,64]{1,0:T(8,128)S(1)} %copy.38), kind=kOutput, calls=%fused_computation.32 | convolution fusion | flops 36306944 | bytes 1179648 | tf_op jit(solution)/shard_map/tka,tkb->tab/dot_general | solution.py:132
  21.3 1.0 copy.44
  22.4 3.8 %fusion.39 = bf16[256,1024,1]{1,0,2:T(8,128)(2,1)S(1)} fusion(bf16[1,2304,1024]{2,1,0:T(8,128)(2,1)} %param.8, bf16[288,8,2,128]{3,2,1,0:T(2,128)(2,1)S(1)} %bitcast.147, f32[32,8,8,128]{3,2,1,0:T(8,128)S(1)} %bitcast.159, f32[1024]{0:T(1024)S(1)} %bitcast.158), kind=kOutput, calls=%fused_computation.34 | convolution fusion | flops 1208745984 | bytes 7475200 | tf_op jit(solution)/shard_map/dot_general | solution.py:124
  26.2 13.9 %select_bitcast_fusion = f32[4,256,2304]{2,1,0:T(8,128)} fusion(bf16[256,1024,1]{1,0,2:T(8,128)(2,1)S(1)} %fusion.39, bf16[1,4,1024,2304]{3,2,1,0:T(8,128)(2,1)} %param.10, pred[4]{0:T(512)(128)(4,1)S(1)} %iota_compare_fusion.8), kind=kOutput, calls=%fused_computation.4 | convolution fusion | flops 4834197504 | bytes 28835844 | tf_op jit(solution)/shard_map/tf,lfd->ltd/dot_general | solution.py:137
  40.0 13.2 %reshape.139 = f32[4,8,32,4,576]{4,3,2,1,0:T(4,128)} reshape(f32[4,256,2304]{2,1,0:T(8,128)} %select_bitcast_fusion) | data formatting | bytes 18874368 | tf_op jit(solution)/shard_map/reshape | solution.py:140
  53.2 5.5 %copy.45 = f32[4,8,32,4,576]{4,2,0,3,1:T(8,128)S(1)} copy(f32[4,8,32,4,576]{4,3,2,1,0:T(4,128)} %reshape.139) | data formatting | bytes 18874368 | tf_op jit(solution)/shard_map/reshape | solution.py:140
  59.8 1.4 constant_dynamic-slice_fusion.10
  63.5 1.6 constant_dynamic-slice_fusion.15
  65.6 1.4 constant_dynamic-slice_fusion.20
  67.1 2.1 dynamic-slice_add_fusion.1
  69.3 1.2 collective-permute-start.17
  70.5 1.7 dynamic-slice_add_fusion.2
  73.1 1.8 dynamic-slice_add_fusion
  75.0 1.1 constant_dynamic-slice_fusion.19
  76.0 1.6 collective-permute-start.7
  77.6 12.3 %collective-permute-done.17 = f32[8,40,576]{2,1,0:T(8,128)S(1)} collective-permute-done((f32[8,40,576]{2,1,0:T(8,128)S(1)}, f32[8,40,576]{2,1,0:T(8,128)S(1)}, u32[]{:S(2)}, u32[]{:S(2)}) %collective-permute-start.17) | collective-permute-done | bytes 737312 | tf_op jit(solution)/shard_map/ppermute | solution.py:70
  90.8 1.7 collective-permute-start.18
  95.4 13.4 %collective-permute-done.18 = f32[4,40,576]{2,1,0:T(8,128)S(1)} collective-permute-done((f32[4,40,576]{2,1,0:T(8,128)}, f32[4,40,576]{2,1,0:T(8,128)S(1)}, u32[]{:S(2)}, u32[]{:S(2)}) %collective-permute-start.18) | collective-permute-done | bytes 368672 | tf_op jit(solution)/shard_map/ppermute | solution.py:70
  108.9 1.1 collective-permute-start.19
  110.0 1.2 dynamic-slice_add_fusion.10
  111.2 1.6 collective-permute-start.14
  112.9 1.3 dynamic-slice_add_fusion.3
  114.2 1.1 collective-permute-start.8
  115.4 2.7 %collective-permute-start.20 = (f32[1,40,576]{2,1,0:T(8,128)S(1)}, f32[1,40,576]{2,1,0:T(8,128)S(1)}, u32[]{:S(2)}, u32[]{:S(2)}) collective-permute-start(f32[1,40,576]{2,1,0:T(8,128)S(1)} %constant_dynamic-slice_fusion.6), channel_id=1, source_target_pairs={{0,16},{8,24},{16,0},{24,8},{1,17},{9,25},{17,1},{25,9},{2,18},{10... | collective-permute-start | bytes 276488 | tf_op jit(solution)/shard_map/ppermute | solution.py:70
  118.1 2.4 %collective-permute-start.15 = (f32[1,40,576]{2,1,0:T(8,128)S(1)}, f32[1,40,576]{2,1,0:T(8,128)S(1)}, u32[]{:S(2)}, u32[]{:S(2)}) collective-permute-start(f32[1,40,576]{2,1,0:T(8,128)S(1)} %constant_dynamic-slice_fusion.11), channel_id=1, source_target_pairs={{0,16},{8,24},{16,0},{24,8},{1,17},{9,25},{17,1},{25,9},{2,18},{10... | collective-permute-start | bytes 276488 | tf_op jit(solution)/shard_map/ppermute | solution.py:70
  120.5 5.4 %collective-permute-done.8 = f32[4,48,576]{2,1,0:T(8,128)S(1)} collective-permute-done((f32[4,48,576]{2,1,0:T(8,128)S(1)}, f32[4,48,576]{2,1,0:T(8,128)S(1)}, u32[]{:S(2)}, u32[]{:S(2)}) %collective-permute-start.8) | collective-permute-done | bytes 442400 | tf_op jit(solution)/shard_map/ppermute | solution.py:70
  126.0 1.7 collective-permute-start.9
  127.9 2.7 %collective-permute-start.26 = (bf16[1,40,576]{2,1,0:T(8,128)(2,1)S(1)}, bf16[1,40,576]{2,1,0:T(8,128)(2,1)S(1)}, u32[]{:S(2)}, u32[]{:S(2)}) collective-permute-start(bf16[1,40,576]{2,1,0:T(8,128)(2,1)S(1)} %bitcast.150), channel_id=1, source_target_pairs={{0,16},{8,24},{16,0},{24,8},{1,17},{9,25},{17,1},{25,9},{2,18},{10... | collective-permute-start | bytes 138248 | tf_op jit(solution)/shard_map/ppermute | solution.py:92
  130.9 3.2 %collective-permute-done.26 = bf16[1,40,576]{2,1,0:T(8,128)(2,1)S(1)} collective-permute-done((bf16[1,40,576]{2,1,0:T(8,128)(2,1)S(1)}, bf16[1,40,576]{2,1,0:T(8,128)(2,1)S(1)}, u32[]{:S(2)}, u32[]{:S(2)}) %collective-permute-start.26) | collective-permute-done | bytes 46112 | tf_op jit(solution)/shard_map/ppermute | solution.py:92
  134.7 2.0 collective-permute-start.10
  136.8 2.1 collective-permute-start.32
  138.9 3.9 %collective-permute-done.10 = f32[1,48,576]{2,1,0:T(8,128)S(1)} collective-permute-done((f32[1,48,576]{2,1,0:T(8,128)S(1)}, f32[1,48,576]{2,1,0:T(8,128)S(1)}, u32[]{:S(2)}, u32[]{:S(2)}) %collective-permute-start.10) | collective-permute-done | bytes 110624 | tf_op jit(solution)/shard_map/ppermute | solution.py:70
  143.0 2.1 collective-permute-start.28
  145.0 3.3 %collective-permute-done.21 = bf16[1,48,576]{2,1,0:T(8,128)(2,1)S(1)} collective-permute-done((bf16[1,48,576]{2,1,0:T(8,128)(2,1)S(1)}, bf16[1,48,576]{2,1,0:T(8,128)(2,1)S(1)}, u32[]{:S(2)}, u32[]{:S(2)}) %collective-permute-start.21) | collective-permute-done | bytes 55328 | tf_op jit(solution)/shard_map/ppermute | solution.py:92
  149.8 4.6 %collective-permute-done.22 = bf16[2,48,576]{2,1,0:T(8,128)(2,1)S(1)} collective-permute-done((bf16[2,48,576]{2,1,0:T(8,128)(2,1)S(1)}, bf16[2,48,576]{2,1,0:T(8,128)(2,1)S(1)}, u32[]{:S(2)}, u32[]{:S(2)}) %collective-permute-start.22) | collective-permute-done | bytes 110624 | tf_op jit(solution)/shard_map/ppermute | solution.py:92
  154.4 1.6 collective-permute-start.23
  157.5 3.2 %collective-permute-done.23 = bf16[4,48,576]{2,1,0:T(8,128)(2,1)S(1)} collective-permute-done((bf16[4,48,576]{2,1,0:T(8,128)(2,1)S(1)}, bf16[4,48,576]{2,1,0:T(8,128)(2,1)S(1)}, u32[]{:S(2)}, u32[]{:S(2)}) %collective-permute-start.23) | collective-permute-done | bytes 221216 | tf_op jit(solution)/shard_map/ppermute | solution.py:92
  160.8 1.6 collective-permute-start.24
  162.4 2.7 %collective-permute-done.29 = bf16[8,40,576]{2,1,0:T(8,128)(2,1)S(1)} collective-permute-done((bf16[8,40,576]{2,1,0:T(8,128)(2,1)S(1)}, bf16[8,40,576]{2,1,0:T(8,128)(2,1)S(1)}, u32[]{:S(2)}, u32[]{:S(2)}) %collective-permute-start.29) | collective-permute-done | bytes 368672 | tf_op jit(solution)/shard_map/ppermute | solution.py:92
  166.2 3.6 %collective-permute-done.24 = bf16[8,48,576]{2,1,0:T(8,128)(2,1)S(1)} collective-permute-done((bf16[8,48,576]{2,1,0:T(8,128)(2,1)S(1)}, bf16[8,48,576]{2,1,0:T(8,128)(2,1)S(1)}, u32[]{:S(2)}, u32[]{:S(2)}) %collective-permute-start.24) | collective-permute-done | bytes 442400 | tf_op jit(solution)/shard_map/ppermute | solution.py:92
  170.7 1.8 maximum_select_fusion.2
  172.8 2.1 maximum_select_fusion
  175.1 1.1 pad_maximum_fusion
  176.2 6.4 %copy.52 = bf16[4,8,32,4,576]{4,3,2,1,0:T(4,128)(2,1)} copy(bf16[4,8,32,4,576]{4,2,0,3,1:T(8,128)(2,1)S(1)} %bitcast.123) | data formatting | bytes 9437184 | tf_op jit(solution)/shard_map/transpose | solution.py:159
  182.6 10.0 %reshape.149 = bf16[4,256,2304]{2,1,0:T(8,128)(2,1)} reshape(bf16[4,8,32,4,576]{4,3,2,1,0:T(4,128)(2,1)} %copy.52) | data formatting | bytes 9437184 | tf_op jit(solution)/shard_map/reshape | solution.py:160
  192.5 10.6 %fusion.34 = bf16[256,1024]{1,0:T(8,128)(2,1)S(1)} fusion(bf16[1,4,1024,2304]{3,2,1,0:T(8,128)(2,1)} %param.10, bf16[4,256,2304]{2,1,0:T(8,128)(2,1)} %reshape.149, pred[4]{0:T(512)(128)(4,1)S(1)} %copy-done.14, f32[32,8,8,128]{3,2,1,0:T(8,128)S(1)} %bitcast.160), kind=kOutput, calls=%fused_computation.33 | convolution fusion | flops 4834721792 | bytes 25165828 | tf_op jit(solution)/shard_map/ltd,lfd->tf/dot_general | solution.py:163
  203.2 1.5 fusion.50
  204.7 2.2 slice_bitcast_fusion.4
  206.9 2.9 %copy.53 = f32[2,2,2,64,576]{4,3,2,1,0:T(8,128)} copy(f32[2,2,2,64,576]{3,4,0,2,1:T(8,128)} %get-tuple-element.6) | data formatting | bytes 2359296 | tf_op jit(solution)/shard_map/transpose | solution.py:61
  209.8 2.0 constant_dynamic-slice_fusion.5
  212.2 1.8 copy.54
  214.0 2.1 constant_dynamic-slice_fusion.2
  216.9 1.2 dynamic-slice_add_fusion.7
  218.1 1.6 collective-permute-start.37
  219.9 8.3 %collective-permute-done.37 = f32[2,64,576]{2,1,0:T(8,128)S(1)} collective-permute-done((f32[2,64,576]{2,1,0:T(8,128)S(1)}, f32[2,64,576]{2,1,0:T(8,128)S(1)}, u32[]{:S(2)}, u32[]{:S(2)}) %collective-permute-start.37) | collective-permute-done | bytes 294944 | tf_op jit(solution)/shard_map/ppermute | solution.py:70
  230.3 3.7 %collective-permute-done.38 = f32[1,64,576]{2,1,0:T(8,128)S(1)} collective-permute-done((f32[1,64,576]{2,1,0:T(8,128)S(1)}, f32[1,64,576]{2,1,0:T(8,128)S(1)}, u32[]{:S(2)}, u32[]{:S(2)}) %collective-permute-start.38) | collective-permute-done | bytes 147488 | tf_op jit(solution)/shard_map/ppermute | solution.py:70
  234.0 1.1 collective-permute-done.41
  (154 shorter events, 23.7 us)
Async XLA Ops:
  1.9 5.5 %collective-permute-start = (bf16[1,64,576]{2,1,0:T(8,128)(2,1)S(1)}, bf16[1,64,576]{2,1,0:T(8,128)(2,1)S(1)}, u32[]{:S(2)}, u32[]{:S(2)}) collective-permute-start(bf16[1,64,576]{2,1,0:T(8,128)(2,1)S(1)} %copy.57), channel_id=1, source_target_pairs={{0,2},{1,3},{2,0},{3,1},{4,6},{5,7},{6,4},{7,5},{8,10},{9,11},{10,... | collective-permute-start | bytes 221192 | tf_op jit(solution)/shard_map/ppermute | solution.py:92
  5.1 4.7 %collective-permute-start.3 = (bf16[1,64,576]{2,1,0:T(8,128)(2,1)S(1)}, bf16[1,64,576]{2,1,0:T(8,128)(2,1)S(1)}, u32[]{:S(2)}, u32[]{:S(2)}) collective-permute-start(bf16[1,64,576]{2,1,0:T(8,128)(2,1)S(1)} %copy.58), channel_id=1, source_target_pairs={{0,4},{4,0},{1,5},{5,1},{2,6},{6,2},{3,7},{7,3},{8,12},{12,8},{9,1... | collective-permute-start | bytes 221192 | tf_op jit(solution)/shard_map/ppermute | solution.py:92
  7.4 5.7 %collective-permute-start.1 = (bf16[2,64,576]{2,1,0:T(8,128)(2,1)S(1)}, bf16[2,64,576]{2,1,0:T(8,128)(2,1)S(1)}, u32[]{:S(2)}, u32[]{:S(2)}) collective-permute-start(bf16[2,64,576]{2,1,0:T(8,128)(2,1)S(1)} %maximum_select_fusion.16), channel_id=1, source_target_pairs={{0,4},{4,0},{1,5},{5,1},{2,6},{6,2},{3,7},{7,3},{8,12},{12,8},{9,1... | collective-permute-start | bytes 442376 | tf_op jit(solution)/shard_map/ppermute | solution.py:92
  9.9 5.4 %collective-permute-start.4 = (bf16[2,64,576]{2,1,0:T(8,128)(2,1)S(1)}, bf16[2,64,576]{2,1,0:T(8,128)(2,1)S(1)}, u32[]{:S(2)}, u32[]{:S(2)}) collective-permute-start(bf16[2,64,576]{2,1,0:T(8,128)(2,1)S(1)} %maximum_select_fusion.17), channel_id=1, source_target_pairs={{0,2},{1,3},{2,0},{3,1},{4,6},{5,7},{6,4},{7,5},{8,10},{9,11},{10,... | collective-permute-start | bytes 442376 | tf_op jit(solution)/shard_map/ppermute | solution.py:92
  13.2 7.5 %collective-permute-start.2 = (bf16[4,64,576]{2,1,0:T(8,128)(2,1)S(1)}, bf16[4,64,576]{2,1,0:T(8,128)(2,1)S(1)}, u32[]{:S(2)}, u32[]{:S(2)}) collective-permute-start(bf16[4,64,576]{2,1,0:T(8,128)(2,1)S(1)} %maximum_select_fusion.11), channel_id=1, source_target_pairs={{0,1},{1,0},{2,3},{3,2},{4,5},{5,4},{6,7},{7,6},{8,9},{9,8},{10,11... | collective-permute-start | bytes 884744 | tf_op jit(solution)/shard_map/ppermute | solution.py:92
  15.3 5.6 %collective-permute-start.5 = (bf16[4,64,576]{2,1,0:T(8,128)(2,1)S(1)}, bf16[4,64,576]{2,1,0:T(8,128)(2,1)S(1)}, u32[]{:S(2)}, u32[]{:S(2)}) collective-permute-start(bf16[4,64,576]{2,1,0:T(8,128)(2,1)S(1)} %maximum_select_fusion.12), channel_id=1, source_target_pairs={{0,1},{1,0},{2,3},{3,2},{4,5},{5,4},{6,7},{7,6},{8,9},{9,8},{10,11... | collective-permute-start | bytes 884744 | tf_op jit(solution)/shard_map/ppermute | solution.py:92
  20.6 1.7 copy-start.11
  20.7 5.5 %copy-start.13 = (pred[4]{0:T(512)(128)(4,1)}, pred[4]{0:T(512)(128)(4,1)S(1)}, u32[]{:S(2)}) copy-start(pred[4]{0:T(512)(128)(4,1)S(1)} %iota_compare_fusion.8) | copy-start | bytes 16
  21.2 1.2 copy-start.10
  59.8 2.2 copy-start.2
  62.0 5.2 %collective-permute-start.16 = (f32[16,40,576]{2,1,0:T(8,128)}, f32[16,40,576]{2,1,0:T(8,128)}, u32[]{:S(2)}, u32[]{:S(2)}) collective-permute-start(f32[16,40,576]{2,1,0:T(8,128)} %constant_dynamic-slice_fusion.10), channel_id=1, source_target_pairs={{0,1},{1,0},{2,3},{3,2},{4,5},{5,4},{6,7},{7,6},{8,9},{9,8},{10,11... | collective-permute-start | bytes 4423688 | tf_op jit(solution)/shard_map/ppermute | solution.py:70
  63.2 2.4 %copy-start = (f32[2,2,2,2,2,48,576]{6,5,4,3,2,1,0:T(8,128)}, f32[2,2,2,2,2,48,576]{6,5,4,3,2,1,0:T(8,128)S(1)}, u32[]{:S(2)}) copy-start(f32[2,2,2,2,2,48,576]{6,5,4,3,2,1,0:T(8,128)S(1)} %copy.46) | copy-start | bytes 10616836
  65.1 5.4 %collective-permute-start.11 = (f32[16,40,576]{2,1,0:T(8,128)}, f32[16,40,576]{2,1,0:T(8,128)}, u32[]{:S(2)}, u32[]{:S(2)}) collective-permute-start(f32[16,40,576]{2,1,0:T(8,128)} %constant_dynamic-slice_fusion.15), channel_id=1, source_target_pairs={{0,1},{1,0},{2,3},{3,2},{4,5},{5,4},{6,7},{7,6},{8,9},{9,8},{10,11... | collective-permute-start | bytes 4423688 | tf_op jit(solution)/shard_map/ppermute | solution.py:70
  67.0 6.0 %collective-permute-start.6 = (f32[16,48,576]{2,1,0:T(8,128)}, f32[16,48,576]{2,1,0:T(8,128)}, u32[]{:S(2)}, u32[]{:S(2)}) collective-permute-start(f32[16,48,576]{2,1,0:T(8,128)} %constant_dynamic-slice_fusion.20), channel_id=1, source_target_pairs={{0,1},{1,0},{2,3},{3,2},{4,5},{5,4},{6,7},{7,6},{8,9},{9,8},{10,11... | collective-permute-start | bytes 5308424 | tf_op jit(solution)/shard_map/ppermute | solution.py:70
  69.3 20.6 %collective-permute-start.17 = (f32[8,40,576]{2,1,0:T(8,128)S(1)}, f32[8,40,576]{2,1,0:T(8,128)S(1)}, u32[]{:S(2)}, u32[]{:S(2)}) collective-permute-start(f32[8,40,576]{2,1,0:T(8,128)S(1)} %constant_dynamic-slice_fusion.9), channel_id=1, source_target_pairs={{0,2},{1,3},{2,0},{3,1},{4,6},{5,7},{6,4},{7,5},{8,10},{9,11},{10,... | collective-permute-start | bytes 2211848 | tf_op jit(solution)/shard_map/ppermute | solution.py:70
  70.5 2.6 %copy-start.1 = (f32[2,2,2,2,2,48,576]{6,5,4,3,2,1,0:T(8,128)S(1)}, f32[2,2,2,2,2,48,576]{6,5,4,3,2,1,0:T(8,128)}, u32[]{:S(2)}) copy-start(f32[2,2,2,2,2,48,576]{6,5,4,3,2,1,0:T(8,128)} %copy-done) | copy-start | bytes 10616836
  72.4 20.4 %collective-permute-start.12 = (f32[8,40,576]{2,1,0:T(8,128)S(1)}, f32[8,40,576]{2,1,0:T(8,128)S(1)}, u32[]{:S(2)}, u32[]{:S(2)}) collective-permute-start(f32[8,40,576]{2,1,0:T(8,128)S(1)} %constant_dynamic-slice_fusion.14), channel_id=1, source_target_pairs={{0,4},{4,0},{1,5},{5,1},{2,6},{6,2},{3,7},{7,3},{8,12},{12,8},{9,1... | collective-permute-start | bytes 2211848 | tf_op jit(solution)/shard_map/ppermute | solution.py:70
  76.0 36.8 %collective-permute-start.7 = (f32[8,48,576]{2,1,0:T(8,128)}, f32[8,48,576]{2,1,0:T(8,128)}, u32[]{:S(2)}, u32[]{:S(2)}) collective-permute-start(f32[8,48,576]{2,1,0:T(8,128)} %constant_dynamic-slice_fusion.19), channel_id=1, source_target_pairs={{0,8},{8,0},{16,24},{24,16},{1,9},{9,1},{17,25},{25,17},{2,10},{10... | collective-permute-start | bytes 2654216 | tf_op jit(solution)/shard_map/ppermute | solution.py:70
  90.0 5.4 %copy-start.8 = (bf16[4,32,576]{2,1,0:T(8,128)(2,1)S(1)}, bf16[4,32,576]{2,1,0:T(8,128)(2,1)}, u32[]{:S(2)}) copy-start(bf16[4,32,576]{2,1,0:T(8,128)(2,1)} %param.13) | copy-start | bytes 442372
  90.8 18.0 %collective-permute-start.18 = (f32[4,40,576]{2,1,0:T(8,128)}, f32[4,40,576]{2,1,0:T(8,128)S(1)}, u32[]{:S(2)}, u32[]{:S(2)}) collective-permute-start(f32[4,40,576]{2,1,0:T(8,128)} %constant_dynamic-slice_fusion.8), channel_id=1, source_target_pairs={{0,8},{8,0},{16,24},{24,16},{1,9},{9,1},{17,25},{25,17},{2,10},{10... | collective-permute-start | bytes 1105928 | tf_op jit(solution)/shard_map/ppermute | solution.py:70
  92.8 0.9 copy-start.5
  94.5 15.5 %collective-permute-start.13 = (f32[4,40,576]{2,1,0:T(8,128)}, f32[4,40,576]{2,1,0:T(8,128)}, u32[]{:S(2)}, u32[]{:S(2)}) collective-permute-start(f32[4,40,576]{2,1,0:T(8,128)} %constant_dynamic-slice_fusion.13), channel_id=1, source_target_pairs={{0,2},{1,3},{2,0},{3,1},{4,6},{5,7},{6,4},{7,5},{8,10},{9,11},{10,... | collective-permute-start | bytes 1105928 | tf_op jit(solution)/shard_map/ppermute | solution.py:70
  108.9 6.4 %collective-permute-start.19 = (f32[2,40,576]{2,1,0:T(8,128)S(1)}, f32[2,40,576]{2,1,0:T(8,128)S(1)}, u32[]{:S(2)}, u32[]{:S(2)}) collective-permute-start(f32[2,40,576]{2,1,0:T(8,128)S(1)} %constant_dynamic-slice_fusion.7), channel_id=1, source_target_pairs={{0,4},{4,0},{1,5},{5,1},{2,6},{6,2},{3,7},{7,3},{8,12},{12,8},{9,1... | collective-permute-start | bytes 552968 | tf_op jit(solution)/shard_map/ppermute | solution.py:70
  111.2 6.8 %collective-permute-start.14 = (f32[2,40,576]{2,1,0:T(8,128)S(1)}, f32[2,40,576]{2,1,0:T(8,128)S(1)}, u32[]{:S(2)}, u32[]{:S(2)}) collective-permute-start(f32[2,40,576]{2,1,0:T(8,128)S(1)} %constant_dynamic-slice_fusion.12), channel_id=1, source_target_pairs={{0,8},{8,0},{16,24},{24,16},{1,9},{9,1},{17,25},{25,17},{2,10},{10... | collective-permute-start | bytes 552968 | tf_op jit(solution)/shard_map/ppermute | solution.py:70
  114.2 13.5 %copy-start.9 = (f32[4,576]{1,0:T(4,128)S(1)}, f32[4,576]{1,0:T(4,128)}, u32[]{:S(2)}) copy-start(f32[4,576]{1,0:T(4,128)} %param.11) | copy-start | bytes 27652
  114.2 11.6 %collective-permute-start.8 = (f32[4,48,576]{2,1,0:T(8,128)S(1)}, f32[4,48,576]{2,1,0:T(8,128)S(1)}, u32[]{:S(2)}, u32[]{:S(2)}) collective-permute-start(f32[4,48,576]{2,1,0:T(8,128)S(1)} %constant_dynamic-slice_fusion.18), channel_id=1, source_target_pairs={{0,4},{4,0},{1,5},{5,1},{2,6},{6,2},{3,7},{7,3},{8,12},{12,8},{9,1... | collective-permute-start | bytes 1327112 | tf_op jit(solution)/shard_map/ppermute | solution.py:70
  115.4 12.4 %collective-permute-start.20 = (f32[1,40,576]{2,1,0:T(8,128)S(1)}, f32[1,40,576]{2,1,0:T(8,128)S(1)}, u32[]{:S(2)}, u32[]{:S(2)}) collective-permute-start(f32[1,40,576]{2,1,0:T(8,128)S(1)} %constant_dynamic-slice_fusion.6), channel_id=1, source_target_pairs={{0,16},{8,24},{16,0},{24,8},{1,17},{9,25},{17,1},{25,9},{2,18},{10... | collective-permute-start | bytes 276488 | tf_op jit(solution)/shard_map/ppermute | solution.py:70
  118.1 9.7 %collective-permute-start.15 = (f32[1,40,576]{2,1,0:T(8,128)S(1)}, f32[1,40,576]{2,1,0:T(8,128)S(1)}, u32[]{:S(2)}, u32[]{:S(2)}) collective-permute-start(f32[1,40,576]{2,1,0:T(8,128)S(1)} %constant_dynamic-slice_fusion.11), channel_id=1, source_target_pairs={{0,16},{8,24},{16,0},{24,8},{1,17},{9,25},{17,1},{25,9},{2,18},{10... | collective-permute-start | bytes 276488 | tf_op jit(solution)/shard_map/ppermute | solution.py:70
  126.0 8.7 %collective-permute-start.9 = (f32[2,48,576]{2,1,0:T(8,128)S(1)}, f32[2,48,576]{2,1,0:T(8,128)S(1)}, u32[]{:S(2)}, u32[]{:S(2)}) collective-permute-start(f32[2,48,576]{2,1,0:T(8,128)S(1)} %constant_dynamic-slice_fusion.17), channel_id=1, source_target_pairs={{0,2},{1,3},{2,0},{3,1},{4,6},{5,7},{6,4},{7,5},{8,10},{9,11},{10,... | collective-permute-start | bytes 663560 | tf_op jit(solution)/shard_map/ppermute | solution.py:70
  127.9 28.3 %copy-start.6 = (bf16[40,576]{1,0:T(8,128)(2,1)}, bf16[40,576]{1,0:T(8,128)(2,1)S(1)}, u32[]{:S(2)}) copy-start(bf16[40,576]{1,0:T(8,128)(2,1)S(1)} %get-tuple-element.9) | copy-start | bytes 138244
  127.9 6.2 %collective-permute-start.26 = (bf16[1,40,576]{2,1,0:T(8,128)(2,1)S(1)}, bf16[1,40,576]{2,1,0:T(8,128)(2,1)S(1)}, u32[]{:S(2)}, u32[]{:S(2)}) collective-permute-start(bf16[1,40,576]{2,1,0:T(8,128)(2,1)S(1)} %bitcast.150), channel_id=1, source_target_pairs={{0,16},{8,24},{16,0},{24,8},{1,17},{9,25},{17,1},{25,9},{2,18},{10... | collective-permute-start | bytes 138248 | tf_op jit(solution)/shard_map/ppermute | solution.py:92
  130.5 6.2 %collective-permute-start.31 = (bf16[1,40,576]{2,1,0:T(8,128)(2,1)S(1)}, bf16[1,40,576]{2,1,0:T(8,128)(2,1)S(1)}, u32[]{:S(2)}, u32[]{:S(2)}) collective-permute-start(bf16[1,40,576]{2,1,0:T(8,128)(2,1)S(1)} %bitcast.152), channel_id=1, source_target_pairs={{0,16},{8,24},{16,0},{24,8},{1,17},{9,25},{17,1},{25,9},{2,18},{10... | collective-permute-start | bytes 138248 | tf_op jit(solution)/shard_map/ppermute | solution.py:92
  134.1 8.8 %collective-permute-start.27 = (bf16[2,40,576]{2,1,0:T(8,128)(2,1)S(1)}, bf16[2,40,576]{2,1,0:T(8,128)(2,1)S(1)}, u32[]{:S(2)}, u32[]{:S(2)}) collective-permute-start(bf16[2,40,576]{2,1,0:T(8,128)(2,1)S(1)} %maximum_select_fusion.19), channel_id=1, source_target_pairs={{0,8},{8,0},{16,24},{24,16},{1,9},{9,1},{17,25},{25,17},{2,10},{10... | collective-permute-start | bytes 276488 | tf_op jit(solution)/shard_map/ppermute | solution.py:92
  134.7 8.1 %collective-permute-start.10 = (f32[1,48,576]{2,1,0:T(8,128)S(1)}, f32[1,48,576]{2,1,0:T(8,128)S(1)}, u32[]{:S(2)}, u32[]{:S(2)}) collective-permute-start(f32[1,48,576]{2,1,0:T(8,128)S(1)} %constant_dynamic-slice_fusion.16), channel_id=1, source_target_pairs={{0,16},{8,24},{16,0},{24,8},{1,17},{9,25},{17,1},{25,9},{2,18},{10... | collective-permute-start | bytes 331784 | tf_op jit(solution)/shard_map/ppermute | solution.py:70
  136.8 12.5 %collective-permute-start.32 = (bf16[2,40,576]{2,1,0:T(8,128)(2,1)S(1)}, bf16[2,40,576]{2,1,0:T(8,128)(2,1)S(1)}, u32[]{:S(2)}, u32[]{:S(2)}) collective-permute-start(bf16[2,40,576]{2,1,0:T(8,128)(2,1)S(1)} %maximum_select_fusion.20), channel_id=1, source_target_pairs={{0,4},{4,0},{1,5},{5,1},{2,6},{6,2},{3,7},{7,3},{8,12},{12,8},{9,1... | collective-permute-start | bytes 276488 | tf_op jit(solution)/shard_map/ppermute | solution.py:92
  142.8 5.5 %collective-permute-start.21 = (bf16[1,48,576]{2,1,0:T(8,128)(2,1)S(1)}, bf16[1,48,576]{2,1,0:T(8,128)(2,1)S(1)}, u32[]{:S(2)}, u32[]{:S(2)}) collective-permute-start(bf16[1,48,576]{2,1,0:T(8,128)(2,1)S(1)} %bitcast.148), channel_id=1, source_target_pairs={{0,16},{8,24},{16,0},{24,8},{1,17},{9,25},{17,1},{25,9},{2,18},{10... | collective-permute-start | bytes 165896 | tf_op jit(solution)/shard_map/ppermute | solution.py:92
  143.0 13.1 %collective-permute-start.28 = (bf16[4,40,576]{2,1,0:T(8,128)(2,1)S(1)}, bf16[4,40,576]{2,1,0:T(8,128)(2,1)S(1)}, u32[]{:S(2)}, u32[]{:S(2)}) collective-permute-start(bf16[4,40,576]{2,1,0:T(8,128)(2,1)S(1)} %maximum_select_fusion.14), channel_id=1, source_target_pairs={{0,2},{1,3},{2,0},{3,1},{4,6},{5,7},{6,4},{7,5},{8,10},{9,11},{10,... | collective-permute-start | bytes 552968 | tf_op jit(solution)/shard_map/ppermute | solution.py:92
  148.3 6.1 %collective-permute-start.22 = (bf16[2,48,576]{2,1,0:T(8,128)(2,1)S(1)}, bf16[2,48,576]{2,1,0:T(8,128)(2,1)S(1)}, u32[]{:S(2)}, u32[]{:S(2)}) collective-permute-start(bf16[2,48,576]{2,1,0:T(8,128)(2,1)S(1)} %maximum_select_fusion.18), channel_id=1, source_target_pairs={{0,2},{1,3},{2,0},{3,1},{4,6},{5,7},{6,4},{7,5},{8,10},{9,11},{10,... | collective-permute-start | bytes 331784 | tf_op jit(solution)/shard_map/ppermute | solution.py:92
  149.3 7.4 %collective-permute-start.33 = (bf16[4,40,576]{2,1,0:T(8,128)(2,1)S(1)}, bf16[4,40,576]{2,1,0:T(8,128)(2,1)S(1)}, u32[]{:S(2)}, u32[]{:S(2)}) collective-permute-start(bf16[4,40,576]{2,1,0:T(8,128)(2,1)S(1)} %maximum_select_fusion.15), channel_id=1, source_target_pairs={{0,8},{8,0},{16,24},{24,16},{1,9},{9,1},{17,25},{25,17},{2,10},{10... | collective-permute-start | bytes 552968 | tf_op jit(solution)/shard_map/ppermute | solution.py:92
  154.4 6.3 %collective-permute-start.23 = (bf16[4,48,576]{2,1,0:T(8,128)(2,1)S(1)}, bf16[4,48,576]{2,1,0:T(8,128)(2,1)S(1)}, u32[]{:S(2)}, u32[]{:S(2)}) collective-permute-start(bf16[4,48,576]{2,1,0:T(8,128)(2,1)S(1)} %maximum_select_fusion.13), channel_id=1, source_target_pairs={{0,4},{4,0},{1,5},{5,1},{2,6},{6,2},{3,7},{7,3},{8,12},{12,8},{9,1... | collective-permute-start | bytes 663560 | tf_op jit(solution)/shard_map/ppermute | solution.py:92
  156.1 9.0 %collective-permute-start.29 = (bf16[8,40,576]{2,1,0:T(8,128)(2,1)S(1)}, bf16[8,40,576]{2,1,0:T(8,128)(2,1)S(1)}, u32[]{:S(2)}, u32[]{:S(2)}) collective-permute-start(bf16[8,40,576]{2,1,0:T(8,128)(2,1)S(1)} %maximum_select_fusion.9), channel_id=1, source_target_pairs={{0,4},{4,0},{1,5},{5,1},{2,6},{6,2},{3,7},{7,3},{8,12},{12,8},{9,1... | collective-permute-start | bytes 1105928 | tf_op jit(solution)/shard_map/ppermute | solution.py:92
  156.9 8.6 %collective-permute-start.34 = (bf16[8,40,576]{2,1,0:T(8,128)(2,1)S(1)}, bf16[8,40,576]{2,1,0:T(8,128)(2,1)S(1)}, u32[]{:S(2)}, u32[]{:S(2)}) collective-permute-start(bf16[8,40,576]{2,1,0:T(8,128)(2,1)S(1)} %maximum_select_fusion.10), channel_id=1, source_target_pairs={{0,2},{1,3},{2,0},{3,1},{4,6},{5,7},{6,4},{7,5},{8,10},{9,11},{10,... | collective-permute-start | bytes 1105928 | tf_op jit(solution)/shard_map/ppermute | solution.py:92
  160.8 8.9 %collective-permute-start.24 = (bf16[8,48,576]{2,1,0:T(8,128)(2,1)S(1)}, bf16[8,48,576]{2,1,0:T(8,128)(2,1)S(1)}, u32[]{:S(2)}, u32[]{:S(2)}) collective-permute-start(bf16[8,48,576]{2,1,0:T(8,128)(2,1)S(1)} %maximum_select_fusion.8), channel_id=1, source_target_pairs={{0,8},{8,0},{16,24},{24,16},{1,9},{9,1},{17,25},{25,17},{2,10},{10... | collective-permute-start | bytes 1327112 | tf_op jit(solution)/shard_map/ppermute | solution.py:92
  165.3 4.8 %collective-permute-start.30 = (bf16[16,40,576]{2,1,0:T(8,128)(2,1)S(1)}, bf16[16,40,576]{2,1,0:T(8,128)(2,1)S(1)}, u32[]{:S(2)}, u32[]{:S(2)}) collective-permute-start(bf16[16,40,576]{2,1,0:T(8,128)(2,1)S(1)} %maximum_select_fusion.4), channel_id=1, source_target_pairs={{0,1},{1,0},{2,3},{3,2},{4,5},{5,4},{6,7},{7,6},{8,9},{9,8},{10,11... | collective-permute-start | bytes 2211848 | tf_op jit(solution)/shard_map/ppermute | solution.py:92
  165.6 5.0 %collective-permute-start.35 = (bf16[16,40,576]{2,1,0:T(8,128)(2,1)S(1)}, bf16[16,40,576]{2,1,0:T(8,128)(2,1)}, u32[]{:S(2)}, u32[]{:S(2)}) collective-permute-start(bf16[16,40,576]{2,1,0:T(8,128)(2,1)S(1)} %maximum_select_fusion.5), channel_id=1, source_target_pairs={{0,1},{1,0},{2,3},{3,2},{4,5},{5,4},{6,7},{7,6},{8,9},{9,8},{10,11... | collective-permute-start | bytes 2211848 | tf_op jit(solution)/shard_map/ppermute | solution.py:92
  170.0 2.8 %collective-permute-start.25 = (bf16[16,48,576]{2,1,0:T(8,128)(2,1)S(1)}, bf16[16,48,576]{2,1,0:T(8,128)(2,1)}, u32[]{:S(2)}, u32[]{:S(2)}) collective-permute-start(bf16[16,48,576]{2,1,0:T(8,128)(2,1)S(1)} %maximum_select_fusion.3), channel_id=1, source_target_pairs={{0,1},{1,0},{2,3},{3,2},{4,5},{5,4},{6,7},{7,6},{8,9},{9,8},{10,11... | collective-permute-start | bytes 2654216 | tf_op jit(solution)/shard_map/ppermute | solution.py:92
  182.6 10.0 %copy-start.12 = (f32[256,8,128]{2,1,0:T(8,128)S(1)}, f32[256,8,128]{2,1,0:T(8,128)}, u32[]{:S(2)}) copy-start(f32[256,8,128]{2,1,0:T(8,128)} %copy-done.11) | copy-start | bytes 3145732
  182.6 10.0 %copy-start.14 = (pred[4]{0:T(512)(128)(4,1)S(1)}, pred[4]{0:T(512)(128)(4,1)}, u32[]{:S(2)}) copy-start(pred[4]{0:T(512)(128)(4,1)} %copy-done.13) | copy-start | bytes 16
  182.6 20.6 %slice-start = ((s8[4718592]{0:T(1024)(128)(4,1)}), s8[524288]{0:T(1024)(128)(4,1)S(1)}, s32[]{:S(2)}) async-start(s8[4718592]{0:T(1024)(128)(4,1)} %bitcast.155), calls=%async_computation | async-start | bytes 1048576
  192.5 10.6 %slice-start.1 = ((s8[4718592]{0:T(1024)(128)(4,1)}), s8[4194304]{0:T(1024)(128)(4,1)S(1)}, s32[]{:S(2)}) async-start(s8[4718592]{0:T(1024)(128)(4,1)} %bitcast.155), calls=%async_computation.1 | async-start | bytes 8388608
  211.8 5.1 %collective-permute-start.36 = (f32[4,64,576]{2,1,0:T(8,128)}, f32[4,64,576]{2,1,0:T(8,128)}, u32[]{:S(2)}, u32[]{:S(2)}) collective-permute-start(f32[4,64,576]{2,1,0:T(8,128)} %constant_dynamic-slice_fusion.5), channel_id=1, source_target_pairs={{0,1},{1,0},{2,3},{3,2},{4,5},{5,4},{6,7},{7,6},{8,9},{9,8},{10,11... | collective-permute-start | bytes 1769480 | tf_op jit(solution)/shard_map/ppermute | solution.py:70
  212.2 4.1 %copy-start.7 = (bf16[40,576]{1,0:T(8,128)(2,1)S(1)}, bf16[40,576]{1,0:T(8,128)(2,1)}, u32[]{:S(2)}) copy-start(bf16[40,576]{1,0:T(8,128)(2,1)} %copy-done.6) | copy-start | bytes 138244
  214.0 3.0 %copy-start.4 = (f32[2,2,2,64,576]{4,3,2,1,0:T(8,128)S(1)}, f32[2,2,2,64,576]{4,3,2,1,0:T(8,128)}, u32[]{:S(2)}) copy-start(f32[2,2,2,64,576]{4,3,2,1,0:T(8,128)} %copy.53) | copy-start | bytes 3538948
  214.0 5.7 %copy-start.3 = (f32[2,2,2,64,576]{4,3,2,1,0:T(8,128)S(1)}, f32[2,2,2,64,576]{4,3,2,1,0:T(8,128)}, u32[]{:S(2)}) copy-start(f32[2,2,2,64,576]{4,3,2,1,0:T(8,128)} %copy.54) | copy-start | bytes 3538948
  216.1 3.6 %collective-permute-start.39 = (f32[4,64,576]{2,1,0:T(8,128)}, f32[4,64,576]{2,1,0:T(8,128)S(1)}, u32[]{:S(2)}, u32[]{:S(2)}) collective-permute-start(f32[4,64,576]{2,1,0:T(8,128)} %constant_dynamic-slice_fusion.2), channel_id=1, source_target_pairs={{0,1},{1,0},{2,3},{3,2},{4,5},{5,4},{6,7},{7,6},{8,9},{9,8},{10,11... | collective-permute-start | bytes 1769480 | tf_op jit(solution)/shard_map/ppermute | solution.py:70
  218.1 10.1 %collective-permute-start.37 = (f32[2,64,576]{2,1,0:T(8,128)S(1)}, f32[2,64,576]{2,1,0:T(8,128)S(1)}, u32[]{:S(2)}, u32[]{:S(2)}) collective-permute-start(f32[2,64,576]{2,1,0:T(8,128)S(1)} %constant_dynamic-slice_fusion.4), channel_id=1, source_target_pairs={{0,4},{4,0},{1,5},{5,1},{2,6},{6,2},{3,7},{7,3},{8,12},{12,8},{9,1... | collective-permute-start | bytes 884744 | tf_op jit(solution)/shard_map/ppermute | solution.py:70
  219.8 9.8 %collective-permute-start.40 = (f32[2,64,576]{2,1,0:T(8,128)S(1)}, f32[2,64,576]{2,1,0:T(8,128)S(1)}, u32[]{:S(2)}, u32[]{:S(2)}) collective-permute-start(f32[2,64,576]{2,1,0:T(8,128)S(1)} %constant_dynamic-slice_fusion.1), channel_id=1, source_target_pairs={{0,2},{1,3},{2,0},{3,1},{4,6},{5,7},{6,4},{7,5},{8,10},{9,11},{10,... | collective-permute-start | bytes 884744 | tf_op jit(solution)/shard_map/ppermute | solution.py:70
  228.3 5.7 %collective-permute-start.38 = (f32[1,64,576]{2,1,0:T(8,128)S(1)}, f32[1,64,576]{2,1,0:T(8,128)S(1)}, u32[]{:S(2)}, u32[]{:S(2)}) collective-permute-start(f32[1,64,576]{2,1,0:T(8,128)S(1)} %constant_dynamic-slice_fusion.3), channel_id=1, source_target_pairs={{0,2},{1,3},{2,0},{3,1},{4,6},{5,7},{6,4},{7,5},{8,10},{9,11},{10,... | collective-permute-start | bytes 442376 | tf_op jit(solution)/shard_map/ppermute | solution.py:70
  229.7 5.4 %collective-permute-start.41 = (f32[1,64,576]{2,1,0:T(8,128)S(1)}, f32[1,64,576]{2,1,0:T(8,128)S(1)}, u32[]{:S(2)}, u32[]{:S(2)}) collective-permute-start(f32[1,64,576]{2,1,0:T(8,128)S(1)} %constant_dynamic-slice_fusion), channel_id=1, source_target_pairs={{0,4},{4,0},{1,5},{5,1},{2,6},{6,2},{3,7},{7,3},{8,12},{12,8},{9,1... | collective-permute-start | bytes 442376 | tf_op jit(solution)/shard_map/ppermute | solution.py:70
